TPU v7x, 32 devices: a whole 2x2x4 slice. The times are simulated.
32 devices in a mesh: outer: 4 (over y, core), inner: 8 (over z, x).
Axes of the slice: x: 2, y: 2, z: 4, core: 2. Of those that a mesh axis runs over, the one named last changes fastest.
Arguments:
- queries: bfloat16 [4, 8, 8, 64, 512], P('outer', None, 'inner'), may hold values from -240 to 240
- keys: bfloat16 [4, 8, 8, 64, 128], P('outer', None, 'inner'), may hold values from -6 to 6
- values: bfloat16 [4, 8, 8, 64, 128], P('outer', None, 'inner'), may hold values from -6 to 6
- grad_out: bfloat16 [4, 8, 8, 64, 512], P('outer', None, 'inner'), may hold values from -6 to 6
- doc_starts: int32 [4, 8, 4], replicated, may hold values from 0 to 512, as said below
Outputs:
- attn_out: bfloat16 [4, 8, 8, 64, 512], P('outer', None, 'inner')
- query_grads: bfloat16 [4, 8, 8, 64, 512], P('outer', None, 'inner')
- key_grads: bfloat16 [4, 8, 8, 64, 128], P('outer', None, 'inner')
- value_grads: bfloat16 [4, 8, 8, 64, 128], P('outer', None, 'inner')
Inputs may be any that keep to these rules, and one draw needn't show every extreme that they name: `doc_starts`: entry [o, u, j] is an offset within unit u of segment o at which a document starts, or 512 for none. The offsets below 512 of a unit are distinct, rise with j and stand before all its 512 entries. Offset 0 starts a document in every even unit except unit 0 of segments o > 0; unit 0 of such a segment and an odd unit may continue the document of the position before them (then their first entry is not 0). The last unit of every segment continues the one before it; position 0 of the sequence starts a document.
All inputs are finite; a program needn't handle non-finite values.
Results may differ from a plain program's by a relative error of at most 0.0075.
Values may be sent and summed in bfloat16 or wider, within the bound.
No kernel may reach another device: no remote copies, remote signals or barrier semaphores. Data moves between devices by JAX's collectives and lax.ppermute only.
A program may use at most 128 MiB of HBM per device.

v0:
```python
import math

import jax
import jax.numpy as jnp
from jax import lax
from jax.sharding import PartitionSpec as P


def passed_along(x, axis, by):
    size = lax.axis_size(axis)
    pairs = [(i, i + by) for i in range(size) if 0 <= i + by < size]
    return lax.ppermute(x, axis, pairs)


def doc_table(doc_starts, tok_dev):
    n_outer, n_inner, n_slots = doc_starts.shape
    flat_starts = doc_starts.reshape(n_outer * n_inner, n_slots)
    start_counts = jnp.sum((flat_starts < tok_dev).astype(jnp.int32), axis=1)
    first_index = jnp.cumsum(start_counts) - start_counts
    offsets = jnp.arange(tok_dev, dtype=jnp.int32)
    inside_count = jnp.sum(
        (flat_starts[:, None, :] <= offsets[None, :, None]).astype(jnp.int32), axis=2
    )
    return (first_index[:, None] + inside_count - 1).reshape(n_outer, n_inner, tok_dev)


def owner_table(doc_starts):
    n_outer, n_inner = (doc_starts.shape[0], doc_starts.shape[1])
    pairs = n_inner // 2
    joined = (doc_starts[:, 1::2, 0] != 0).astype(jnp.int32)
    pair_ids = jnp.arange(pairs, dtype=jnp.int32)
    relative = jnp.where(pair_ids == 0, 0, jnp.where(pair_ids == pairs - 1, 1, pair_ids + 1))
    pair_owner = (jnp.arange(n_outer, dtype=jnp.int32)[:, None] + relative[None, :]) % pairs
    even_owner = 2 * pair_owner
    owner = jnp.stack([even_owner, even_owner + 1 - joined], axis=2)
    return owner.reshape(n_outer, n_inner)


def slot_table(unit_owner):
    n_inner = unit_owner.shape[1]
    same_owner = unit_owner[:, :, None] == unit_owner[:, None, :]
    earlier = jnp.arange(n_inner)[None, :] < jnp.arange(n_inner)[:, None]
    return jnp.sum((same_owner & earlier[None]).astype(jnp.int32), axis=2)


def route_table(target_row, slot_row, slot_count):
    n_units = target_row.shape[0]
    unit_ids = jnp.arange(n_units, dtype=jnp.int32)
    tables = []
    for slot_id in range(slot_count):
        matched = (target_row[None, :] == unit_ids[:, None]) & (slot_row[None, :] == slot_id)
        present = jnp.any(matched, axis=1)
        chosen = jnp.sum(jnp.where(matched, unit_ids[None, :], 0), axis=1)
        tables.append(jnp.where(present, chosen, n_units))
    return jnp.stack(tables)


def pack_rows(piece_rows, index_table):
    padded = jnp.concatenate(
        [piece_rows, jnp.zeros((1,) + piece_rows.shape[1:], piece_rows.dtype)], axis=0
    )
    return padded[index_table]


def unpack(arrived, target_row, slot_row):
    n_slots, n_inner = (arrived.shape[0], arrived.shape[1])
    flat_rows = arrived.reshape((n_slots * n_inner,) + arrived.shape[2:])
    return flat_rows[slot_row * n_inner + target_row]


def holder_meta(owner_row, slot_row, docs_row, holder, seg_start, is_valid, missing):
    n_inner, tok_dev = docs_row.shape
    unit_ids = jnp.arange(n_inner, dtype=jnp.int32)
    offsets = jnp.arange(tok_dev, dtype=jnp.int32)
    places, labels = ([], [])
    for slot_id in range(2):
        matched = (owner_row == holder) & (slot_row == slot_id)
        unit_id = jnp.sum(jnp.where(matched, unit_ids, 0))
        present = jnp.any(matched) & is_valid
        places.append(seg_start + unit_id * tok_dev + offsets)
        labels.append(jnp.where(present, docs_row[unit_id], missing))
    return (jnp.concatenate(places), jnp.concatenate(labels))


def attend(
    query_buf, grad_buf, query_pos, query_doc, key_buf, value_buf, key_pos, key_doc, n_heads
):
    n_rows = query_buf.shape[0]
    head_dim = key_buf.shape[1]
    scaling = 1.0 / math.sqrt(head_dim)
    q_three = query_buf.reshape(n_rows, n_heads, head_dim)
    g_three = grad_buf.reshape(n_rows, n_heads, head_dim)
    scores = (
        jnp.einsum("qhd,kd->hqk", q_three, key_buf, preferred_element_type=jnp.float32) * scaling
    )
    allowed = (query_doc[:, None] == key_doc[None, :]) & (key_pos[None, :] <= query_pos[:, None])
    scores = jnp.where(allowed[None], scores, -jnp.inf)
    row_max = jnp.max(scores, axis=2, keepdims=True)
    log_total = row_max + jnp.log(jnp.sum(jnp.exp(scores - row_max), axis=2, keepdims=True))
    probs = jnp.exp(scores - log_total)
    probs_low = probs.astype(jnp.bfloat16)
    attn = jnp.einsum(
        "hqk,kd->qhd", probs_low, value_buf, preferred_element_type=jnp.float32
    ).astype(jnp.bfloat16)
    inner_prod = jnp.sum(g_three.astype(jnp.float32) * attn.astype(jnp.float32), axis=2)
    grad_probs = jnp.einsum("qhd,kd->hqk", g_three, value_buf, preferred_element_type=jnp.float32)
    score_grads = (probs * (grad_probs - inner_prod.T[:, :, None])).astype(jnp.bfloat16)
    q_grads = (
        jnp.einsum("hqk,kd->qhd", score_grads, key_buf, preferred_element_type=jnp.float32)
        * scaling
    )
    k_grads = (
        jnp.einsum("hqk,qhd->kd", score_grads, q_three, preferred_element_type=jnp.float32)
        * scaling
    )
    v_grads = jnp.einsum("hqk,qhd->kd", probs_low, g_three, preferred_element_type=jnp.float32)
    return (
        attn.reshape(n_rows, -1),
        q_grads.astype(jnp.bfloat16).reshape(n_rows, -1),
        k_grads,
        v_grads,
    )


def shards(queries, keys, values, grad_out, doc_starts):
    n_inner = lax.axis_size("inner")
    piece_len = queries.shape[3]
    width_q = queries.shape[4]
    head_dim = keys.shape[4]
    n_heads = width_q // head_dim
    tok_dev = piece_len * n_inner
    seg_len = tok_dev * n_inner
    outer_id = lax.axis_index("outer")
    inner_id = lax.axis_index("inner")
    unit_owner = owner_table(doc_starts)
    slot_all = slot_table(unit_owner)
    docs_all = doc_table(doc_starts, tok_dev)
    own_owner = unit_owner[outer_id]
    own_slot = slot_all[outer_id]
    own_docs = docs_all[outer_id]
    before = jnp.maximum(outer_id - 1, 0)
    prev_owner = unit_owner[before]
    prev_slot = slot_all[before]
    prev_docs = docs_all[before]
    has_before = outer_id > 0
    seg_start = outer_id * seg_len
    prev_start = before * seg_len
    query_rows = queries[0, :, 0]
    key_rows = keys[0, :, 0]
    value_rows = values[0, :, 0]
    grad_rows = grad_out[0, :, 0]
    hold_index = route_table(own_owner, own_slot, 2)
    q_in, k_in, v_in, g_in = (
        lax.all_to_all(
            pack_rows(query_rows, hold_index), "inner", split_axis=1, concat_axis=1, tiled=True
        ),
        lax.all_to_all(
            pack_rows(key_rows, hold_index), "inner", split_axis=1, concat_axis=1, tiled=True
        ),
        lax.all_to_all(
            pack_rows(value_rows, hold_index), "inner", split_axis=1, concat_axis=1, tiled=True
        ),
        lax.all_to_all(
            pack_rows(grad_rows, hold_index), "inner", split_axis=1, concat_axis=1, tiled=True
        ),
    )
    query_buf = q_in.reshape(2 * tok_dev, width_q)
    grad_buf = g_in.reshape(2 * tok_dev, width_q)
    key_buf = k_in.reshape(2 * tok_dev, head_dim)
    value_buf = v_in.reshape(2 * tok_dev, head_dim)
    prev_keys, prev_values = passed_along((key_buf, value_buf), "outer", 1)
    query_pos, query_doc = holder_meta(
        own_owner, own_slot, own_docs, inner_id, seg_start, outer_id >= 0, -1
    )
    ctx_keys = jnp.concatenate([key_buf, prev_keys])
    ctx_values = jnp.concatenate([value_buf, prev_values])
    own_pos, own_doc = holder_meta(
        own_owner, own_slot, own_docs, inner_id, seg_start, outer_id >= 0, -1
    )
    back_pos, back_doc = holder_meta(
        prev_owner, prev_slot, prev_docs, inner_id, prev_start, has_before, -2
    )
    key_pos = jnp.concatenate([own_pos, back_pos])
    key_doc = jnp.concatenate([own_doc, back_doc])
    attn, q_grads, k_grads, v_grads = attend(
        query_buf, grad_buf, query_pos, query_doc, ctx_keys, ctx_values, key_pos, key_doc, n_heads
    )
    later_kg, later_vg = passed_along((k_grads[2 * tok_dev :], v_grads[2 * tok_dev :]), "outer", -1)
    key_total = (
        (k_grads[: 2 * tok_dev] + later_kg)
        .astype(jnp.bfloat16)
        .reshape(2, n_inner, piece_len, head_dim)
    )
    value_total = (
        (v_grads[: 2 * tok_dev] + later_vg)
        .astype(jnp.bfloat16)
        .reshape(2, n_inner, piece_len, head_dim)
    )
    attn_back, qg_back, kg_back, vg_back = (
        lax.all_to_all(
            attn.reshape(2, n_inner, piece_len, width_q),
            "inner",
            split_axis=1,
            concat_axis=1,
            tiled=True,
        ),
        lax.all_to_all(
            q_grads.reshape(2, n_inner, piece_len, width_q),
            "inner",
            split_axis=1,
            concat_axis=1,
            tiled=True,
        ),
        lax.all_to_all(key_total, "inner", split_axis=1, concat_axis=1, tiled=True),
        lax.all_to_all(value_total, "inner", split_axis=1, concat_axis=1, tiled=True),
    )
    attn_rows = unpack(attn_back, own_owner, own_slot)
    qgrad_rows = unpack(qg_back, own_owner, own_slot)
    kgrad_rows = unpack(kg_back, own_owner, own_slot)
    vgrad_rows = unpack(vg_back, own_owner, own_slot)
    shape_q = (1, n_inner, 1, piece_len, width_q)
    shape_k = (1, n_inner, 1, piece_len, head_dim)
    return (
        attn_rows.reshape(shape_q),
        qgrad_rows.reshape(shape_q),
        kgrad_rows.reshape(shape_k),
        vgrad_rows.reshape(shape_k),
    )


def solution(mesh):
    return jax.shard_map(
        shards,
        mesh=mesh,
        in_specs=(
            P("outer", None, "inner", None, None),
            P("outer", None, "inner", None, None),
            P("outer", None, "inner", None, None),
            P("outer", None, "inner", None, None),
            P(),
        ),
        out_specs=(
            P("outer", None, "inner", None, None),
            P("outer", None, "inner", None, None),
            P("outer", None, "inner", None, None),
            P("outer", None, "inner", None, None),
        ),
        check_vma=False,
    )
```

profile of v0, /device:TPU:1, one launch (start us, length us, event | category | flops | bytes accessed | tf_op | source)
XLA Modules:
  0.0 294.7 jit_solution(16554586157267958369)
XLA Ops:
  5.2 6.3 %all-to-all-start.1 = ((bf16[2,8,64,128]{3,2,0,1:T(8,128)(2,1)}), bf16[2,8,64,128]{3,2,0,1:T(8,128)(2,1)S(1)}, u32[]{:S(2)}, u32[]{:S(2)}) async-start(bf16[2,8,64,128]{3,2,0,1:T(8,128)(2,1)} %copy.125), calls=%async_computation.1 | async-start | bytes 524288 | tf_op jit(solution)/shard_map/all_to_all | solution.py:157
  13.8 5.2 %all-to-all-done.1 = bf16[2,8,64,128]{3,2,0,1:T(8,128)(2,1)S(1)} async-done(((bf16[2,8,64,128]{3,2,0,1:T(8,128)(2,1)}), bf16[2,8,64,128]{3,2,0,1:T(8,128)(2,1)S(1)}, u32[]{:S(2)}, u32[]{:S(2)}) %all-to-all-start.1) | async-done | bytes 262176 | tf_op jit(solution)/shard_map/all_to_all | solution.py:157
  19.0 4.7 %all-to-all-start = ((bf16[2,8,64,128]{3,2,0,1:T(8,128)(2,1)}), bf16[2,8,64,128]{3,2,0,1:T(8,128)(2,1)S(1)}, u32[]{:S(2)}, u32[]{:S(2)}) async-start(bf16[2,8,64,128]{3,2,0,1:T(8,128)(2,1)} %copy.118), calls=%async_computation | async-start | bytes 524288 | tf_op jit(solution)/shard_map/all_to_all | solution.py:160
  23.7 1.1 concatenate.57
  25.5 1.1 copy.127
  26.6 4.3 %all-to-all-done = bf16[2,8,64,128]{3,2,0,1:T(8,128)(2,1)S(1)} async-done(((bf16[2,8,64,128]{3,2,0,1:T(8,128)(2,1)}), bf16[2,8,64,128]{3,2,0,1:T(8,128)(2,1)S(1)}, u32[]{:S(2)}, u32[]{:S(2)}) %all-to-all-start) | async-done | bytes 262176 | tf_op jit(solution)/shard_map/all_to_all | solution.py:160
  30.9 4.9 %all-to-all-start.2 = ((bf16[2,8,64,512]{3,2,0,1:T(8,128)(2,1)}), bf16[2,8,64,512]{3,2,0,1:T(8,128)(2,1)S(1)}, u32[]{:S(2)}, u32[]{:S(2)}) async-start(bf16[2,8,64,512]{3,2,0,1:T(8,128)(2,1)} %copy.127), calls=%async_computation.2 | async-start | bytes 2097152 | tf_op jit(solution)/shard_map/all_to_all | solution.py:154
  35.8 1.1 concatenate.58
  37.5 1.1 copy.134
  40.7 19.8 %all-to-all-done.2 = bf16[2,8,64,512]{3,2,0,1:T(8,128)(2,1)S(1)} async-done(((bf16[2,8,64,512]{3,2,0,1:T(8,128)(2,1)}), bf16[2,8,64,512]{3,2,0,1:T(8,128)(2,1)S(1)}, u32[]{:S(2)}, u32[]{:S(2)}) %all-to-all-start.2) | async-done | bytes 1048608 | tf_op jit(solution)/shard_map/all_to_all | solution.py:154
  60.4 4.9 %all-to-all-start.4 = ((bf16[2,8,64,512]{3,2,0,1:T(8,128)(2,1)}), bf16[2,8,64,512]{3,2,0,1:T(8,128)(2,1)S(1)}, u32[]{:S(2)}, u32[]{:S(2)}) async-start(bf16[2,8,64,512]{3,2,0,1:T(8,128)(2,1)} %copy.134), calls=%async_computation.4 | async-start | bytes 2097152 | tf_op jit(solution)/shard_map/all_to_all | solution.py:163
  80.8 4.0 %collective-permute-start.1 = (bf16[1024,128]{1,0:T(8,128)(2,1)S(1)}, bf16[1024,128]{1,0:T(8,128)(2,1)}, u32[]{:S(2)}, u32[]{:S(2)}) collective-permute-start(bf16[1024,128]{1,0:T(8,128)(2,1)S(1)} %bitcast.127), channel_id=1, source_target_pairs={{0,8},{8,16},{16,24},{1,9},{9,17},{17,25},{2,10},{10,18},{18,26},{... | collective-permute-start | bytes 786440 | tf_op jit(solution)/shard_map/ppermute | solution.py:12
  84.8 2.3 compare_and_fusion
  87.2 1.9 copy.119
  89.0 1.8 copy.121
  90.8 2.1 collective-permute-start
  92.9 2.3 copy.128
  95.2 2.1 reshape_reshape.12
  97.4 2.9 copy.164
  100.3 3.2 %reshape.537 = bf16[1024,4,128]{0,2,1:T(8,128)(2,1)S(1)} reshape(bf16[2,8,64,512]{2,1,0,3:T(8,128)(2,1)} %copy.164) | data formatting | bytes 2097152 | tf_op jit(solution)/shard_map/reshape;reshape | solution.py:92
  103.5 15.2 %fusion.3 = (f32[4,1024]{1,0:T(4,128)S(1)}, f32[2048,1024,4]{1,0,2:T(8,128)}) fusion(pred[1024,2048]{0,1:T(8,128)(4,1)S(1)} %compare_and_fusion, bf16[1024,4,128]{2,1,0:T(4,128)(2,1)} %reshape_reshape.12, bf16[1024,128]{1,0:T(8,128)(2,1)} %collective-permute-done.1, bf16[1024,128]{1,0:T(8,128)(2,1)S(1)} %bitcast.128), kind=kOutput, calls=%fused_computation.15 | convolution fusion | flops 2173693952 | bytes 37240832 | tf_op jit(solution)/shard_map/qhd,kd->hqk/dot_general | solution.py:94
  118.8 14.3 %exponential_reduce_fusion = f32[4,1024]{1,0:T(4,128)S(1)} fusion(f32[2048,1024,4]{1,0,2:T(8,128)} %get-tuple-element.44, f32[4,1024]{1,0:T(4,128)S(1)} %get-tuple-element.43, pred[1024,2048]{0,1:T(8,128)(4,1)S(1)} %compare_and_fusion), kind=kLoop, calls=%fused_computation.13 | loop fusion | flops 33550336 | bytes 35684352 | tf_op jit(solution)/shard_map/reduce_sum | solution.py:99
  133.1 15.2 %convolution_bitcast_fusion = f32[2048,128]{1,0:T(8,128)} fusion(bf16[1024,4,128]{0,2,1:T(8,128)(2,1)S(1)} %reshape.537, f32[2048,1024,4]{1,0,2:T(8,128)} %get-tuple-element.44, f32[4,1024]{1,0:T(4,128)S(1)} %log_add_fusion, pred[1024,2048]{0,1:T(8,128)(4,1)S(1)} %compare_and_fusion), kind=kOutput, calls=%fused_computation.17 | convolution fusion | flops 2181038080 | bytes 37765120 | tf_op jit(solution)/shard_map/hqk,qhd->kd/dot_general | solution.py:116
  148.3 1.9 slice.39
  150.2 3.1 %collective-permute-start.3 = (f32[1024,128]{1,0:T(8,128)}, f32[1024,128]{1,0:T(8,128)}, u32[]{:S(2)}, u32[]{:S(2)}) collective-permute-start(f32[1024,128]{1,0:T(8,128)} %slice.39), channel_id=1, source_target_pairs={{8,0},{16,8},{24,16},{9,1},{17,9},{25,17},{10,2},{18,10},{26,18},{... | collective-permute-start | bytes 1572872 | tf_op jit(solution)/shard_map/ppermute | solution.py:12
  153.4 16.4 %multiply_reduce_fusion = (f32[1024,4]{0,1:T(4,128)S(1)}, bf16[1024,4,128]{0,2,1:T(8,128)(2,1)}) fusion(bf16[1024,4,128]{0,2,1:T(8,128)(2,1)S(1)} %reshape.537, f32[2048,1024,4]{1,0,2:T(8,128)} %get-tuple-element.44, f32[4,1024]{1,0:T(4,128)S(1)} %log_add_fusion, pred[1024,2048]{0,1:T(8,128)(4,1)S(1)} %compare_and_fusion, ...), kind=kOutput, calls=%fused_computation.21 | convolution fusion | flops 2184704000 | bytes 38305792 | tf_op jit(solution)/shard_map/hqk,kd->qhd/dot_general | solution.py:102
  169.7 16.5 %fusion.1 = bf16[4,1024,2048]{1,2,0:T(8,128)(2,1)S(1)} fusion(f32[2048,1024,4]{1,0,2:T(8,128)} %get-tuple-element.44, bf16[1024,4,128]{0,2,1:T(8,128)(2,1)} %copy-done.3, f32[4,1024]{1,0:T(4,128)S(1)} %bitcast.152, f32[4,1024]{1,0:T(4,128)S(1)} %log_add_fusion, pred[1024,2048]{0,1:T(8,128)(4,1)} %copy-done.1, bf16[1024,128]{0,1:T(8,128)(2,1)} %collective-permute-done, ...), kind=kOutput, calls=%fused_computation.10 | convolution fusion | flops 2198863872 | bytes 54034432 | tf_op jit(solution)/shard_map/qhd,kd->hqk/dot_general | solution.py:106
  186.2 5.7 %copy-done = bf16[4,1024,2048]{1,2,0:T(8,128)(2,1)} copy-done((bf16[4,1024,2048]{1,2,0:T(8,128)(2,1)}, bf16[4,1024,2048]{1,2,0:T(8,128)(2,1)S(1)}, u32[]{:S(2)}) %copy-start) | copy-done | bytes 16777240
  191.9 6.0 %fusion.4 = f32[2048,128]{1,0:T(8,128)S(1)} fusion(bf16[4,1024,2048]{1,2,0:T(8,128)(2,1)S(1)} %fusion.1, bf16[1024,4,128]{2,1,0:T(4,128)(2,1)} %reshape_reshape.12), kind=kOutput, calls=%fused_computation.19 | convolution fusion | flops 2147745792 | bytes 18874368 | tf_op jit(solution)/shard_map/hqk,qhd->kd/dot_general | solution.py:113
  198.0 1.9 collective-permute-start.2
  199.9 1.3 fusion.10
  201.9 5.7 %all-to-all-start.7 = ((bf16[2,8,64,128]{3,2,0,1:T(8,128)(2,1)}), bf16[2,8,64,128]{3,2,0,1:T(8,128)(2,1)S(1)}, u32[]{:S(2)}, u32[]{:S(2)}) async-start(bf16[2,8,64,128]{3,2,0,1:T(8,128)(2,1)} %copy.148), calls=%async_computation.7 | async-start | bytes 524288 | tf_op jit(solution)/shard_map/all_to_all | solution.py:215
  208.5 1.1 fusion.11
  210.3 5.9 %all-to-all-done.7 = bf16[2,8,64,128]{3,2,0,1:T(8,128)(2,1)S(1)} async-done(((bf16[2,8,64,128]{3,2,0,1:T(8,128)(2,1)}), bf16[2,8,64,128]{3,2,0,1:T(8,128)(2,1)S(1)}, u32[]{:S(2)}, u32[]{:S(2)}) %all-to-all-start.7) | async-done | bytes 262176 | tf_op jit(solution)/shard_map/all_to_all | solution.py:215
  216.9 4.0 %all-to-all-start.6 = ((bf16[2,8,64,128]{3,2,0,1:T(8,128)(2,1)}), bf16[2,8,64,128]{3,2,0,1:T(8,128)(2,1)}, u32[]{:S(2)}, u32[]{:S(2)}) async-start(bf16[2,8,64,128]{3,2,0,1:T(8,128)(2,1)} %copy.145), calls=%async_computation.6 | async-start | bytes 524288 | tf_op jit(solution)/shard_map/all_to_all | solution.py:214
  221.0 8.3 %fusion.6 = bf16[1024,4,128]{0,2,1:T(8,128)(2,1)S(1)} fusion(bf16[4,1024,2048]{1,2,0:T(8,128)(2,1)} %copy-done, bf16[1024,128]{1,0:T(8,128)(2,1)} %collective-permute-done.1, bf16[1024,128]{1,0:T(8,128)(2,1)S(1)} %bitcast.129), kind=kOutput, calls=%fused_computation.24 | convolution fusion | flops 2149580800 | bytes 18350080 | tf_op jit(solution)/shard_map/hqk,kd->qhd/dot_general | solution.py:109
  229.3 1.3 reshape.529
  230.6 2.5 copy.142
  233.1 5.4 %all-to-all-start.5 = ((bf16[2,8,64,512]{3,2,0,1:T(8,128)(2,1)}), bf16[2,8,64,512]{3,2,0,1:T(8,128)(2,1)S(1)}, u32[]{:S(2)}, u32[]{:S(2)}) async-start(bf16[2,8,64,512]{3,2,0,1:T(8,128)(2,1)} %copy.142), calls=%async_computation.5 | async-start | bytes 2097152 | tf_op jit(solution)/shard_map/all_to_all | solution.py:207
  238.5 3.0 %reshape.528 = bf16[2,8,64,512]{2,1,0,3:T(8,128)(2,1)S(1)} reshape(bf16[1024,4,128]{0,2,1:T(8,128)(2,1)} %get-tuple-element.46) | data formatting | bytes 2097152 | tf_op jit(solution)/shard_map/reshape;reshape | solution.py:201
  241.4 2.5 copy.132
  243.9 19.6 %all-to-all-done.5 = bf16[2,8,64,512]{3,2,0,1:T(8,128)(2,1)S(1)} async-done(((bf16[2,8,64,512]{3,2,0,1:T(8,128)(2,1)}), bf16[2,8,64,512]{3,2,0,1:T(8,128)(2,1)S(1)}, u32[]{:S(2)}, u32[]{:S(2)}) %all-to-all-start.5) | async-done | bytes 1048608 | tf_op jit(solution)/shard_map/all_to_all | solution.py:207
  263.6 4.5 %all-to-all-start.3 = ((bf16[2,8,64,512]{3,2,0,1:T(8,128)(2,1)}), bf16[2,8,64,512]{3,2,0,1:T(8,128)(2,1)S(1)}, u32[]{:S(2)}, u32[]{:S(2)}) async-start(bf16[2,8,64,512]{3,2,0,1:T(8,128)(2,1)} %copy.132), calls=%async_computation.3 | async-start | bytes 2097152 | tf_op jit(solution)/shard_map/all_to_all | solution.py:200
  269.1 1.2 gather_fusion.7
  271.3 1.2 gather_fusion.6
  272.6 1.4 gather_fusion.5
  273.9 19.3 %all-to-all-done.3 = bf16[2,8,64,512]{3,2,0,1:T(8,128)(2,1)S(1)} async-done(((bf16[2,8,64,512]{3,2,0,1:T(8,128)(2,1)}), bf16[2,8,64,512]{3,2,0,1:T(8,128)(2,1)S(1)}, u32[]{:S(2)}, u32[]{:S(2)}) %all-to-all-start.3) | async-done | bytes 1048608 | tf_op jit(solution)/shard_map/all_to_all | solution.py:200
  293.3 1.4 gather_fusion.3
  (76 shorter events, 18.3 us)
Async XLA Ops:
  5.2 13.8 %all-to-all-start.1 = ((bf16[2,8,64,128]{3,2,0,1:T(8,128)(2,1)}), bf16[2,8,64,128]{3,2,0,1:T(8,128)(2,1)S(1)}, u32[]{:S(2)}, u32[]{:S(2)}) async-start(bf16[2,8,64,128]{3,2,0,1:T(8,128)(2,1)} %copy.125), calls=%async_computation.1 | async-start | bytes 524288 | tf_op jit(solution)/shard_map/all_to_all | solution.py:157
  19.0 4.7 %copy-start.5 = (bf16[2,8,64,128]{3,2,0,1:T(8,128)(2,1)}, bf16[2,8,64,128]{3,2,0,1:T(8,128)(2,1)S(1)}, u32[]{:S(2)}) copy-start(bf16[2,8,64,128]{3,2,0,1:T(8,128)(2,1)S(1)} %all-to-all-done.1) | copy-start | bytes 786436
  19.0 11.9 %all-to-all-start = ((bf16[2,8,64,128]{3,2,0,1:T(8,128)(2,1)}), bf16[2,8,64,128]{3,2,0,1:T(8,128)(2,1)S(1)}, u32[]{:S(2)}, u32[]{:S(2)}) async-start(bf16[2,8,64,128]{3,2,0,1:T(8,128)(2,1)} %copy.118), calls=%async_computation | async-start | bytes 524288 | tf_op jit(solution)/shard_map/all_to_all | solution.py:160
  30.9 4.9 %copy-start.6 = (bf16[2,8,64,128]{3,2,0,1:T(8,128)(2,1)}, bf16[2,8,64,128]{3,2,0,1:T(8,128)(2,1)S(1)}, u32[]{:S(2)}) copy-start(bf16[2,8,64,128]{3,2,0,1:T(8,128)(2,1)S(1)} %all-to-all-done) | copy-start | bytes 786436
  30.9 29.5 %all-to-all-start.2 = ((bf16[2,8,64,512]{3,2,0,1:T(8,128)(2,1)}), bf16[2,8,64,512]{3,2,0,1:T(8,128)(2,1)S(1)}, u32[]{:S(2)}, u32[]{:S(2)}) async-start(bf16[2,8,64,512]{3,2,0,1:T(8,128)(2,1)} %copy.127), calls=%async_computation.2 | async-start | bytes 2097152 | tf_op jit(solution)/shard_map/all_to_all | solution.py:154
  60.4 20.4 %copy-start.2 = (bf16[2,8,64,512]{3,2,0,1:T(8,128)(2,1)}, bf16[2,8,64,512]{3,2,0,1:T(8,128)(2,1)S(1)}, u32[]{:S(2)}) copy-start(bf16[2,8,64,512]{3,2,0,1:T(8,128)(2,1)S(1)} %all-to-all-done.2) | copy-start | bytes 3145732
  60.4 36.9 %all-to-all-start.4 = ((bf16[2,8,64,512]{3,2,0,1:T(8,128)(2,1)}), bf16[2,8,64,512]{3,2,0,1:T(8,128)(2,1)S(1)}, u32[]{:S(2)}, u32[]{:S(2)}) async-start(bf16[2,8,64,512]{3,2,0,1:T(8,128)(2,1)} %copy.134), calls=%async_computation.4 | async-start | bytes 2097152 | tf_op jit(solution)/shard_map/all_to_all | solution.py:163
  80.8 22.7 %collective-permute-start.1 = (bf16[1024,128]{1,0:T(8,128)(2,1)S(1)}, bf16[1024,128]{1,0:T(8,128)(2,1)}, u32[]{:S(2)}, u32[]{:S(2)}) collective-permute-start(bf16[1024,128]{1,0:T(8,128)(2,1)S(1)} %bitcast.127), channel_id=1, source_target_pairs={{0,8},{8,16},{16,24},{1,9},{9,17},{17,25},{2,10},{10,18},{18,26},{... | collective-permute-start | bytes 786440 | tf_op jit(solution)/shard_map/ppermute | solution.py:12
  87.1 66.2 %copy-start.1 = (pred[1024,2048]{0,1:T(8,128)(4,1)}, pred[1024,2048]{0,1:T(8,128)(4,1)S(1)}, u32[]{:S(2)}) copy-start(pred[1024,2048]{0,1:T(8,128)(4,1)S(1)} %compare_and_fusion) | copy-start | bytes 6291460
  90.8 62.5 %collective-permute-start = (bf16[1024,128]{0,1:T(8,128)(2,1)}, bf16[1024,128]{0,1:T(8,128)(2,1)}, u32[]{:S(2)}, u32[]{:S(2)}) collective-permute-start(bf16[1024,128]{0,1:T(8,128)(2,1)} %copy.121), channel_id=1, source_target_pairs={{0,8},{8,16},{16,24},{1,9},{9,17},{17,25},{2,10},{10,18},{18,26},{... | collective-permute-start | bytes 786440 | tf_op jit(solution)/shard_map/ppermute | solution.py:12
  103.5 49.9 %copy-start.3 = (bf16[1024,4,128]{0,2,1:T(8,128)(2,1)}, bf16[1024,4,128]{0,2,1:T(8,128)(2,1)S(1)}, u32[]{:S(2)}) copy-start(bf16[1024,4,128]{0,2,1:T(8,128)(2,1)S(1)} %reshape.537) | copy-start | bytes 3145732
  150.2 49.7 %collective-permute-start.3 = (f32[1024,128]{1,0:T(8,128)}, f32[1024,128]{1,0:T(8,128)}, u32[]{:S(2)}, u32[]{:S(2)}) collective-permute-start(f32[1024,128]{1,0:T(8,128)} %slice.39), channel_id=1, source_target_pairs={{8,0},{16,8},{24,16},{9,1},{17,9},{25,17},{10,2},{18,10},{26,18},{... | collective-permute-start | bytes 1572872 | tf_op jit(solution)/shard_map/ppermute | solution.py:12
  186.2 5.7 %copy-start = (bf16[4,1024,2048]{1,2,0:T(8,128)(2,1)}, bf16[4,1024,2048]{1,2,0:T(8,128)(2,1)S(1)}, u32[]{:S(2)}) copy-start(bf16[4,1024,2048]{1,2,0:T(8,128)(2,1)S(1)} %fusion.1) | copy-start | bytes 50331652
  197.9 2.0 copy-start.4
  198.0 10.5 %collective-permute-start.2 = (f32[1024,128]{1,0:T(8,128)S(1)}, f32[1024,128]{1,0:T(8,128)S(1)}, u32[]{:S(2)}, u32[]{:S(2)}) collective-permute-start(f32[1024,128]{1,0:T(8,128)S(1)} %slice.37), channel_id=1, source_target_pairs={{8,0},{16,8},{24,16},{9,1},{17,9},{25,17},{10,2},{18,10},{26,18},{... | collective-permute-start | bytes 1572872 | tf_op jit(solution)/shard_map/ppermute | solution.py:12
  201.9 14.3 %all-to-all-start.7 = ((bf16[2,8,64,128]{3,2,0,1:T(8,128)(2,1)}), bf16[2,8,64,128]{3,2,0,1:T(8,128)(2,1)S(1)}, u32[]{:S(2)}, u32[]{:S(2)}) async-start(bf16[2,8,64,128]{3,2,0,1:T(8,128)(2,1)} %copy.148), calls=%async_computation.7 | async-start | bytes 524288 | tf_op jit(solution)/shard_map/all_to_all | solution.py:215
  216.2 0.7 copy-start.7
  216.9 16.2 %all-to-all-start.6 = ((bf16[2,8,64,128]{3,2,0,1:T(8,128)(2,1)}), bf16[2,8,64,128]{3,2,0,1:T(8,128)(2,1)}, u32[]{:S(2)}, u32[]{:S(2)}) async-start(bf16[2,8,64,128]{3,2,0,1:T(8,128)(2,1)} %copy.145), calls=%async_computation.6 | async-start | bytes 524288 | tf_op jit(solution)/shard_map/all_to_all | solution.py:214
  233.1 30.4 %all-to-all-start.5 = ((bf16[2,8,64,512]{3,2,0,1:T(8,128)(2,1)}), bf16[2,8,64,512]{3,2,0,1:T(8,128)(2,1)S(1)}, u32[]{:S(2)}, u32[]{:S(2)}) async-start(bf16[2,8,64,512]{3,2,0,1:T(8,128)(2,1)} %copy.142), calls=%async_computation.5 | async-start | bytes 2097152 | tf_op jit(solution)/shard_map/all_to_all | solution.py:207
  263.6 29.6 %all-to-all-start.3 = ((bf16[2,8,64,512]{3,2,0,1:T(8,128)(2,1)}), bf16[2,8,64,512]{3,2,0,1:T(8,128)(2,1)S(1)}, u32[]{:S(2)}, u32[]{:S(2)}) async-start(bf16[2,8,64,512]{3,2,0,1:T(8,128)(2,1)} %copy.132), calls=%async_computation.3 | async-start | bytes 2097152 | tf_op jit(solution)/shard_map/all_to_all | solution.py:200
where the time goes:
time: 298 us; the launch traced here: 295 us
  matrix products  77.5 us (26%)
  waiting for transfers between devices  75 us (25%)
  local copies, waits for them, and re-layouts  53.7 us (18%)
  starting transfers between devices  51.6 us (17%)
  other arithmetic  23.4 us (8%)
  between operations  13.4 us (4%)
    all_to_all x1, waiting for transfers between devices, shards(): lax.all_to_all(pack_rows(query_rows, hold_index), 'inner', split_axis=1,...  19.8 us
    all_to_all x1, waiting for transfers between devices, shards(): lax.all_to_all(q_grads.reshape(2, n_inner, piece_len, width_q), 'inner',...  19.6 us
    all_to_all x1, waiting for transfers between devices, shards(): lax.all_to_all(attn.reshape(2, n_inner, piece_len, width_q), 'inner', spl...  19.3 us
    dot_general x1, matrix products, attend(): jnp.einsum('qhd,kd->hqk', g_three, value_buf, preferred_element_type=jnp....  16.5 us
    dot_general x1, matrix products, attend(): jnp.einsum('hqk,kd->qhd', probs_low, value_buf, preferred_element_type=jn...  16.4 us
    dot_general x1, matrix products, attend(): jnp.einsum('qhd,kd->hqk', q_three, key_buf, preferred_element_type=jnp.fl...  15.2 us
    dot_general x1, matrix products, attend(): jnp.einsum('hqk,qhd->kd', probs_low, g_three, preferred_element_type=jnp....  15.2 us
    reduce_sum x1, other arithmetic, attend(): jnp.sum(jnp.exp(scores - row_max), axis=2, keepdims=True)  14.3 us
  transfers between devices with their start and end apart: 12, of which 7 were waited for; matrix products, arithmetic and copies ran while one was open for 48% of the time, Pallas kernels for 0%

commit v1 on v0

v1 whole, which is shorter than its diff:
```python
import math

import jax
import jax.numpy as jnp
from jax import lax
from jax.sharding import PartitionSpec as P


def doc_table(doc_starts, tok_dev):
    n_outer, n_inner, n_slots = doc_starts.shape
    flat_starts = doc_starts.reshape(n_outer * n_inner, n_slots)
    start_counts = jnp.sum((flat_starts < tok_dev).astype(jnp.int32), axis=1)
    first_index = jnp.cumsum(start_counts) - start_counts
    offsets = jnp.arange(tok_dev, dtype=jnp.int32)
    inside_count = jnp.sum(
        (flat_starts[:, None, :] <= offsets[None, :, None]).astype(jnp.int32), axis=2
    )
    return (first_index[:, None] + inside_count - 1).reshape(n_outer, n_inner, tok_dev)


def attend(
    query_buf, grad_buf, query_pos, query_doc, key_buf, value_buf, key_pos, key_doc, n_heads
):
    n_rows = query_buf.shape[0]
    head_dim = key_buf.shape[1]
    scaling = 1.0 / math.sqrt(head_dim)
    q_three = query_buf.reshape(n_rows, n_heads, head_dim)
    g_three = grad_buf.reshape(n_rows, n_heads, head_dim)
    scores = (
        jnp.einsum("qhd,kd->hqk", q_three, key_buf, preferred_element_type=jnp.float32) * scaling
    )
    allowed = (query_doc[:, None] == key_doc[None, :]) & (key_pos[None, :] <= query_pos[:, None])
    scores = jnp.where(allowed[None], scores, -jnp.inf)
    row_max = jnp.max(scores, axis=2, keepdims=True)
    log_total = row_max + jnp.log(jnp.sum(jnp.exp(scores - row_max), axis=2, keepdims=True))
    probs = jnp.exp(scores - log_total)
    probs_low = probs.astype(jnp.bfloat16)
    attn = jnp.einsum(
        "hqk,kd->qhd", probs_low, value_buf, preferred_element_type=jnp.float32
    ).astype(jnp.bfloat16)
    inner_prod = jnp.sum(g_three.astype(jnp.float32) * attn.astype(jnp.float32), axis=2)
    grad_probs = jnp.einsum("qhd,kd->hqk", g_three, value_buf, preferred_element_type=jnp.float32)
    score_grads = (probs * (grad_probs - inner_prod.T[:, :, None])).astype(jnp.bfloat16)
    q_grads = (
        jnp.einsum("hqk,kd->qhd", score_grads, key_buf, preferred_element_type=jnp.float32)
        * scaling
    )
    k_grads = (
        jnp.einsum("hqk,qhd->kd", score_grads, q_three, preferred_element_type=jnp.float32)
        * scaling
    )
    v_grads = jnp.einsum("hqk,qhd->kd", probs_low, g_three, preferred_element_type=jnp.float32)
    return (
        attn.reshape(n_rows, -1),
        q_grads.astype(jnp.bfloat16).reshape(n_rows, -1),
        k_grads,
        v_grads,
    )


def shards(queries, keys, values, grad_out, doc_starts):
    n_inner = lax.axis_size("inner")
    n_outer = lax.axis_size("outer")
    n_units = queries.shape[1]
    piece_len = queries.shape[3]
    width_q = queries.shape[4]
    head_dim = keys.shape[4]
    n_heads = width_q // head_dim
    tok_dev = piece_len * n_inner
    outer_id = lax.axis_index("outer")
    inner_id = lax.axis_index("inner")
    docs_all = doc_table(doc_starts, tok_dev)
    offsets = jnp.arange(tok_dev, dtype=jnp.int32)

    packed = jnp.concatenate(
        [queries[0, :, 0], keys[0, :, 0], values[0, :, 0], grad_out[0, :, 0]], axis=-1
    )
    arrived = lax.all_to_all(packed, "inner", 0, 0, tiled=True).reshape(tok_dev, -1)
    query_buf = arrived[:, :width_q]
    kv_own = arrived[:, width_q : width_q + 2 * head_dim]
    grad_buf = arrived[:, width_q + 2 * head_dim :]

    pairs_up = [(2 * p, 2 * p + 1) for p in range(n_inner // 2)]
    kv_partner = lax.ppermute(kv_own, "inner", pairs_up)

    both = ("outer", "inner")
    last_a, last_b = n_inner - 2, n_inner - 1
    send_a = [((o - 1) * n_inner + last_a, o * n_inner) for o in range(1, n_outer)] + [
        ((o - 1) * n_inner + last_b, o * n_inner + 1) for o in range(1, n_outer)
    ]
    send_b = [((o - 1) * n_inner + last_a, o * n_inner + 1) for o in range(1, n_outer)] + [
        ((o - 1) * n_inner + last_b, o * n_inner) for o in range(1, n_outer)
    ]
    recv_a = lax.ppermute(kv_own, both, send_a)
    recv_b = lax.ppermute(kv_own, both, send_b)
    first = inner_id == 0
    kv_prev_a = jnp.where(first, recv_a, recv_b)
    kv_prev_b = jnp.where(first, recv_b, recv_a)

    unit_id = outer_id * n_units + inner_id
    before = jnp.maximum(outer_id - 1, 0)
    has_prev = (outer_id > 0) & (inner_id < 2)
    has_partner = inner_id % 2 == 1
    query_doc = docs_all[outer_id, inner_id]
    query_pos = unit_id * tok_dev + offsets
    partner_doc = jnp.where(has_partner, docs_all[outer_id, jnp.maximum(inner_id - 1, 0)], -3)
    prev_a_doc = jnp.where(has_prev, docs_all[before, last_a], -4)
    prev_b_doc = jnp.where(has_prev, docs_all[before, last_b], -5)
    key_doc = jnp.concatenate([prev_a_doc, prev_b_doc, partner_doc, query_doc])
    key_pos = jnp.concatenate(
        [
            (before * n_units + last_a) * tok_dev + offsets,
            (before * n_units + last_b) * tok_dev + offsets,
            (unit_id - 1) * tok_dev + offsets,
            query_pos,
        ]
    )
    ctx = jnp.concatenate([kv_prev_a, kv_prev_b, kv_partner, kv_own])
    attn, q_grads, k_grads, v_grads = attend(
        query_buf,
        grad_buf,
        query_pos,
        query_doc,
        ctx[:, :head_dim],
        ctx[:, head_dim:],
        key_pos,
        key_doc,
        n_heads,
    )
    kv_grads = jnp.concatenate([k_grads, v_grads], axis=1).reshape(4, tok_dev, 2 * head_dim)

    pairs_down = [(b, a) for a, b in pairs_up]
    from_partner = lax.ppermute(kv_grads[2], "inner", pairs_down)
    back_a = [(b, a) for a, b in send_a]
    back_b = [(b, a) for a, b in send_b]
    grads_a = jnp.where(first, kv_grads[0], kv_grads[1])
    grads_b = jnp.where(first, kv_grads[1], kv_grads[0])
    from_next_a = lax.ppermute(grads_a, both, back_a)
    from_next_b = lax.ppermute(grads_b, both, back_b)
    kv_total = (kv_grads[3] + from_partner + from_next_a + from_next_b).astype(jnp.bfloat16)

    result = jnp.concatenate([attn, q_grads, kv_total], axis=-1).reshape(
        n_inner, piece_len, -1
    )
    returned = lax.all_to_all(result, "inner", 0, 0, tiled=True)
    shape_q = (1, n_units, 1, piece_len, width_q)
    shape_k = (1, n_units, 1, piece_len, head_dim)
    return (
        returned[..., :width_q].reshape(shape_q),
        returned[..., width_q : 2 * width_q].reshape(shape_q),
        returned[..., 2 * width_q : 2 * width_q + head_dim].reshape(shape_k),
        returned[..., 2 * width_q + head_dim :].reshape(shape_k),
    )


def solution(mesh):
    return jax.shard_map(
        shards,
        mesh=mesh,
        in_specs=(
            P("outer", None, "inner", None, None),
            P("outer", None, "inner", None, None),
            P("outer", None, "inner", None, None),
            P("outer", None, "inner", None, None),
            P(),
        ),
        out_specs=(
            P("outer", None, "inner", None, None),
            P("outer", None, "inner", None, None),
            P("outer", None, "inner", None, None),
            P("outer", None, "inner", None, None),
        ),
        check_vma=False,
    )
```

time: 298 us -> 151 us (0.51)
  matrix products: 77.5 us -> 25.1 us
  local copies, waits for them, and re-layouts: 53.7 us -> 7.89 us
  blocking collectives: 0 us -> 38.4 us
  waiting for transfers between devices: 75 us -> 41.4 us
  starting transfers between devices: 51.6 us -> 20.6 us
  between operations: 13.4 us -> 0.86 us
  other arithmetic: 23.4 us -> 14.7 us
    all_to_all x8 -> x1, waiting for transfers between devices: 74.1 us -> 26.9 us  [shards(): lax.all_to_all(packed, 'inner', 0, 0, tiled=True).reshape(tok_dev, -1)]
    all_to_all x0 -> x1, blocking collectives: none -> 38.4 us  [shards(): returned = lax.all_to_all(result, 'inner', 0, 0, tiled=True)]
    all_to_all x8 -> x1, starting transfers between devices: 40.5 us -> 6.34 us  [shards(): lax.all_to_all(packed, 'inner', 0, 0, tiled=True).reshape(tok_dev, -1)]
    another operation x9 -> x1, local copies, waits for them, and re-layouts: 17.8 us -> 0.08 us  [the longest x2 6.13 us: attend(): g_three = grad_buf.reshape(n_rows, n_heads, head_dim)]
    ppermute x4 -> x6, waiting for transfers between devices: 0.92 us -> 14.5 us  [the longest x1 7.21 us: shards(): recv_b = lax.ppermute(kv_own, both, send_b)]
    dot_general x1, matrix products: 15.2 us -> 2.94 us  [attend(): jnp.einsum('qhd,kd->hqk', q_three, key_buf, preferred_element_type=jnp.fl...]
    gather x12 -> x0, local copies, waits for them, and re-layouts: 11.3 us -> none  [the longest x8 6.09 us: pack_rows(): return padded[index_table]]
    dot_general x1, matrix products: 16.4 us -> 5.3 us  [attend(): jnp.einsum('hqk,kd->qhd', probs_low, value_buf, preferred_element_type=jn...]
  transfers between devices with their start and end apart: 12 -> 7, of which waited for: 7 -> 5; matrix products, arithmetic and copies ran while one was open for 48% -> 7% of each run, Pallas kernels for 0% -> 0%
where the time goes in v1:
time: 151 us; the launch traced here: 149 us
  waiting for transfers between devices  41.4 us (27%)
  blocking collectives  38.4 us (25%)
  matrix products  25.1 us (17%)
  starting transfers between devices  20.6 us (14%)
  other arithmetic  14.7 us (10%)
  local copies, waits for them, and re-layouts  7.89 us (5%)
    all_to_all x1, blocking collectives, shards(): returned = lax.all_to_all(result, 'inner', 0, 0, tiled=True)  38.4 us
    all_to_all x1, waiting for transfers between devices, shards(): lax.all_to_all(packed, 'inner', 0, 0, tiled=True).reshape(tok_dev, -1)  26.9 us
    dot_general x1, matrix products, attend(): jnp.einsum('qhd,kd->hqk', g_three, value_buf, preferred_element_type=jnp....  8.96 us
    ppermute x1, waiting for transfers between devices, shards(): recv_b = lax.ppermute(kv_own, both, send_b)  7.21 us
    all_to_all x1, starting transfers between devices, shards(): lax.all_to_all(packed, 'inner', 0, 0, tiled=True).reshape(tok_dev, -1)  6.34 us
    dot_general x1, matrix products, attend(): jnp.einsum('hqk,kd->qhd', probs_low, value_buf, preferred_element_type=jn...  5.3 us
    dot_general x1, matrix products, attend(): jnp.einsum('hqk,qhd->kd', probs_low, g_three, preferred_element_type=jnp....  4.17 us
    ppermute x1, starting transfers between devices, shards(): from_next_b = lax.ppermute(grads_b, both, back_b)  4.15 us
  transfers between devices with their start and end apart: 7, of which 5 were waited for; matrix products, arithmetic and copies ran while one was open for 7% of the time, Pallas kernels for 0%

profile of v1, /device:TPU:1, one launch (start us, length us, event | category | flops | bytes accessed | tf_op | source)
XLA Modules:
  0.0 148.9 jit_solution(11811836576815216265)
XLA Ops:
  0.6 2.5 %pad_maximum_fusion = bf16[8,64,1280]{2,1,0:T(8,128)(2,1)} fusion(bf16[8,64,512]{2,1,0:T(8,128)(2,1)} %bitcast.89, bf16[8,64,128]{2,1,0:T(8,128)(2,1)} %bitcast.95, bf16[8,64,128]{2,1,0:T(8,128)(2,1)} %bitcast.96, bf16[8,64,512]{2,1,0:T(8,128)(2,1)} %bitcast.90), kind=kLoop, calls=%fused_computation.19 | loop fusion | flops 5242880 | bytes 2621440 | tf_op jit(solution)/shard_map/concatenate | solution.py:75
  3.1 6.3 %all-to-all-start = ((bf16[8,64,1280]{2,1,0:T(8,128)(2,1)}), bf16[8,64,1280]{2,1,0:T(8,128)(2,1)S(1)}, u32[]{:S(2)}, u32[]{:S(2)}) async-start(bf16[8,64,1280]{2,1,0:T(8,128)(2,1)} %pad_maximum_fusion), calls=%async_computation | async-start | bytes 2621440 | tf_op jit(solution)/shard_map/all_to_all | solution.py:78
  9.5 0.7 copy.49
  10.2 0.7 convert_reduce_fusion.1
  10.9 0.1 reshape.167
  11.0 0.1 reduce-window.4
  11.0 0.1 reduce.1
  11.1 0.1 reshape.154
  11.2 0.1 le.32
  11.3 0.1 convert_reduce_fusion
  11.4 0.1 fusion.16
  11.6 1.6 %compare_and_fusion = pred[512,2048]{0,1:T(8,128)(4,1)S(1)} fusion(s32[512]{0:T(512)S(1)} %iota_add_fusion, s32[512]{0:T(512)S(1)} %bitcast.98, s32[2048]{0:T(1024)S(1)} %pad_add_fusion.1, s32[2048]{0:T(1024)S(1)} %pad_add_fusion), kind=kLoop, calls=%fused_computation.8 | loop fusion | flops 3145728 | bytes 1069056 | tf_op jit(solution)/shard_map/and | solution.py:32
  13.2 26.9 %all-to-all-done = bf16[8,64,1280]{2,1,0:T(8,128)(2,1)S(1)} async-done(((bf16[8,64,1280]{2,1,0:T(8,128)(2,1)}), bf16[8,64,1280]{2,1,0:T(8,128)(2,1)S(1)}, u32[]{:S(2)}, u32[]{:S(2)}) %all-to-all-start) | async-done | bytes 1310752 | tf_op jit(solution)/shard_map/all_to_all | solution.py:78
  40.1 0.7 slice.58
  40.8 1.3 collective-permute-start
  42.1 1.3 collective-permute-start.1
  43.4 4.1 %collective-permute-start.2 = (bf16[512,256]{1,0:T(8,128)(2,1)}, bf16[512,256]{1,0:T(8,128)(2,1)}, u32[]{:S(2)}, u32[]{:S(2)}) collective-permute-start(bf16[512,256]{1,0:T(8,128)(2,1)} %slice.58), channel_id=1, source_target_pairs={{0,1},{2,3},{4,5},{6,7},{8,9},{10,11},{12,13},{14,15},{16,17},{18,... | collective-permute-start | bytes 786440 | tf_op jit(solution)/shard_map/ppermute | solution.py:84
  47.5 0.1 fusion.19
  47.6 0.2 copy.50
  47.8 0.2 copy.82
  48.0 3.3 %collective-permute-done = bf16[512,256]{1,0:T(8,128)(2,1)} collective-permute-done((bf16[512,256]{1,0:T(8,128)(2,1)}, bf16[512,256]{1,0:T(8,128)(2,1)}, u32[]{:S(2)}, u32[]{:S(2)}) %collective-permute-start) | collective-permute-done | bytes 262176 | tf_op jit(solution)/shard_map/ppermute | solution.py:94
  51.3 7.2 %collective-permute-done.1 = bf16[512,256]{1,0:T(8,128)(2,1)} collective-permute-done((bf16[512,256]{1,0:T(8,128)(2,1)}, bf16[512,256]{1,0:T(8,128)(2,1)}, u32[]{:S(2)}, u32[]{:S(2)}) %collective-permute-start.1) | collective-permute-done | bytes 262176 | tf_op jit(solution)/shard_map/ppermute | solution.py:95
  58.5 1.1 broadcast_select_fusion.3
  59.6 1.1 pad_maximum_fusion.2
  60.7 2.9 %fusion.3 = (f32[4,512]{1,0:T(4,128)S(1)}, f32[2048,512,4]{1,0,2:T(8,128)S(1)}) fusion(pred[512,2048]{0,1:T(8,128)(4,1)S(1)} %compare_and_fusion, bf16[512,4,128]{0,2,1:T(8,128)(2,1)S(1)} %bitcast.91, bf16[2048,256]{1,0:T(8,128)(2,1)S(1)} %pad_maximum_fusion.2), kind=kOutput, calls=%fused_computation.7 | convolution fusion | flops 1086322688 | bytes 18882560 | tf_op jit(solution)/shard_map/qhd,kd->hqk/dot_general | solution.py:30
  63.7 3.8 %exponential_reduce_fusion = f32[4,512]{1,0:T(4,128)S(1)} fusion(f32[2048,512,4]{1,0,2:T(8,128)S(1)} %get-tuple-element.29, f32[4,512]{1,0:T(4,128)S(1)} %get-tuple-element.28, pred[512,2048]{0,1:T(8,128)(4,1)S(1)} %compare_and_fusion), kind=kLoop, calls=%fused_computation.5 | loop fusion | flops 16775168 | bytes 17842176 | tf_op jit(solution)/shard_map/reduce_sum | solution.py:35
  67.5 5.3 %multiply_reduce_fusion = (f32[512,4]{0,1:T(4,128)S(1)}, bf16[512,4,128]{0,2,1:T(8,128)(2,1)}) fusion(bf16[512,512]{0,1:T(8,128)(2,1)S(1)} %copy.82, f32[2048,512,4]{1,0,2:T(8,128)S(1)} %get-tuple-element.29, f32[4,512]{1,0:T(4,128)S(1)} %log_add_fusion, pred[512,2048]{0,1:T(8,128)(4,1)S(1)} %compare_and_fusion, bf16[2048,256]{1,0:T(8,128)(2,1)S(1)} %pad_maximum_fusion.2), kind=kOutput, calls=%fused_computation.26 | convolution fusion | flops 1091827712 | bytes 19415040 | tf_op jit(solution)/shard_map/hqk,kd->qhd/dot_general | solution.py:38
  72.8 4.2 %convolution_bitcast_fusion = f32[2048,128]{1,0:T(8,128)S(1)} fusion(bf16[512,4,128]{0,2,1:T(8,128)(2,1)S(1)} %bitcast.93, f32[2048,512,4]{1,0,2:T(8,128)S(1)} %get-tuple-element.29, f32[4,512]{1,0:T(4,128)S(1)} %log_add_fusion, pred[512,2048]{0,1:T(8,128)(4,1)S(1)} %compare_and_fusion), kind=kOutput, calls=%fused_computation.15 | convolution fusion | flops 1090519040 | bytes 19406848 | tf_op jit(solution)/shard_map/hqk,qhd->kd/dot_general | solution.py:52
  77.0 0.0 copy-start.2
  77.0 9.0 %fusion.1 = bf16[4,512,2048]{1,2,0:T(8,128)(2,1)S(1)} fusion(f32[2048,512,4]{1,0,2:T(8,128)} %copy-done, f32[4,512]{1,0:T(4,128)S(1)} %bitcast.102, f32[4,512]{1,0:T(4,128)S(1)} %log_add_fusion, pred[512,2048]{0,1:T(8,128)(4,1)S(1)} %compare_and_fusion, bf16[512,4,128]{0,2,1:T(8,128)(2,1)S(1)} %bitcast.94, bf16[2048,256]{1,0:T(8,128)(2,1)S(1)} %pad_maximum_fusion.2), kind=kOutput, calls=%fused_computation.2 | convolution fusion | flops 1098907648 | bytes 27279360 | tf_op jit(solution)/shard_map/qhd,kd->hqk/dot_general | solution.py:42
  86.0 2.4 %fusion.4 = f32[2048,128]{1,0:T(8,128)S(1)} fusion(bf16[4,512,2048]{1,2,0:T(8,128)(2,1)S(1)} %fusion.1, bf16[512,4,128]{0,2,1:T(8,128)(2,1)S(1)} %bitcast.92), kind=kOutput, calls=%fused_computation.17 | convolution fusion | flops 1074003968 | bytes 9961472 | tf_op jit(solution)/shard_map/hqk,qhd->kd/dot_general | solution.py:49
  88.4 0.9 broadcast_select_fusion.1
  89.3 1.1 fusion.14
  90.4 1.3 collective-permute-start.3
  91.7 4.2 %collective-permute-start.5 = (f32[512,256]{1,0:T(8,128)}, f32[512,256]{1,0:T(8,128)}, u32[]{:S(2)}, u32[]{:S(2)}) collective-permute-start(f32[512,256]{1,0:T(8,128)} %get-tuple-element.15), channel_id=1, source_target_pairs={{9,6},{17,14},{25,22},{8,7},{16,15},{24,23}} | collective-permute-start | bytes 1572872 | tf_op jit(solution)/shard_map/ppermute | solution.py:139
  95.8 2.1 %collective-permute-start.4 = (f32[512,256]{1,0:T(8,128)}, f32[512,256]{1,0:T(8,128)}, u32[]{:S(2)}, u32[]{:S(2)}) collective-permute-start(f32[512,256]{1,0:T(8,128)} %get-tuple-element.12), channel_id=1, source_target_pairs={{8,6},{16,14},{24,22},{9,7},{17,15},{25,23}} | collective-permute-start | bytes 1572872 | tf_op jit(solution)/shard_map/ppermute | solution.py:138
  97.9 1.3 fusion.7
  99.2 0.3 copy.59
  99.5 0.2 concatenate.30
  99.7 2.1 %copy.54 = bf16[512,4,128]{2,1,0:T(4,128)(2,1)} copy(bf16[512,4,128]{0,2,1:T(8,128)(2,1)} %get-tuple-element.31) | data formatting | bytes 1048576 | tf_op jit(solution)/shard_map/convert_element_type | solution.py:40
  101.9 1.2 concatenate.29
  103.1 3.3 %collective-permute-done.3 = f32[512,256]{1,0:T(8,128)} collective-permute-done((f32[512,256]{1,0:T(8,128)}, f32[512,256]{1,0:T(8,128)}, u32[]{:S(2)}, u32[]{:S(2)}) %collective-permute-start.3) | collective-permute-done | bytes 524320 | tf_op jit(solution)/shard_map/ppermute | solution.py:133
  106.5 0.6 collective-permute-done.4
  107.1 1.5 fusion.13
  108.5 0.1 pad_maximum_fusion.1
  108.6 38.4 %all_to_all.10 = bf16[8,64,1280]{2,1,0:T(8,128)(2,1)S(1)} all-to-all(bf16[8,64,1280]{2,1,0:T(8,128)(2,1)S(1)} %pad_maximum_fusion.1), channel_id=1, replica_groups=mesh['outer'=4,'inner'=8] {'inner'}, dimensions={0} | all-to-all | bytes 2621440 | tf_op jit(solution)/shard_map/all_to_all | solution.py:145
  147.1 1.1 slice_bitcast_fusion
  148.2 0.8 slice_bitcast_fusion.8
  (15 shorter events, 0.1 us)
Async XLA Ops:
  3.1 36.9 %all-to-all-start = ((bf16[8,64,1280]{2,1,0:T(8,128)(2,1)}), bf16[8,64,1280]{2,1,0:T(8,128)(2,1)S(1)}, u32[]{:S(2)}, u32[]{:S(2)}) async-start(bf16[8,64,1280]{2,1,0:T(8,128)(2,1)} %pad_maximum_fusion), calls=%async_computation | async-start | bytes 2621440 | tf_op jit(solution)/shard_map/all_to_all | solution.py:78
  40.8 10.6 %collective-permute-start = (bf16[512,256]{1,0:T(8,128)(2,1)}, bf16[512,256]{1,0:T(8,128)(2,1)}, u32[]{:S(2)}, u32[]{:S(2)}) collective-permute-start(bf16[512,256]{1,0:T(8,128)(2,1)} %slice.58), channel_id=1, source_target_pairs={{6,8},{14,16},{22,24},{7,9},{15,17},{23,25}} | collective-permute-start | bytes 786440 | tf_op jit(solution)/shard_map/ppermute | solution.py:94
  42.1 16.5 %collective-permute-start.1 = (bf16[512,256]{1,0:T(8,128)(2,1)}, bf16[512,256]{1,0:T(8,128)(2,1)}, u32[]{:S(2)}, u32[]{:S(2)}) collective-permute-start(bf16[512,256]{1,0:T(8,128)(2,1)} %slice.58), channel_id=1, source_target_pairs={{6,9},{14,17},{22,25},{7,8},{15,16},{23,24}} | collective-permute-start | bytes 786440 | tf_op jit(solution)/shard_map/ppermute | solution.py:95
  43.4 16.3 %collective-permute-start.2 = (bf16[512,256]{1,0:T(8,128)(2,1)}, bf16[512,256]{1,0:T(8,128)(2,1)}, u32[]{:S(2)}, u32[]{:S(2)}) collective-permute-start(bf16[512,256]{1,0:T(8,128)(2,1)} %slice.58), channel_id=1, source_target_pairs={{0,1},{2,3},{4,5},{6,7},{8,9},{10,11},{12,13},{14,15},{16,17},{18,... | collective-permute-start | bytes 786440 | tf_op jit(solution)/shard_map/ppermute | solution.py:84
  47.8 15.9 %copy-start.1 = (bf16[512,512]{0,1:T(8,128)(2,1)}, bf16[512,512]{0,1:T(8,128)(2,1)S(1)}, u32[]{:S(2)}) copy-start(bf16[512,512]{0,1:T(8,128)(2,1)S(1)} %copy.50) | copy-start | bytes 1572868
  63.7 9.2 %copy-start = (f32[2048,512,4]{1,0,2:T(8,128)}, f32[2048,512,4]{1,0,2:T(8,128)S(1)}, u32[]{:S(2)}) copy-start(f32[2048,512,4]{1,0,2:T(8,128)S(1)} %get-tuple-element.29) | copy-start | bytes 50331652
  77.0 9.0 %copy-start.2 = (bf16[512,512]{0,1:T(8,128)(2,1)S(1)}, bf16[512,512]{0,1:T(8,128)(2,1)}, u32[]{:S(2)}) copy-start(bf16[512,512]{0,1:T(8,128)(2,1)} %copy-done.1) | copy-start | bytes 1572868
  90.4 16.1 %collective-permute-start.3 = (f32[512,256]{1,0:T(8,128)}, f32[512,256]{1,0:T(8,128)}, u32[]{:S(2)}, u32[]{:S(2)}) collective-permute-start(f32[512,256]{1,0:T(8,128)} %get-tuple-element.14), channel_id=1, source_target_pairs={{1,0},{3,2},{5,4},{7,6},{9,8},{11,10},{13,12},{15,14},{17,16},{19,... | collective-permute-start | bytes 1572872 | tf_op jit(solution)/shard_map/ppermute | solution.py:133
  91.7 14.8 %collective-permute-start.5 = (f32[512,256]{1,0:T(8,128)}, f32[512,256]{1,0:T(8,128)}, u32[]{:S(2)}, u32[]{:S(2)}) collective-permute-start(f32[512,256]{1,0:T(8,128)} %get-tuple-element.15), channel_id=1, source_target_pairs={{9,6},{17,14},{25,22},{8,7},{16,15},{24,23}} | collective-permute-start | bytes 1572872 | tf_op jit(solution)/shard_map/ppermute | solution.py:139
  95.8 11.2 %collective-permute-start.4 = (f32[512,256]{1,0:T(8,128)}, f32[512,256]{1,0:T(8,128)}, u32[]{:S(2)}, u32[]{:S(2)}) collective-permute-start(f32[512,256]{1,0:T(8,128)} %get-tuple-element.12), channel_id=1, source_target_pairs={{8,6},{16,14},{24,22},{9,7},{17,15},{25,23}} | collective-permute-start | bytes 1572872 | tf_op jit(solution)/shard_map/ppermute | solution.py:138

commit v2 on v1

--- a/solution.py
+++ b/solution.py
@@ -72,13 +72,12 @@
     docs_all = doc_table(doc_starts, tok_dev)
     offsets = jnp.arange(tok_dev, dtype=jnp.int32)
 
-    packed = jnp.concatenate(
-        [queries[0, :, 0], keys[0, :, 0], values[0, :, 0], grad_out[0, :, 0]], axis=-1
-    )
-    arrived = lax.all_to_all(packed, "inner", 0, 0, tiled=True).reshape(tok_dev, -1)
-    query_buf = arrived[:, :width_q]
-    kv_own = arrived[:, width_q : width_q + 2 * head_dim]
-    grad_buf = arrived[:, width_q + 2 * head_dim :]
+    kv_packed = jnp.concatenate([keys[0, :, 0], values[0, :, 0]], axis=-1)
+    kv_own = lax.all_to_all(kv_packed, "inner", 0, 0, tiled=True).reshape(tok_dev, -1)
+    qg_packed = jnp.concatenate([queries[0, :, 0], grad_out[0, :, 0]], axis=-1)
+    qg_own = lax.all_to_all(qg_packed, "inner", 0, 0, tiled=True).reshape(tok_dev, -1)
+    query_buf = qg_own[:, :width_q]
+    grad_buf = qg_own[:, width_q:]
 
     pairs_up = [(2 * p, 2 * p + 1) for p in range(n_inner // 2)]
     kv_partner = lax.ppermute(kv_own, "inner", pairs_up)
@@ -139,17 +138,18 @@
     from_next_b = lax.ppermute(grads_b, both, back_b)
     kv_total = (kv_grads[3] + from_partner + from_next_a + from_next_b).astype(jnp.bfloat16)
 
-    result = jnp.concatenate([attn, q_grads, kv_total], axis=-1).reshape(
-        n_inner, piece_len, -1
+    out_rows = jnp.concatenate([attn, q_grads], axis=-1).reshape(n_inner, piece_len, -1)
+    out_back = lax.all_to_all(out_rows, "inner", 0, 0, tiled=True)
+    kv_back = lax.all_to_all(
+        kv_total.reshape(n_inner, piece_len, -1), "inner", 0, 0, tiled=True
     )
-    returned = lax.all_to_all(result, "inner", 0, 0, tiled=True)
     shape_q = (1, n_units, 1, piece_len, width_q)
     shape_k = (1, n_units, 1, piece_len, head_dim)
     return (
-        returned[..., :width_q].reshape(shape_q),
-        returned[..., width_q : 2 * width_q].reshape(shape_q),
-        returned[..., 2 * width_q : 2 * width_q + head_dim].reshape(shape_k),
-        returned[..., 2 * width_q + head_dim :].reshape(shape_k),
+        out_back[..., :width_q].reshape(shape_q),
+        out_back[..., width_q:].reshape(shape_q),
+        kv_back[..., :head_dim].reshape(shape_k),
+        kv_back[..., head_dim:].reshape(shape_k),
     )
 
 

time: 151 us -> 158 us (1.046)
  blocking collectives: 38.4 us -> 0 us
  waiting for transfers between devices: 41.4 us -> 65.8 us
  starting transfers between devices: 20.6 us -> 35.4 us
  matrix products: 25.1 us -> 29.6 us
  local copies, waits for them, and re-layouts: 7.89 us -> 11.5 us
    all_to_all x1 -> x0, blocking collectives: 38.4 us -> none  [shards(): returned = lax.all_to_all(result, 'inner', 0, 0, tiled=True)]
    all_to_all x1 -> x4, starting transfers between devices: 6.34 us -> 25.5 us  [the longest x1 9.17 us: shards(): lax.all_to_all(kv_total.reshape(n_inner, piece_len, -1), 'inner', 0, 0, t...]
    ppermute x1, waiting for transfers between devices: 3.34 us -> 20.8 us  [shards(): recv_a = lax.ppermute(kv_own, both, send_a)]
    ppermute x1, waiting for transfers between devices: 0.6 us -> 5.62 us  [shards(): from_next_a = lax.ppermute(grads_a, both, back_a)]
    ppermute x1, waiting for transfers between devices: 0.01 us -> 3.44 us  [shards(): from_next_b = lax.ppermute(grads_b, both, back_b)]
    dot_general x1, matrix products: 1.29 us -> 4.68 us  [attend(): jnp.einsum('hqk,kd->qhd', score_grads, key_buf, preferred_element_type=jn...]
    unnamed x9 -> x18, local copies, waits for them, and re-layouts: 2.56 us -> 5.72 us
    ppermute x1, starting transfers between devices: 4.15 us -> 1.32 us  [shards(): from_next_b = lax.ppermute(grads_b, both, back_b)]
  transfers between devices with their start and end apart: 7 -> 10, of which waited for: 5 -> 9; matrix products, arithmetic and copies ran while one was open for 7% -> 9% of each run, Pallas kernels for 0% -> 0%
where the time goes in v2:
time: 158 us; the launch traced here: 157 us
  waiting for transfers between devices  65.8 us (42%)
  starting transfers between devices  35.4 us (22%)
  matrix products  29.6 us (19%)
  other arithmetic  13.5 us (9%)
  local copies, waits for them, and re-layouts  11.5 us (7%)
    all_to_all x1, waiting for transfers between devices, shards(): out_back = lax.all_to_all(out_rows, 'inner', 0, 0, tiled=True)  23 us
    ppermute x1, waiting for transfers between devices, shards(): recv_a = lax.ppermute(kv_own, both, send_a)  20.8 us
    all_to_all x1, starting transfers between devices, shards(): lax.all_to_all(kv_total.reshape(n_inner, piece_len, -1), 'inner', 0, 0, t...  9.17 us
    dot_general x1, matrix products, attend(): jnp.einsum('qhd,kd->hqk', g_three, value_buf, preferred_element_type=jnp....  9.12 us
    all_to_all x1, starting transfers between devices, shards(): lax.all_to_all(kv_packed, 'inner', 0, 0, tiled=True).reshape(tok_dev, -1)  6.34 us
    unnamed x18, local copies, waits for them, and re-layouts  5.72 us
    ppermute x1, waiting for transfers between devices, shards(): from_next_a = lax.ppermute(grads_a, both, back_a)  5.62 us
    dot_general x1, matrix products, attend(): jnp.einsum('hqk,kd->qhd', probs_low, value_buf, preferred_element_type=jn...  5.28 us
  transfers between devices with their start and end apart: 10, of which 9 were waited for; matrix products, arithmetic and copies ran while one was open for 9% of the time, Pallas kernels for 0%

profile of v2, /device:TPU:1, one launch (start us, length us, event | category | flops | bytes accessed | tf_op | source)
XLA Modules:
  0.0 156.8 jit_solution(10157597359664454214)
XLA Ops:
  0.6 1.7 %pad_maximum_fusion.4 = bf16[8,64,256]{2,1,0:T(8,128)(2,1)} fusion(bf16[8,64,128]{2,1,0:T(8,128)(2,1)} %bitcast.94, bf16[8,64,128]{2,1,0:T(8,128)(2,1)} %bitcast.95), kind=kLoop, calls=%fused_computation.40 | loop fusion | flops 524288 | bytes 524288 | tf_op jit(solution)/shard_map/concatenate | solution.py:75
  2.3 6.3 %all-to-all-start = ((bf16[8,64,256]{2,1,0:T(8,128)(2,1)}), bf16[8,64,256]{2,1,0:T(8,128)(2,1)S(1)}, u32[]{:S(2)}, u32[]{:S(2)}) async-start(bf16[8,64,256]{2,1,0:T(8,128)(2,1)} %pad_maximum_fusion.4), calls=%async_computation | async-start | bytes 524288 | tf_op jit(solution)/shard_map/all_to_all | solution.py:76
  8.7 0.7 copy.63
  9.5 0.7 convert_reduce_fusion.1
  10.3 0.1 reduce.1
  10.5 2.3 %pad_maximum_fusion.1 = bf16[8,64,1024]{2,1,0:T(8,128)(2,1)} fusion(bf16[8,64,512]{2,1,0:T(8,128)(2,1)} %bitcast.92, bf16[8,64,512]{2,1,0:T(8,128)(2,1)} %bitcast.93), kind=kLoop, calls=%fused_computation.24 | loop fusion | flops 2097152 | bytes 2097152 | tf_op jit(solution)/shard_map/concatenate | solution.py:77
  12.8 3.3 %all-to-all-done = bf16[8,64,256]{2,1,0:T(8,128)(2,1)S(1)} async-done(((bf16[8,64,256]{2,1,0:T(8,128)(2,1)}), bf16[8,64,256]{2,1,0:T(8,128)(2,1)S(1)}, u32[]{:S(2)}, u32[]{:S(2)}) %all-to-all-start) | async-done | bytes 262176 | tf_op jit(solution)/shard_map/all_to_all | solution.py:76
  16.1 4.7 %all-to-all-start.1 = ((bf16[8,64,1024]{2,1,0:T(8,128)(2,1)}), bf16[8,64,1024]{2,1,0:T(8,128)(2,1)S(1)}, u32[]{:S(2)}, u32[]{:S(2)}) async-start(bf16[8,64,1024]{2,1,0:T(8,128)(2,1)} %pad_maximum_fusion.1), calls=%async_computation.1 | async-start | bytes 2097152 | tf_op jit(solution)/shard_map/all_to_all | solution.py:78
  20.9 0.1 convert_reduce_fusion
  21.1 3.4 %collective-permute-start.2 = (bf16[512,256]{1,0:T(8,128)(2,1)S(1)}, bf16[512,256]{1,0:T(8,128)(2,1)S(1)}, u32[]{:S(2)}, u32[]{:S(2)}) collective-permute-start(bf16[512,256]{1,0:T(8,128)(2,1)S(1)} %bitcast.84), channel_id=1, source_target_pairs={{0,1},{2,3},{4,5},{6,7},{8,9},{10,11},{12,13},{14,15},{16,17},{18,... | collective-permute-start | bytes 786440 | tf_op jit(solution)/shard_map/ppermute | solution.py:83
  24.5 1.3 collective-permute-start
  25.8 1.3 collective-permute-start.1
  27.1 1.6 %compare_and_fusion = pred[512,2048]{0,1:T(8,128)(4,1)S(1)} fusion(s32[512]{0:T(512)S(1)} %iota_add_fusion, s32[512]{0:T(512)S(1)} %bitcast.97, s32[2048]{0:T(1024)S(1)} %pad_add_fusion.1, s32[2048]{0:T(1024)S(1)} %pad_add_fusion), kind=kLoop, calls=%fused_computation.8 | loop fusion | flops 3145728 | bytes 1069056 | tf_op jit(solution)/shard_map/and | solution.py:32
  28.6 20.8 %collective-permute-done = bf16[512,256]{1,0:T(8,128)(2,1)S(1)} collective-permute-done((bf16[512,256]{1,0:T(8,128)(2,1)S(1)}, bf16[512,256]{1,0:T(8,128)(2,1)S(1)}, u32[]{:S(2)}, u32[]{:S(2)}) %collective-permute-start) | collective-permute-done | bytes 262176 | tf_op jit(solution)/shard_map/ppermute | solution.py:93
  49.5 4.8 %collective-permute-done.1 = bf16[512,256]{1,0:T(8,128)(2,1)S(1)} collective-permute-done((bf16[512,256]{1,0:T(8,128)(2,1)S(1)}, bf16[512,256]{1,0:T(8,128)(2,1)S(1)}, u32[]{:S(2)}, u32[]{:S(2)}) %collective-permute-start.1) | collective-permute-done | bytes 262176 | tf_op jit(solution)/shard_map/ppermute | solution.py:94
  54.4 0.7 copy-done.7
  55.1 1.0 pad_maximum_fusion
  56.1 0.6 all-to-all-done.1
  56.7 1.0 fusion.19
  57.7 1.3 copy.64
  59.0 1.4 copy.69
  60.5 2.9 %fusion.3 = (f32[4,512]{1,0:T(4,128)S(1)}, f32[2048,512,4]{1,0,2:T(8,128)S(1)}) fusion(pred[512,2048]{0,1:T(8,128)(4,1)S(1)} %compare_and_fusion, bf16[512,4,128]{0,2,1:T(8,128)(2,1)S(1)} %bitcast.88, bf16[2048,256]{1,0:T(8,128)(2,1)S(1)} %pad_maximum_fusion), kind=kOutput, calls=%fused_computation.7 | convolution fusion | flops 1086322688 | bytes 18882560 | tf_op jit(solution)/shard_map/qhd,kd->hqk/dot_general | solution.py:30
  63.4 3.6 %exponential_reduce_fusion = f32[4,512]{1,0:T(4,128)S(1)} fusion(f32[2048,512,4]{1,0,2:T(8,128)S(1)} %get-tuple-element.33, f32[4,512]{1,0:T(4,128)S(1)} %get-tuple-element.32, pred[512,2048]{0,1:T(8,128)(4,1)S(1)} %compare_and_fusion), kind=kLoop, calls=%fused_computation.5 | loop fusion | flops 16775168 | bytes 17842176 | tf_op jit(solution)/shard_map/reduce_sum | solution.py:35
  67.1 5.3 %multiply_reduce_fusion = (f32[512,4]{0,1:T(4,128)S(1)}, bf16[512,4,128]{0,2,1:T(8,128)(2,1)}) fusion(bf16[512,512]{0,1:T(8,128)(2,1)S(1)} %copy.69, f32[2048,512,4]{1,0,2:T(8,128)S(1)} %get-tuple-element.33, f32[4,512]{1,0:T(4,128)S(1)} %log_add_fusion, pred[512,2048]{0,1:T(8,128)(4,1)S(1)} %compare_and_fusion, bf16[2048,256]{1,0:T(8,128)(2,1)S(1)} %pad_maximum_fusion), kind=kOutput, calls=%fused_computation.26 | convolution fusion | flops 1091827712 | bytes 19415040 | tf_op jit(solution)/shard_map/hqk,kd->qhd/dot_general | solution.py:38
  72.3 5.2 %convolution_bitcast_fusion = f32[2048,128]{1,0:T(8,128)S(1)} fusion(bf16[512,4,128]{0,2,1:T(8,128)(2,1)} %bitcast.90, f32[2048,512,4]{1,0,2:T(8,128)S(1)} %get-tuple-element.33, f32[4,512]{1,0:T(4,128)S(1)} %log_add_fusion, pred[512,2048]{0,1:T(8,128)(4,1)S(1)} %compare_and_fusion), kind=kOutput, calls=%fused_computation.15 | convolution fusion | flops 1090519040 | bytes 19406848 | tf_op jit(solution)/shard_map/hqk,qhd->kd/dot_general | solution.py:52
  77.6 9.1 %fusion.1 = bf16[4,512,2048]{1,2,0:T(8,128)(2,1)S(1)} fusion(f32[2048,512,4]{1,0,2:T(8,128)} %copy-done.1, f32[4,512]{1,0:T(4,128)S(1)} %bitcast.101, f32[4,512]{1,0:T(4,128)S(1)} %log_add_fusion, pred[512,2048]{0,1:T(8,128)(4,1)S(1)} %compare_and_fusion, bf16[512,4,128]{0,2,1:T(8,128)(2,1)S(1)} %bitcast.91, bf16[2048,256]{1,0:T(8,128)(2,1)S(1)} %pad_maximum_fusion), kind=kOutput, calls=%fused_computation.2 | convolution fusion | flops 1098907648 | bytes 27279360 | tf_op jit(solution)/shard_map/qhd,kd->hqk/dot_general | solution.py:42
  86.8 3.2 %copy-done = bf16[4,512,2048]{1,2,0:T(8,128)(2,1)} copy-done((bf16[4,512,2048]{1,2,0:T(8,128)(2,1)}, bf16[4,512,2048]{1,2,0:T(8,128)(2,1)S(1)}, u32[]{:S(2)}) %copy-start) | copy-done | bytes 8388632
  90.0 2.4 %fusion.4 = f32[2048,128]{1,0:T(8,128)S(1)} fusion(bf16[4,512,2048]{1,2,0:T(8,128)(2,1)S(1)} %fusion.1, bf16[512,4,128]{0,2,1:T(8,128)(2,1)S(1)} %bitcast.89), kind=kOutput, calls=%fused_computation.17 | convolution fusion | flops 1074003968 | bytes 9961472 | tf_op jit(solution)/shard_map/hqk,qhd->kd/dot_general | solution.py:49
  92.5 0.1 fusion.14
  92.6 1.3 collective-permute-start.5
  93.9 1.3 collective-permute-start.4
  95.2 1.3 collective-permute-start.3
  96.5 3.4 %collective-permute-done.5 = f32[512,256]{1,0:T(8,128)S(1)} collective-permute-done((f32[512,256]{1,0:T(8,128)S(1)}, f32[512,256]{1,0:T(8,128)S(1)}, u32[]{:S(2)}, u32[]{:S(2)}) %collective-permute-start.5) | collective-permute-done | bytes 524320 | tf_op jit(solution)/shard_map/ppermute | solution.py:138
  100.0 5.6 %collective-permute-done.4 = f32[512,256]{1,0:T(8,128)S(1)} collective-permute-done((f32[512,256]{1,0:T(8,128)S(1)}, f32[512,256]{1,0:T(8,128)S(1)}, u32[]{:S(2)}, u32[]{:S(2)}) %collective-permute-start.4) | collective-permute-done | bytes 524320 | tf_op jit(solution)/shard_map/ppermute | solution.py:137
  105.6 4.0 %collective-permute-done.3 = f32[512,256]{1,0:T(8,128)S(1)} collective-permute-done((f32[512,256]{1,0:T(8,128)S(1)}, f32[512,256]{1,0:T(8,128)S(1)}, u32[]{:S(2)}, u32[]{:S(2)}) %collective-permute-start.3) | collective-permute-done | bytes 524320 | tf_op jit(solution)/shard_map/ppermute | solution.py:132
  109.6 0.8 fusion.13
  110.4 9.2 %all-to-all-start.3 = ((bf16[8,64,256]{2,1,0:T(8,128)(2,1)}), bf16[8,64,256]{2,1,0:T(8,128)(2,1)S(1)}, u32[]{:S(2)}, u32[]{:S(2)}) async-start(bf16[8,64,256]{2,1,0:T(8,128)(2,1)} %bitcast.28), calls=%async_computation.3 | async-start | bytes 524288 | tf_op jit(solution)/shard_map/all_to_all | solution.py:143
  119.6 4.7 %fusion.7 = bf16[512,4,128]{0,2,1:T(8,128)(2,1)S(1)} fusion(bf16[4,512,2048]{1,2,0:T(8,128)(2,1)} %copy-done, bf16[2048,256]{1,0:T(8,128)(2,1)S(1)} %pad_maximum_fusion), kind=kOutput, calls=%fused_computation.22 | convolution fusion | flops 1074266112 | bytes 9437184 | tf_op jit(solution)/shard_map/hqk,kd->qhd/dot_general | solution.py:45
  124.3 0.3 copy.73
  124.6 0.2 concatenate.32
  124.8 0.3 copy.68
  125.2 0.2 concatenate.31
  125.4 1.1 pad_maximum_fusion.2
  126.5 0.2 all-to-all-done.3
  126.7 5.2 %all-to-all-start.2 = ((bf16[8,64,1024]{2,1,0:T(8,128)(2,1)}), bf16[8,64,1024]{2,1,0:T(8,128)(2,1)S(1)}, u32[]{:S(2)}, u32[]{:S(2)}) async-start(bf16[8,64,1024]{2,1,0:T(8,128)(2,1)} %pad_maximum_fusion.2), calls=%async_computation.2 | async-start | bytes 2097152 | tf_op jit(solution)/shard_map/all_to_all | solution.py:142
  131.9 0.8 slice_bitcast_fusion.8
  132.7 23.0 %all-to-all-done.2 = bf16[8,64,1024]{2,1,0:T(8,128)(2,1)S(1)} async-done(((bf16[8,64,1024]{2,1,0:T(8,128)(2,1)}), bf16[8,64,1024]{2,1,0:T(8,128)(2,1)S(1)}, u32[]{:S(2)}, u32[]{:S(2)}) %all-to-all-start.2) | async-done | bytes 1048608 | tf_op jit(solution)/shard_map/all_to_all | solution.py:142
  155.7 1.1 slice_bitcast_fusion
  (30 shorter events, 0.6 us)
Async XLA Ops:
  2.3 13.8 %all-to-all-start = ((bf16[8,64,256]{2,1,0:T(8,128)(2,1)}), bf16[8,64,256]{2,1,0:T(8,128)(2,1)S(1)}, u32[]{:S(2)}, u32[]{:S(2)}) async-start(bf16[8,64,256]{2,1,0:T(8,128)(2,1)} %pad_maximum_fusion.4), calls=%async_computation | async-start | bytes 524288 | tf_op jit(solution)/shard_map/all_to_all | solution.py:76
  16.1 40.6 %all-to-all-start.1 = ((bf16[8,64,1024]{2,1,0:T(8,128)(2,1)}), bf16[8,64,1024]{2,1,0:T(8,128)(2,1)S(1)}, u32[]{:S(2)}, u32[]{:S(2)}) async-start(bf16[8,64,1024]{2,1,0:T(8,128)(2,1)} %pad_maximum_fusion.1), calls=%async_computation.1 | async-start | bytes 2097152 | tf_op jit(solution)/shard_map/all_to_all | solution.py:78
  21.1 33.3 %collective-permute-start.2 = (bf16[512,256]{1,0:T(8,128)(2,1)S(1)}, bf16[512,256]{1,0:T(8,128)(2,1)S(1)}, u32[]{:S(2)}, u32[]{:S(2)}) collective-permute-start(bf16[512,256]{1,0:T(8,128)(2,1)S(1)} %bitcast.84), channel_id=1, source_target_pairs={{0,1},{2,3},{4,5},{6,7},{8,9},{10,11},{12,13},{14,15},{16,17},{18,... | collective-permute-start | bytes 786440 | tf_op jit(solution)/shard_map/ppermute | solution.py:83
  24.5 25.0 %collective-permute-start = (bf16[512,256]{1,0:T(8,128)(2,1)S(1)}, bf16[512,256]{1,0:T(8,128)(2,1)S(1)}, u32[]{:S(2)}, u32[]{:S(2)}) collective-permute-start(bf16[512,256]{1,0:T(8,128)(2,1)S(1)} %bitcast.85), channel_id=1, source_target_pairs={{6,8},{14,16},{22,24},{7,9},{15,17},{23,25}} | collective-permute-start | bytes 786440 | tf_op jit(solution)/shard_map/ppermute | solution.py:93
  25.8 28.5 %collective-permute-start.1 = (bf16[512,256]{1,0:T(8,128)(2,1)S(1)}, bf16[512,256]{1,0:T(8,128)(2,1)S(1)}, u32[]{:S(2)}, u32[]{:S(2)}) collective-permute-start(bf16[512,256]{1,0:T(8,128)(2,1)S(1)} %bitcast.86), channel_id=1, source_target_pairs={{6,9},{14,17},{22,25},{7,8},{15,16},{23,24}} | collective-permute-start | bytes 786440 | tf_op jit(solution)/shard_map/ppermute | solution.py:94
  54.3 0.7 copy-start.7
  59.0 8.0 %copy-start.3 = (bf16[512,512]{0,1:T(8,128)(2,1)}, bf16[512,512]{0,1:T(8,128)(2,1)S(1)}, u32[]{:S(2)}) copy-start(bf16[512,512]{0,1:T(8,128)(2,1)S(1)} %copy.64) | copy-start | bytes 1572868
  60.4 6.6 %copy-start.5 = (bf16[512,512]{0,1:T(8,128)(2,1)}, bf16[512,512]{0,1:T(8,128)(2,1)S(1)}, u32[]{:S(2)}) copy-start(bf16[512,512]{0,1:T(8,128)(2,1)S(1)} %copy.69) | copy-start | bytes 1572868
  63.4 9.0 %copy-start.1 = (f32[2048,512,4]{1,0,2:T(8,128)}, f32[2048,512,4]{1,0,2:T(8,128)S(1)}, u32[]{:S(2)}) copy-start(f32[2048,512,4]{1,0,2:T(8,128)S(1)} %get-tuple-element.33) | copy-start | bytes 50331652
  72.3 5.3 %copy-start.6 = (bf16[512,512]{0,1:T(8,128)(2,1)S(1)}, bf16[512,512]{0,1:T(8,128)(2,1)}, u32[]{:S(2)}) copy-start(bf16[512,512]{0,1:T(8,128)(2,1)} %copy-done.5) | copy-start | bytes 1572868
  77.6 12.4 %copy-start.4 = (bf16[512,512]{0,1:T(8,128)(2,1)S(1)}, bf16[512,512]{0,1:T(8,128)(2,1)}, u32[]{:S(2)}) copy-start(bf16[512,512]{0,1:T(8,128)(2,1)} %copy-done.3) | copy-start | bytes 1572868
  86.7 3.2 %copy-start = (bf16[4,512,2048]{1,2,0:T(8,128)(2,1)}, bf16[4,512,2048]{1,2,0:T(8,128)(2,1)S(1)}, u32[]{:S(2)}) copy-start(bf16[4,512,2048]{1,2,0:T(8,128)(2,1)S(1)} %fusion.1) | copy-start | bytes 25165828
  92.4 32.5 %copy-start.2 = (bf16[512,4,128]{0,2,1:T(8,128)(2,1)S(1)}, bf16[512,4,128]{0,2,1:T(8,128)(2,1)}, u32[]{:S(2)}) copy-start(bf16[512,4,128]{0,2,1:T(8,128)(2,1)} %get-tuple-element.35) | copy-start | bytes 1572868
  92.6 7.4 %collective-permute-start.5 = (f32[512,256]{1,0:T(8,128)S(1)}, f32[512,256]{1,0:T(8,128)S(1)}, u32[]{:S(2)}, u32[]{:S(2)}) collective-permute-start(f32[512,256]{1,0:T(8,128)S(1)} %get-tuple-element.19), channel_id=1, source_target_pairs={{9,6},{17,14},{25,22},{8,7},{16,15},{24,23}} | collective-permute-start | bytes 1572872 | tf_op jit(solution)/shard_map/ppermute | solution.py:138
  93.9 11.7 %collective-permute-start.4 = (f32[512,256]{1,0:T(8,128)S(1)}, f32[512,256]{1,0:T(8,128)S(1)}, u32[]{:S(2)}, u32[]{:S(2)}) collective-permute-start(f32[512,256]{1,0:T(8,128)S(1)} %get-tuple-element.16), channel_id=1, source_target_pairs={{8,6},{16,14},{24,22},{9,7},{17,15},{25,23}} | collective-permute-start | bytes 1572872 | tf_op jit(solution)/shard_map/ppermute | solution.py:137
  95.2 14.4 %collective-permute-start.3 = (f32[512,256]{1,0:T(8,128)S(1)}, f32[512,256]{1,0:T(8,128)S(1)}, u32[]{:S(2)}, u32[]{:S(2)}) collective-permute-start(f32[512,256]{1,0:T(8,128)S(1)} %get-tuple-element.18), channel_id=1, source_target_pairs={{1,0},{3,2},{5,4},{7,6},{9,8},{11,10},{13,12},{15,14},{17,16},{19,... | collective-permute-start | bytes 1572872 | tf_op jit(solution)/shard_map/ppermute | solution.py:132
  110.4 16.2 %all-to-all-start.3 = ((bf16[8,64,256]{2,1,0:T(8,128)(2,1)}), bf16[8,64,256]{2,1,0:T(8,128)(2,1)S(1)}, u32[]{:S(2)}, u32[]{:S(2)}) async-start(bf16[8,64,256]{2,1,0:T(8,128)(2,1)} %bitcast.28), calls=%async_computation.3 | async-start | bytes 524288 | tf_op jit(solution)/shard_map/all_to_all | solution.py:143
  126.7 29.0 %all-to-all-start.2 = ((bf16[8,64,1024]{2,1,0:T(8,128)(2,1)}), bf16[8,64,1024]{2,1,0:T(8,128)(2,1)S(1)}, u32[]{:S(2)}, u32[]{:S(2)}) async-start(bf16[8,64,1024]{2,1,0:T(8,128)(2,1)} %pad_maximum_fusion.2), calls=%async_computation.2 | async-start | bytes 2097152 | tf_op jit(solution)/shard_map/all_to_all | solution.py:142

commit v3 on v1

--- a/solution.py
+++ b/solution.py
@@ -1,8 +1,11 @@
+import functools
 import math
 
 import jax
 import jax.numpy as jnp
 from jax import lax
+from jax.experimental import pallas as pl
+from jax.experimental.pallas import tpu as pltpu
 from jax.sharding import PartitionSpec as P
 
 
@@ -18,44 +21,83 @@
     return (first_index[:, None] + inside_count - 1).reshape(n_outer, n_inner, tok_dev)
 
 
+def attention_kernel(
+    qdoc_ref, qpos_ref, kdoc_ref, kpos_ref, q_ref, g_ref, k_ref, v_ref,
+    o_ref, dq_ref, dk_ref, dv_ref, *, scaling
+):
+    @pl.when((pl.program_id(0) == 0) & (pl.program_id(1) == 0))
+    def _():
+        dk_ref[...] = jnp.zeros_like(dk_ref)
+        dv_ref[...] = jnp.zeros_like(dv_ref)
+
+    q = q_ref[...]
+    g = g_ref[...]
+    k = k_ref[...]
+    v = v_ref[...]
+    contract_last = (((1,), (1,)), ((), ()))
+    contract_first = (((0,), (0,)), ((), ()))
+    scores = lax.dot_general(q, k, contract_last, preferred_element_type=jnp.float32) * scaling
+    allowed = (qdoc_ref[...] == kdoc_ref[...]) & (kpos_ref[...] <= qpos_ref[...])
+    scores = jnp.where(allowed, scores, -jnp.inf)
+    row_max = jnp.max(scores, axis=1, keepdims=True)
+    log_total = row_max + jnp.log(jnp.sum(jnp.exp(scores - row_max), axis=1, keepdims=True))
+    probs = jnp.exp(scores - log_total)
+    probs_low = probs.astype(jnp.bfloat16)
+    attn = jnp.dot(probs_low, v, preferred_element_type=jnp.float32).astype(jnp.bfloat16)
+    o_ref[...] = attn
+    inner_prod = jnp.sum(
+        g.astype(jnp.float32) * attn.astype(jnp.float32), axis=1, keepdims=True
+    )
+    grad_probs = lax.dot_general(g, v, contract_last, preferred_element_type=jnp.float32)
+    score_grads = (probs * (grad_probs - inner_prod)).astype(jnp.bfloat16)
+    dq_ref[...] = (
+        jnp.dot(score_grads, k, preferred_element_type=jnp.float32) * scaling
+    ).astype(jnp.bfloat16)
+    dk_ref[...] += (
+        lax.dot_general(score_grads, q, contract_first, preferred_element_type=jnp.float32)
+        * scaling
+    )
+    dv_ref[...] += lax.dot_general(
+        probs_low, g, contract_first, preferred_element_type=jnp.float32
+    )
+
+
 def attend(
     query_buf, grad_buf, query_pos, query_doc, key_buf, value_buf, key_pos, key_doc, n_heads
 ):
-    n_rows = query_buf.shape[0]
-    head_dim = key_buf.shape[1]
-    scaling = 1.0 / math.sqrt(head_dim)
-    q_three = query_buf.reshape(n_rows, n_heads, head_dim)
-    g_three = grad_buf.reshape(n_rows, n_heads, head_dim)
-    scores = (
-        jnp.einsum("qhd,kd->hqk", q_three, key_buf, preferred_element_type=jnp.float32) * scaling
-    )
-    allowed = (query_doc[:, None] == key_doc[None, :]) & (key_pos[None, :] <= query_pos[:, None])
-    scores = jnp.where(allowed[None], scores, -jnp.inf)
-    row_max = jnp.max(scores, axis=2, keepdims=True)
-    log_total = row_max + jnp.log(jnp.sum(jnp.exp(scores - row_max), axis=2, keepdims=True))
-    probs = jnp.exp(scores - log_total)
-    probs_low = probs.astype(jnp.bfloat16)
-    attn = jnp.einsum(
-        "hqk,kd->qhd", probs_low, value_buf, preferred_element_type=jnp.float32
-    ).astype(jnp.bfloat16)
-    inner_prod = jnp.sum(g_three.astype(jnp.float32) * attn.astype(jnp.float32), axis=2)
-    grad_probs = jnp.einsum("qhd,kd->hqk", g_three, value_buf, preferred_element_type=jnp.float32)
-    score_grads = (probs * (grad_probs - inner_prod.T[:, :, None])).astype(jnp.bfloat16)
-    q_grads = (
-        jnp.einsum("hqk,kd->qhd", score_grads, key_buf, preferred_element_type=jnp.float32)
-        * scaling
-    )
-    k_grads = (
-        jnp.einsum("hqk,qhd->kd", score_grads, q_three, preferred_element_type=jnp.float32)
-        * scaling
-    )
-    v_grads = jnp.einsum("hqk,qhd->kd", probs_low, g_three, preferred_element_type=jnp.float32)
-    return (
-        attn.reshape(n_rows, -1),
-        q_grads.astype(jnp.bfloat16).reshape(n_rows, -1),
-        k_grads,
-        v_grads,
-    )
+    n_rows, width_q = query_buf.shape
+    n_keys, head_dim = key_buf.shape
+    block_q = min(256, n_rows)
+    grid = (n_rows // block_q, n_heads)
+    row_spec = pl.BlockSpec((block_q, head_dim), lambda i, h: (i, h))
+    col_spec = pl.BlockSpec((block_q, 1), lambda i, h: (i, 0))
+    key_meta_spec = pl.BlockSpec((1, n_keys), lambda i, h: (0, 0))
+    key_spec = pl.BlockSpec((n_keys, head_dim), lambda i, h: (0, 0))
+    kernel = functools.partial(attention_kernel, scaling=1.0 / math.sqrt(head_dim))
+    attn, q_grads, k_grads, v_grads = pl.pallas_call(
+        kernel,
+        grid=grid,
+        in_specs=[col_spec, col_spec, key_meta_spec, key_meta_spec,
+                  row_spec, row_spec, key_spec, key_spec],
+        out_specs=[row_spec, row_spec, key_spec, key_spec],
+        out_shape=[
+            jax.ShapeDtypeStruct((n_rows, width_q), jnp.bfloat16),
+            jax.ShapeDtypeStruct((n_rows, width_q), jnp.bfloat16),
+            jax.ShapeDtypeStruct((n_keys, head_dim), jnp.float32),
+            jax.ShapeDtypeStruct((n_keys, head_dim), jnp.float32),
+        ],
+        compiler_params=pltpu.CompilerParams(dimension_semantics=("arbitrary", "arbitrary")),
+    )(
+        query_doc.reshape(n_rows, 1),
+        query_pos.reshape(n_rows, 1),
+        key_doc.reshape(1, n_keys),
+        key_pos.reshape(1, n_keys),
+        query_buf,
+        grad_buf,
+        key_buf,
+        value_buf,
+    )
+    return attn, q_grads, k_grads, v_grads
 
 
 def shards(queries, keys, values, grad_out, doc_starts):

time: 151 us -> 143 us (0.947); the launches traced: 149 us -> 143 us
  matrix products: 25.1 us -> 0 us
  Pallas kernels: 0 us -> 23.6 us
  other arithmetic: 14.7 us -> 5.36 us
  waiting for transfers between devices: 41.4 us -> 47.1 us
  blocking collectives: 38.4 us -> 40.1 us
  starting transfers between devices: 20.6 us -> 18.9 us
    dot_general x6 -> x0, matrix products: 25.1 us -> none  [the longest x1 8.96 us: attend(): jnp.einsum('qhd,kd->hqk', g_three, value_buf, preferred_element_type=jnp....]
    pallas_call x0 -> x1, Pallas kernels: none -> 23.6 us  [attend(): pl.pallas_call(kernel, grid=grid, in_specs=[col_spec, col_spec, key_meta_...]
    reduce_sum x1 -> x0, other arithmetic: 3.82 us -> none  [attend(): jnp.sum(jnp.exp(scores - row_max), axis=2, keepdims=True)]
    ppermute x1, waiting for transfers between devices: 0.01 us -> 2.87 us  [shards(): from_next_b = lax.ppermute(grads_b, both, back_b)]
    convert_element_type x2 -> x0, local copies, waits for them, and re-layouts: 2.43 us -> none  [the longest x1 2.12 us: attend(): attn = jnp.einsum('hqk,kd->qhd', probs_low, value_buf, preferred_element_...]
    ppermute x1, waiting for transfers between devices: 3.34 us -> 5.41 us  [shards(): from_partner = lax.ppermute(kv_grads[2], 'inner', pairs_down)]
    slice x2, local copies, waits for them, and re-layouts: 0.29 us -> 2.11 us  [the longest x1 1.06 us: shards(): ctx[:, head_dim:]]
    all_to_all x1, blocking collectives: 38.4 us -> 40.1 us  [shards(): returned = lax.all_to_all(result, 'inner', 0, 0, tiled=True)]
  transfers between devices with their start and end apart: 7 -> 7, of which waited for: 5 -> 5; matrix products, arithmetic and copies ran while one was open for 7% -> 3% of each run, Pallas kernels for 0% -> 0%
where the time goes in v3:
time: 143 us
  waiting for transfers between devices  47.1 us (33%)
  blocking collectives  40.1 us (28%)
  Pallas kernels  23.6 us (17%)
  starting transfers between devices  18.9 us (13%)
  local copies, waits for them, and re-layouts  6.69 us (5%)
  other arithmetic  5.36 us (4%)
    all_to_all x1, blocking collectives, shards(): returned = lax.all_to_all(result, 'inner', 0, 0, tiled=True)  40.1 us
    all_to_all x1, waiting for transfers between devices, shards(): lax.all_to_all(packed, 'inner', 0, 0, tiled=True).reshape(tok_dev, -1)  27.1 us
    pallas_call x1, Pallas kernels, attend(): pl.pallas_call(kernel, grid=grid, in_specs=[col_spec, col_spec, key_meta_...  23.6 us
    ppermute x1, waiting for transfers between devices, shards(): recv_b = lax.ppermute(kv_own, both, send_b)  7.6 us
    all_to_all x1, starting transfers between devices, shards(): lax.all_to_all(packed, 'inner', 0, 0, tiled=True).reshape(tok_dev, -1)  6.34 us
    ppermute x1, waiting for transfers between devices, shards(): from_partner = lax.ppermute(kv_grads[2], 'inner', pairs_down)  5.41 us
    ppermute x1, waiting for transfers between devices, shards(): recv_a = lax.ppermute(kv_own, both, send_a)  4.13 us
    ppermute x1, starting transfers between devices, shards(): kv_partner = lax.ppermute(kv_own, 'inner', pairs_up)  3.43 us
  transfers between devices with their start and end apart: 7, of which 5 were waited for; matrix products, arithmetic and copies ran while one was open for 3% of the time, Pallas kernels for 0%

profile of v3, /device:TPU:1, one launch (start us, length us, event | category | flops | bytes accessed | tf_op | source)
XLA Modules:
  0.0 142.6 jit_solution(2372851876188440911)
XLA Ops:
  0.6 0.0 copy-start.3
  0.6 2.5 %pad_maximum_fusion = bf16[8,64,1280]{2,1,0:T(8,128)(2,1)} fusion(bf16[8,64,512]{2,1,0:T(8,128)(2,1)} %bitcast.30, bf16[8,64,128]{2,1,0:T(8,128)(2,1)} %bitcast.32, bf16[8,64,128]{2,1,0:T(8,128)(2,1)} %bitcast.33, bf16[8,64,512]{2,1,0:T(8,128)(2,1)} %bitcast.31), kind=kLoop, calls=%fused_computation | loop fusion | flops 5242880 | bytes 2621440 | tf_op jit(solution)/shard_map/concatenate | solution.py:117
  3.2 6.3 %all-to-all-start = ((bf16[8,64,1280]{2,1,0:T(8,128)(2,1)}), bf16[8,64,1280]{2,1,0:T(8,128)(2,1)S(1)}, u32[]{:S(2)}, u32[]{:S(2)}) async-start(bf16[8,64,1280]{2,1,0:T(8,128)(2,1)} %pad_maximum_fusion), calls=%async_computation | async-start | bytes 2621440 | tf_op jit(solution)/shard_map/all_to_all | solution.py:120
  9.5 0.0 copy-done.3
  9.5 0.1 le.15
  9.6 0.1 reshape.92
  9.7 0.1 reduce-window.4
  9.8 0.1 reduce.1
  9.9 0.1 reshape.83
  10.0 0.1 convert_reduce_fusion
  10.1 0.1 fusion.3
  10.2 0.9 copy.18.qdoc_ref
  11.0 0.6 pad_add_fusion.1
  11.6 0.6 pad_add_fusion
  12.3 0.7 iota_add_fusion.qpos_ref
  13.0 27.1 %all-to-all-done = bf16[8,64,1280]{2,1,0:T(8,128)(2,1)S(1)} async-done(((bf16[8,64,1280]{2,1,0:T(8,128)(2,1)}), bf16[8,64,1280]{2,1,0:T(8,128)(2,1)S(1)}, u32[]{:S(2)}, u32[]{:S(2)}) %all-to-all-start) | async-done | bytes 1310752 | tf_op jit(solution)/shard_map/all_to_all | solution.py:120
  40.1 3.4 %collective-permute-start.2 = (bf16[512,256]{1,0:T(8,128)(2,1)S(1)}, bf16[512,256]{1,0:T(8,128)(2,1)S(1)}, u32[]{:S(2)}, u32[]{:S(2)}) collective-permute-start(bf16[512,256]{1,0:T(8,128)(2,1)S(1)} %slice.60), channel_id=1, source_target_pairs={{0,1},{2,3},{4,5},{6,7},{8,9},{10,11},{12,13},{14,15},{16,17},{18,... | collective-permute-start | bytes 786440 | tf_op jit(solution)/shard_map/ppermute | solution.py:126
  43.5 1.3 collective-permute-start.1
  44.8 1.3 collective-permute-start
  46.1 1.0 fusion.5
  47.2 7.6 %collective-permute-done.1 = bf16[512,256]{1,0:T(8,128)(2,1)S(1)} collective-permute-done((bf16[512,256]{1,0:T(8,128)(2,1)S(1)}, bf16[512,256]{1,0:T(8,128)(2,1)S(1)}, u32[]{:S(2)}, u32[]{:S(2)}) %collective-permute-start.1) | collective-permute-done | bytes 262176 | tf_op jit(solution)/shard_map/ppermute | solution.py:137
  54.8 4.1 %collective-permute-done = bf16[512,256]{1,0:T(8,128)(2,1)S(1)} collective-permute-done((bf16[512,256]{1,0:T(8,128)(2,1)S(1)}, bf16[512,256]{1,0:T(8,128)(2,1)S(1)}, u32[]{:S(2)}, u32[]{:S(2)}) %collective-permute-start) | collective-permute-done | bytes 262176 | tf_op jit(solution)/shard_map/ppermute | solution.py:136
  59.0 0.0 collective-permute-done.2
  59.0 0.1 pad_maximum_fusion.2
  59.1 1.1 fusion.6
  60.1 23.6 %shard_map.84 = (bf16[512,512]{1,0:T(8,128)(2,1)}, bf16[512,512]{1,0:T(8,128)(2,1)}, f32[2048,128]{1,0:T(8,128)}, f32[2048,128]{1,0:T(8,128)}) custom-call(s32[512,1]{1,0:T(8,128)} %copy.18.qdoc_ref, s32[512,1]{1,0:T(8,128)} %iota_add_fusion.qpos_ref, s32[1,2048]{1,0:T(1,128)} %bitcast.35, s32[1,2048]{1,0:T(1,128)} %bitcast.34, ...), custom_call_target="tpu_custom_call" | custom-call | tf_op jit(solution)/shard_map/pallas_call | solution.py:77
  83.7 0.0 copy-start
  83.7 1.4 constant_dynamic-update-slice_fusion.1
  85.1 0.1 copy-done
  85.2 0.1 constant_dynamic-update-slice_fusion
  85.3 0.0 copy-start.1
  85.3 0.0 copy-start.2
  85.3 0.2 fusion.4
  85.5 1.4 collective-permute-start.3
  86.9 1.7 %collective-permute-start.4 = (f32[512,256]{1,0:T(8,128)S(1)}, f32[512,256]{1,0:T(8,128)S(1)}, u32[]{:S(2)}, u32[]{:S(2)}) collective-permute-start(f32[512,256]{1,0:T(8,128)S(1)} %get-tuple-element.13), channel_id=1, source_target_pairs={{8,6},{16,14},{24,22},{9,7},{17,15},{25,23}} | collective-permute-start | bytes 1572872 | tf_op jit(solution)/shard_map/ppermute | solution.py:180
  88.6 3.4 %collective-permute-start.5 = (f32[512,256]{1,0:T(8,128)S(1)}, f32[512,256]{1,0:T(8,128)S(1)}, u32[]{:S(2)}, u32[]{:S(2)}) collective-permute-start(f32[512,256]{1,0:T(8,128)S(1)} %get-tuple-element.14), channel_id=1, source_target_pairs={{9,6},{17,14},{25,22},{8,7},{16,15},{24,23}} | collective-permute-start | bytes 1572872 | tf_op jit(solution)/shard_map/ppermute | solution.py:181
  92.1 5.4 %collective-permute-done.3 = f32[512,256]{1,0:T(8,128)S(1)} collective-permute-done((f32[512,256]{1,0:T(8,128)S(1)}, f32[512,256]{1,0:T(8,128)S(1)}, u32[]{:S(2)}, u32[]{:S(2)}) %collective-permute-start.3) | collective-permute-done | bytes 524320 | tf_op jit(solution)/shard_map/ppermute | solution.py:175
  97.5 0.0 collective-permute-done.4
  97.5 2.9 %collective-permute-done.5 = f32[512,256]{1,0:T(8,128)S(1)} collective-permute-done((f32[512,256]{1,0:T(8,128)S(1)}, f32[512,256]{1,0:T(8,128)S(1)}, u32[]{:S(2)}, u32[]{:S(2)}) %collective-permute-start.5) | collective-permute-done | bytes 524320 | tf_op jit(solution)/shard_map/ppermute | solution.py:181
  100.3 0.1 fusion.2
  100.5 0.0 copy-done.1
  100.5 0.0 copy-done.2
  100.5 0.1 pad_maximum_fusion.1
  100.6 40.1 %all_to_all.10 = bf16[8,64,1280]{2,1,0:T(8,128)(2,1)S(1)} all-to-all(bf16[8,64,1280]{2,1,0:T(8,128)(2,1)S(1)} %bitcast.29), channel_id=1, replica_groups=mesh['outer'=4,'inner'=8] {'inner'}, dimensions={0} | all-to-all | bytes 2621440 | tf_op jit(solution)/shard_map/all_to_all | solution.py:187
  140.7 0.8 slice_bitcast_fusion.2
  141.5 1.1 slice_bitcast_fusion
  (8 shorter events, 0.1 us)
Async XLA Ops:
  0.6 8.9 %copy-start.3 = (s32[4,8,4]{1,2,0:T(4,128)S(1)}, s32[4,8,4]{1,2,0:T(4,128)}, u32[]{:S(2)}) copy-start(s32[4,8,4]{1,2,0:T(4,128)} %param.9) | copy-start | bytes 1540
  3.2 36.9 %all-to-all-start = ((bf16[8,64,1280]{2,1,0:T(8,128)(2,1)}), bf16[8,64,1280]{2,1,0:T(8,128)(2,1)S(1)}, u32[]{:S(2)}, u32[]{:S(2)}) async-start(bf16[8,64,1280]{2,1,0:T(8,128)(2,1)} %pad_maximum_fusion), calls=%async_computation | async-start | bytes 2621440 | tf_op jit(solution)/shard_map/all_to_all | solution.py:120
  40.1 18.9 %collective-permute-start.2 = (bf16[512,256]{1,0:T(8,128)(2,1)S(1)}, bf16[512,256]{1,0:T(8,128)(2,1)S(1)}, u32[]{:S(2)}, u32[]{:S(2)}) collective-permute-start(bf16[512,256]{1,0:T(8,128)(2,1)S(1)} %slice.60), channel_id=1, source_target_pairs={{0,1},{2,3},{4,5},{6,7},{8,9},{10,11},{12,13},{14,15},{16,17},{18,... | collective-permute-start | bytes 786440 | tf_op jit(solution)/shard_map/ppermute | solution.py:126
  43.5 11.2 %collective-permute-start.1 = (bf16[512,256]{1,0:T(8,128)(2,1)S(1)}, bf16[512,256]{1,0:T(8,128)(2,1)S(1)}, u32[]{:S(2)}, u32[]{:S(2)}) collective-permute-start(bf16[512,256]{1,0:T(8,128)(2,1)S(1)} %slice.60), channel_id=1, source_target_pairs={{6,9},{14,17},{22,25},{7,8},{15,16},{23,24}} | collective-permute-start | bytes 786440 | tf_op jit(solution)/shard_map/ppermute | solution.py:137
  44.8 14.1 %collective-permute-start = (bf16[512,256]{1,0:T(8,128)(2,1)S(1)}, bf16[512,256]{1,0:T(8,128)(2,1)S(1)}, u32[]{:S(2)}, u32[]{:S(2)}) collective-permute-start(bf16[512,256]{1,0:T(8,128)(2,1)S(1)} %slice.60), channel_id=1, source_target_pairs={{6,8},{14,16},{22,24},{7,9},{15,17},{23,25}} | collective-permute-start | bytes 786440 | tf_op jit(solution)/shard_map/ppermute | solution.py:136
  83.7 1.5 %copy-start = (f32[2048,128]{1,0:T(8,128)S(1)}, f32[2048,128]{1,0:T(8,128)}, u32[]{:S(2)}) copy-start(f32[2048,128]{1,0:T(8,128)} %get-tuple-element.11) | copy-start | bytes 3145732
  85.3 15.2 %copy-start.1 = (bf16[512,512]{1,0:T(8,128)(2,1)S(1)}, bf16[512,512]{1,0:T(8,128)(2,1)}, u32[]{:S(2)}) copy-start(bf16[512,512]{1,0:T(8,128)(2,1)} %get-tuple-element.8) | copy-start | bytes 1572868
  85.3 15.2 %copy-start.2 = (bf16[512,512]{1,0:T(8,128)(2,1)S(1)}, bf16[512,512]{1,0:T(8,128)(2,1)}, u32[]{:S(2)}) copy-start(bf16[512,512]{1,0:T(8,128)(2,1)} %get-tuple-element.9) | copy-start | bytes 1572868
  85.5 12.0 %collective-permute-start.3 = (f32[512,256]{1,0:T(8,128)S(1)}, f32[512,256]{1,0:T(8,128)S(1)}, u32[]{:S(2)}, u32[]{:S(2)}) collective-permute-start(f32[512,256]{1,0:T(8,128)S(1)} %get-tuple-element.12), channel_id=1, source_target_pairs={{1,0},{3,2},{5,4},{7,6},{9,8},{11,10},{13,12},{15,14},{17,16},{19,... | collective-permute-start | bytes 1572872 | tf_op jit(solution)/shard_map/ppermute | solution.py:175
  86.9 10.5 %collective-permute-start.4 = (f32[512,256]{1,0:T(8,128)S(1)}, f32[512,256]{1,0:T(8,128)S(1)}, u32[]{:S(2)}, u32[]{:S(2)}) collective-permute-start(f32[512,256]{1,0:T(8,128)S(1)} %get-tuple-element.13), channel_id=1, source_target_pairs={{8,6},{16,14},{24,22},{9,7},{17,15},{25,23}} | collective-permute-start | bytes 1572872 | tf_op jit(solution)/shard_map/ppermute | solution.py:180
  88.6 11.7 %collective-permute-start.5 = (f32[512,256]{1,0:T(8,128)S(1)}, f32[512,256]{1,0:T(8,128)S(1)}, u32[]{:S(2)}, u32[]{:S(2)}) collective-permute-start(f32[512,256]{1,0:T(8,128)S(1)} %get-tuple-element.14), channel_id=1, source_target_pairs={{9,6},{17,14},{25,22},{8,7},{16,15},{24,23}} | collective-permute-start | bytes 1572872 | tf_op jit(solution)/shard_map/ppermute | solution.py:181

commit v4 on v3

--- a/solution.py
+++ b/solution.py
@@ -22,21 +22,20 @@
 
 
 def attention_kernel(
-    qdoc_ref, qpos_ref, kdoc_ref, kpos_ref, q_ref, g_ref, k_ref, v_ref,
-    o_ref, dq_ref, dk_ref, dv_ref, *, scaling
+    qdoc_ref, qpos_ref, kdoc_ref, kpos_ref, q_ref, g_ref, k_ref, v_ref, kt_ref, vt_ref,
+    o_ref, dq_ref, dkt_ref, dvt_ref, *, scaling
 ):
     @pl.when((pl.program_id(0) == 0) & (pl.program_id(1) == 0))
     def _():
-        dk_ref[...] = jnp.zeros_like(dk_ref)
-        dv_ref[...] = jnp.zeros_like(dv_ref)
+        dkt_ref[...] = jnp.zeros_like(dkt_ref)
+        dvt_ref[...] = jnp.zeros_like(dvt_ref)
 
     q = q_ref[...]
     g = g_ref[...]
     k = k_ref[...]
     v = v_ref[...]
-    contract_last = (((1,), (1,)), ((), ()))
     contract_first = (((0,), (0,)), ((), ()))
-    scores = lax.dot_general(q, k, contract_last, preferred_element_type=jnp.float32) * scaling
+    scores = jnp.dot(q, kt_ref[...], preferred_element_type=jnp.float32) * scaling
     allowed = (qdoc_ref[...] == kdoc_ref[...]) & (kpos_ref[...] <= qpos_ref[...])
     scores = jnp.where(allowed, scores, -jnp.inf)
     row_max = jnp.max(scores, axis=1, keepdims=True)
@@ -48,17 +47,17 @@
     inner_prod = jnp.sum(
         g.astype(jnp.float32) * attn.astype(jnp.float32), axis=1, keepdims=True
     )
-    grad_probs = lax.dot_general(g, v, contract_last, preferred_element_type=jnp.float32)
+    grad_probs = jnp.dot(g, vt_ref[...], preferred_element_type=jnp.float32)
     score_grads = (probs * (grad_probs - inner_prod)).astype(jnp.bfloat16)
     dq_ref[...] = (
         jnp.dot(score_grads, k, preferred_element_type=jnp.float32) * scaling
     ).astype(jnp.bfloat16)
-    dk_ref[...] += (
-        lax.dot_general(score_grads, q, contract_first, preferred_element_type=jnp.float32)
+    dkt_ref[...] += (
+        lax.dot_general(q, score_grads, contract_first, preferred_element_type=jnp.float32)
         * scaling
     )
-    dv_ref[...] += lax.dot_general(
-        probs_low, g, contract_first, preferred_element_type=jnp.float32
+    dvt_ref[...] += lax.dot_general(
+        g, probs_low, contract_first, preferred_element_type=jnp.float32
     )
 
 
@@ -73,18 +72,19 @@
     col_spec = pl.BlockSpec((block_q, 1), lambda i, h: (i, 0))
     key_meta_spec = pl.BlockSpec((1, n_keys), lambda i, h: (0, 0))
     key_spec = pl.BlockSpec((n_keys, head_dim), lambda i, h: (0, 0))
+    key_t_spec = pl.BlockSpec((head_dim, n_keys), lambda i, h: (0, 0))
     kernel = functools.partial(attention_kernel, scaling=1.0 / math.sqrt(head_dim))
-    attn, q_grads, k_grads, v_grads = pl.pallas_call(
+    attn, q_grads, k_grads_t, v_grads_t = pl.pallas_call(
         kernel,
         grid=grid,
         in_specs=[col_spec, col_spec, key_meta_spec, key_meta_spec,
-                  row_spec, row_spec, key_spec, key_spec],
-        out_specs=[row_spec, row_spec, key_spec, key_spec],
+                  row_spec, row_spec, key_spec, key_spec, key_t_spec, key_t_spec],
+        out_specs=[row_spec, row_spec, key_t_spec, key_t_spec],
         out_shape=[
             jax.ShapeDtypeStruct((n_rows, width_q), jnp.bfloat16),
             jax.ShapeDtypeStruct((n_rows, width_q), jnp.bfloat16),
-            jax.ShapeDtypeStruct((n_keys, head_dim), jnp.float32),
-            jax.ShapeDtypeStruct((n_keys, head_dim), jnp.float32),
+            jax.ShapeDtypeStruct((head_dim, n_keys), jnp.float32),
+            jax.ShapeDtypeStruct((head_dim, n_keys), jnp.float32),
         ],
         compiler_params=pltpu.CompilerParams(dimension_semantics=("arbitrary", "arbitrary")),
     )(
@@ -96,8 +96,10 @@
         grad_buf,
         key_buf,
         value_buf,
-    )
-    return attn, q_grads, k_grads, v_grads
+        key_buf.T,
+        value_buf.T,
+    )
+    return attn, q_grads, k_grads_t.T, v_grads_t.T
 
 
 def shards(queries, keys, values, grad_out, doc_starts):

time: 143 us -> 145 us (1.014)
  blocking collectives: 40.1 us -> 43 us
  Pallas kernels: 23.6 us -> 21.8 us
  waiting for transfers between devices: 47.1 us -> 45.5 us
  other arithmetic: 5.36 us -> 6.92 us
    all_to_all x1, blocking collectives: 40.1 us -> 43 us  [shards(): returned = lax.all_to_all(result, 'inner', 0, 0, tiled=True)]
    ppermute x1, waiting for transfers between devices: 2.87 us -> 0.76 us  [shards(): from_next_b = lax.ppermute(grads_b, both, back_b)]
    pallas_call x1, Pallas kernels: 23.6 us -> 21.8 us  [attend(): pl.pallas_call(kernel, grid=grid, in_specs=[col_spec, col_spec, key_meta_...]
  transfers between devices with their start and end apart: 7 -> 7, of which waited for: 5 -> 6; matrix products, arithmetic and copies ran while one was open for 3% -> 3% of each run, Pallas kernels for 0% -> 0%
where the time goes in v4:
time: 145 us
  waiting for transfers between devices  45.5 us (31%)
  blocking collectives  43 us (30%)
  Pallas kernels  21.8 us (15%)
  starting transfers between devices  19 us (13%)
  local copies, waits for them, and re-layouts  7.58 us (5%)
  other arithmetic  6.92 us (5%)
    all_to_all x1, blocking collectives, shards(): returned = lax.all_to_all(result, 'inner', 0, 0, tiled=True)  43 us
    all_to_all x1, waiting for transfers between devices, shards(): lax.all_to_all(packed, 'inner', 0, 0, tiled=True).reshape(tok_dev, -1)  27.1 us
    pallas_call x1, Pallas kernels, attend(): pl.pallas_call(kernel, grid=grid, in_specs=[col_spec, col_spec, key_meta_...  21.8 us
    ppermute x1, waiting for transfers between devices, shards(): recv_b = lax.ppermute(kv_own, both, send_b)  7.6 us
    all_to_all x1, starting transfers between devices, shards(): lax.all_to_all(packed, 'inner', 0, 0, tiled=True).reshape(tok_dev, -1)  6.47 us
    ppermute x1, waiting for transfers between devices, shards(): from_partner = lax.ppermute(kv_grads[2], 'inner', pairs_down)  4.86 us
    ppermute x1, waiting for transfers between devices, shards(): recv_a = lax.ppermute(kv_own, both, send_a)  4.13 us
    ppermute x1, starting transfers between devices, shards(): from_next_b = lax.ppermute(grads_b, both, back_b)  3.53 us
  transfers between devices with their start and end apart: 7, of which 6 were waited for; matrix products, arithmetic and copies ran while one was open for 3% of the time, Pallas kernels for 0%

profile of v4, /device:TPU:1, one launch (start us, length us, event | category | flops | bytes accessed | tf_op | source)
XLA Modules:
  0.0 144.6 jit_solution(7260950863386486400)
XLA Ops:
  0.6 2.5 %pad_maximum_fusion = bf16[8,64,1280]{2,1,0:T(8,128)(2,1)} fusion(bf16[8,64,512]{2,1,0:T(8,128)(2,1)} %bitcast.42, bf16[8,64,128]{2,1,0:T(8,128)(2,1)} %bitcast.44, bf16[8,64,128]{2,1,0:T(8,128)(2,1)} %bitcast.45, bf16[8,64,512]{2,1,0:T(8,128)(2,1)} %bitcast.43), kind=kLoop, calls=%fused_computation.6 | loop fusion | flops 5242880 | bytes 2621440 | tf_op jit(solution)/shard_map/concatenate | solution.py:119
  3.1 6.5 %all-to-all-start = ((bf16[8,64,1280]{2,1,0:T(8,128)(2,1)}), bf16[8,64,1280]{2,1,0:T(8,128)(2,1)S(1)}, u32[]{:S(2)}, u32[]{:S(2)}) async-start(bf16[8,64,1280]{2,1,0:T(8,128)(2,1)} %pad_maximum_fusion), calls=%async_computation | async-start | bytes 2621440 | tf_op jit(solution)/shard_map/all_to_all | solution.py:122
  9.6 0.0 copy-done.4
  9.6 0.1 le.15
  9.7 0.1 reshape.92
  9.8 0.1 reduce-window.4
  9.9 0.1 reduce.1
  10.0 0.1 reshape.83
  10.1 0.1 convert_reduce_fusion
  10.2 0.1 fusion.7
  10.3 0.9 copy.29.qdoc_ref
  11.2 0.6 pad_add_fusion.1
  11.8 0.6 pad_add_fusion
  12.4 0.7 iota_add_fusion.qpos_ref
  13.1 27.1 %all-to-all-done = bf16[8,64,1280]{2,1,0:T(8,128)(2,1)S(1)} async-done(((bf16[8,64,1280]{2,1,0:T(8,128)(2,1)}), bf16[8,64,1280]{2,1,0:T(8,128)(2,1)S(1)}, u32[]{:S(2)}, u32[]{:S(2)}) %all-to-all-start) | async-done | bytes 1310752 | tf_op jit(solution)/shard_map/all_to_all | solution.py:122
  40.2 0.1 copy.33
  40.4 3.4 %collective-permute-start.2 = (bf16[512,256]{0,1:T(8,128)(2,1)S(1)}, bf16[512,256]{0,1:T(8,128)(2,1)S(1)}, u32[]{:S(2)}, u32[]{:S(2)}) collective-permute-start(bf16[512,256]{0,1:T(8,128)(2,1)S(1)} %copy.33), channel_id=1, source_target_pairs={{0,1},{2,3},{4,5},{6,7},{8,9},{10,11},{12,13},{14,15},{16,17},{18,... | collective-permute-start | bytes 786440 | tf_op jit(solution)/shard_map/ppermute | solution.py:128
  43.8 1.3 collective-permute-start.1
  45.1 1.3 collective-permute-start
  46.4 1.0 fusion.8
  47.4 7.6 %collective-permute-done.1 = bf16[512,256]{0,1:T(8,128)(2,1)S(1)} collective-permute-done((bf16[512,256]{0,1:T(8,128)(2,1)S(1)}, bf16[512,256]{0,1:T(8,128)(2,1)S(1)}, u32[]{:S(2)}, u32[]{:S(2)}) %collective-permute-start.1) | collective-permute-done | bytes 262176 | tf_op jit(solution)/shard_map/ppermute | solution.py:139
  55.0 4.1 %collective-permute-done = bf16[512,256]{0,1:T(8,128)(2,1)S(1)} collective-permute-done((bf16[512,256]{0,1:T(8,128)(2,1)S(1)}, bf16[512,256]{0,1:T(8,128)(2,1)S(1)}, u32[]{:S(2)}, u32[]{:S(2)}) %collective-permute-start) | collective-permute-done | bytes 262176 | tf_op jit(solution)/shard_map/ppermute | solution.py:138
  59.2 0.0 collective-permute-done.2
  59.2 0.1 pad_maximum_fusion.2
  59.4 1.2 slice_bitcast_fusion.4
  60.6 1.0 copy.31.v_ref
  61.6 1.0 copy.30.k_ref
  62.6 21.8 %shard_map.84 = (bf16[512,512]{1,0:T(8,128)(2,1)}, bf16[512,512]{1,0:T(8,128)(2,1)}, f32[128,2048]{1,0:T(8,128)}, f32[128,2048]{1,0:T(8,128)}) custom-call(s32[512,1]{1,0:T(8,128)} %copy.29.qdoc_ref, s32[512,1]{1,0:T(8,128)} %iota_add_fusion.qpos_ref, s32[1,2048]{1,0:T(1,128)} %bitcast.47, s32[1,2048]{1,0:T(1,128)} %bitcast.46, ...), custom_call_target="tpu_custom_call" | custom-call | tf_op jit(solution)/shard_map/pallas_call | solution.py:77
  84.4 0.0 copy-start
  84.4 0.0 copy-start.1
  84.4 1.4 broadcast_select_fusion.1
  85.9 1.7 %collective-permute-start.4 = (f32[512,256]{0,1:T(8,128)S(1)}, f32[512,256]{0,1:T(8,128)S(1)}, u32[]{:S(2)}, u32[]{:S(2)}) collective-permute-start(f32[512,256]{0,1:T(8,128)S(1)} %get-tuple-element.12), channel_id=1, source_target_pairs={{8,6},{16,14},{24,22},{9,7},{17,15},{25,23}} | collective-permute-start | bytes 1572872 | tf_op jit(solution)/shard_map/ppermute | solution.py:182
  87.6 0.0 copy-done
  87.6 0.0 copy-done.1
  87.6 0.1 fusion.6
  87.8 1.3 collective-permute-start.3
  89.1 0.0 copy-start.2
  89.1 0.0 copy-start.3
  89.1 3.5 %collective-permute-start.5 = (f32[512,256]{0,1:T(8,128)S(1)}, f32[512,256]{0,1:T(8,128)S(1)}, u32[]{:S(2)}, u32[]{:S(2)}) collective-permute-start(f32[512,256]{0,1:T(8,128)S(1)} %get-tuple-element.15), channel_id=1, source_target_pairs={{9,6},{17,14},{25,22},{8,7},{16,15},{24,23}} | collective-permute-start | bytes 1572872 | tf_op jit(solution)/shard_map/ppermute | solution.py:183
  92.6 1.0 collective-permute-done.4
  93.7 4.9 %collective-permute-done.3 = f32[512,256]{0,1:T(8,128)S(1)} collective-permute-done((f32[512,256]{0,1:T(8,128)S(1)}, f32[512,256]{0,1:T(8,128)S(1)}, u32[]{:S(2)}, u32[]{:S(2)}) %collective-permute-start.3) | collective-permute-done | bytes 524320 | tf_op jit(solution)/shard_map/ppermute | solution.py:177
  98.5 0.8 collective-permute-done.5
  99.3 0.2 fusion.5
  99.5 0.1 copy.32
  99.7 0.1 pad_maximum_fusion.1
  99.8 43.0 %all_to_all.10 = bf16[8,64,1280]{2,1,0:T(8,128)(2,1)S(1)} all-to-all(bf16[8,64,1280]{2,1,0:T(8,128)(2,1)S(1)} %bitcast.41), channel_id=1, replica_groups=mesh['outer'=4,'inner'=8] {'inner'}, dimensions={0} | all-to-all | bytes 2621440 | tf_op jit(solution)/shard_map/all_to_all | solution.py:189
  142.7 0.8 slice_bitcast_fusion.2
  143.5 1.1 slice_bitcast_fusion
  (11 shorter events, 0.1 us)
Async XLA Ops:
  3.1 6.5 %copy-start.4 = (s32[4,8,4]{1,2,0:T(4,128)S(1)}, s32[4,8,4]{1,2,0:T(4,128)}, u32[]{:S(2)}) copy-start(s32[4,8,4]{1,2,0:T(4,128)} %param.9) | copy-start | bytes 1540
  3.1 37.0 %all-to-all-start = ((bf16[8,64,1280]{2,1,0:T(8,128)(2,1)}), bf16[8,64,1280]{2,1,0:T(8,128)(2,1)S(1)}, u32[]{:S(2)}, u32[]{:S(2)}) async-start(bf16[8,64,1280]{2,1,0:T(8,128)(2,1)} %pad_maximum_fusion), calls=%async_computation | async-start | bytes 2621440 | tf_op jit(solution)/shard_map/all_to_all | solution.py:122
  40.4 18.9 %collective-permute-start.2 = (bf16[512,256]{0,1:T(8,128)(2,1)S(1)}, bf16[512,256]{0,1:T(8,128)(2,1)S(1)}, u32[]{:S(2)}, u32[]{:S(2)}) collective-permute-start(bf16[512,256]{0,1:T(8,128)(2,1)S(1)} %copy.33), channel_id=1, source_target_pairs={{0,1},{2,3},{4,5},{6,7},{8,9},{10,11},{12,13},{14,15},{16,17},{18,... | collective-permute-start | bytes 786440 | tf_op jit(solution)/shard_map/ppermute | solution.py:128
  43.8 11.2 %collective-permute-start.1 = (bf16[512,256]{0,1:T(8,128)(2,1)S(1)}, bf16[512,256]{0,1:T(8,128)(2,1)S(1)}, u32[]{:S(2)}, u32[]{:S(2)}) collective-permute-start(bf16[512,256]{0,1:T(8,128)(2,1)S(1)} %copy.33), channel_id=1, source_target_pairs={{6,9},{14,17},{22,25},{7,8},{15,16},{23,24}} | collective-permute-start | bytes 786440 | tf_op jit(solution)/shard_map/ppermute | solution.py:139
  45.1 14.1 %collective-permute-start = (bf16[512,256]{0,1:T(8,128)(2,1)S(1)}, bf16[512,256]{0,1:T(8,128)(2,1)S(1)}, u32[]{:S(2)}, u32[]{:S(2)}) collective-permute-start(bf16[512,256]{0,1:T(8,128)(2,1)S(1)} %copy.33), channel_id=1, source_target_pairs={{6,8},{14,16},{22,24},{7,9},{15,17},{23,25}} | collective-permute-start | bytes 786440 | tf_op jit(solution)/shard_map/ppermute | solution.py:138
  84.4 3.2 %copy-start = (f32[128,2048]{1,0:T(8,128)S(1)}, f32[128,2048]{1,0:T(8,128)}, u32[]{:S(2)}) copy-start(f32[128,2048]{1,0:T(8,128)} %get-tuple-element.10) | copy-start | bytes 3145732
  84.4 3.2 %copy-start.1 = (f32[128,2048]{1,0:T(8,128)S(1)}, f32[128,2048]{1,0:T(8,128)}, u32[]{:S(2)}) copy-start(f32[128,2048]{1,0:T(8,128)} %get-tuple-element.11) | copy-start | bytes 3145732
  85.9 7.8 %collective-permute-start.4 = (f32[512,256]{0,1:T(8,128)S(1)}, f32[512,256]{0,1:T(8,128)S(1)}, u32[]{:S(2)}, u32[]{:S(2)}) collective-permute-start(f32[512,256]{0,1:T(8,128)S(1)} %get-tuple-element.12), channel_id=1, source_target_pairs={{8,6},{16,14},{24,22},{9,7},{17,15},{25,23}} | collective-permute-start | bytes 1572872 | tf_op jit(solution)/shard_map/ppermute | solution.py:182
  87.8 10.8 %collective-permute-start.3 = (f32[512,256]{0,1:T(8,128)S(1)}, f32[512,256]{0,1:T(8,128)S(1)}, u32[]{:S(2)}, u32[]{:S(2)}) collective-permute-start(f32[512,256]{0,1:T(8,128)S(1)} %get-tuple-element.14), channel_id=1, source_target_pairs={{1,0},{3,2},{5,4},{7,6},{9,8},{11,10},{13,12},{15,14},{17,16},{19,... | collective-permute-start | bytes 1572872 | tf_op jit(solution)/shard_map/ppermute | solution.py:177
  89.1 10.6 %copy-start.2 = (bf16[512,512]{1,0:T(8,128)(2,1)S(1)}, bf16[512,512]{1,0:T(8,128)(2,1)}, u32[]{:S(2)}) copy-start(bf16[512,512]{1,0:T(8,128)(2,1)} %get-tuple-element.8) | copy-start | bytes 1572868
  89.1 10.6 %copy-start.3 = (bf16[512,512]{1,0:T(8,128)(2,1)S(1)}, bf16[512,512]{1,0:T(8,128)(2,1)}, u32[]{:S(2)}) copy-start(bf16[512,512]{1,0:T(8,128)(2,1)} %get-tuple-element.9) | copy-start | bytes 1572868
  89.1 10.2 %collective-permute-start.5 = (f32[512,256]{0,1:T(8,128)S(1)}, f32[512,256]{0,1:T(8,128)S(1)}, u32[]{:S(2)}, u32[]{:S(2)}) collective-permute-start(f32[512,256]{0,1:T(8,128)S(1)} %get-tuple-element.15), channel_id=1, source_target_pairs={{9,6},{17,14},{25,22},{8,7},{16,15},{24,23}} | collective-permute-start | bytes 1572872 | tf_op jit(solution)/shard_map/ppermute | solution.py:183

commit v5 on v4

--- a/solution.py
+++ b/solution.py
@@ -22,43 +22,85 @@
 
 
 def attention_kernel(
-    qdoc_ref, qpos_ref, kdoc_ref, kpos_ref, q_ref, g_ref, k_ref, v_ref, kt_ref, vt_ref,
-    o_ref, dq_ref, dkt_ref, dvt_ref, *, scaling
+    flags_ref, qdoc_ref, qpos_ref, kdoc_ref, kpos_ref, q_ref, g_ref, k_ref, v_ref, kt_ref,
+    vt_ref, o_ref, dq_ref, dkt_ref, dvt_ref, scores_ref, max_ref, sum_ref, acc_ref,
+    *, scaling, n_chunks, chunk
 ):
-    @pl.when((pl.program_id(0) == 0) & (pl.program_id(1) == 0))
+    block = pl.program_id(0)
+
+    @pl.when((block == 0) & (pl.program_id(1) == 0))
     def _():
         dkt_ref[...] = jnp.zeros_like(dkt_ref)
         dvt_ref[...] = jnp.zeros_like(dvt_ref)
 
+    contract_first = (((0,), (0,)), ((), ()))
     q = q_ref[...]
     g = g_ref[...]
-    k = k_ref[...]
-    v = v_ref[...]
-    contract_first = (((0,), (0,)), ((), ()))
-    scores = jnp.dot(q, kt_ref[...], preferred_element_type=jnp.float32) * scaling
-    allowed = (qdoc_ref[...] == kdoc_ref[...]) & (kpos_ref[...] <= qpos_ref[...])
-    scores = jnp.where(allowed, scores, -jnp.inf)
-    row_max = jnp.max(scores, axis=1, keepdims=True)
-    log_total = row_max + jnp.log(jnp.sum(jnp.exp(scores - row_max), axis=1, keepdims=True))
-    probs = jnp.exp(scores - log_total)
-    probs_low = probs.astype(jnp.bfloat16)
-    attn = jnp.dot(probs_low, v, preferred_element_type=jnp.float32).astype(jnp.bfloat16)
+    qdoc = qdoc_ref[...]
+    qpos = qpos_ref[...]
+    max_ref[...] = jnp.full_like(max_ref, -jnp.inf)
+    sum_ref[...] = jnp.zeros_like(sum_ref)
+    acc_ref[...] = jnp.zeros_like(acc_ref)
+
+    def cols(c):
+        return slice(c * chunk, (c + 1) * chunk)
+
+    for c in range(n_chunks):
+        @pl.when(flags_ref[block, c] != 0)
+        def _():
+            scores = (
+                jnp.dot(q, kt_ref[:, cols(c)], preferred_element_type=jnp.float32) * scaling
+            )
+            allowed = (qdoc == kdoc_ref[:, cols(c)]) & (kpos_ref[:, cols(c)] <= qpos)
+            scores = jnp.where(allowed, scores, -jnp.inf)
+            scores_ref[:, cols(c)] = scores
+            max_ref[...] = jnp.maximum(max_ref[...], jnp.max(scores, axis=1, keepdims=True))
+
+    row_max = max_ref[...]
+    for c in range(n_chunks):
+        @pl.when(flags_ref[block, c] != 0)
+        def _():
+            sum_ref[...] += jnp.sum(
+                jnp.exp(scores_ref[:, cols(c)] - row_max), axis=1, keepdims=True
+            )
+
+    log_total = row_max + jnp.log(sum_ref[...])
+    for c in range(n_chunks):
+        @pl.when(flags_ref[block, c] != 0)
+        def _():
+            probs = jnp.exp(scores_ref[:, cols(c)] - log_total)
+            scores_ref[:, cols(c)] = probs
+            acc_ref[...] += jnp.dot(
+                probs.astype(jnp.bfloat16), v_ref[cols(c), :],
+                preferred_element_type=jnp.float32,
+            )
+
+    attn = acc_ref[...].astype(jnp.bfloat16)
     o_ref[...] = attn
     inner_prod = jnp.sum(
         g.astype(jnp.float32) * attn.astype(jnp.float32), axis=1, keepdims=True
     )
-    grad_probs = jnp.dot(g, vt_ref[...], preferred_element_type=jnp.float32)
-    score_grads = (probs * (grad_probs - inner_prod)).astype(jnp.bfloat16)
-    dq_ref[...] = (
-        jnp.dot(score_grads, k, preferred_element_type=jnp.float32) * scaling
-    ).astype(jnp.bfloat16)
-    dkt_ref[...] += (
-        lax.dot_general(q, score_grads, contract_first, preferred_element_type=jnp.float32)
-        * scaling
-    )
-    dvt_ref[...] += lax.dot_general(
-        g, probs_low, contract_first, preferred_element_type=jnp.float32
-    )
+    acc_ref[...] = jnp.zeros_like(acc_ref)
+    for c in range(n_chunks):
+        @pl.when(flags_ref[block, c] != 0)
+        def _():
+            probs = scores_ref[:, cols(c)]
+            probs_low = probs.astype(jnp.bfloat16)
+            grad_probs = jnp.dot(g, vt_ref[:, cols(c)], preferred_element_type=jnp.float32)
+            score_grads = (probs * (grad_probs - inner_prod)).astype(jnp.bfloat16)
+            acc_ref[...] += jnp.dot(
+                score_grads, k_ref[cols(c), :], preferred_element_type=jnp.float32
+            )
+            dkt_ref[:, cols(c)] += (
+                lax.dot_general(q, score_grads, contract_first,
+                                preferred_element_type=jnp.float32)
+                * scaling
+            )
+            dvt_ref[:, cols(c)] += lax.dot_general(
+                g, probs_low, contract_first, preferred_element_type=jnp.float32
+            )
+
+    dq_ref[...] = (acc_ref[...] * scaling).astype(jnp.bfloat16)
 
 
 def attend(
@@ -67,19 +109,42 @@
     n_rows, width_q = query_buf.shape
     n_keys, head_dim = key_buf.shape
     block_q = min(256, n_rows)
-    grid = (n_rows // block_q, n_heads)
-    row_spec = pl.BlockSpec((block_q, head_dim), lambda i, h: (i, h))
-    col_spec = pl.BlockSpec((block_q, 1), lambda i, h: (i, 0))
-    key_meta_spec = pl.BlockSpec((1, n_keys), lambda i, h: (0, 0))
-    key_spec = pl.BlockSpec((n_keys, head_dim), lambda i, h: (0, 0))
-    key_t_spec = pl.BlockSpec((head_dim, n_keys), lambda i, h: (0, 0))
-    kernel = functools.partial(attention_kernel, scaling=1.0 / math.sqrt(head_dim))
+    chunk = min(256, n_keys)
+    n_blocks = n_rows // block_q
+    n_chunks = n_keys // chunk
+    qd = query_doc.reshape(n_blocks, block_q)
+    kd = key_doc.reshape(n_chunks, chunk)
+    qp = query_pos.reshape(n_blocks, block_q)
+    kp = key_pos.reshape(n_chunks, chunk)
+    flags = (
+        (jnp.min(qd, axis=1)[:, None] <= jnp.max(kd, axis=1)[None, :])
+        & (jnp.min(kd, axis=1)[None, :] <= jnp.max(qd, axis=1)[:, None])
+        & (jnp.min(kp, axis=1)[None, :] <= jnp.max(qp, axis=1)[:, None])
+    ).astype(jnp.int32)
+    grid = (n_blocks, n_heads)
+    row_spec = pl.BlockSpec((block_q, head_dim), lambda i, h, f: (i, h))
+    col_spec = pl.BlockSpec((block_q, 1), lambda i, h, f: (i, 0))
+    key_meta_spec = pl.BlockSpec((1, n_keys), lambda i, h, f: (0, 0))
+    key_spec = pl.BlockSpec((n_keys, head_dim), lambda i, h, f: (0, 0))
+    key_t_spec = pl.BlockSpec((head_dim, n_keys), lambda i, h, f: (0, 0))
+    kernel = functools.partial(
+        attention_kernel, scaling=1.0 / math.sqrt(head_dim), n_chunks=n_chunks, chunk=chunk
+    )
     attn, q_grads, k_grads_t, v_grads_t = pl.pallas_call(
         kernel,
-        grid=grid,
-        in_specs=[col_spec, col_spec, key_meta_spec, key_meta_spec,
-                  row_spec, row_spec, key_spec, key_spec, key_t_spec, key_t_spec],
-        out_specs=[row_spec, row_spec, key_t_spec, key_t_spec],
+        grid_spec=pltpu.PrefetchScalarGridSpec(
+            num_scalar_prefetch=1,
+            grid=grid,
+            in_specs=[col_spec, col_spec, key_meta_spec, key_meta_spec,
+                      row_spec, row_spec, key_spec, key_spec, key_t_spec, key_t_spec],
+            out_specs=[row_spec, row_spec, key_t_spec, key_t_spec],
+            scratch_shapes=[
+                pltpu.VMEM((block_q, n_keys), jnp.float32),
+                pltpu.VMEM((block_q, 1), jnp.float32),
+                pltpu.VMEM((block_q, 1), jnp.float32),
+                pltpu.VMEM((block_q, head_dim), jnp.float32),
+            ],
+        ),
         out_shape=[
             jax.ShapeDtypeStruct((n_rows, width_q), jnp.bfloat16),
             jax.ShapeDtypeStruct((n_rows, width_q), jnp.bfloat16),
@@ -88,6 +153,7 @@
         ],
         compiler_params=pltpu.CompilerParams(dimension_semantics=("arbitrary", "arbitrary")),
     )(
+        flags,
         query_doc.reshape(n_rows, 1),
         query_pos.reshape(n_rows, 1),
         key_doc.reshape(1, n_keys),

time: 145 us -> 152 us (1.048); the launches traced: 145 us -> 150 us
  starting transfers between devices: 19 us -> 22.6 us
  waiting for transfers between devices: 45.5 us -> 42.4 us
  Pallas kernels: 21.8 us -> 24.3 us
  other arithmetic: 6.92 us -> 8.79 us
    ppermute x1, starting transfers between devices: 3.53 us -> 7.46 us  [shards(): from_next_b = lax.ppermute(grads_b, both, back_b)]
    pallas_call x1, Pallas kernels: 21.8 us -> 24.3 us  [attend(): pl.pallas_call(kernel, grid_spec=pltpu.PrefetchScalarGridSpec(num_scalar_...]
    all_to_all x1, waiting for transfers between devices: 27.1 us -> 24.6 us  [shards(): lax.all_to_all(packed, 'inner', 0, 0, tiled=True).reshape(tok_dev, -1)]
  transfers between devices with their start and end apart: 7 -> 7, of which waited for: 6 -> 5; matrix products, arithmetic and copies ran while one was open for 3% -> 5% of each run, Pallas kernels for 0% -> 0%
where the time goes in v5:
time: 152 us; the launch traced here: 150 us
  blocking collectives  42.9 us (28%)
  waiting for transfers between devices  42.4 us (28%)
  Pallas kernels  24.3 us (16%)
  starting transfers between devices  22.6 us (15%)
  other arithmetic  8.79 us (6%)
  local copies, waits for them, and re-layouts  8.14 us (5%)
    all_to_all x1, blocking collectives, shards(): returned = lax.all_to_all(result, 'inner', 0, 0, tiled=True)  42.9 us
    all_to_all x1, waiting for transfers between devices, shards(): lax.all_to_all(packed, 'inner', 0, 0, tiled=True).reshape(tok_dev, -1)  24.6 us
    pallas_call x1, Pallas kernels, attend(): pl.pallas_call(kernel, grid_spec=pltpu.PrefetchScalarGridSpec(num_scalar_...  24.3 us
    ppermute x1, waiting for transfers between devices, shards(): recv_b = lax.ppermute(kv_own, both, send_b)  7.6 us
    ppermute x1, starting transfers between devices, shards(): from_next_b = lax.ppermute(grads_b, both, back_b)  7.46 us
    all_to_all x1, starting transfers between devices, shards(): lax.all_to_all(packed, 'inner', 0, 0, tiled=True).reshape(tok_dev, -1)  6.47 us
    ppermute x1, waiting for transfers between devices, shards(): from_partner = lax.ppermute(kv_grads[2], 'inner', pairs_down)  5.34 us
    ppermute x1, waiting for transfers between devices, shards(): recv_a = lax.ppermute(kv_own, both, send_a)  4.13 us
  transfers between devices with their start and end apart: 7, of which 5 were waited for; matrix products, arithmetic and copies ran while one was open for 5% of the time, Pallas kernels for 0%

profile of v5, /device:TPU:1, one launch (start us, length us, event | category | flops | bytes accessed | tf_op | source)
XLA Modules:
  0.0 150.0 jit_solution(7191245789824121962)
XLA Ops:
  0.6 2.5 %pad_maximum_fusion = bf16[8,64,1280]{2,1,0:T(8,128)(2,1)} fusion(bf16[8,64,512]{2,1,0:T(8,128)(2,1)} %bitcast.42, bf16[8,64,128]{2,1,0:T(8,128)(2,1)} %bitcast.44, bf16[8,64,128]{2,1,0:T(8,128)(2,1)} %bitcast.45, bf16[8,64,512]{2,1,0:T(8,128)(2,1)} %bitcast.43), kind=kLoop, calls=%fused_computation.6 | loop fusion | flops 5242880 | bytes 2621440 | tf_op jit(solution)/shard_map/concatenate | solution.py:185
  3.1 6.5 %all-to-all-start = ((bf16[8,64,1280]{2,1,0:T(8,128)(2,1)}), bf16[8,64,1280]{2,1,0:T(8,128)(2,1)S(1)}, u32[]{:S(2)}, u32[]{:S(2)}) async-start(bf16[8,64,1280]{2,1,0:T(8,128)(2,1)} %pad_maximum_fusion), calls=%async_computation | async-start | bytes 2621440 | tf_op jit(solution)/shard_map/all_to_all | solution.py:188
  9.6 0.1 le.26
  9.7 0.1 reshape.127
  9.8 0.1 reduce-window.4
  9.9 0.1 reduce.1
  10.0 0.1 reshape.118
  10.1 0.1 convert_reduce_fusion
  10.2 0.1 fusion.7
  10.3 0.5 broadcast.79
  10.8 0.7 fusion.16
  11.5 0.9 copy.29.qdoc_ref
  12.4 0.1 fusion.14
  12.5 0.1 add_reduce_fusion
  12.6 0.2 fusion.9
  12.8 0.1 fusion.15
  13.0 0.6 pad_add_fusion.2
  13.6 0.6 pad_add_fusion.1
  14.2 0.7 iota_add_fusion.qpos_ref
  14.9 0.7 and_convert_fusion.flags_ref
  15.6 24.6 %all-to-all-done = bf16[8,64,1280]{2,1,0:T(8,128)(2,1)S(1)} async-done(((bf16[8,64,1280]{2,1,0:T(8,128)(2,1)}), bf16[8,64,1280]{2,1,0:T(8,128)(2,1)S(1)}, u32[]{:S(2)}, u32[]{:S(2)}) %all-to-all-start) | async-done | bytes 1310752 | tf_op jit(solution)/shard_map/all_to_all | solution.py:188
  40.2 0.1 copy.33
  40.3 3.4 %collective-permute-start.2 = (bf16[512,256]{0,1:T(8,128)(2,1)S(1)}, bf16[512,256]{0,1:T(8,128)(2,1)S(1)}, u32[]{:S(2)}, u32[]{:S(2)}) collective-permute-start(bf16[512,256]{0,1:T(8,128)(2,1)S(1)} %copy.33), channel_id=1, source_target_pairs={{0,1},{2,3},{4,5},{6,7},{8,9},{10,11},{12,13},{14,15},{16,17},{18,... | collective-permute-start | bytes 786440 | tf_op jit(solution)/shard_map/ppermute | solution.py:194
  43.8 1.3 collective-permute-start.1
  45.1 1.3 collective-permute-start
  46.4 1.0 fusion.20
  47.4 7.6 %collective-permute-done.1 = bf16[512,256]{0,1:T(8,128)(2,1)S(1)} collective-permute-done((bf16[512,256]{0,1:T(8,128)(2,1)S(1)}, bf16[512,256]{0,1:T(8,128)(2,1)S(1)}, u32[]{:S(2)}, u32[]{:S(2)}) %collective-permute-start.1) | collective-permute-done | bytes 262176 | tf_op jit(solution)/shard_map/ppermute | solution.py:205
  55.0 4.1 %collective-permute-done = bf16[512,256]{0,1:T(8,128)(2,1)S(1)} collective-permute-done((bf16[512,256]{0,1:T(8,128)(2,1)S(1)}, bf16[512,256]{0,1:T(8,128)(2,1)S(1)}, u32[]{:S(2)}, u32[]{:S(2)}) %collective-permute-start) | collective-permute-done | bytes 262176 | tf_op jit(solution)/shard_map/ppermute | solution.py:204
  59.2 0.0 collective-permute-done.2
  59.2 0.1 pad_maximum_fusion.2
  59.3 1.2 slice_bitcast_fusion.4
  60.6 1.0 copy.31.v_ref
  61.6 1.0 copy.30.k_ref
  62.6 24.3 %shard_map.84 = (bf16[512,512]{1,0:T(8,128)(2,1)}, bf16[512,512]{1,0:T(8,128)(2,1)}, f32[128,2048]{1,0:T(8,128)}, f32[128,2048]{1,0:T(8,128)}) custom-call(s32[2,8]{1,0:T(2,128)} %and_convert_fusion.flags_ref, s32[512,1]{1,0:T(8,128)} %copy.29.qdoc_ref, s32[512,1]{1,0:T(8,128)} %iota_add_fusion.qpos_ref, s32[1,2048]{1,0:T(1,128)} %bitcast.47, ...), custom_call_target="tpu_custom_call" | custom-call | tf_op jit(solution)/shard_map/pallas_call | solution.py:133
  86.9 1.4 broadcast_select_fusion.1
  88.4 1.3 collective-permute-start.4
  89.7 0.1 fusion.6
  89.9 1.3 collective-permute-start.3
  91.2 7.5 %collective-permute-start.5 = (f32[512,256]{0,1:T(8,128)S(1)}, f32[512,256]{0,1:T(8,128)S(1)}, u32[]{:S(2)}, u32[]{:S(2)}) collective-permute-start(f32[512,256]{0,1:T(8,128)S(1)} %get-tuple-element.27), channel_id=1, source_target_pairs={{9,6},{17,14},{25,22},{8,7},{16,15},{24,23}} | collective-permute-start | bytes 1572872 | tf_op jit(solution)/shard_map/ppermute | solution.py:249
  98.7 0.0 collective-permute-done.4
  98.7 5.3 %collective-permute-done.3 = f32[512,256]{0,1:T(8,128)S(1)} collective-permute-done((f32[512,256]{0,1:T(8,128)S(1)}, f32[512,256]{0,1:T(8,128)S(1)}, u32[]{:S(2)}, u32[]{:S(2)}) %collective-permute-start.3) | collective-permute-done | bytes 524320 | tf_op jit(solution)/shard_map/ppermute | solution.py:243
  104.0 0.7 collective-permute-done.5
  104.7 0.2 fusion.5
  105.0 0.1 copy.32
  105.1 0.1 pad_maximum_fusion.1
  105.2 42.9 %all_to_all.10 = bf16[8,64,1280]{2,1,0:T(8,128)(2,1)S(1)} all-to-all(bf16[8,64,1280]{2,1,0:T(8,128)(2,1)S(1)} %bitcast.41), channel_id=1, replica_groups=mesh['outer'=4,'inner'=8] {'inner'}, dimensions={0} | all-to-all | bytes 2621440 | tf_op jit(solution)/shard_map/all_to_all | solution.py:255
  148.1 0.8 slice_bitcast_fusion.2
  148.9 1.1 slice_bitcast_fusion
  (23 shorter events, 0.2 us)
Async XLA Ops:
  3.1 6.5 %copy-start.4 = (s32[4,8,4]{1,2,0:T(4,128)S(1)}, s32[4,8,4]{1,2,0:T(4,128)}, u32[]{:S(2)}) copy-start(s32[4,8,4]{1,2,0:T(4,128)} %param.9) | copy-start | bytes 1540
  3.1 37.0 %all-to-all-start = ((bf16[8,64,1280]{2,1,0:T(8,128)(2,1)}), bf16[8,64,1280]{2,1,0:T(8,128)(2,1)S(1)}, u32[]{:S(2)}, u32[]{:S(2)}) async-start(bf16[8,64,1280]{2,1,0:T(8,128)(2,1)} %pad_maximum_fusion), calls=%async_computation | async-start | bytes 2621440 | tf_op jit(solution)/shard_map/all_to_all | solution.py:188
  40.3 18.9 %collective-permute-start.2 = (bf16[512,256]{0,1:T(8,128)(2,1)S(1)}, bf16[512,256]{0,1:T(8,128)(2,1)S(1)}, u32[]{:S(2)}, u32[]{:S(2)}) collective-permute-start(bf16[512,256]{0,1:T(8,128)(2,1)S(1)} %copy.33), channel_id=1, source_target_pairs={{0,1},{2,3},{4,5},{6,7},{8,9},{10,11},{12,13},{14,15},{16,17},{18,... | collective-permute-start | bytes 786440 | tf_op jit(solution)/shard_map/ppermute | solution.py:194
  43.8 11.2 %collective-permute-start.1 = (bf16[512,256]{0,1:T(8,128)(2,1)S(1)}, bf16[512,256]{0,1:T(8,128)(2,1)S(1)}, u32[]{:S(2)}, u32[]{:S(2)}) collective-permute-start(bf16[512,256]{0,1:T(8,128)(2,1)S(1)} %copy.33), channel_id=1, source_target_pairs={{6,9},{14,17},{22,25},{7,8},{15,16},{23,24}} | collective-permute-start | bytes 786440 | tf_op jit(solution)/shard_map/ppermute | solution.py:205
  45.1 14.1 %collective-permute-start = (bf16[512,256]{0,1:T(8,128)(2,1)S(1)}, bf16[512,256]{0,1:T(8,128)(2,1)S(1)}, u32[]{:S(2)}, u32[]{:S(2)}) collective-permute-start(bf16[512,256]{0,1:T(8,128)(2,1)S(1)} %copy.33), channel_id=1, source_target_pairs={{6,8},{14,16},{22,24},{7,9},{15,17},{23,25}} | collective-permute-start | bytes 786440 | tf_op jit(solution)/shard_map/ppermute | solution.py:204
  86.9 2.8 %copy-start = (f32[128,2048]{1,0:T(8,128)S(1)}, f32[128,2048]{1,0:T(8,128)}, u32[]{:S(2)}) copy-start(f32[128,2048]{1,0:T(8,128)} %get-tuple-element.10) | copy-start | bytes 3145732
  86.9 2.8 %copy-start.1 = (f32[128,2048]{1,0:T(8,128)S(1)}, f32[128,2048]{1,0:T(8,128)}, u32[]{:S(2)}) copy-start(f32[128,2048]{1,0:T(8,128)} %get-tuple-element.11) | copy-start | bytes 3145732
  88.4 10.3 %collective-permute-start.4 = (f32[512,256]{0,1:T(8,128)S(1)}, f32[512,256]{0,1:T(8,128)S(1)}, u32[]{:S(2)}, u32[]{:S(2)}) collective-permute-start(f32[512,256]{0,1:T(8,128)S(1)} %get-tuple-element.16), channel_id=1, source_target_pairs={{8,6},{16,14},{24,22},{9,7},{17,15},{25,23}} | collective-permute-start | bytes 1572872 | tf_op jit(solution)/shard_map/ppermute | solution.py:248
  89.9 14.1 %collective-permute-start.3 = (f32[512,256]{0,1:T(8,128)S(1)}, f32[512,256]{0,1:T(8,128)S(1)}, u32[]{:S(2)}, u32[]{:S(2)}) collective-permute-start(f32[512,256]{0,1:T(8,128)S(1)} %get-tuple-element.26), channel_id=1, source_target_pairs={{1,0},{3,2},{5,4},{7,6},{9,8},{11,10},{13,12},{15,14},{17,16},{19,... | collective-permute-start | bytes 1572872 | tf_op jit(solution)/shard_map/ppermute | solution.py:243
  91.2 13.9 %copy-start.2 = (bf16[512,512]{1,0:T(8,128)(2,1)S(1)}, bf16[512,512]{1,0:T(8,128)(2,1)}, u32[]{:S(2)}) copy-start(bf16[512,512]{1,0:T(8,128)(2,1)} %get-tuple-element.8) | copy-start | bytes 1572868
  91.2 13.9 %copy-start.3 = (bf16[512,512]{1,0:T(8,128)(2,1)S(1)}, bf16[512,512]{1,0:T(8,128)(2,1)}, u32[]{:S(2)}) copy-start(bf16[512,512]{1,0:T(8,128)(2,1)} %get-tuple-element.9) | copy-start | bytes 1572868
  91.2 13.5 %collective-permute-start.5 = (f32[512,256]{0,1:T(8,128)S(1)}, f32[512,256]{0,1:T(8,128)S(1)}, u32[]{:S(2)}, u32[]{:S(2)}) collective-permute-start(f32[512,256]{0,1:T(8,128)S(1)} %get-tuple-element.27), channel_id=1, source_target_pairs={{9,6},{17,14},{25,22},{8,7},{16,15},{24,23}} | collective-permute-start | bytes 1572872 | tf_op jit(solution)/shard_map/ppermute | solution.py:249

commit v6 on v4

--- a/solution.py
+++ b/solution.py
@@ -159,19 +159,57 @@
             query_pos,
         ]
     )
-    ctx = jnp.concatenate([kv_prev_a, kv_prev_b, kv_partner, kv_own])
-    attn, q_grads, k_grads, v_grads = attend(
-        query_buf,
-        grad_buf,
-        query_pos,
-        query_doc,
-        ctx[:, :head_dim],
-        ctx[:, head_dim:],
-        key_pos,
-        key_doc,
-        n_heads,
-    )
-    kv_grads = jnp.concatenate([k_grads, v_grads], axis=1).reshape(4, tok_dev, 2 * head_dim)
+    n_slots = 4
+    slot_kv = jnp.stack([kv_prev_a, kv_prev_b, kv_partner, kv_own])
+    slot_doc = key_doc.reshape(n_slots, tok_dev)
+    slot_pos = key_pos.reshape(n_slots, tok_dev)
+    needed = (
+        (jnp.min(slot_doc, axis=1) <= jnp.max(query_doc))
+        & (jnp.max(slot_doc, axis=1) >= jnp.min(query_doc))
+        & (jnp.min(slot_pos, axis=1) <= jnp.max(query_pos))
+    )
+    needed = needed | (jnp.arange(n_slots) == n_slots - 1)
+    needed_i = needed.astype(jnp.int32)
+    count = jnp.sum(needed_i)
+    rank = jnp.where(
+        needed, jnp.cumsum(needed_i) - 1, count + jnp.cumsum(1 - needed_i) - 1
+    )
+    slot_ids = jnp.arange(n_slots, dtype=jnp.int32)
+    order = jnp.sum(
+        jnp.where(rank[None, :] == slot_ids[:, None], slot_ids[None, :], 0), axis=1
+    )
+    kv_sorted = slot_kv[order]
+    doc_sorted = slot_doc[order]
+    pos_sorted = slot_pos[order]
+
+    def branch(n_used):
+        def run(kv_sorted, doc_sorted, pos_sorted):
+            ctx = kv_sorted[:n_used].reshape(n_used * tok_dev, 2 * head_dim)
+            attn, q_grads, k_grads, v_grads = attend(
+                query_buf,
+                grad_buf,
+                query_pos,
+                query_doc,
+                ctx[:, :head_dim],
+                ctx[:, head_dim:],
+                pos_sorted[:n_used].reshape(-1),
+                doc_sorted[:n_used].reshape(-1),
+                n_heads,
+            )
+            grads = jnp.concatenate([k_grads, v_grads], axis=1).reshape(
+                n_used, tok_dev, 2 * head_dim
+            )
+            grads = jnp.concatenate(
+                [grads, jnp.zeros((n_slots - n_used, tok_dev, 2 * head_dim), jnp.float32)]
+            )
+            return attn, q_grads, grads
+
+        return run
+
+    attn, q_grads, grads_sorted = lax.switch(
+        count - 1, [branch(n) for n in range(1, n_slots + 1)], kv_sorted, doc_sorted, pos_sorted
+    )
+    kv_grads = grads_sorted[rank]
 
     pairs_down = [(b, a) for a, b in pairs_up]
     from_partner = lax.ppermute(kv_grads[2], "inner", pairs_down)

time: 145 us -> 145 us (level)
  local copies, waits for them, and re-layouts: 7.58 us -> 16.7 us
  Pallas kernels: 21.8 us -> 13 us
  other arithmetic: 6.92 us -> 12.8 us
  blocking collectives: 43 us -> 39.8 us
  waiting for transfers between devices: 45.5 us -> 42.3 us
    pallas_call x1, Pallas kernels: 21.8 us -> 13 us  [attend(): pl.pallas_call(kernel, grid=grid, in_specs=[col_spec, col_spec, key_meta_...]
    gather x0 -> x4, local copies, waits for them, and re-layouts: none -> 4.01 us  [the longest x1 2.27 us: shards(): kv_grads = grads_sorted[rank]]
    all_to_all x1, waiting for transfers between devices: 27.1 us -> 23.9 us  [shards(): lax.all_to_all(packed, 'inner', 0, 0, tiled=True).reshape(tok_dev, -1)]
    all_to_all x1, blocking collectives: 43 us -> 39.8 us  [shards(): returned = lax.all_to_all(result, 'inner', 0, 0, tiled=True)]
    ppermute x1, waiting for transfers between devices: 4.86 us -> 7.42 us  [shards(): from_partner = lax.ppermute(kv_grads[2], 'inner', pairs_down)]
    ppermute x1, waiting for transfers between devices: 4.13 us -> 1.74 us  [shards(): recv_a = lax.ppermute(kv_own, both, send_a)]
    sub x0 -> x1, other arithmetic: none -> 1.95 us  [shards(): 1 - needed_i]
    cond x0 -> x5, local copies, waits for them, and re-layouts: none -> 1.6 us
  transfers between devices with their start and end apart: 7 -> 7, of which waited for: 6 -> 5; matrix products, arithmetic and copies ran while one was open for 3% -> 5% of each run, Pallas kernels for 0% -> 0%
where the time goes in v6:
time: 145 us; the launch traced here: 144 us
  waiting for transfers between devices  42.3 us (29%)
  blocking collectives  39.8 us (27%)
  starting transfers between devices  17.9 us (12%)
  local copies, waits for them, and re-layouts  16.7 us (12%)
  Pallas kernels  13 us (9%)
  other arithmetic  12.8 us (9%)
  between operations  1.51 us (1%)
    all_to_all x1, blocking collectives, shards(): returned = lax.all_to_all(result, 'inner', 0, 0, tiled=True)  39.8 us
    all_to_all x1, waiting for transfers between devices, shards(): lax.all_to_all(packed, 'inner', 0, 0, tiled=True).reshape(tok_dev, -1)  23.9 us
    pallas_call x1, Pallas kernels, attend(): pl.pallas_call(kernel, grid=grid, in_specs=[col_spec, col_spec, key_meta_...  13 us
    ppermute x1, waiting for transfers between devices, shards(): from_partner = lax.ppermute(kv_grads[2], 'inner', pairs_down)  7.42 us
    ppermute x1, waiting for transfers between devices, shards(): recv_b = lax.ppermute(kv_own, both, send_b)  7.21 us
    all_to_all x1, starting transfers between devices, shards(): lax.all_to_all(packed, 'inner', 0, 0, tiled=True).reshape(tok_dev, -1)  6.34 us
    ppermute x1, starting transfers between devices, shards(): kv_partner = lax.ppermute(kv_own, 'inner', pairs_up)  4.11 us
  transfers between devices with their start and end apart: 7, of which 5 were waited for; matrix products, arithmetic and copies ran while one was open for 5% of the time, Pallas kernels for 0%

profile of v6, /device:TPU:1, one launch (start us, length us, event | category | flops | bytes accessed | tf_op | source)
XLA Modules:
  0.0 144.1 jit_solution(16772041654090072849)
XLA Ops:
  0.6 2.5 %pad_maximum_fusion.3 = bf16[8,64,1280]{2,1,0:T(8,128)(2,1)} fusion(bf16[8,64,512]{2,1,0:T(8,128)(2,1)} %bitcast.152, bf16[8,64,128]{2,1,0:T(8,128)(2,1)} %bitcast.158, bf16[8,64,128]{2,1,0:T(8,128)(2,1)} %bitcast.159, bf16[8,64,512]{2,1,0:T(8,128)(2,1)} %bitcast.153), kind=kLoop, calls=%fused_computation.17 | loop fusion | flops 5242880 | bytes 2621440 | tf_op jit(solution)/shard_map/concatenate | solution.py:119
  3.1 6.3 %all-to-all-start = ((bf16[8,64,1280]{2,1,0:T(8,128)(2,1)}), bf16[8,64,1280]{2,1,0:T(8,128)(2,1)S(1)}, u32[]{:S(2)}, u32[]{:S(2)}) async-start(bf16[8,64,1280]{2,1,0:T(8,128)(2,1)} %pad_maximum_fusion.3), calls=%async_computation | async-start | bytes 2621440 | tf_op jit(solution)/shard_map/all_to_all | solution.py:122
  10.2 0.6 fusion.10
  10.8 0.6 fusion.5
  11.6 0.2 fusion.9
  11.8 1.9 %broadcast_subtract_fusion = (s32[4,1]{0,1:T(1,128)S(1)}, pred[4]{0:T(512)(128)(4,1)S(1)}) fusion(s32[4]{0:T(128)S(1)} %reduce_min.29, s32[]{:T(128)} %fusion.5, s32[4]{0:T(128)S(1)} %get-tuple-element.184, s32[]{:T(128)} %get-tuple-element.186, s32[4]{0:T(128)S(1)} %get-tuple-element.183, s32[]{:T(128)} %get-tuple-element.185), kind=kLoop, calls=%fused_computation.64 | loop fusion | flops 36 | bytes 80 | tf_op jit(solution)/shard_map/sub | solution.py:175
  13.8 0.2 reduce-window.11
  13.9 0.2 reduce-window.14
  14.1 0.6 convert_reduce_fusion.2
  14.7 0.6 bitcast_select_fusion
  15.5 0.7 fusion.7
  16.2 23.9 %all-to-all-done = bf16[8,64,1280]{2,1,0:T(8,128)(2,1)S(1)} async-done(((bf16[8,64,1280]{2,1,0:T(8,128)(2,1)}), bf16[8,64,1280]{2,1,0:T(8,128)(2,1)S(1)}, u32[]{:S(2)}, u32[]{:S(2)}) %all-to-all-start) | async-done | bytes 1310752 | tf_op jit(solution)/shard_map/all_to_all | solution.py:122
  40.1 1.3 collective-permute-start
  41.4 1.3 collective-permute-start.1
  42.7 4.1 %collective-permute-start.2 = (bf16[512,256]{1,0:T(8,128)(2,1)S(1)}, bf16[512,256]{1,0:T(8,128)(2,1)}, u32[]{:S(2)}, u32[]{:S(2)}) collective-permute-start(bf16[512,256]{1,0:T(8,128)(2,1)S(1)} %get-tuple-element.213), channel_id=1, source_target_pairs={{0,1},{2,3},{4,5},{6,7},{8,9},{10,11},{12,13},{14,15},{16,17},{18,... | collective-permute-start | bytes 786440 | tf_op jit(solution)/shard_map/ppermute | solution.py:128
  46.8 0.6 gather_fusion.1
  47.4 0.6 gather_fusion
  48.6 1.7 %collective-permute-done = bf16[512,256]{1,0:T(8,128)(2,1)S(1)} collective-permute-done((bf16[512,256]{1,0:T(8,128)(2,1)S(1)}, bf16[512,256]{1,0:T(8,128)(2,1)S(1)}, u32[]{:S(2)}, u32[]{:S(2)}) %collective-permute-start) | collective-permute-done | bytes 262176 | tf_op jit(solution)/shard_map/ppermute | solution.py:138
  50.4 7.2 %collective-permute-done.1 = bf16[512,256]{1,0:T(8,128)(2,1)S(1)} collective-permute-done((bf16[512,256]{1,0:T(8,128)(2,1)S(1)}, bf16[512,256]{1,0:T(8,128)(2,1)S(1)}, u32[]{:S(2)}, u32[]{:S(2)}) %collective-permute-start.1) | collective-permute-done | bytes 262176 | tf_op jit(solution)/shard_map/ppermute | solution.py:139
  57.6 1.1 pad_maximum_fusion.5
  58.7 0.6 gather_fusion.2
  59.3 24.9 %conditional.1 = (bf16[512,512]{1,0:T(8,128)(2,1)}, bf16[512,512]{1,0:T(8,128)(2,1)}, f32[4,512,256]{2,1,0:T(8,128)}) conditional(s32[]{:T(128)} %clamp.3, (s32[1,1,512]{2,1,0:T(1,128)S(1)}, s32[512]{0:T(512)S(1)}, s32[4,512]{1,0:T(4,128)S(1)}, s32[4,512]{1,0:T(4,128)S(1)}, bf16[4,512,256]{2,1,0:T(8,128)(2,1)S(1)}, ...), branch_computations={%region_13.14_spmd, %region_14.15_spmd, %region_15.16_spmd, %regio... | conditional | flops 524288 | bytes 19980372 | solution.py:209
  59.3 1.0 copy.81
  60.4 0.4 slice.116
  60.8 0.9 slice_bitcast_fusion.5
  61.8 0.9 copy.64.k_ref
  62.6 0.8 copy.65.v_ref
  63.5 0.6 copy.98
  64.1 0.6 copy.99
  64.7 0.8 slice.102.g_ref
  65.5 0.8 slice.98.q_ref
  66.3 0.9 copy.62.qdoc_ref
  67.2 0.9 copy.63.qpos_ref
  68.1 13.0 %branch_1_fun.1 = (bf16[512,512]{1,0:T(8,128)(2,1)}, bf16[512,512]{1,0:T(8,128)(2,1)}, f32[128,1024]{1,0:T(8,128)}, f32[128,1024]{1,0:T(8,128)}) custom-call(s32[512,1]{1,0:T(8,128)} %copy.62.qdoc_ref, s32[512,1]{1,0:T(8,128)} %copy.63.qpos_ref, s32[1,1024]{1,0:T(1,128)} %bitcast.175, s32[1,1024]{1,0:T(1,128)} %bitcast.176, bf16[512,512]{1,0:T(8,128)(2,1)} %slice.98.q_ref, ...), custom_call_target="tpu_custom_call" | custom-call | tf_op jit(solution)/shard_map/cond/branch_1_fun/pallas_call | solution.py:77
  81.1 1.3 pad_maximum_fusion
  82.4 0.3 copy.97
  82.7 1.5 %concatenate.25.clone = f32[4,512,256]{2,1,0:T(8,128)} pad(f32[2,512,256]{2,1,0:T(8,128)S(1)} %bitcast.140, f32[]{:T(128)} %constant.26.clone), padding=0_2x0_0x0_0 | pad | bytes 3145732 | tf_op jit(solution)/shard_map/cond/branch_1_fun/concatenate | solution.py:202
  84.2 2.3 %gather_fusion.3 = f32[4,512,256]{2,1,0:T(8,128)S(1)} fusion(f32[4,512,256]{2,1,0:T(8,128)} %get-tuple-element.174, s32[1024]{0:T(1024)S(1)} %pad_clamp_fusion), kind=kCustom, calls=%fused_computation.3 | custom fusion | bytes 4194320 | tf_op jit(solution)/shard_map/gather | solution.py:212
  86.5 0.2 slice_bitcast_fusion.11
  86.7 1.3 collective-permute-start.3
  88.0 1.3 collective-permute-start.4
  89.3 2.2 %collective-permute-start.5 = (f32[512,256]{1,0:T(8,128)S(1)}, f32[512,256]{1,0:T(8,128)S(1)}, u32[]{:S(2)}, u32[]{:S(2)}) collective-permute-start(f32[512,256]{1,0:T(8,128)S(1)} %get-tuple-element.207), channel_id=1, source_target_pairs={{9,6},{17,14},{25,22},{8,7},{16,15},{24,23}} | collective-permute-start | bytes 1572872 | tf_op jit(solution)/shard_map/ppermute | solution.py:221
  91.5 7.4 %collective-permute-done.3 = f32[512,256]{1,0:T(8,128)S(1)} collective-permute-done((f32[512,256]{1,0:T(8,128)S(1)}, f32[512,256]{1,0:T(8,128)S(1)}, u32[]{:S(2)}, u32[]{:S(2)}) %collective-permute-start.3) | collective-permute-done | bytes 524320 | tf_op jit(solution)/shard_map/ppermute | solution.py:215
  98.9 2.1 %collective-permute-done.5 = f32[512,256]{1,0:T(8,128)S(1)} collective-permute-done((f32[512,256]{1,0:T(8,128)S(1)}, f32[512,256]{1,0:T(8,128)S(1)}, u32[]{:S(2)}, u32[]{:S(2)}) %collective-permute-start.5) | collective-permute-done | bytes 524320 | tf_op jit(solution)/shard_map/ppermute | solution.py:221
  101.1 1.3 pad_maximum_fusion.4
  102.4 39.8 %all_to_all.10 = bf16[8,64,1280]{2,1,0:T(8,128)(2,1)S(1)} all-to-all(bf16[8,64,1280]{2,1,0:T(8,128)(2,1)S(1)} %bitcast.139), channel_id=1, replica_groups=mesh['outer'=4,'inner'=8] {'inner'}, dimensions={0} | all-to-all | bytes 2621440 | tf_op jit(solution)/shard_map/all_to_all | solution.py:227
  142.2 1.1 slice_bitcast_fusion.9
  143.3 0.8 slice_bitcast_fusion.13
  (32 shorter events, 1.2 us)
Async XLA Ops:
  0.6 8.8 %copy-start.4 = (s32[4,8,4]{1,2,0:T(4,128)S(1)}, s32[4,8,4]{1,2,0:T(4,128)}, u32[]{:S(2)}) copy-start(s32[4,8,4]{1,2,0:T(4,128)} %param.13) | copy-start | bytes 1540
  3.1 36.9 %all-to-all-start = ((bf16[8,64,1280]{2,1,0:T(8,128)(2,1)}), bf16[8,64,1280]{2,1,0:T(8,128)(2,1)S(1)}, u32[]{:S(2)}, u32[]{:S(2)}) async-start(bf16[8,64,1280]{2,1,0:T(8,128)(2,1)} %pad_maximum_fusion.3), calls=%async_computation | async-start | bytes 2621440 | tf_op jit(solution)/shard_map/all_to_all | solution.py:122
  40.1 10.3 %collective-permute-start = (bf16[512,256]{1,0:T(8,128)(2,1)S(1)}, bf16[512,256]{1,0:T(8,128)(2,1)S(1)}, u32[]{:S(2)}, u32[]{:S(2)}) collective-permute-start(bf16[512,256]{1,0:T(8,128)(2,1)S(1)} %get-tuple-element.213), channel_id=1, source_target_pairs={{6,8},{14,16},{22,24},{7,9},{15,17},{23,25}} | collective-permute-start | bytes 786440 | tf_op jit(solution)/shard_map/ppermute | solution.py:138
  41.4 16.2 %collective-permute-start.1 = (bf16[512,256]{1,0:T(8,128)(2,1)S(1)}, bf16[512,256]{1,0:T(8,128)(2,1)S(1)}, u32[]{:S(2)}, u32[]{:S(2)}) collective-permute-start(bf16[512,256]{1,0:T(8,128)(2,1)S(1)} %get-tuple-element.213), channel_id=1, source_target_pairs={{6,9},{14,17},{22,25},{7,8},{15,16},{23,24}} | collective-permute-start | bytes 786440 | tf_op jit(solution)/shard_map/ppermute | solution.py:139
  42.7 14.9 %collective-permute-start.2 = (bf16[512,256]{1,0:T(8,128)(2,1)S(1)}, bf16[512,256]{1,0:T(8,128)(2,1)}, u32[]{:S(2)}, u32[]{:S(2)}) collective-permute-start(bf16[512,256]{1,0:T(8,128)(2,1)S(1)} %get-tuple-element.213), channel_id=1, source_target_pairs={{0,1},{2,3},{4,5},{6,7},{8,9},{10,11},{12,13},{14,15},{16,17},{18,... | collective-permute-start | bytes 786440 | tf_op jit(solution)/shard_map/ppermute | solution.py:128
  86.7 12.3 %collective-permute-start.3 = (f32[512,256]{1,0:T(8,128)S(1)}, f32[512,256]{1,0:T(8,128)S(1)}, u32[]{:S(2)}, u32[]{:S(2)}) collective-permute-start(f32[512,256]{1,0:T(8,128)S(1)} %get-tuple-element.206), channel_id=1, source_target_pairs={{1,0},{3,2},{5,4},{7,6},{9,8},{11,10},{13,12},{15,14},{17,16},{19,... | collective-permute-start | bytes 1572872 | tf_op jit(solution)/shard_map/ppermute | solution.py:215
  88.0 11.0 %collective-permute-start.4 = (f32[512,256]{1,0:T(8,128)S(1)}, f32[512,256]{1,0:T(8,128)S(1)}, u32[]{:S(2)}, u32[]{:S(2)}) collective-permute-start(f32[512,256]{1,0:T(8,128)S(1)} %get-tuple-element.208), channel_id=1, source_target_pairs={{8,6},{16,14},{24,22},{9,7},{17,15},{25,23}} | collective-permute-start | bytes 1572872 | tf_op jit(solution)/shard_map/ppermute | solution.py:220
  89.3 11.7 %collective-permute-start.5 = (f32[512,256]{1,0:T(8,128)S(1)}, f32[512,256]{1,0:T(8,128)S(1)}, u32[]{:S(2)}, u32[]{:S(2)}) collective-permute-start(f32[512,256]{1,0:T(8,128)S(1)} %get-tuple-element.207), channel_id=1, source_target_pairs={{9,6},{17,14},{25,22},{8,7},{16,15},{24,23}} | collective-permute-start | bytes 1572872 | tf_op jit(solution)/shard_map/ppermute | solution.py:221

commit v7 on v6

--- a/solution.py
+++ b/solution.py
@@ -61,24 +61,30 @@
     )
 
 
-def attend(
-    query_buf, grad_buf, query_pos, query_doc, key_buf, value_buf, key_pos, key_doc, n_heads
-):
-    n_rows, width_q = query_buf.shape
-    n_keys, head_dim = key_buf.shape
+def attend(rows, q_first, g_first, query_pos, query_doc, ctx, key_pos, key_doc, n_heads):
+    n_rows = rows.shape[0]
+    n_keys, kv_width = ctx.shape
+    head_dim = kv_width // 2
+    width_q = n_heads * head_dim
     block_q = min(256, n_rows)
     grid = (n_rows // block_q, n_heads)
+    q_spec = pl.BlockSpec((block_q, head_dim), lambda i, h: (i, q_first + h))
+    g_spec = pl.BlockSpec((block_q, head_dim), lambda i, h: (i, g_first + h))
     row_spec = pl.BlockSpec((block_q, head_dim), lambda i, h: (i, h))
     col_spec = pl.BlockSpec((block_q, 1), lambda i, h: (i, 0))
     key_meta_spec = pl.BlockSpec((1, n_keys), lambda i, h: (0, 0))
-    key_spec = pl.BlockSpec((n_keys, head_dim), lambda i, h: (0, 0))
+    k_spec = pl.BlockSpec((n_keys, head_dim), lambda i, h: (0, 0))
+    v_spec = pl.BlockSpec((n_keys, head_dim), lambda i, h: (0, 1))
+    kt_spec = pl.BlockSpec((head_dim, n_keys), lambda i, h: (0, 0))
+    vt_spec = pl.BlockSpec((head_dim, n_keys), lambda i, h: (1, 0))
     key_t_spec = pl.BlockSpec((head_dim, n_keys), lambda i, h: (0, 0))
+    ctx_t = ctx.T
     kernel = functools.partial(attention_kernel, scaling=1.0 / math.sqrt(head_dim))
     attn, q_grads, k_grads_t, v_grads_t = pl.pallas_call(
         kernel,
         grid=grid,
         in_specs=[col_spec, col_spec, key_meta_spec, key_meta_spec,
-                  row_spec, row_spec, key_spec, key_spec, key_t_spec, key_t_spec],
+                  q_spec, g_spec, k_spec, v_spec, kt_spec, vt_spec],
         out_specs=[row_spec, row_spec, key_t_spec, key_t_spec],
         out_shape=[
             jax.ShapeDtypeStruct((n_rows, width_q), jnp.bfloat16),
@@ -92,14 +98,14 @@
         query_pos.reshape(n_rows, 1),
         key_doc.reshape(1, n_keys),
         key_pos.reshape(1, n_keys),
-        query_buf,
-        grad_buf,
-        key_buf,
-        value_buf,
-        key_buf.T,
-        value_buf.T,
-    )
-    return attn, q_grads, k_grads_t.T, v_grads_t.T
+        rows,
+        rows,
+        ctx,
+        ctx,
+        ctx_t,
+        ctx_t,
+    )
+    return attn, q_grads, k_grads_t, v_grads_t
 
 
 def shards(queries, keys, values, grad_out, doc_starts):
@@ -120,9 +126,7 @@
         [queries[0, :, 0], keys[0, :, 0], values[0, :, 0], grad_out[0, :, 0]], axis=-1
     )
     arrived = lax.all_to_all(packed, "inner", 0, 0, tiled=True).reshape(tok_dev, -1)
-    query_buf = arrived[:, :width_q]
     kv_own = arrived[:, width_q : width_q + 2 * head_dim]
-    grad_buf = arrived[:, width_q + 2 * head_dim :]
 
     pairs_up = [(2 * p, 2 * p + 1) for p in range(n_inner // 2)]
     kv_partner = lax.ppermute(kv_own, "inner", pairs_up)
@@ -185,18 +189,18 @@
     def branch(n_used):
         def run(kv_sorted, doc_sorted, pos_sorted):
             ctx = kv_sorted[:n_used].reshape(n_used * tok_dev, 2 * head_dim)
-            attn, q_grads, k_grads, v_grads = attend(
-                query_buf,
-                grad_buf,
+            attn, q_grads, k_grads_t, v_grads_t = attend(
+                arrived,
+                0,
+                width_q // head_dim + 2,
                 query_pos,
                 query_doc,
-                ctx[:, :head_dim],
-                ctx[:, head_dim:],
+                ctx,
                 pos_sorted[:n_used].reshape(-1),
                 doc_sorted[:n_used].reshape(-1),
                 n_heads,
             )
-            grads = jnp.concatenate([k_grads, v_grads], axis=1).reshape(
+            grads = jnp.concatenate([k_grads_t, v_grads_t], axis=0).T.reshape(
                 n_used, tok_dev, 2 * head_dim
             )
             grads = jnp.concatenate(

time: 145 us -> 144 us (level); the launches traced: 144 us -> 145 us
  Pallas kernels: 13 us -> 17.4 us
  local copies, waits for them, and re-layouts: 16.7 us -> 13 us
  starting transfers between devices: 17.9 us -> 16.3 us
  waiting for transfers between devices: 42.3 us -> 43.8 us
    pallas_call x1, Pallas kernels: 13 us -> 17.4 us  [attend(): pl.pallas_call(kernel, grid=grid, in_specs=[col_spec, col_spec, key_meta_...]
    slice x4 -> x0, local copies, waits for them, and re-layouts: 3.38 us -> none  [the longest x1 0.86 us: run(): ctx[:, :head_dim]]
    ppermute x1, waiting for transfers between devices: 2.06 us -> 4.39 us  [shards(): from_next_b = lax.ppermute(grads_b, both, back_b)]
    transpose x0 -> x1, other arithmetic: none -> 1.47 us  [run(): jnp.concatenate([k_grads_t, v_grads_t], axis=0)]
    ppermute x1, waiting for transfers between devices: 7.42 us -> 5.96 us  [shards(): from_partner = lax.ppermute(kv_grads[2], 'inner', pairs_down)]
where the time goes in v7:
time: 144 us; the launch traced here: 145 us
  waiting for transfers between devices  43.8 us (30%)
  blocking collectives  39.7 us (28%)
  Pallas kernels  17.4 us (12%)
  starting transfers between devices  16.3 us (11%)
  local copies, waits for them, and re-layouts  13 us (9%)
  other arithmetic  13 us (9%)
  between operations  1.54 us (1%)
    all_to_all x1, blocking collectives, shards(): returned = lax.all_to_all(result, 'inner', 0, 0, tiled=True)  39.7 us
    all_to_all x1, waiting for transfers between devices, shards(): lax.all_to_all(packed, 'inner', 0, 0, tiled=True).reshape(tok_dev, -1)  23.9 us
    pallas_call x1, Pallas kernels, attend(): pl.pallas_call(kernel, grid=grid, in_specs=[col_spec, col_spec, key_meta_...  17.4 us
    ppermute x1, waiting for transfers between devices, shards(): recv_b = lax.ppermute(kv_own, both, send_b)  7.21 us
    all_to_all x1, starting transfers between devices, shards(): lax.all_to_all(packed, 'inner', 0, 0, tiled=True).reshape(tok_dev, -1)  6.34 us
    ppermute x1, waiting for transfers between devices, shards(): from_partner = lax.ppermute(kv_grads[2], 'inner', pairs_down)  5.96 us
    ppermute x1, waiting for transfers between devices, shards(): from_next_b = lax.ppermute(grads_b, both, back_b)  4.39 us
    ppermute x1, starting transfers between devices, shards(): kv_partner = lax.ppermute(kv_own, 'inner', pairs_up)  3.43 us
  transfers between devices with their start and end apart: 7, of which 5 were waited for; matrix products, arithmetic and copies ran while one was open for 5% of the time, Pallas kernels for 0%

profile of v7, /device:TPU:1, one launch (start us, length us, event | category | flops | bytes accessed | tf_op | source)
XLA Modules:
  0.0 144.9 jit_solution(8415896068117867522)
XLA Ops:
  0.6 2.5 %pad_maximum_fusion = bf16[8,64,1280]{2,1,0:T(8,128)(2,1)} fusion(bf16[8,64,512]{2,1,0:T(8,128)(2,1)} %bitcast.145, bf16[8,64,128]{2,1,0:T(8,128)(2,1)} %bitcast.148, bf16[8,64,128]{2,1,0:T(8,128)(2,1)} %bitcast.149, bf16[8,64,512]{2,1,0:T(8,128)(2,1)} %bitcast.146), kind=kLoop, calls=%fused_computation.14 | loop fusion | flops 5242880 | bytes 2621440 | tf_op jit(solution)/shard_map/concatenate | solution.py:125
  3.1 6.3 %all-to-all-start = ((bf16[8,64,1280]{2,1,0:T(8,128)(2,1)}), bf16[8,64,1280]{2,1,0:T(8,128)(2,1)S(1)}, u32[]{:S(2)}, u32[]{:S(2)}) async-start(bf16[8,64,1280]{2,1,0:T(8,128)(2,1)} %pad_maximum_fusion), calls=%async_computation | async-start | bytes 2621440 | tf_op jit(solution)/shard_map/all_to_all | solution.py:128
  9.7 0.1 reduce.3
  10.0 0.1 convert_reduce_fusion
  10.2 0.6 fusion.10
  10.8 0.6 fusion.5
  11.5 0.1 reduce_min.29
  11.6 0.2 fusion.9
  11.8 1.9 %broadcast_subtract_fusion = (s32[4,1]{0,1:T(1,128)S(1)}, pred[4]{0:T(512)(128)(4,1)S(1)}) fusion(s32[4]{0:T(128)S(1)} %reduce_min.29, s32[]{:T(128)} %fusion.5, s32[4]{0:T(128)S(1)} %get-tuple-element.157, s32[]{:T(128)} %get-tuple-element.159, s32[4]{0:T(128)S(1)} %get-tuple-element.156, s32[]{:T(128)} %get-tuple-element.158), kind=kLoop, calls=%fused_computation.61 | loop fusion | flops 36 | bytes 80 | tf_op jit(solution)/shard_map/sub | solution.py:179
  13.8 0.2 reduce-window.11
  13.9 0.2 reduce-window.14
  14.1 0.6 convert_reduce_fusion.2
  14.7 0.6 bitcast_select_fusion
  15.4 0.1 select_reduce_fusion
  15.5 0.7 fusion.7
  16.2 23.9 %all-to-all-done = bf16[8,64,1280]{2,1,0:T(8,128)(2,1)S(1)} async-done(((bf16[8,64,1280]{2,1,0:T(8,128)(2,1)}), bf16[8,64,1280]{2,1,0:T(8,128)(2,1)S(1)}, u32[]{:S(2)}, u32[]{:S(2)}) %all-to-all-start) | async-done | bytes 1310752 | tf_op jit(solution)/shard_map/all_to_all | solution.py:128
  40.1 1.3 collective-permute-start
  41.4 1.3 collective-permute-start.1
  42.7 3.4 %collective-permute-start.2 = (bf16[512,256]{1,0:T(8,128)(2,1)S(1)}, bf16[512,256]{1,0:T(8,128)(2,1)S(1)}, u32[]{:S(2)}, u32[]{:S(2)}) collective-permute-start(bf16[512,256]{1,0:T(8,128)(2,1)S(1)} %get-tuple-element.176), channel_id=1, source_target_pairs={{0,1},{2,3},{4,5},{6,7},{8,9},{10,11},{12,13},{14,15},{16,17},{18,... | collective-permute-start | bytes 786440 | tf_op jit(solution)/shard_map/ppermute | solution.py:132
  46.2 0.6 gather_fusion.1
  46.7 0.6 gather_fusion
  47.9 2.4 %collective-permute-done = bf16[512,256]{1,0:T(8,128)(2,1)S(1)} collective-permute-done((bf16[512,256]{1,0:T(8,128)(2,1)S(1)}, bf16[512,256]{1,0:T(8,128)(2,1)S(1)}, u32[]{:S(2)}, u32[]{:S(2)}) %collective-permute-start) | collective-permute-done | bytes 262176 | tf_op jit(solution)/shard_map/ppermute | solution.py:142
  50.4 7.2 %collective-permute-done.1 = bf16[512,256]{1,0:T(8,128)(2,1)S(1)} collective-permute-done((bf16[512,256]{1,0:T(8,128)(2,1)S(1)}, bf16[512,256]{1,0:T(8,128)(2,1)S(1)}, u32[]{:S(2)}, u32[]{:S(2)}) %collective-permute-start.1) | collective-permute-done | bytes 262176 | tf_op jit(solution)/shard_map/ppermute | solution.py:143
  57.6 0.7 copy-done.2
  58.3 1.1 pad_maximum_fusion.2
  59.4 0.6 gather_fusion.2
  60.0 25.1 %conditional.1 = (bf16[512,512]{1,0:T(8,128)(2,1)}, bf16[512,512]{1,0:T(8,128)(2,1)}, f32[4,512,256]{2,1,0:T(8,128)}) conditional(s32[]{:T(128)} %clamp.3, (s32[1,1,512]{2,1,0:T(1,128)S(1)}, s32[512]{0:T(512)S(1)}, s32[4,512]{1,0:T(4,128)S(1)}, s32[4,512]{1,0:T(4,128)S(1)}, bf16[4,512,256]{2,1,0:T(8,128)(2,1)S(1)}, ...), branch_computations={%region_13.14_spmd, %region_14.15_spmd, %region_15.16_spmd, %regio... | conditional | flops 524288 | bytes 16310328 | solution.py:213
  60.1 1.2 copy.63
  61.3 0.6 copy.91
  61.9 0.6 copy.92
  62.5 0.9 copy.64.qdoc_ref
  63.4 0.9 copy.65.qpos_ref
  64.3 17.4 %branch_2_fun.1 = (bf16[512,512]{1,0:T(8,128)(2,1)}, bf16[512,512]{1,0:T(8,128)(2,1)}, f32[128,1536]{1,0:T(8,128)}, f32[128,1536]{1,0:T(8,128)}) custom-call(s32[512,1]{1,0:T(8,128)} %copy.64.qdoc_ref, s32[512,1]{1,0:T(8,128)} %copy.65.qpos_ref, s32[1,1536]{1,0:T(1,128)} %bitcast.163, s32[1,1536]{1,0:T(1,128)} %bitcast.164, ...), custom_call_target="tpu_custom_call" | custom-call | tf_op jit(solution)/shard_map/cond/branch_2_fun/pallas_call | solution.py:83
  81.7 1.5 %maximum_bitcast_fusion.2 = f32[1536,256]{0,1:T(8,128)S(1)} fusion(f32[128,1536]{1,0:T(8,128)} %get-tuple-element.77, f32[128,1536]{1,0:T(8,128)} %get-tuple-element.76), kind=kLoop, calls=%fused_computation.10 | loop fusion | flops 393216 | bytes 3145728 | tf_op jit(solution)/shard_map/cond/branch_2_fun/transpose | solution.py:203
  83.2 0.5 copy.66
  83.6 1.5 %concatenate.27 = f32[4,512,256]{2,1,0:T(8,128)} pad(f32[3,512,256]{2,1,0:T(8,128)S(1)} %bitcast.141, f32[]{:T(128)} %constant.29.clone), padding=0_1x0_0x0_0 | pad | bytes 3670020 | tf_op jit(solution)/shard_map/cond/branch_2_fun/concatenate | solution.py:206
  85.2 2.3 %gather_fusion.3 = f32[4,512,256]{2,1,0:T(8,128)S(1)} fusion(f32[4,512,256]{2,1,0:T(8,128)} %get-tuple-element.155, s32[1024]{0:T(1024)S(1)} %pad_clamp_fusion), kind=kCustom, calls=%fused_computation.3 | custom fusion | bytes 4194320 | tf_op jit(solution)/shard_map/gather | solution.py:216
  87.4 0.2 slice_bitcast_fusion.8
  87.6 1.3 collective-permute-start.3
  88.9 1.3 collective-permute-start.4
  90.2 1.3 collective-permute-start.5
  91.6 6.0 %collective-permute-done.3 = f32[512,256]{1,0:T(8,128)S(1)} collective-permute-done((f32[512,256]{1,0:T(8,128)S(1)}, f32[512,256]{1,0:T(8,128)S(1)}, u32[]{:S(2)}, u32[]{:S(2)}) %collective-permute-start.3) | collective-permute-done | bytes 524320 | tf_op jit(solution)/shard_map/ppermute | solution.py:219
  97.5 4.4 %collective-permute-done.5 = f32[512,256]{1,0:T(8,128)S(1)} collective-permute-done((f32[512,256]{1,0:T(8,128)S(1)}, f32[512,256]{1,0:T(8,128)S(1)}, u32[]{:S(2)}, u32[]{:S(2)}) %collective-permute-start.5) | collective-permute-done | bytes 524320 | tf_op jit(solution)/shard_map/ppermute | solution.py:225
  101.9 0.1 fusion.3
  102.1 1.3 pad_maximum_fusion.1
  103.4 39.7 %all_to_all.10 = bf16[8,64,1280]{2,1,0:T(8,128)(2,1)S(1)} all-to-all(bf16[8,64,1280]{2,1,0:T(8,128)(2,1)S(1)} %bitcast.142), channel_id=1, replica_groups=mesh['outer'=4,'inner'=8] {'inner'}, dimensions={0} | all-to-all | bytes 2621440 | tf_op jit(solution)/shard_map/all_to_all | solution.py:231
  143.0 1.1 slice_bitcast_fusion.6
  144.1 0.8 slice_bitcast_fusion.10
  (30 shorter events, 0.6 us)
Async XLA Ops:
  0.6 8.8 %copy-start.3 = (s32[4,8,4]{1,2,0:T(4,128)S(1)}, s32[4,8,4]{1,2,0:T(4,128)}, u32[]{:S(2)}) copy-start(s32[4,8,4]{1,2,0:T(4,128)} %param.13) | copy-start | bytes 1540
  3.1 36.9 %all-to-all-start = ((bf16[8,64,1280]{2,1,0:T(8,128)(2,1)}), bf16[8,64,1280]{2,1,0:T(8,128)(2,1)S(1)}, u32[]{:S(2)}, u32[]{:S(2)}) async-start(bf16[8,64,1280]{2,1,0:T(8,128)(2,1)} %pad_maximum_fusion), calls=%async_computation | async-start | bytes 2621440 | tf_op jit(solution)/shard_map/all_to_all | solution.py:128
  40.1 10.3 %collective-permute-start = (bf16[512,256]{1,0:T(8,128)(2,1)S(1)}, bf16[512,256]{1,0:T(8,128)(2,1)S(1)}, u32[]{:S(2)}, u32[]{:S(2)}) collective-permute-start(bf16[512,256]{1,0:T(8,128)(2,1)S(1)} %get-tuple-element.176), channel_id=1, source_target_pairs={{6,8},{14,16},{22,24},{7,9},{15,17},{23,25}} | collective-permute-start | bytes 786440 | tf_op jit(solution)/shard_map/ppermute | solution.py:142
  41.4 16.2 %collective-permute-start.1 = (bf16[512,256]{1,0:T(8,128)(2,1)S(1)}, bf16[512,256]{1,0:T(8,128)(2,1)S(1)}, u32[]{:S(2)}, u32[]{:S(2)}) collective-permute-start(bf16[512,256]{1,0:T(8,128)(2,1)S(1)} %get-tuple-element.176), channel_id=1, source_target_pairs={{6,9},{14,17},{22,25},{7,8},{15,16},{23,24}} | collective-permute-start | bytes 786440 | tf_op jit(solution)/shard_map/ppermute | solution.py:143
  42.7 14.9 %collective-permute-start.2 = (bf16[512,256]{1,0:T(8,128)(2,1)S(1)}, bf16[512,256]{1,0:T(8,128)(2,1)S(1)}, u32[]{:S(2)}, u32[]{:S(2)}) collective-permute-start(bf16[512,256]{1,0:T(8,128)(2,1)S(1)} %get-tuple-element.176), channel_id=1, source_target_pairs={{0,1},{2,3},{4,5},{6,7},{8,9},{10,11},{12,13},{14,15},{16,17},{18,... | collective-permute-start | bytes 786440 | tf_op jit(solution)/shard_map/ppermute | solution.py:132
  57.6 0.7 copy-start.2
  60.1 4.1 %copy-start = (bf16[3,512,256]{2,1,0:T(8,128)(2,1)}, bf16[3,512,256]{2,1,0:T(8,128)(2,1)S(1)}, u32[]{:S(2)}) copy-start(bf16[3,512,256]{2,1,0:T(8,128)(2,1)S(1)} %slice.46) | copy-start | bytes 2359300 | tf_op jit(solution)/shard_map/cond
  87.6 9.9 %collective-permute-start.3 = (f32[512,256]{1,0:T(8,128)S(1)}, f32[512,256]{1,0:T(8,128)S(1)}, u32[]{:S(2)}, u32[]{:S(2)}) collective-permute-start(f32[512,256]{1,0:T(8,128)S(1)} %get-tuple-element.169), channel_id=1, source_target_pairs={{1,0},{3,2},{5,4},{7,6},{9,8},{11,10},{13,12},{15,14},{17,16},{19,... | collective-permute-start | bytes 1572872 | tf_op jit(solution)/shard_map/ppermute | solution.py:219
  88.9 8.6 %collective-permute-start.4 = (f32[512,256]{1,0:T(8,128)S(1)}, f32[512,256]{1,0:T(8,128)S(1)}, u32[]{:S(2)}, u32[]{:S(2)}) collective-permute-start(f32[512,256]{1,0:T(8,128)S(1)} %get-tuple-element.171), channel_id=1, source_target_pairs={{8,6},{16,14},{24,22},{9,7},{17,15},{25,23}} | collective-permute-start | bytes 1572872 | tf_op jit(solution)/shard_map/ppermute | solution.py:224
  90.2 11.7 %collective-permute-start.5 = (f32[512,256]{1,0:T(8,128)S(1)}, f32[512,256]{1,0:T(8,128)S(1)}, u32[]{:S(2)}, u32[]{:S(2)}) collective-permute-start(f32[512,256]{1,0:T(8,128)S(1)} %get-tuple-element.170), channel_id=1, source_target_pairs={{9,6},{17,14},{25,22},{8,7},{16,15},{24,23}} | collective-permute-start | bytes 1572872 | tf_op jit(solution)/shard_map/ppermute | solution.py:225

commit v8 on v7

--- a/solution.py
+++ b/solution.py
@@ -22,82 +22,92 @@
 
 
 def attention_kernel(
-    qdoc_ref, qpos_ref, kdoc_ref, kpos_ref, q_ref, g_ref, k_ref, v_ref, kt_ref, vt_ref,
-    o_ref, dq_ref, dkt_ref, dvt_ref, *, scaling
+    qmeta_ref, kmeta_ref, q_ref, g_ref, k_ref, v_ref, kt_ref, vt_ref,
+    o_ref, dq_ref, dkt_ref, dvt_ref, *, scaling, n_heads, head_dim
 ):
-    @pl.when((pl.program_id(0) == 0) & (pl.program_id(1) == 0))
+    @pl.when(pl.program_id(0) == 0)
     def _():
         dkt_ref[...] = jnp.zeros_like(dkt_ref)
         dvt_ref[...] = jnp.zeros_like(dvt_ref)
 
-    q = q_ref[...]
-    g = g_ref[...]
     k = k_ref[...]
     v = v_ref[...]
+    kt = kt_ref[...]
+    vt = vt_ref[...]
     contract_first = (((0,), (0,)), ((), ()))
-    scores = jnp.dot(q, kt_ref[...], preferred_element_type=jnp.float32) * scaling
-    allowed = (qdoc_ref[...] == kdoc_ref[...]) & (kpos_ref[...] <= qpos_ref[...])
-    scores = jnp.where(allowed, scores, -jnp.inf)
-    row_max = jnp.max(scores, axis=1, keepdims=True)
-    log_total = row_max + jnp.log(jnp.sum(jnp.exp(scores - row_max), axis=1, keepdims=True))
-    probs = jnp.exp(scores - log_total)
-    probs_low = probs.astype(jnp.bfloat16)
-    attn = jnp.dot(probs_low, v, preferred_element_type=jnp.float32).astype(jnp.bfloat16)
-    o_ref[...] = attn
-    inner_prod = jnp.sum(
-        g.astype(jnp.float32) * attn.astype(jnp.float32), axis=1, keepdims=True
-    )
-    grad_probs = jnp.dot(g, vt_ref[...], preferred_element_type=jnp.float32)
-    score_grads = (probs * (grad_probs - inner_prod)).astype(jnp.bfloat16)
-    dq_ref[...] = (
-        jnp.dot(score_grads, k, preferred_element_type=jnp.float32) * scaling
-    ).astype(jnp.bfloat16)
-    dkt_ref[...] += (
-        lax.dot_general(q, score_grads, contract_first, preferred_element_type=jnp.float32)
-        * scaling
-    )
-    dvt_ref[...] += lax.dot_general(
-        g, probs_low, contract_first, preferred_element_type=jnp.float32
-    )
-
-
-def attend(rows, q_first, g_first, query_pos, query_doc, ctx, key_pos, key_doc, n_heads):
+    allowed = (qmeta_ref[:, 0:1] == kmeta_ref[0:1, :]) & (
+        kmeta_ref[1:2, :] <= qmeta_ref[:, 1:2]
+    )
+    for h in range(n_heads):
+        cols = slice(h * head_dim, (h + 1) * head_dim)
+        q = q_ref[:, cols]
+        g = g_ref[:, cols]
+        scores = jnp.dot(q, kt, preferred_element_type=jnp.float32) * scaling
+        scores = jnp.where(allowed, scores, -jnp.inf)
+        row_max = jnp.max(scores, axis=1, keepdims=True)
+        log_total = row_max + jnp.log(
+            jnp.sum(jnp.exp(scores - row_max), axis=1, keepdims=True)
+        )
+        probs = jnp.exp(scores - log_total)
+        probs_low = probs.astype(jnp.bfloat16)
+        attn = jnp.dot(probs_low, v, preferred_element_type=jnp.float32).astype(jnp.bfloat16)
+        o_ref[:, cols] = attn
+        inner_prod = jnp.sum(
+            g.astype(jnp.float32) * attn.astype(jnp.float32), axis=1, keepdims=True
+        )
+        grad_probs = jnp.dot(g, vt, preferred_element_type=jnp.float32)
+        score_grads = (probs * (grad_probs - inner_prod)).astype(jnp.bfloat16)
+        dq_ref[:, cols] = (
+            jnp.dot(score_grads, k, preferred_element_type=jnp.float32) * scaling
+        ).astype(jnp.bfloat16)
+        dkt_ref[...] += (
+            lax.dot_general(q, score_grads, contract_first, preferred_element_type=jnp.float32)
+            * scaling
+        )
+        dvt_ref[...] += lax.dot_general(
+            g, probs_low, contract_first, preferred_element_type=jnp.float32
+        )
+
+
+def attend(rows, query_pos, query_doc, ctx, key_pos, key_doc, n_heads):
     n_rows = rows.shape[0]
     n_keys, kv_width = ctx.shape
     head_dim = kv_width // 2
     width_q = n_heads * head_dim
     block_q = min(256, n_rows)
-    grid = (n_rows // block_q, n_heads)
-    q_spec = pl.BlockSpec((block_q, head_dim), lambda i, h: (i, q_first + h))
-    g_spec = pl.BlockSpec((block_q, head_dim), lambda i, h: (i, g_first + h))
-    row_spec = pl.BlockSpec((block_q, head_dim), lambda i, h: (i, h))
-    col_spec = pl.BlockSpec((block_q, 1), lambda i, h: (i, 0))
-    key_meta_spec = pl.BlockSpec((1, n_keys), lambda i, h: (0, 0))
-    k_spec = pl.BlockSpec((n_keys, head_dim), lambda i, h: (0, 0))
-    v_spec = pl.BlockSpec((n_keys, head_dim), lambda i, h: (0, 1))
-    kt_spec = pl.BlockSpec((head_dim, n_keys), lambda i, h: (0, 0))
-    vt_spec = pl.BlockSpec((head_dim, n_keys), lambda i, h: (1, 0))
-    key_t_spec = pl.BlockSpec((head_dim, n_keys), lambda i, h: (0, 0))
+    grid = (n_rows // block_q,)
+    q_spec = pl.BlockSpec((block_q, width_q), lambda i: (i, 0))
+    g_spec = pl.BlockSpec((block_q, width_q), lambda i: (i, 1))
+    qmeta_spec = pl.BlockSpec((block_q, 2), lambda i: (i, 0))
+    kmeta_spec = pl.BlockSpec((2, n_keys), lambda i: (0, 0))
+    k_spec = pl.BlockSpec((n_keys, head_dim), lambda i: (0, 0))
+    v_spec = pl.BlockSpec((n_keys, head_dim), lambda i: (0, 1))
+    kt_spec = pl.BlockSpec((head_dim, n_keys), lambda i: (0, 0))
+    vt_spec = pl.BlockSpec((head_dim, n_keys), lambda i: (1, 0))
+    out_spec = pl.BlockSpec((block_q, width_q), lambda i: (i, 0))
+    key_t_spec = pl.BlockSpec((head_dim, n_keys), lambda i: (0, 0))
     ctx_t = ctx.T
-    kernel = functools.partial(attention_kernel, scaling=1.0 / math.sqrt(head_dim))
-    attn, q_grads, k_grads_t, v_grads_t = pl.pallas_call(
+    kernel = functools.partial(
+        attention_kernel,
+        scaling=1.0 / math.sqrt(head_dim),
+        n_heads=n_heads,
+        head_dim=head_dim,
+    )
+    return pl.pallas_call(
         kernel,
         grid=grid,
-        in_specs=[col_spec, col_spec, key_meta_spec, key_meta_spec,
-                  q_spec, g_spec, k_spec, v_spec, kt_spec, vt_spec],
-        out_specs=[row_spec, row_spec, key_t_spec, key_t_spec],
+        in_specs=[qmeta_spec, kmeta_spec, q_spec, g_spec, k_spec, v_spec, kt_spec, vt_spec],
+        out_specs=[out_spec, out_spec, key_t_spec, key_t_spec],
         out_shape=[
             jax.ShapeDtypeStruct((n_rows, width_q), jnp.bfloat16),
             jax.ShapeDtypeStruct((n_rows, width_q), jnp.bfloat16),
             jax.ShapeDtypeStruct((head_dim, n_keys), jnp.float32),
             jax.ShapeDtypeStruct((head_dim, n_keys), jnp.float32),
         ],
-        compiler_params=pltpu.CompilerParams(dimension_semantics=("arbitrary", "arbitrary")),
+        compiler_params=pltpu.CompilerParams(dimension_semantics=("arbitrary",)),
     )(
-        query_doc.reshape(n_rows, 1),
-        query_pos.reshape(n_rows, 1),
-        key_doc.reshape(1, n_keys),
-        key_pos.reshape(1, n_keys),
+        jnp.stack([query_doc, query_pos], axis=1),
+        jnp.stack([key_doc, key_pos]),
         rows,
         rows,
         ctx,
@@ -105,7 +115,6 @@
         ctx_t,
         ctx_t,
     )
-    return attn, q_grads, k_grads_t, v_grads_t
 
 
 def shards(queries, keys, values, grad_out, doc_starts):
@@ -123,10 +132,10 @@
     offsets = jnp.arange(tok_dev, dtype=jnp.int32)
 
     packed = jnp.concatenate(
-        [queries[0, :, 0], keys[0, :, 0], values[0, :, 0], grad_out[0, :, 0]], axis=-1
+        [queries[0, :, 0], grad_out[0, :, 0], keys[0, :, 0], values[0, :, 0]], axis=-1
     )
     arrived = lax.all_to_all(packed, "inner", 0, 0, tiled=True).reshape(tok_dev, -1)
-    kv_own = arrived[:, width_q : width_q + 2 * head_dim]
+    kv_own = arrived[:, 2 * width_q :]
 
     pairs_up = [(2 * p, 2 * p + 1) for p in range(n_inner // 2)]
     kv_partner = lax.ppermute(kv_own, "inner", pairs_up)
@@ -191,8 +200,6 @@
             ctx = kv_sorted[:n_used].reshape(n_used * tok_dev, 2 * head_dim)
             attn, q_grads, k_grads_t, v_grads_t = attend(
                 arrived,
-                0,
-                width_q // head_dim + 2,
                 query_pos,
                 query_doc,
                 ctx,

time: 144 us -> 139 us (0.965)
  Pallas kernels: 17.4 us -> 11.6 us
    pallas_call x1, Pallas kernels: 17.4 us -> 11.6 us  [attend(): pl.pallas_call(kernel, grid=grid, in_specs=[qmeta_spec, kmeta_spec, q_spe...]
    ppermute x1, waiting for transfers between devices: 4.39 us -> 1.57 us  [shards(): from_next_b = lax.ppermute(grads_b, both, back_b)]
    ppermute x1, waiting for transfers between devices: 5.96 us -> 8.01 us  [shards(): from_partner = lax.ppermute(kv_grads[2], 'inner', pairs_down)]
  transfers between devices with their start and end apart: 7 -> 7, of which waited for: 5 -> 5; matrix products, arithmetic and copies ran while one was open for 5% -> 6% of each run, Pallas kernels for 0% -> 0%
where the time goes in v8:
time: 139 us
  waiting for transfers between devices  43.1 us (31%)
  blocking collectives  39.7 us (29%)
  starting transfers between devices  17.1 us (12%)
  other arithmetic  13.4 us (10%)
  local copies, waits for them, and re-layouts  12 us (9%)
  Pallas kernels  11.6 us (8%)
  between operations  1.54 us (1%)
    all_to_all x1, blocking collectives, shards(): returned = lax.all_to_all(result, 'inner', 0, 0, tiled=True)  39.7 us
    all_to_all x1, waiting for transfers between devices, shards(): lax.all_to_all(packed, 'inner', 0, 0, tiled=True).reshape(tok_dev, -1)  23.9 us
    pallas_call x1, Pallas kernels, attend(): pl.pallas_call(kernel, grid=grid, in_specs=[qmeta_spec, kmeta_spec, q_spe...  11.6 us
    ppermute x1, waiting for transfers between devices, shards(): from_partner = lax.ppermute(kv_grads[2], 'inner', pairs_down)  8.01 us
    ppermute x1, waiting for transfers between devices, shards(): recv_b = lax.ppermute(kv_own, both, send_b)  7.21 us
    all_to_all x1, starting transfers between devices, shards(): lax.all_to_all(packed, 'inner', 0, 0, tiled=True).reshape(tok_dev, -1)  6.34 us
    ppermute x1, starting transfers between devices, shards(): kv_partner = lax.ppermute(kv_own, 'inner', pairs_up)  3.43 us
  transfers between devices with their start and end apart: 7, of which 5 were waited for; matrix products, arithmetic and copies ran while one was open for 6% of the time, Pallas kernels for 0%

profile of v8, /device:TPU:1, one launch (start us, length us, event | category | flops | bytes accessed | tf_op | source)
XLA Modules:
  0.0 138.5 jit_solution(8688028709649128469)
XLA Ops:
  0.6 2.5 %pad_maximum_fusion = bf16[8,64,1280]{2,1,0:T(8,128)(2,1)} fusion(bf16[8,64,128]{2,1,0:T(8,128)(2,1)} %bitcast.148, bf16[8,64,128]{2,1,0:T(8,128)(2,1)} %bitcast.149, bf16[8,64,512]{2,1,0:T(8,128)(2,1)} %bitcast.145, bf16[8,64,512]{2,1,0:T(8,128)(2,1)} %bitcast.146), kind=kLoop, calls=%fused_computation.22 | loop fusion | flops 5242880 | bytes 2621440 | tf_op jit(solution)/shard_map/concatenate | solution.py:134
  3.1 6.3 %all-to-all-start = ((bf16[8,64,1280]{2,1,0:T(8,128)(2,1)}), bf16[8,64,1280]{2,1,0:T(8,128)(2,1)S(1)}, u32[]{:S(2)}, u32[]{:S(2)}) async-start(bf16[8,64,1280]{2,1,0:T(8,128)(2,1)} %pad_maximum_fusion), calls=%async_computation | async-start | bytes 2621440 | tf_op jit(solution)/shard_map/all_to_all | solution.py:137
  9.7 0.1 reduce.3
  10.0 0.1 convert_reduce_fusion
  10.2 0.6 fusion.10
  10.9 0.6 fusion.5
  11.5 0.1 reduce_min.29
  11.6 0.2 fusion.9
  11.8 1.9 %broadcast_subtract_fusion = (s32[4,1]{0,1:T(1,128)S(1)}, pred[4]{0:T(512)(128)(4,1)S(1)}) fusion(s32[4]{0:T(128)S(1)} %reduce_min.29, s32[]{:T(128)} %fusion.5, s32[4]{0:T(128)S(1)} %get-tuple-element.181, s32[]{:T(128)} %get-tuple-element.183, s32[4]{0:T(128)S(1)} %get-tuple-element.180, s32[]{:T(128)} %get-tuple-element.182), kind=kLoop, calls=%fused_computation.69 | loop fusion | flops 36 | bytes 80 | tf_op jit(solution)/shard_map/sub | solution.py:188
  13.8 0.2 reduce-window.11
  13.9 0.2 reduce-window.14
  14.1 0.6 convert_reduce_fusion.2
  14.8 0.6 bitcast_select_fusion
  15.4 0.1 select_reduce_fusion
  15.5 0.7 fusion.7
  16.2 23.9 %all-to-all-done = bf16[8,64,1280]{2,1,0:T(8,128)(2,1)S(1)} async-done(((bf16[8,64,1280]{2,1,0:T(8,128)(2,1)}), bf16[8,64,1280]{2,1,0:T(8,128)(2,1)S(1)}, u32[]{:S(2)}, u32[]{:S(2)}) %all-to-all-start) | async-done | bytes 1310752 | tf_op jit(solution)/shard_map/all_to_all | solution.py:137
  40.1 1.3 collective-permute-start
  41.4 1.3 collective-permute-start.1
  42.7 3.4 %collective-permute-start.2 = (bf16[512,256]{1,0:T(8,128)(2,1)S(1)}, bf16[512,256]{1,0:T(8,128)(2,1)S(1)}, u32[]{:S(2)}, u32[]{:S(2)}) collective-permute-start(bf16[512,256]{1,0:T(8,128)(2,1)S(1)} %get-tuple-element.200), channel_id=1, source_target_pairs={{0,1},{2,3},{4,5},{6,7},{8,9},{10,11},{12,13},{14,15},{16,17},{18,... | collective-permute-start | bytes 786440 | tf_op jit(solution)/shard_map/ppermute | solution.py:141
  46.2 0.6 gather_fusion.1
  46.7 0.6 gather_fusion
  48.0 2.4 %collective-permute-done = bf16[512,256]{1,0:T(8,128)(2,1)S(1)} collective-permute-done((bf16[512,256]{1,0:T(8,128)(2,1)S(1)}, bf16[512,256]{1,0:T(8,128)(2,1)S(1)}, u32[]{:S(2)}, u32[]{:S(2)}) %collective-permute-start) | collective-permute-done | bytes 262176 | tf_op jit(solution)/shard_map/ppermute | solution.py:151
  50.4 7.2 %collective-permute-done.1 = bf16[512,256]{1,0:T(8,128)(2,1)S(1)} collective-permute-done((bf16[512,256]{1,0:T(8,128)(2,1)S(1)}, bf16[512,256]{1,0:T(8,128)(2,1)S(1)}, u32[]{:S(2)}, u32[]{:S(2)}) %collective-permute-start.1) | collective-permute-done | bytes 262176 | tf_op jit(solution)/shard_map/ppermute | solution.py:152
  57.6 0.7 copy-done.2
  58.3 1.1 pad_maximum_fusion.2
  59.4 0.6 gather_fusion.2
  60.0 18.8 %conditional.1 = (bf16[512,512]{1,0:T(8,128)(2,1)}, bf16[512,512]{1,0:T(8,128)(2,1)}, f32[4,512,256]{2,1,0:T(8,128)}) conditional(s32[]{:T(128)} %clamp.3, (s32[1,1,512]{2,1,0:T(1,128)S(1)}, s32[512]{0:T(512)S(1)}, s32[4,512]{1,0:T(4,128)S(1)}, s32[4,512]{1,0:T(4,128)S(1)}, bf16[4,512,256]{2,1,0:T(8,128)(2,1)S(1)}, ...), branch_computations={%region_13.14_spmd, %region_14.15_spmd, %region_15.16_spmd, %regio... | conditional | flops 529408 | bytes 16343096 | solution.py:220
  60.1 0.6 pad_add_fusion.2.kmeta_ref
  60.7 1.0 copy.92
  61.7 0.4 slice.74
  62.2 1.0 copy.80.k_ref.v_ref
  63.2 0.9 copy.79.qmeta_ref
  64.1 11.6 %branch_1_fun.1 = (bf16[512,512]{1,0:T(8,128)(2,1)}, bf16[512,512]{1,0:T(8,128)(2,1)}, f32[128,1024]{1,0:T(8,128)}, f32[128,1024]{1,0:T(8,128)}) custom-call(s32[512,2]{1,0:T(8,128)} %copy.79.qmeta_ref, s32[2,1024]{1,0:T(2,128)} %pad_add_fusion.2.kmeta_ref, bf16[512,1280]{1,0:T(8,128)(2,1)S(1)} %get-tuple-element.62.q_ref.g_ref, ...), custom_call_target="tpu_custom_call" | custom-call | tf_op jit(solution)/shard_map/cond/branch_1_fun/pallas_call | solution.py:96
  75.7 1.3 maximum_bitcast_fusion.1
  77.0 0.3 copy.104
  77.3 1.5 %concatenate.25.clone = f32[4,512,256]{2,1,0:T(8,128)} pad(f32[2,512,256]{2,1,0:T(8,128)S(1)} %bitcast.143, f32[]{:T(128)} %constant.26.clone), padding=0_2x0_0x0_0 | pad | bytes 3145732 | tf_op jit(solution)/shard_map/cond/branch_1_fun/concatenate | solution.py:213
  78.8 2.3 %gather_fusion.3 = f32[4,512,256]{2,1,0:T(8,128)S(1)} fusion(f32[4,512,256]{2,1,0:T(8,128)} %get-tuple-element.179, s32[1024]{0:T(1024)S(1)} %pad_clamp_fusion), kind=kCustom, calls=%fused_computation.3 | custom fusion | bytes 4194320 | tf_op jit(solution)/shard_map/gather | solution.py:223
  81.1 0.2 slice_bitcast_fusion.8
  81.3 1.3 collective-permute-start.3
  82.6 1.3 collective-permute-start.4
  83.9 2.1 %collective-permute-start.5 = (f32[512,256]{1,0:T(8,128)S(1)}, f32[512,256]{1,0:T(8,128)S(1)}, u32[]{:S(2)}, u32[]{:S(2)}) collective-permute-start(f32[512,256]{1,0:T(8,128)S(1)} %get-tuple-element.194), channel_id=1, source_target_pairs={{9,6},{17,14},{25,22},{8,7},{16,15},{24,23}} | collective-permute-start | bytes 1572872 | tf_op jit(solution)/shard_map/ppermute | solution.py:232
  86.0 8.0 %collective-permute-done.3 = f32[512,256]{1,0:T(8,128)S(1)} collective-permute-done((f32[512,256]{1,0:T(8,128)S(1)}, f32[512,256]{1,0:T(8,128)S(1)}, u32[]{:S(2)}, u32[]{:S(2)}) %collective-permute-start.3) | collective-permute-done | bytes 524320 | tf_op jit(solution)/shard_map/ppermute | solution.py:226
  94.0 1.6 %collective-permute-done.5 = f32[512,256]{1,0:T(8,128)S(1)} collective-permute-done((f32[512,256]{1,0:T(8,128)S(1)}, f32[512,256]{1,0:T(8,128)S(1)}, u32[]{:S(2)}, u32[]{:S(2)}) %collective-permute-start.5) | collective-permute-done | bytes 524320 | tf_op jit(solution)/shard_map/ppermute | solution.py:232
  95.6 0.1 fusion.3
  95.7 1.3 pad_maximum_fusion.1
  97.0 39.7 %all_to_all.10 = bf16[8,64,1280]{2,1,0:T(8,128)(2,1)S(1)} all-to-all(bf16[8,64,1280]{2,1,0:T(8,128)(2,1)S(1)} %bitcast.142), channel_id=1, replica_groups=mesh['outer'=4,'inner'=8] {'inner'}, dimensions={0} | all-to-all | bytes 2621440 | tf_op jit(solution)/shard_map/all_to_all | solution.py:238
  136.7 1.1 slice_bitcast_fusion.6
  137.8 0.8 slice_bitcast_fusion.10
  (33 shorter events, 0.7 us)
Async XLA Ops:
  0.6 8.9 %copy-start.3 = (s32[4,8,4]{1,2,0:T(4,128)S(1)}, s32[4,8,4]{1,2,0:T(4,128)}, u32[]{:S(2)}) copy-start(s32[4,8,4]{1,2,0:T(4,128)} %param.13) | copy-start | bytes 1540
  3.1 36.9 %all-to-all-start = ((bf16[8,64,1280]{2,1,0:T(8,128)(2,1)}), bf16[8,64,1280]{2,1,0:T(8,128)(2,1)S(1)}, u32[]{:S(2)}, u32[]{:S(2)}) async-start(bf16[8,64,1280]{2,1,0:T(8,128)(2,1)} %pad_maximum_fusion), calls=%async_computation | async-start | bytes 2621440 | tf_op jit(solution)/shard_map/all_to_all | solution.py:137
  40.1 10.3 %collective-permute-start = (bf16[512,256]{1,0:T(8,128)(2,1)S(1)}, bf16[512,256]{1,0:T(8,128)(2,1)S(1)}, u32[]{:S(2)}, u32[]{:S(2)}) collective-permute-start(bf16[512,256]{1,0:T(8,128)(2,1)S(1)} %get-tuple-element.200), channel_id=1, source_target_pairs={{6,8},{14,16},{22,24},{7,9},{15,17},{23,25}} | collective-permute-start | bytes 786440 | tf_op jit(solution)/shard_map/ppermute | solution.py:151
  41.4 16.2 %collective-permute-start.1 = (bf16[512,256]{1,0:T(8,128)(2,1)S(1)}, bf16[512,256]{1,0:T(8,128)(2,1)S(1)}, u32[]{:S(2)}, u32[]{:S(2)}) collective-permute-start(bf16[512,256]{1,0:T(8,128)(2,1)S(1)} %get-tuple-element.200), channel_id=1, source_target_pairs={{6,9},{14,17},{22,25},{7,8},{15,16},{23,24}} | collective-permute-start | bytes 786440 | tf_op jit(solution)/shard_map/ppermute | solution.py:152
  42.7 14.9 %collective-permute-start.2 = (bf16[512,256]{1,0:T(8,128)(2,1)S(1)}, bf16[512,256]{1,0:T(8,128)(2,1)S(1)}, u32[]{:S(2)}, u32[]{:S(2)}) collective-permute-start(bf16[512,256]{1,0:T(8,128)(2,1)S(1)} %get-tuple-element.200), channel_id=1, source_target_pairs={{0,1},{2,3},{4,5},{6,7},{8,9},{10,11},{12,13},{14,15},{16,17},{18,... | collective-permute-start | bytes 786440 | tf_op jit(solution)/shard_map/ppermute | solution.py:141
  57.6 0.7 copy-start.2
  62.2 1.9 %copy-start.1 = (bf16[32,8,2,512]{3,1,2,0:T(8,128)(2,1)}, bf16[32,8,2,512]{3,1,2,0:T(8,128)(2,1)S(1)}, u32[]{:S(2)}) copy-start(bf16[32,8,2,512]{3,1,2,0:T(8,128)(2,1)S(1)} %copy.107) | copy-start | bytes 1572868 | tf_op jit(solution)/shard_map/cond
  81.3 12.7 %collective-permute-start.3 = (f32[512,256]{1,0:T(8,128)S(1)}, f32[512,256]{1,0:T(8,128)S(1)}, u32[]{:S(2)}, u32[]{:S(2)}) collective-permute-start(f32[512,256]{1,0:T(8,128)S(1)} %get-tuple-element.193), channel_id=1, source_target_pairs={{1,0},{3,2},{5,4},{7,6},{9,8},{11,10},{13,12},{15,14},{17,16},{19,... | collective-permute-start | bytes 1572872 | tf_op jit(solution)/shard_map/ppermute | solution.py:226
  82.6 11.5 %collective-permute-start.4 = (f32[512,256]{1,0:T(8,128)S(1)}, f32[512,256]{1,0:T(8,128)S(1)}, u32[]{:S(2)}, u32[]{:S(2)}) collective-permute-start(f32[512,256]{1,0:T(8,128)S(1)} %get-tuple-element.195), channel_id=1, source_target_pairs={{8,6},{16,14},{24,22},{9,7},{17,15},{25,23}} | collective-permute-start | bytes 1572872 | tf_op jit(solution)/shard_map/ppermute | solution.py:231
  83.9 11.7 %collective-permute-start.5 = (f32[512,256]{1,0:T(8,128)S(1)}, f32[512,256]{1,0:T(8,128)S(1)}, u32[]{:S(2)}, u32[]{:S(2)}) collective-permute-start(f32[512,256]{1,0:T(8,128)S(1)} %get-tuple-element.194), channel_id=1, source_target_pairs={{9,6},{17,14},{25,22},{8,7},{16,15},{24,23}} | collective-permute-start | bytes 1572872 | tf_op jit(solution)/shard_map/ppermute | solution.py:232

commit v9 on v8

--- a/solution.py
+++ b/solution.py
@@ -134,6 +134,8 @@
     packed = jnp.concatenate(
         [queries[0, :, 0], grad_out[0, :, 0], keys[0, :, 0], values[0, :, 0]], axis=-1
     )
+    unit_local = (inner_id + 2 * outer_id) % n_units
+    packed = jnp.roll(packed, -2 * outer_id, axis=0)
     arrived = lax.all_to_all(packed, "inner", 0, 0, tiled=True).reshape(tok_dev, -1)
     kv_own = arrived[:, 2 * width_q :]
 
@@ -142,25 +144,24 @@
 
     both = ("outer", "inner")
     last_a, last_b = n_inner - 2, n_inner - 1
-    send_a = [((o - 1) * n_inner + last_a, o * n_inner) for o in range(1, n_outer)] + [
-        ((o - 1) * n_inner + last_b, o * n_inner + 1) for o in range(1, n_outer)
-    ]
-    send_b = [((o - 1) * n_inner + last_a, o * n_inner + 1) for o in range(1, n_outer)] + [
-        ((o - 1) * n_inner + last_b, o * n_inner) for o in range(1, n_outer)
-    ]
+    lead = [(-2 * o) % n_inner for o in range(n_outer)]
+    send_a = [((o - 1) * n_inner + lead[o] + r, o * n_inner + lead[o] + r)
+              for o in range(1, n_outer) for r in range(2)]
+    send_b = [((o - 1) * n_inner + lead[o] + r, o * n_inner + lead[o] + 1 - r)
+              for o in range(1, n_outer) for r in range(2)]
     recv_a = lax.ppermute(kv_own, both, send_a)
     recv_b = lax.ppermute(kv_own, both, send_b)
-    first = inner_id == 0
+    first = unit_local == 0
     kv_prev_a = jnp.where(first, recv_a, recv_b)
     kv_prev_b = jnp.where(first, recv_b, recv_a)
 
-    unit_id = outer_id * n_units + inner_id
+    unit_id = outer_id * n_units + unit_local
     before = jnp.maximum(outer_id - 1, 0)
-    has_prev = (outer_id > 0) & (inner_id < 2)
-    has_partner = inner_id % 2 == 1
-    query_doc = docs_all[outer_id, inner_id]
+    has_prev = (outer_id > 0) & (unit_local < 2)
+    has_partner = unit_local % 2 == 1
+    query_doc = docs_all[outer_id, unit_local]
     query_pos = unit_id * tok_dev + offsets
-    partner_doc = jnp.where(has_partner, docs_all[outer_id, jnp.maximum(inner_id - 1, 0)], -3)
+    partner_doc = jnp.where(has_partner, docs_all[outer_id, jnp.maximum(unit_local - 1, 0)], -3)
     prev_a_doc = jnp.where(has_prev, docs_all[before, last_a], -4)
     prev_b_doc = jnp.where(has_prev, docs_all[before, last_b], -5)
     key_doc = jnp.concatenate([prev_a_doc, prev_b_doc, partner_doc, query_doc])
@@ -235,7 +236,9 @@
     result = jnp.concatenate([attn, q_grads, kv_total], axis=-1).reshape(
         n_inner, piece_len, -1
     )
-    returned = lax.all_to_all(result, "inner", 0, 0, tiled=True)
+    returned = jnp.roll(
+        lax.all_to_all(result, "inner", 0, 0, tiled=True), 2 * outer_id, axis=0
+    )
     shape_q = (1, n_units, 1, piece_len, width_q)
     shape_k = (1, n_units, 1, piece_len, head_dim)
     return (

time: 139 us -> 139 us (level)
  the two profiles are of different devices: /device:TPU:1 before, /device:TPU:0 now
where the time goes in v9:
time: 139 us; the launch traced here: 138 us
  waiting for transfers between devices  69.3 us (50%)
  starting transfers between devices  31.6 us (23%)
  other arithmetic  16.3 us (12%)
  local copies, waits for them, and re-layouts  10.8 us (8%)
  Pallas kernels  8.44 us (6%)
  between operations  1.59 us (1%)
    all_to_all x1, waiting for transfers between devices, shards(): lax.all_to_all(result, 'inner', 0, 0, tiled=True)  30.8 us
    all_to_all x1, waiting for transfers between devices, shards(): lax.all_to_all(packed, 'inner', 0, 0, tiled=True).reshape(tok_dev, -1)  24.7 us
    all_to_all x1, starting transfers between devices, shards(): lax.all_to_all(result, 'inner', 0, 0, tiled=True)  16.2 us
    ppermute x1, waiting for transfers between devices, shards(): from_partner = lax.ppermute(kv_grads[2], 'inner', pairs_down)  11.5 us
    pallas_call x1, Pallas kernels, attend(): pl.pallas_call(kernel, grid=grid, in_specs=[qmeta_spec, kmeta_spec, q_spe...  8.44 us
    all_to_all x1, starting transfers between devices, shards(): lax.all_to_all(packed, 'inner', 0, 0, tiled=True).reshape(tok_dev, -1)  7.28 us
    concatenate x1, other arithmetic, shards(): packed = jnp.roll(packed, -2 * outer_id, axis=0)  4.08 us
    ppermute x1, starting transfers between devices, shards(): kv_partner = lax.ppermute(kv_own, 'inner', pairs_up)  4.02 us
  transfers between devices with their start and end apart: 8, of which 4 were waited for; matrix products, arithmetic and copies ran while one was open for 6% of the time, Pallas kernels for 0%

profile of v9, /device:TPU:0, one launch (start us, length us, event | category | flops | bytes accessed | tf_op | source)
XLA Modules:
  0.0 138.1 jit_solution(6162951140764503161)
XLA Ops:
  0.7 4.1 %fusion.4 = bf16[8,64,1280]{2,1,0:T(8,128)(2,1)} fusion(s32[]{:T(128)S(6)} %select_n.158, bf16[8,64,512]{2,1,0:T(8,128)(2,1)} %bitcast.144, bf16[8,64,512]{2,1,0:T(8,128)(2,1)} %bitcast.145, bf16[8,64,128]{2,1,0:T(8,128)(2,1)} %bitcast.146, bf16[8,64,128]{2,1,0:T(8,128)(2,1)} %bitcast.147), kind=kLoop, calls=%fused_computation.36 | loop fusion | flops 10485760 | bytes 2621444 | tf_op jit(solution)/shard_map/jit(_roll_dynamic)/concatenate | solution.py:138
  4.7 7.3 %all-to-all-start = ((bf16[8,64,1280]{2,1,0:T(8,128)(2,1)}), bf16[8,64,1280]{2,1,0:T(8,128)(2,1)S(1)}, u32[]{:S(2)}, u32[]{:S(2)}) async-start(bf16[8,64,1280]{2,1,0:T(8,128)(2,1)} %fusion.4), calls=%async_computation | async-start | bytes 2621440 | tf_op jit(solution)/shard_map/all_to_all | solution.py:139
  12.3 0.1 reduce.3
  12.4 0.1 reshape.267
  12.6 0.1 convert_reduce_fusion
  12.7 0.6 fusion.18
  13.4 0.6 fusion.13
  14.1 0.1 reduce_min.29
  14.2 0.2 fusion.17
  14.4 1.9 %broadcast_subtract_fusion = (s32[4,1]{0,1:T(1,128)S(1)}, pred[4]{0:T(512)(128)(4,1)S(1)}) fusion(s32[4]{0:T(128)S(1)} %reduce_min.29, s32[]{:T(128)} %fusion.13, s32[4]{0:T(128)S(1)} %get-tuple-element.182, s32[]{:T(128)} %get-tuple-element.184, s32[4]{0:T(128)S(1)} %get-tuple-element.181, s32[]{:T(128)} %get-tuple-element.183), kind=kLoop, calls=%fused_computation.89 | loop fusion | flops 36 | bytes 80 | tf_op jit(solution)/shard_map/sub | solution.py:189
  16.3 0.2 reduce-window.11
  16.5 0.2 reduce-window.14
  16.7 0.6 convert_reduce_fusion.2
  17.3 0.6 bitcast_select_fusion
  18.0 0.1 select_reduce_fusion
  18.1 0.7 fusion.15
  18.8 24.7 %all-to-all-done = bf16[8,64,1280]{2,1,0:T(8,128)(2,1)S(1)} async-done(((bf16[8,64,1280]{2,1,0:T(8,128)(2,1)}), bf16[8,64,1280]{2,1,0:T(8,128)(2,1)S(1)}, u32[]{:S(2)}, u32[]{:S(2)}) %all-to-all-start) | async-done | bytes 1310752 | tf_op jit(solution)/shard_map/all_to_all | solution.py:139
  43.5 0.7 collective-permute-start
  44.2 0.7 collective-permute-start.1
  44.9 4.0 %collective-permute-start.2 = (bf16[512,256]{1,0:T(8,128)(2,1)S(1)}, bf16[512,256]{1,0:T(8,128)(2,1)}, u32[]{:S(2)}, u32[]{:S(2)}) collective-permute-start(bf16[512,256]{1,0:T(8,128)(2,1)S(1)} %get-tuple-element.201), channel_id=1, source_target_pairs={{0,1},{2,3},{4,5},{6,7},{8,9},{10,11},{12,13},{14,15},{16,17},{18,... | collective-permute-start | bytes 786440 | tf_op jit(solution)/shard_map/ppermute | solution.py:143
  48.9 0.6 gather_fusion.1
  49.5 0.6 gather_fusion
  50.7 2.3 %collective-permute-done.2 = bf16[512,256]{1,0:T(8,128)(2,1)} collective-permute-done((bf16[512,256]{1,0:T(8,128)(2,1)S(1)}, bf16[512,256]{1,0:T(8,128)(2,1)}, u32[]{:S(2)}, u32[]{:S(2)}) %collective-permute-start.2) | collective-permute-done | bytes 262176 | tf_op jit(solution)/shard_map/ppermute | solution.py:143
  53.0 1.1 pad_maximum_fusion.1
  54.1 0.6 gather_fusion.2
  54.7 14.8 %conditional.1 = (bf16[512,512]{1,0:T(8,128)(2,1)}, bf16[512,512]{1,0:T(8,128)(2,1)}, f32[4,512,256]{2,1,0:T(8,128)}) conditional(s32[]{:T(128)} %clamp.3, (s32[1,1,512]{2,1,0:T(1,128)S(1)}, s32[512]{0:T(512)S(1)}, s32[4,512]{1,0:T(4,128)S(1)}, s32[4,512]{1,0:T(4,128)S(1)}, bf16[4,512,256]{2,1,0:T(8,128)(2,1)S(1)}, ...), branch_computations={%region_13.15_spmd, %region_14.16_spmd, %region_15.17_spmd, %regio... | conditional | flops 529408 | bytes 16343096 | solution.py:221
  54.7 0.5 copy.91
  55.3 0.7 slice_bitcast_fusion
  56.0 0.8 copy.76.k_ref.v_ref
  56.9 0.9 copy.75.qmeta_ref
  57.7 0.6 pad_add_fusion.1.kmeta_ref
  58.3 8.4 %branch_0_fun.1 = (bf16[512,512]{1,0:T(8,128)(2,1)}, bf16[512,512]{1,0:T(8,128)(2,1)}, f32[128,512]{1,0:T(8,128)}, f32[128,512]{1,0:T(8,128)}) custom-call(s32[512,2]{1,0:T(8,128)} %copy.75.qmeta_ref, s32[2,512]{1,0:T(2,128)} %pad_add_fusion.1.kmeta_ref, bf16[512,1280]{1,0:T(8,128)(2,1)S(1)} %get-tuple-element.53.q_ref.g_ref, ...), custom_call_target="tpu_custom_call" | custom-call | tf_op jit(solution)/shard_map/cond/branch_0_fun/pallas_call | solution.py:96
  66.8 1.1 maximum_bitcast_fusion
  67.9 0.2 copy.102
  68.1 1.5 %concatenate.26.clone = f32[4,512,256]{2,1,0:T(8,128)} pad(f32[1,512,256]{2,1,0:T(8,128)S(1)} %copy.102, f32[]{:T(128)} %constant.79.clone), padding=0_3x0_0x0_0 | pad | bytes 2621444 | tf_op jit(solution)/shard_map/cond/branch_0_fun/concatenate | solution.py:214
  69.6 2.3 %gather_fusion.3 = f32[4,512,256]{2,1,0:T(8,128)S(1)} fusion(f32[4,512,256]{2,1,0:T(8,128)} %get-tuple-element.180, s32[1024]{0:T(1024)S(1)} %pad_clamp_fusion), kind=kCustom, calls=%fused_computation.3 | custom fusion | bytes 4194320 | tf_op jit(solution)/shard_map/gather | solution.py:224
  71.9 0.2 slice_bitcast_fusion.8
  72.0 1.3 collective-permute-start.3
  73.3 0.7 collective-permute-start.4
  74.0 0.7 collective-permute-start.5
  74.7 11.5 %collective-permute-done.3 = f32[512,256]{1,0:T(8,128)S(1)} collective-permute-done((f32[512,256]{1,0:T(8,128)S(1)}, f32[512,256]{1,0:T(8,128)S(1)}, u32[]{:S(2)}, u32[]{:S(2)}) %collective-permute-start.3) | collective-permute-done | bytes 524320 | tf_op jit(solution)/shard_map/ppermute | solution.py:227
  86.2 0.1 fusion.11
  86.4 2.3 %pad_maximum_fusion = bf16[512,1280]{1,0:T(8,128)(2,1)} fusion(bf16[512,256]{1,0:T(8,128)(2,1)S(1)} %fusion.11, bf16[512,512]{1,0:T(8,128)(2,1)} %get-tuple-element.97, bf16[512,512]{1,0:T(8,128)(2,1)} %get-tuple-element.96), kind=kLoop, calls=%fused_computation.40 | loop fusion | flops 3932160 | bytes 2621440 | tf_op jit(solution)/shard_map/concatenate | solution.py:236
  88.7 16.2 %all-to-all-start.1 = ((bf16[8,64,1280]{2,1,0:T(8,128)(2,1)}), bf16[8,64,1280]{2,1,0:T(8,128)(2,1)S(1)}, u32[]{:S(2)}, u32[]{:S(2)}) async-start(bf16[8,64,1280]{2,1,0:T(8,128)(2,1)} %bitcast.48), calls=%async_computation.1 | async-start | bytes 2621440 | tf_op jit(solution)/shard_map/all_to_all | solution.py:240
  105.0 30.8 %all-to-all-done.1 = bf16[8,64,1280]{2,1,0:T(8,128)(2,1)S(1)} async-done(((bf16[8,64,1280]{2,1,0:T(8,128)(2,1)}), bf16[8,64,1280]{2,1,0:T(8,128)(2,1)S(1)}, u32[]{:S(2)}, u32[]{:S(2)}) %all-to-all-start.1) | async-done | bytes 1310752 | tf_op jit(solution)/shard_map/all_to_all | solution.py:240
  135.8 0.5 fusion
  136.3 1.1 slice_bitcast_fusion.6
  137.3 0.8 slice_bitcast_fusion.10
  (29 shorter events, 0.5 us)
Async XLA Ops:
  0.7 11.4 %copy-start.2 = (s32[4,8,4]{1,2,0:T(4,128)S(1)}, s32[4,8,4]{1,2,0:T(4,128)}, u32[]{:S(2)}) copy-start(s32[4,8,4]{1,2,0:T(4,128)} %param.15) | copy-start | bytes 1540
  4.7 38.7 %all-to-all-start = ((bf16[8,64,1280]{2,1,0:T(8,128)(2,1)}), bf16[8,64,1280]{2,1,0:T(8,128)(2,1)S(1)}, u32[]{:S(2)}, u32[]{:S(2)}) async-start(bf16[8,64,1280]{2,1,0:T(8,128)(2,1)} %fusion.4), calls=%async_computation | async-start | bytes 2621440 | tf_op jit(solution)/shard_map/all_to_all | solution.py:139
  43.5 7.2 %collective-permute-start = (bf16[512,256]{1,0:T(8,128)(2,1)S(1)}, bf16[512,256]{1,0:T(8,128)(2,1)S(1)}, u32[]{:S(2)}, u32[]{:S(2)}) collective-permute-start(bf16[512,256]{1,0:T(8,128)(2,1)S(1)} %get-tuple-element.201), channel_id=1, source_target_pairs={{6,14},{7,15},{12,20},{13,21},{18,26},{19,27}} | collective-permute-start | bytes 786440 | tf_op jit(solution)/shard_map/ppermute | solution.py:152
  44.2 6.5 %collective-permute-start.1 = (bf16[512,256]{1,0:T(8,128)(2,1)S(1)}, bf16[512,256]{1,0:T(8,128)(2,1)S(1)}, u32[]{:S(2)}, u32[]{:S(2)}) collective-permute-start(bf16[512,256]{1,0:T(8,128)(2,1)S(1)} %get-tuple-element.201), channel_id=1, source_target_pairs={{6,15},{7,14},{12,21},{13,20},{18,27},{19,26}} | collective-permute-start | bytes 786440 | tf_op jit(solution)/shard_map/ppermute | solution.py:153
  44.9 8.2 %collective-permute-start.2 = (bf16[512,256]{1,0:T(8,128)(2,1)S(1)}, bf16[512,256]{1,0:T(8,128)(2,1)}, u32[]{:S(2)}, u32[]{:S(2)}) collective-permute-start(bf16[512,256]{1,0:T(8,128)(2,1)S(1)} %get-tuple-element.201), channel_id=1, source_target_pairs={{0,1},{2,3},{4,5},{6,7},{8,9},{10,11},{12,13},{14,15},{16,17},{18,... | collective-permute-start | bytes 786440 | tf_op jit(solution)/shard_map/ppermute | solution.py:143
  72.0 14.2 %collective-permute-start.3 = (f32[512,256]{1,0:T(8,128)S(1)}, f32[512,256]{1,0:T(8,128)S(1)}, u32[]{:S(2)}, u32[]{:S(2)}) collective-permute-start(f32[512,256]{1,0:T(8,128)S(1)} %get-tuple-element.194), channel_id=1, source_target_pairs={{1,0},{3,2},{5,4},{7,6},{9,8},{11,10},{13,12},{15,14},{17,16},{19,... | collective-permute-start | bytes 1572872 | tf_op jit(solution)/shard_map/ppermute | solution.py:227
  73.3 12.9 %collective-permute-start.4 = (f32[512,256]{1,0:T(8,128)S(1)}, f32[512,256]{1,0:T(8,128)S(1)}, u32[]{:S(2)}, u32[]{:S(2)}) collective-permute-start(f32[512,256]{1,0:T(8,128)S(1)} %get-tuple-element.196), channel_id=1, source_target_pairs={{14,6},{15,7},{20,12},{21,13},{26,18},{27,19}} | collective-permute-start | bytes 1572872 | tf_op jit(solution)/shard_map/ppermute | solution.py:232
  74.0 12.2 %collective-permute-start.5 = (f32[512,256]{1,0:T(8,128)S(1)}, f32[512,256]{1,0:T(8,128)S(1)}, u32[]{:S(2)}, u32[]{:S(2)}) collective-permute-start(f32[512,256]{1,0:T(8,128)S(1)} %get-tuple-element.195), channel_id=1, source_target_pairs={{15,6},{14,7},{21,12},{20,13},{27,18},{26,19}} | collective-permute-start | bytes 1572872 | tf_op jit(solution)/shard_map/ppermute | solution.py:233
  88.7 47.1 %all-to-all-start.1 = ((bf16[8,64,1280]{2,1,0:T(8,128)(2,1)}), bf16[8,64,1280]{2,1,0:T(8,128)(2,1)S(1)}, u32[]{:S(2)}, u32[]{:S(2)}) async-start(bf16[8,64,1280]{2,1,0:T(8,128)(2,1)} %bitcast.48), calls=%async_computation.1 | async-start | bytes 2621440 | tf_op jit(solution)/shard_map/all_to_all | solution.py:240

commit v10 on v9

--- a/solution.py
+++ b/solution.py
@@ -45,10 +45,8 @@
         scores = jnp.dot(q, kt, preferred_element_type=jnp.float32) * scaling
         scores = jnp.where(allowed, scores, -jnp.inf)
         row_max = jnp.max(scores, axis=1, keepdims=True)
-        log_total = row_max + jnp.log(
-            jnp.sum(jnp.exp(scores - row_max), axis=1, keepdims=True)
-        )
-        probs = jnp.exp(scores - log_total)
+        shifted = jnp.exp(scores - row_max)
+        probs = shifted * (1.0 / jnp.sum(shifted, axis=1, keepdims=True))
         probs_low = probs.astype(jnp.bfloat16)
         attn = jnp.dot(probs_low, v, preferred_element_type=jnp.float32).astype(jnp.bfloat16)
         o_ref[:, cols] = attn
@@ -131,11 +129,13 @@
     docs_all = doc_table(doc_starts, tok_dev)
     offsets = jnp.arange(tok_dev, dtype=jnp.int32)
 
+    rotated = (jnp.arange(n_units, dtype=jnp.int32) + 2 * outer_id) % n_units
     packed = jnp.concatenate(
-        [queries[0, :, 0], grad_out[0, :, 0], keys[0, :, 0], values[0, :, 0]], axis=-1
+        [queries[0, rotated, 0], grad_out[0, rotated, 0], keys[0, rotated, 0],
+         values[0, rotated, 0]],
+        axis=-1,
     )
     unit_local = (inner_id + 2 * outer_id) % n_units
-    packed = jnp.roll(packed, -2 * outer_id, axis=0)
     arrived = lax.all_to_all(packed, "inner", 0, 0, tiled=True).reshape(tok_dev, -1)
     kv_own = arrived[:, 2 * width_q :]
 
@@ -236,9 +236,8 @@
     result = jnp.concatenate([attn, q_grads, kv_total], axis=-1).reshape(
         n_inner, piece_len, -1
     )
-    returned = jnp.roll(
-        lax.all_to_all(result, "inner", 0, 0, tiled=True), 2 * outer_id, axis=0
-    )
+    restored = (jnp.arange(n_units, dtype=jnp.int32) - 2 * outer_id) % n_units
+    returned = lax.all_to_all(result, "inner", 0, 0, tiled=True)[restored]
     shape_q = (1, n_units, 1, piece_len, width_q)
     shape_k = (1, n_units, 1, piece_len, head_dim)
     return (

time: 139 us -> 147 us (1.058)
  local copies, waits for them, and re-layouts: 10.8 us -> 20.1 us
  starting transfers between devices: 31.6 us -> 27 us
  waiting for transfers between devices: 69.3 us -> 73.7 us
  other arithmetic: 16.3 us -> 14.3 us
    gather x0 -> x5, local copies, waits for them, and re-layouts: none -> 3.98 us  [the longest x1 1.62 us: shards(): grad_out[0, rotated, 0]]
    all_to_all x1, starting transfers between devices: 16.2 us -> 12.4 us  [shards(): returned = lax.all_to_all(result, 'inner', 0, 0, tiled=True)[restored]]
    ppermute x1, waiting for transfers between devices: 11.5 us -> 15.3 us  [shards(): from_partner = lax.ppermute(kv_grads[2], 'inner', pairs_down)]
    concatenate x2, other arithmetic: 4.55 us -> 1.2 us  [the longest x1 1.19 us: shards(): jnp.concatenate([queries[0, rotated, 0], grad_out[0, rotated, 0], keys[0,...]
  transfers between devices with their start and end apart: 8 -> 8, of which waited for: 4 -> 4; matrix products, arithmetic and copies ran while one was open for 6% -> 5% of each run, Pallas kernels for 0% -> 0%
where the time goes in v10:
time: 147 us; the launch traced here: 145 us
  waiting for transfers between devices  73.7 us (50%)
  starting transfers between devices  27 us (18%)
  local copies, waits for them, and re-layouts  20.1 us (14%)
  other arithmetic  14.3 us (10%)
  Pallas kernels  8.48 us (6%)
  between operations  1.67 us (1%)
    all_to_all x1, waiting for transfers between devices, shards(): returned = lax.all_to_all(result, 'inner', 0, 0, tiled=True)[restored]  30.8 us
    all_to_all x1, waiting for transfers between devices, shards(): lax.all_to_all(packed, 'inner', 0, 0, tiled=True).reshape(tok_dev, -1)  24.7 us
    ppermute x1, waiting for transfers between devices, shards(): from_partner = lax.ppermute(kv_grads[2], 'inner', pairs_down)  15.3 us
    all_to_all x1, starting transfers between devices, shards(): returned = lax.all_to_all(result, 'inner', 0, 0, tiled=True)[restored]  12.4 us
    pallas_call x1, Pallas kernels, attend(): pl.pallas_call(kernel, grid=grid, in_specs=[qmeta_spec, kmeta_spec, q_spe...  8.48 us
    all_to_all x1, starting transfers between devices, shards(): lax.all_to_all(packed, 'inner', 0, 0, tiled=True).reshape(tok_dev, -1)  7.28 us
    gather x1, local copies, waits for them, and re-layouts, shards(): kv_grads = grads_sorted[rank]  3.62 us
    ppermute x1, starting transfers between devices, shards(): kv_partner = lax.ppermute(kv_own, 'inner', pairs_up)  3.34 us
  transfers between devices with their start and end apart: 8, of which 4 were waited for; matrix products, arithmetic and copies ran while one was open for 5% of the time, Pallas kernels for 0%

profile of v10, /device:TPU:0, one launch (start us, length us, event | category | flops | bytes accessed | tf_op | source)
XLA Modules:
  0.0 145.3 jit_solution(10657396026343512467)
XLA Ops:
  0.7 1.0 copy-done
  1.7 0.6 gather_fusion.2
  2.3 1.6 %gather_fusion.3 = bf16[8,64,512]{2,1,0:T(8,128)(2,1)S(1)} fusion(bf16[1,8,1,64,512]{4,3,2,1,0:T(8,128)(2,1)} %param.12, s32[8]{0:T(128)S(1)} %fusion.11), kind=kCustom, calls=%fused_computation.3 | custom fusion | bytes 1048672 | tf_op jit(solution)/shard_map/gather | solution.py:134
  3.9 0.6 gather_fusion.4
  4.5 0.6 gather_fusion.5
  5.1 1.2 pad_maximum_fusion
  6.3 7.3 %all-to-all-start = ((bf16[8,64,1280]{2,1,0:T(8,128)(2,1)}), bf16[8,64,1280]{2,1,0:T(8,128)(2,1)S(1)}, u32[]{:S(2)}, u32[]{:S(2)}) async-start(bf16[8,64,1280]{2,1,0:T(8,128)(2,1)} %pad_maximum_fusion), calls=%async_computation | async-start | bytes 2621440 | tf_op jit(solution)/shard_map/all_to_all | solution.py:139
  14.3 0.6 fusion.16
  15.0 0.6 fusion.5
  15.8 0.2 fusion.15
  15.9 1.9 %broadcast_subtract_fusion = (s32[4,1]{0,1:T(1,128)S(1)}, pred[4]{0:T(512)(128)(4,1)S(1)}) fusion(s32[4]{0:T(128)S(1)} %reduce_min.29, s32[]{:T(128)} %fusion.5, s32[4]{0:T(128)S(1)} %get-tuple-element.181, s32[]{:T(128)} %get-tuple-element.183, s32[4]{0:T(128)S(1)} %get-tuple-element.180, s32[]{:T(128)} %get-tuple-element.182), kind=kLoop, calls=%fused_computation.89 | loop fusion | flops 36 | bytes 80 | tf_op jit(solution)/shard_map/sub | solution.py:189
  17.9 0.2 reduce-window.11
  18.1 0.2 reduce-window.14
  18.2 0.6 convert_reduce_fusion.2
  18.9 0.6 bitcast_select_fusion
  19.6 0.7 fusion.12
  20.3 24.7 %all-to-all-done = bf16[8,64,1280]{2,1,0:T(8,128)(2,1)S(1)} async-done(((bf16[8,64,1280]{2,1,0:T(8,128)(2,1)}), bf16[8,64,1280]{2,1,0:T(8,128)(2,1)S(1)}, u32[]{:S(2)}, u32[]{:S(2)}) %all-to-all-start) | async-done | bytes 1310752 | tf_op jit(solution)/shard_map/all_to_all | solution.py:139
  45.0 0.7 collective-permute-start
  45.7 0.7 collective-permute-start.1
  46.4 3.3 %collective-permute-start.2 = (bf16[512,256]{1,0:T(8,128)(2,1)S(1)}, bf16[512,256]{1,0:T(8,128)(2,1)S(1)}, u32[]{:S(2)}, u32[]{:S(2)}) collective-permute-start(bf16[512,256]{1,0:T(8,128)(2,1)S(1)} %get-tuple-element.200), channel_id=1, source_target_pairs={{0,1},{2,3},{4,5},{6,7},{8,9},{10,11},{12,13},{14,15},{16,17},{18,... | collective-permute-start | bytes 786440 | tf_op jit(solution)/shard_map/ppermute | solution.py:143
  49.7 0.6 gather_fusion.1
  50.3 0.6 gather_fusion
  51.6 2.9 %collective-permute-done.2 = bf16[512,256]{1,0:T(8,128)(2,1)S(1)} collective-permute-done((bf16[512,256]{1,0:T(8,128)(2,1)S(1)}, bf16[512,256]{1,0:T(8,128)(2,1)S(1)}, u32[]{:S(2)}, u32[]{:S(2)}) %collective-permute-start.2) | collective-permute-done | bytes 262176 | tf_op jit(solution)/shard_map/ppermute | solution.py:143
  54.5 1.1 pad_maximum_fusion.2
  55.7 1.8 %gather_fusion.6 = bf16[4,512,256]{2,1,0:T(8,128)(2,1)S(1)} fusion(bf16[4,512,256]{2,1,0:T(8,128)(2,1)} %pad_maximum_fusion.2, s32[1024]{0:T(1024)S(1)} %pad_clamp_fusion.2), kind=kCustom, calls=%fused_computation.6 | custom fusion | bytes 2097168 | tf_op jit(solution)/shard_map/gather | solution.py:195
  57.5 16.6 %conditional.1 = (bf16[512,512]{1,0:T(8,128)(2,1)}, bf16[512,512]{1,0:T(8,128)(2,1)}, f32[4,512,256]{2,1,0:T(8,128)}) conditional(s32[]{:T(128)} %clamp.3, (s32[1,1,512]{2,1,0:T(1,128)S(1)}, s32[512]{0:T(512)S(1)}, s32[4,512]{1,0:T(4,128)S(1)}, s32[4,512]{1,0:T(4,128)S(1)}, bf16[4,512,256]{2,1,0:T(8,128)(2,1)S(1)}, ...), branch_computations={%region_13.14_spmd, %region_14.15_spmd, %region_15.16_spmd, %regio... | conditional | flops 529408 | bytes 14745656 | solution.py:221
  57.5 1.3 copy.91
  58.9 1.7 %slice_bitcast_fusion = (bf16[256,512]{1,0:T(8,128)(2,1)}, bf16[512,256]{0,1:T(8,128)(2,1)S(1)}) fusion(bf16[4,512,256]{1,2,0:T(8,128)(2,1)} %copy.91), kind=kLoop, calls=%fused_computation.10 | loop fusion | bytes 786432 | tf_op jit(solution)/shard_map/cond/branch_0_fun/transpose | solution.py:87
  60.6 0.8 copy.76.k_ref.v_ref
  61.4 0.9 copy.75.qmeta_ref
  62.3 0.6 pad_add_fusion.1.kmeta_ref
  62.9 8.5 %branch_0_fun.1 = (bf16[512,512]{1,0:T(8,128)(2,1)}, bf16[512,512]{1,0:T(8,128)(2,1)}, f32[128,512]{1,0:T(8,128)}, f32[128,512]{1,0:T(8,128)}) custom-call(s32[512,2]{1,0:T(8,128)} %copy.75.qmeta_ref, s32[2,512]{1,0:T(2,128)} %pad_add_fusion.1.kmeta_ref, bf16[512,1280]{1,0:T(8,128)(2,1)S(1)} %get-tuple-element.52.q_ref.g_ref, ...), custom_call_target="tpu_custom_call" | custom-call | tf_op jit(solution)/shard_map/cond/branch_0_fun/pallas_call | solution.py:94
  71.4 1.1 maximum_bitcast_fusion
  72.4 0.2 copy.102
  72.6 1.5 %concatenate.12.clone = f32[4,512,256]{2,1,0:T(8,128)} pad(f32[1,512,256]{2,1,0:T(8,128)S(1)} %copy.102, f32[]{:T(128)} %constant.77.clone), padding=0_3x0_0x0_0 | pad | bytes 2621444 | tf_op jit(solution)/shard_map/cond/branch_0_fun/concatenate | solution.py:214
  74.1 3.6 %gather_fusion.7 = f32[4,512,256]{2,1,0:T(8,128)} fusion(f32[4,512,256]{2,1,0:T(8,128)} %get-tuple-element.179, s32[1024]{0:T(1024)S(1)} %pad_clamp_fusion.1), kind=kCustom, calls=%fused_computation.7 | custom fusion | bytes 4194320 | tf_op jit(solution)/shard_map/gather | solution.py:224
  77.7 1.6 %slice_bitcast_fusion.8 = (f32[512,256]{1,0:T(8,128)S(1)}, f32[512,256]{1,0:T(8,128)S(1)}, f32[512,256]{1,0:T(8,128)S(1)}) fusion(f32[4,512,256]{2,1,0:T(8,128)} %gather_fusion.7, pred[]{:T(512)S(6)} %eq.55), kind=kLoop, calls=%fused_computation.32 | loop fusion | flops 262144 | bytes 3145729 | tf_op jit(solution)/shard_map/squeeze | solution.py:227
  79.3 1.3 collective-permute-start.3
  80.6 0.7 collective-permute-start.4
  81.3 0.7 collective-permute-start.5
  82.0 15.3 %collective-permute-done.3 = f32[512,256]{1,0:T(8,128)S(1)} collective-permute-done((f32[512,256]{1,0:T(8,128)S(1)}, f32[512,256]{1,0:T(8,128)S(1)}, u32[]{:S(2)}, u32[]{:S(2)}) %collective-permute-start.3) | collective-permute-done | bytes 524320 | tf_op jit(solution)/shard_map/ppermute | solution.py:227
  97.3 1.2 fusion.3
  98.5 1.1 pad_maximum_fusion.1
  99.6 12.4 %all-to-all-start.1 = ((bf16[8,64,1280]{2,1,0:T(8,128)(2,1)}), bf16[8,64,1280]{2,1,0:T(8,128)(2,1)S(1)}, u32[]{:S(2)}, u32[]{:S(2)}) async-start(bf16[8,64,1280]{2,1,0:T(8,128)(2,1)} %bitcast.45), calls=%async_computation.1 | async-start | bytes 2621440 | tf_op jit(solution)/shard_map/all_to_all | solution.py:240
  112.0 30.8 %all-to-all-done.1 = bf16[8,64,1280]{2,1,0:T(8,128)(2,1)S(1)} async-done(((bf16[8,64,1280]{2,1,0:T(8,128)(2,1)}), bf16[8,64,1280]{2,1,0:T(8,128)(2,1)S(1)}, u32[]{:S(2)}, u32[]{:S(2)}) %all-to-all-start.1) | async-done | bytes 1310752 | tf_op jit(solution)/shard_map/all_to_all | solution.py:240
  142.8 0.6 gather_fusion.8
  143.5 1.1 slice_bitcast_fusion.6
  144.5 0.8 slice_bitcast_fusion.10
  (46 shorter events, 1.1 us)
Async XLA Ops:
  0.6 1.0 copy-start
  0.6 3.3 %copy-start.4 = (bf16[1,8,1,64,128]{4,3,2,1,0:T(8,128)(2,1)S(1)}, bf16[1,8,1,64,128]{4,3,2,1,0:T(8,128)(2,1)}, u32[]{:S(2)}) copy-start(bf16[1,8,1,64,128]{4,3,2,1,0:T(8,128)(2,1)} %param.10) | copy-start | bytes 393220
  0.7 3.8 %copy-start.5 = (bf16[1,8,1,64,128]{4,3,2,1,0:T(8,128)(2,1)S(1)}, bf16[1,8,1,64,128]{4,3,2,1,0:T(8,128)(2,1)}, u32[]{:S(2)}) copy-start(bf16[1,8,1,64,128]{4,3,2,1,0:T(8,128)(2,1)} %param.11) | copy-start | bytes 393220
  5.1 8.5 %copy-start.6 = (s32[4,8,4]{1,2,0:T(4,128)S(1)}, s32[4,8,4]{1,2,0:T(4,128)}, u32[]{:S(2)}) copy-start(s32[4,8,4]{1,2,0:T(4,128)} %param.13) | copy-start | bytes 1540
  6.3 38.7 %all-to-all-start = ((bf16[8,64,1280]{2,1,0:T(8,128)(2,1)}), bf16[8,64,1280]{2,1,0:T(8,128)(2,1)S(1)}, u32[]{:S(2)}, u32[]{:S(2)}) async-start(bf16[8,64,1280]{2,1,0:T(8,128)(2,1)} %pad_maximum_fusion), calls=%async_computation | async-start | bytes 2621440 | tf_op jit(solution)/shard_map/all_to_all | solution.py:139
  45.0 6.5 %collective-permute-start = (bf16[512,256]{1,0:T(8,128)(2,1)S(1)}, bf16[512,256]{1,0:T(8,128)(2,1)S(1)}, u32[]{:S(2)}, u32[]{:S(2)}) collective-permute-start(bf16[512,256]{1,0:T(8,128)(2,1)S(1)} %get-tuple-element.200), channel_id=1, source_target_pairs={{6,14},{7,15},{12,20},{13,21},{18,26},{19,27}} | collective-permute-start | bytes 786440 | tf_op jit(solution)/shard_map/ppermute | solution.py:152
  45.7 5.9 %collective-permute-start.1 = (bf16[512,256]{1,0:T(8,128)(2,1)S(1)}, bf16[512,256]{1,0:T(8,128)(2,1)S(1)}, u32[]{:S(2)}, u32[]{:S(2)}) collective-permute-start(bf16[512,256]{1,0:T(8,128)(2,1)S(1)} %get-tuple-element.200), channel_id=1, source_target_pairs={{6,15},{7,14},{12,21},{13,20},{18,27},{19,26}} | collective-permute-start | bytes 786440 | tf_op jit(solution)/shard_map/ppermute | solution.py:153
  46.4 8.2 %collective-permute-start.2 = (bf16[512,256]{1,0:T(8,128)(2,1)S(1)}, bf16[512,256]{1,0:T(8,128)(2,1)S(1)}, u32[]{:S(2)}, u32[]{:S(2)}) collective-permute-start(bf16[512,256]{1,0:T(8,128)(2,1)S(1)} %get-tuple-element.200), channel_id=1, source_target_pairs={{0,1},{2,3},{4,5},{6,7},{8,9},{10,11},{12,13},{14,15},{16,17},{18,... | collective-permute-start | bytes 786440 | tf_op jit(solution)/shard_map/ppermute | solution.py:143
  77.7 20.8 %copy-start.2 = (bf16[512,512]{1,0:T(8,128)(2,1)S(1)}, bf16[512,512]{1,0:T(8,128)(2,1)}, u32[]{:S(2)}) copy-start(bf16[512,512]{1,0:T(8,128)(2,1)} %get-tuple-element.95) | copy-start | bytes 1572868
  77.7 20.8 %copy-start.3 = (bf16[512,512]{1,0:T(8,128)(2,1)S(1)}, bf16[512,512]{1,0:T(8,128)(2,1)}, u32[]{:S(2)}) copy-start(bf16[512,512]{1,0:T(8,128)(2,1)} %get-tuple-element.96) | copy-start | bytes 1572868
  79.3 18.0 %collective-permute-start.3 = (f32[512,256]{1,0:T(8,128)S(1)}, f32[512,256]{1,0:T(8,128)S(1)}, u32[]{:S(2)}, u32[]{:S(2)}) collective-permute-start(f32[512,256]{1,0:T(8,128)S(1)} %get-tuple-element.193), channel_id=1, source_target_pairs={{1,0},{3,2},{5,4},{7,6},{9,8},{11,10},{13,12},{15,14},{17,16},{19,... | collective-permute-start | bytes 1572872 | tf_op jit(solution)/shard_map/ppermute | solution.py:227
  80.6 16.7 %collective-permute-start.4 = (f32[512,256]{1,0:T(8,128)S(1)}, f32[512,256]{1,0:T(8,128)S(1)}, u32[]{:S(2)}, u32[]{:S(2)}) collective-permute-start(f32[512,256]{1,0:T(8,128)S(1)} %get-tuple-element.195), channel_id=1, source_target_pairs={{14,6},{15,7},{20,12},{21,13},{26,18},{27,19}} | collective-permute-start | bytes 1572872 | tf_op jit(solution)/shard_map/ppermute | solution.py:232
  81.3 16.0 %collective-permute-start.5 = (f32[512,256]{1,0:T(8,128)S(1)}, f32[512,256]{1,0:T(8,128)S(1)}, u32[]{:S(2)}, u32[]{:S(2)}) collective-permute-start(f32[512,256]{1,0:T(8,128)S(1)} %get-tuple-element.194), channel_id=1, source_target_pairs={{15,6},{14,7},{21,12},{20,13},{27,18},{26,19}} | collective-permute-start | bytes 1572872 | tf_op jit(solution)/shard_map/ppermute | solution.py:233
  99.6 43.2 %all-to-all-start.1 = ((bf16[8,64,1280]{2,1,0:T(8,128)(2,1)}), bf16[8,64,1280]{2,1,0:T(8,128)(2,1)S(1)}, u32[]{:S(2)}, u32[]{:S(2)}) async-start(bf16[8,64,1280]{2,1,0:T(8,128)(2,1)} %bitcast.45), calls=%async_computation.1 | async-start | bytes 2621440 | tf_op jit(solution)/shard_map/all_to_all | solution.py:240

commit v11 on v9

--- a/solution.py
+++ b/solution.py
@@ -22,7 +22,7 @@
 
 
 def attention_kernel(
-    qmeta_ref, kmeta_ref, q_ref, g_ref, k_ref, v_ref, kt_ref, vt_ref,
+    qmeta_ref, kmeta_ref, q_ref, g_ref, k_ref, v_ref,
     o_ref, dq_ref, dkt_ref, dvt_ref, *, scaling, n_heads, head_dim
 ):
     @pl.when(pl.program_id(0) == 0)
@@ -32,8 +32,8 @@
 
     k = k_ref[...]
     v = v_ref[...]
-    kt = kt_ref[...]
-    vt = vt_ref[...]
+    kt = k.T
+    vt = v.T
     contract_first = (((0,), (0,)), ((), ()))
     allowed = (qmeta_ref[:, 0:1] == kmeta_ref[0:1, :]) & (
         kmeta_ref[1:2, :] <= qmeta_ref[:, 1:2]
@@ -69,10 +69,9 @@
         )
 
 
-def attend(rows, query_pos, query_doc, ctx, key_pos, key_doc, n_heads):
+def attend(rows, qmeta, ctx_all, kmeta_all, n_keys, n_heads):
     n_rows = rows.shape[0]
-    n_keys, kv_width = ctx.shape
-    head_dim = kv_width // 2
+    head_dim = ctx_all.shape[1] // 2
     width_q = n_heads * head_dim
     block_q = min(256, n_rows)
     grid = (n_rows // block_q,)
@@ -82,11 +81,8 @@
     kmeta_spec = pl.BlockSpec((2, n_keys), lambda i: (0, 0))
     k_spec = pl.BlockSpec((n_keys, head_dim), lambda i: (0, 0))
     v_spec = pl.BlockSpec((n_keys, head_dim), lambda i: (0, 1))
-    kt_spec = pl.BlockSpec((head_dim, n_keys), lambda i: (0, 0))
-    vt_spec = pl.BlockSpec((head_dim, n_keys), lambda i: (1, 0))
     out_spec = pl.BlockSpec((block_q, width_q), lambda i: (i, 0))
     key_t_spec = pl.BlockSpec((head_dim, n_keys), lambda i: (0, 0))
-    ctx_t = ctx.T
     kernel = functools.partial(
         attention_kernel,
         scaling=1.0 / math.sqrt(head_dim),
@@ -96,7 +92,7 @@
     return pl.pallas_call(
         kernel,
         grid=grid,
-        in_specs=[qmeta_spec, kmeta_spec, q_spec, g_spec, k_spec, v_spec, kt_spec, vt_spec],
+        in_specs=[qmeta_spec, kmeta_spec, q_spec, g_spec, k_spec, v_spec],
         out_specs=[out_spec, out_spec, key_t_spec, key_t_spec],
         out_shape=[
             jax.ShapeDtypeStruct((n_rows, width_q), jnp.bfloat16),
@@ -105,16 +101,7 @@
             jax.ShapeDtypeStruct((head_dim, n_keys), jnp.float32),
         ],
         compiler_params=pltpu.CompilerParams(dimension_semantics=("arbitrary",)),
-    )(
-        jnp.stack([query_doc, query_pos], axis=1),
-        jnp.stack([key_doc, key_pos]),
-        rows,
-        rows,
-        ctx,
-        ctx,
-        ctx_t,
-        ctx_t,
-    )
+    )(qmeta, kmeta_all, rows, rows, ctx_all, ctx_all)
 
 
 def shards(queries, keys, values, grad_out, doc_starts):
@@ -192,21 +179,14 @@
     order = jnp.sum(
         jnp.where(rank[None, :] == slot_ids[:, None], slot_ids[None, :], 0), axis=1
     )
-    kv_sorted = slot_kv[order]
-    doc_sorted = slot_doc[order]
-    pos_sorted = slot_pos[order]
+    kv_sorted = slot_kv[order].reshape(n_slots * tok_dev, 2 * head_dim)
+    kmeta_sorted = jnp.stack([slot_doc[order].reshape(-1), slot_pos[order].reshape(-1)])
+    qmeta = jnp.stack([query_doc, query_pos], axis=1)
 
     def branch(n_used):
-        def run(kv_sorted, doc_sorted, pos_sorted):
-            ctx = kv_sorted[:n_used].reshape(n_used * tok_dev, 2 * head_dim)
+        def run(kv_sorted, kmeta_sorted, qmeta):
             attn, q_grads, k_grads_t, v_grads_t = attend(
-                arrived,
-                query_pos,
-                query_doc,
-                ctx,
-                pos_sorted[:n_used].reshape(-1),
-                doc_sorted[:n_used].reshape(-1),
-                n_heads,
+                arrived, qmeta, kv_sorted, kmeta_sorted, n_used * tok_dev, n_heads
             )
             grads = jnp.concatenate([k_grads_t, v_grads_t], axis=0).T.reshape(
                 n_used, tok_dev, 2 * head_dim
@@ -219,7 +199,7 @@
         return run
 
     attn, q_grads, grads_sorted = lax.switch(
-        count - 1, [branch(n) for n in range(1, n_slots + 1)], kv_sorted, doc_sorted, pos_sorted
+        count - 1, [branch(n) for n in range(1, n_slots + 1)], kv_sorted, kmeta_sorted, qmeta
     )
     kv_grads = grads_sorted[rank]
 

time: 139 us -> 135 us (0.971)
  the two profiles are of different devices: /device:TPU:0 before, /device:TPU:1 now
where the time goes in v11:
time: 135 us; the launch traced here: 133 us
  waiting for transfers between devices  64.3 us (48%)
  starting transfers between devices  35.1 us (26%)
  other arithmetic  14.7 us (11%)
  local copies, waits for them, and re-layouts  9.5 us (7%)
  Pallas kernels  8.11 us (6%)
  between operations  1.62 us (1%)
    all_to_all x1, waiting for transfers between devices, shards(): lax.all_to_all(result, 'inner', 0, 0, tiled=True)  30.7 us
    all_to_all x1, waiting for transfers between devices, shards(): lax.all_to_all(packed, 'inner', 0, 0, tiled=True).reshape(tok_dev, -1)  22.7 us
    all_to_all x1, starting transfers between devices, shards(): lax.all_to_all(result, 'inner', 0, 0, tiled=True)  21.1 us
    pallas_call x1, Pallas kernels, attend(): pl.pallas_call(kernel, grid=grid, in_specs=[qmeta_spec, kmeta_spec, q_spe...  8.11 us
    ppermute x1, waiting for transfers between devices, shards(): from_partner = lax.ppermute(kv_grads[2], 'inner', pairs_down)  7.34 us
    all_to_all x1, starting transfers between devices, shards(): lax.all_to_all(packed, 'inner', 0, 0, tiled=True).reshape(tok_dev, -1)  6.34 us
    concatenate x1, other arithmetic, shards(): packed = jnp.roll(packed, -2 * outer_id, axis=0)  4.09 us
    ppermute x1, waiting for transfers between devices, shards(): kv_partner = lax.ppermute(kv_own, 'inner', pairs_up)  3.49 us
  transfers between devices with their start and end apart: 8, of which 4 were waited for; matrix products, arithmetic and copies ran while one was open for 6% of the time, Pallas kernels for 0%

profile of v11, /device:TPU:1, one launch (start us, length us, event | category | flops | bytes accessed | tf_op | source)
XLA Modules:
  0.0 133.3 jit_solution(8343440763514360026)
XLA Ops:
  0.7 4.1 %fusion.4 = bf16[8,64,1280]{2,1,0:T(8,128)(2,1)} fusion(s32[]{:T(128)S(6)} %select_n.158, bf16[8,64,512]{2,1,0:T(8,128)(2,1)} %bitcast.103, bf16[8,64,512]{2,1,0:T(8,128)(2,1)} %bitcast.104, bf16[8,64,128]{2,1,0:T(8,128)(2,1)} %bitcast.106, bf16[8,64,128]{2,1,0:T(8,128)(2,1)} %bitcast.107), kind=kLoop, calls=%fused_computation.24 | loop fusion | flops 10485760 | bytes 2621444 | tf_op jit(solution)/shard_map/jit(_roll_dynamic)/concatenate | solution.py:125
  4.8 6.3 %all-to-all-start = ((bf16[8,64,1280]{2,1,0:T(8,128)(2,1)}), bf16[8,64,1280]{2,1,0:T(8,128)(2,1)S(1)}, u32[]{:S(2)}, u32[]{:S(2)}) async-start(bf16[8,64,1280]{2,1,0:T(8,128)(2,1)} %fusion.4), calls=%async_computation | async-start | bytes 2621440 | tf_op jit(solution)/shard_map/all_to_all | solution.py:126
  11.2 0.1 reshape.289
  11.3 0.1 reduce.3
  11.4 0.1 reshape.247
  11.5 0.1 le.67
  11.6 0.1 convert_reduce_fusion
  11.7 0.1 fusion.12
  11.8 0.6 fusion.18
  12.5 0.6 iota_add_fusion.1
  13.1 0.1 reduce_min.29
  13.2 0.1 fusion.17
  13.4 1.9 %broadcast_subtract_fusion = (s32[4,1]{0,1:T(1,128)S(1)}, pred[4]{0:T(512)(128)(4,1)S(1)}) fusion(s32[4]{0:T(128)S(1)} %reduce_min.29, s32[]{:T(128)} %get-tuple-element.144, s32[4]{0:T(128)S(1)} %get-tuple-element.123, s32[]{:T(128)} %get-tuple-element.125, s32[4]{0:T(128)S(1)} %get-tuple-element.122, s32[]{:T(128)} %get-tuple-element.124), kind=kLoop, calls=%fused_computation.80 | loop fusion | flops 36 | bytes 80 | tf_op jit(solution)/shard_map/sub | solution.py:176
  15.4 0.2 reduce-window.11
  15.5 0.2 reduce-window.14
  15.7 0.6 convert_reduce_fusion.2
  16.4 0.6 bitcast_select_fusion
  17.0 0.1 select_reduce_fusion
  17.1 0.6 gather_fusion
  17.7 0.6 gather_fusion.1
  18.3 0.7 fusion.15
  19.0 22.7 %all-to-all-done = bf16[8,64,1280]{2,1,0:T(8,128)(2,1)S(1)} async-done(((bf16[8,64,1280]{2,1,0:T(8,128)(2,1)}), bf16[8,64,1280]{2,1,0:T(8,128)(2,1)S(1)}, u32[]{:S(2)}, u32[]{:S(2)}) %all-to-all-start) | async-done | bytes 1310752 | tf_op jit(solution)/shard_map/all_to_all | solution.py:126
  41.7 0.7 collective-permute-start
  42.4 0.7 collective-permute-start.1
  43.1 3.4 %collective-permute-start.2 = (bf16[512,256]{1,0:T(8,128)(2,1)S(1)}, bf16[512,256]{1,0:T(8,128)(2,1)S(1)}, u32[]{:S(2)}, u32[]{:S(2)}) collective-permute-start(bf16[512,256]{1,0:T(8,128)(2,1)S(1)} %get-tuple-element.136), channel_id=1, source_target_pairs={{0,1},{2,3},{4,5},{6,7},{8,9},{10,11},{12,13},{14,15},{16,17},{18,... | collective-permute-start | bytes 786440 | tf_op jit(solution)/shard_map/ppermute | solution.py:130
  47.3 3.5 %collective-permute-done.2 = bf16[512,256]{1,0:T(8,128)(2,1)S(1)} collective-permute-done((bf16[512,256]{1,0:T(8,128)(2,1)S(1)}, bf16[512,256]{1,0:T(8,128)(2,1)S(1)}, u32[]{:S(2)}, u32[]{:S(2)}) %collective-permute-start.2) | collective-permute-done | bytes 262176 | tf_op jit(solution)/shard_map/ppermute | solution.py:130
  50.8 0.7 copy-done.2
  51.5 1.1 pad_maximum_fusion.3
  52.6 0.6 gather_fusion.2
  53.2 11.7 %conditional.1 = (bf16[512,512]{1,0:T(8,128)(2,1)}, bf16[512,512]{1,0:T(8,128)(2,1)}, f32[4,512,256]{1,2,0:T(8,128)}) conditional(s32[]{:T(128)} %clamp.3, (s32[512,2]{0,1:T(2,128)S(1)}, s32[2,2048]{1,0:T(2,128)S(1)}, bf16[512,1280]{1,0:T(8,128)(2,1)S(1)}, bf16[2048,256]{1,0:T(8,128)(2,1)S(1)}) %tuple.63, ...), branch_computations={%region_13.15_spmd, %region_14.16_spmd, %region_15.17_spmd, %regio... | conditional | flops 524288 | bytes 13115420 | solution.py:201
  53.2 0.8 copy.34.qmeta_ref
  54.1 8.1 %branch_0_fun.1 = (bf16[512,512]{1,0:T(8,128)(2,1)}, bf16[512,512]{1,0:T(8,128)(2,1)}, f32[128,512]{1,0:T(8,128)}, f32[128,512]{1,0:T(8,128)}) custom-call(s32[512,2]{1,0:T(8,128)} %copy.34.qmeta_ref, s32[2,2048]{1,0:T(2,128)S(1)} %get-tuple-element.34.kmeta_ref, bf16[512,1280]{1,0:T(8,128)(2,1)S(1)} %get-tuple-element.35.q_ref.g_ref, ...), custom_call_target="tpu_custom_call" | custom-call | tf_op jit(solution)/shard_map/cond/branch_0_fun/pallas_call | solution.py:92
  62.2 1.1 maximum_bitcast_fusion
  63.2 1.6 %concatenate.26 = f32[4,512,256]{1,2,0:T(8,128)} pad(f32[1,512,256]{1,2,0:T(8,128)S(1)} %maximum_bitcast_fusion, f32[]{:T(128)} %constant.79.clone), padding=0_3x0_0x0_0 | pad | bytes 2621444 | tf_op jit(solution)/shard_map/cond/branch_0_fun/concatenate | solution.py:194
  64.9 2.3 %gather_fusion.3 = f32[4,512,256]{1,2,0:T(8,128)S(1)} fusion(f32[4,512,256]{1,2,0:T(8,128)} %get-tuple-element.74, s32[1024]{0:T(1024)S(1)} %pad_clamp_fusion), kind=kCustom, calls=%fused_computation.3 | custom fusion | bytes 4194320 | tf_op jit(solution)/shard_map/gather | solution.py:204
  67.1 0.2 slice_bitcast_fusion.2
  67.4 1.4 %collective-permute-start.3 = (f32[512,256]{0,1:T(8,128)S(1)}, f32[512,256]{0,1:T(8,128)S(1)}, u32[]{:S(2)}, u32[]{:S(2)}) collective-permute-start(f32[512,256]{0,1:T(8,128)S(1)} %get-tuple-element.129), channel_id=1, source_target_pairs={{1,0},{3,2},{5,4},{7,6},{9,8},{11,10},{13,12},{15,14},{17,16},{19,... | collective-permute-start | bytes 1572872 | tf_op jit(solution)/shard_map/ppermute | solution.py:207
  68.8 0.7 collective-permute-start.4
  69.5 0.7 collective-permute-start.5
  70.2 7.3 %collective-permute-done.3 = f32[512,256]{0,1:T(8,128)S(1)} collective-permute-done((f32[512,256]{0,1:T(8,128)S(1)}, f32[512,256]{0,1:T(8,128)S(1)}, u32[]{:S(2)}, u32[]{:S(2)}) %collective-permute-start.3) | collective-permute-done | bytes 524320 | tf_op jit(solution)/shard_map/ppermute | solution.py:207
  77.6 0.2 fusion.11
  77.8 0.1 copy.38
  78.0 1.1 pad_maximum_fusion.2
  79.1 21.1 %all-to-all-start.1 = ((bf16[8,64,1280]{2,1,0:T(8,128)(2,1)}), bf16[8,64,1280]{2,1,0:T(8,128)(2,1)S(1)}, u32[]{:S(2)}, u32[]{:S(2)}) async-start(bf16[8,64,1280]{2,1,0:T(8,128)(2,1)} %bitcast.33), calls=%async_computation.1 | async-start | bytes 2621440 | tf_op jit(solution)/shard_map/all_to_all | solution.py:220
  100.3 30.7 %all-to-all-done.1 = bf16[8,64,1280]{2,1,0:T(8,128)(2,1)S(1)} async-done(((bf16[8,64,1280]{2,1,0:T(8,128)(2,1)}), bf16[8,64,1280]{2,1,0:T(8,128)(2,1)S(1)}, u32[]{:S(2)}, u32[]{:S(2)}) %all-to-all-start.1) | async-done | bytes 1310752 | tf_op jit(solution)/shard_map/all_to_all | solution.py:220
  131.0 0.5 fusion
  131.5 1.1 slice_bitcast_fusion
  132.5 0.8 slice_bitcast_fusion.4
  (32 shorter events, 0.3 us)
Async XLA Ops:
  0.7 10.4 %copy-start.3 = (s32[4,8,4]{1,2,0:T(4,128)S(1)}, s32[4,8,4]{1,2,0:T(4,128)}, u32[]{:S(2)}) copy-start(s32[4,8,4]{1,2,0:T(4,128)} %param.15) | copy-start | bytes 1540
  4.8 36.9 %all-to-all-start = ((bf16[8,64,1280]{2,1,0:T(8,128)(2,1)}), bf16[8,64,1280]{2,1,0:T(8,128)(2,1)S(1)}, u32[]{:S(2)}, u32[]{:S(2)}) async-start(bf16[8,64,1280]{2,1,0:T(8,128)(2,1)} %fusion.4), calls=%async_computation | async-start | bytes 2621440 | tf_op jit(solution)/shard_map/all_to_all | solution.py:126
  41.7 5.5 %collective-permute-start = (bf16[512,256]{1,0:T(8,128)(2,1)S(1)}, bf16[512,256]{1,0:T(8,128)(2,1)S(1)}, u32[]{:S(2)}, u32[]{:S(2)}) collective-permute-start(bf16[512,256]{1,0:T(8,128)(2,1)S(1)} %get-tuple-element.136), channel_id=1, source_target_pairs={{6,14},{7,15},{12,20},{13,21},{18,26},{19,27}} | collective-permute-start | bytes 786440 | tf_op jit(solution)/shard_map/ppermute | solution.py:139
  42.4 4.8 %collective-permute-start.1 = (bf16[512,256]{1,0:T(8,128)(2,1)S(1)}, bf16[512,256]{1,0:T(8,128)(2,1)S(1)}, u32[]{:S(2)}, u32[]{:S(2)}) collective-permute-start(bf16[512,256]{1,0:T(8,128)(2,1)S(1)} %get-tuple-element.136), channel_id=1, source_target_pairs={{6,15},{7,14},{12,21},{13,20},{18,27},{19,26}} | collective-permute-start | bytes 786440 | tf_op jit(solution)/shard_map/ppermute | solution.py:140
  43.1 7.7 %collective-permute-start.2 = (bf16[512,256]{1,0:T(8,128)(2,1)S(1)}, bf16[512,256]{1,0:T(8,128)(2,1)S(1)}, u32[]{:S(2)}, u32[]{:S(2)}) collective-permute-start(bf16[512,256]{1,0:T(8,128)(2,1)S(1)} %get-tuple-element.136), channel_id=1, source_target_pairs={{0,1},{2,3},{4,5},{6,7},{8,9},{10,11},{12,13},{14,15},{16,17},{18,... | collective-permute-start | bytes 786440 | tf_op jit(solution)/shard_map/ppermute | solution.py:130
  50.8 0.7 copy-start.2
  67.4 10.6 %copy-start = (bf16[512,512]{1,0:T(8,128)(2,1)S(1)}, bf16[512,512]{1,0:T(8,128)(2,1)}, u32[]{:S(2)}) copy-start(bf16[512,512]{1,0:T(8,128)(2,1)} %get-tuple-element.72) | copy-start | bytes 1572868
  67.4 10.6 %copy-start.1 = (bf16[512,512]{1,0:T(8,128)(2,1)S(1)}, bf16[512,512]{1,0:T(8,128)(2,1)}, u32[]{:S(2)}) copy-start(bf16[512,512]{1,0:T(8,128)(2,1)} %get-tuple-element.73) | copy-start | bytes 1572868
  67.4 10.2 %collective-permute-start.3 = (f32[512,256]{0,1:T(8,128)S(1)}, f32[512,256]{0,1:T(8,128)S(1)}, u32[]{:S(2)}, u32[]{:S(2)}) collective-permute-start(f32[512,256]{0,1:T(8,128)S(1)} %get-tuple-element.129), channel_id=1, source_target_pairs={{1,0},{3,2},{5,4},{7,6},{9,8},{11,10},{13,12},{15,14},{17,16},{19,... | collective-permute-start | bytes 1572872 | tf_op jit(solution)/shard_map/ppermute | solution.py:207
  68.8 8.8 %collective-permute-start.4 = (f32[512,256]{0,1:T(8,128)S(1)}, f32[512,256]{0,1:T(8,128)S(1)}, u32[]{:S(2)}, u32[]{:S(2)}) collective-permute-start(f32[512,256]{0,1:T(8,128)S(1)} %get-tuple-element.131), channel_id=1, source_target_pairs={{14,6},{15,7},{20,12},{21,13},{26,18},{27,19}} | collective-permute-start | bytes 1572872 | tf_op jit(solution)/shard_map/ppermute | solution.py:212
  69.5 8.1 %collective-permute-start.5 = (f32[512,256]{0,1:T(8,128)S(1)}, f32[512,256]{0,1:T(8,128)S(1)}, u32[]{:S(2)}, u32[]{:S(2)}) collective-permute-start(f32[512,256]{0,1:T(8,128)S(1)} %get-tuple-element.130), channel_id=1, source_target_pairs={{15,6},{14,7},{21,12},{20,13},{27,18},{26,19}} | collective-permute-start | bytes 1572872 | tf_op jit(solution)/shard_map/ppermute | solution.py:213
  79.1 51.9 %all-to-all-start.1 = ((bf16[8,64,1280]{2,1,0:T(8,128)(2,1)}), bf16[8,64,1280]{2,1,0:T(8,128)(2,1)S(1)}, u32[]{:S(2)}, u32[]{:S(2)}) async-start(bf16[8,64,1280]{2,1,0:T(8,128)(2,1)} %bitcast.33), calls=%async_computation.1 | async-start | bytes 2621440 | tf_op jit(solution)/shard_map/all_to_all | solution.py:220

commit v12 on v11

--- a/solution.py
+++ b/solution.py
@@ -204,14 +204,20 @@
     kv_grads = grads_sorted[rank]
 
     pairs_down = [(b, a) for a, b in pairs_up]
-    from_partner = lax.ppermute(kv_grads[2], "inner", pairs_down)
+    low = jnp.bfloat16
+    from_partner = lax.ppermute(kv_grads[2].astype(low), "inner", pairs_down)
     back_a = [(b, a) for a, b in send_a]
     back_b = [(b, a) for a, b in send_b]
     grads_a = jnp.where(first, kv_grads[0], kv_grads[1])
     grads_b = jnp.where(first, kv_grads[1], kv_grads[0])
-    from_next_a = lax.ppermute(grads_a, both, back_a)
-    from_next_b = lax.ppermute(grads_b, both, back_b)
-    kv_total = (kv_grads[3] + from_partner + from_next_a + from_next_b).astype(jnp.bfloat16)
+    from_next_a = lax.ppermute(grads_a.astype(low), both, back_a)
+    from_next_b = lax.ppermute(grads_b.astype(low), both, back_b)
+    kv_total = (
+        kv_grads[3]
+        + from_partner.astype(jnp.float32)
+        + from_next_a.astype(jnp.float32)
+        + from_next_b.astype(jnp.float32)
+    ).astype(jnp.bfloat16)
 
     result = jnp.concatenate([attn, q_grads, kv_total], axis=-1).reshape(
         n_inner, piece_len, -1

time: 135 us -> 129 us (0.956)
  starting transfers between devices: 35.1 us -> 31.7 us
    all_to_all x1, starting transfers between devices: 21.1 us -> 17.8 us  [shards(): lax.all_to_all(result, 'inner', 0, 0, tiled=True)]
    ppermute x3, waiting for transfers between devices: 7.35 us -> 5.08 us  [the longest x1 5.08 us: shards(): from_partner = lax.ppermute(kv_grads[2].astype(low), 'inner', pairs_down)]
where the time goes in v12:
time: 129 us
  waiting for transfers between devices  63.1 us (49%)
  starting transfers between devices  31.7 us (25%)
  other arithmetic  14.5 us (11%)
  local copies, waits for them, and re-layouts  9.5 us (7%)
  Pallas kernels  8.11 us (6%)
  between operations  1.62 us (1%)
    all_to_all x1, waiting for transfers between devices, shards(): lax.all_to_all(result, 'inner', 0, 0, tiled=True)  31.8 us
    all_to_all x1, waiting for transfers between devices, shards(): lax.all_to_all(packed, 'inner', 0, 0, tiled=True).reshape(tok_dev, -1)  22.7 us
    all_to_all x1, starting transfers between devices, shards(): lax.all_to_all(result, 'inner', 0, 0, tiled=True)  17.8 us
    pallas_call x1, Pallas kernels, attend(): pl.pallas_call(kernel, grid=grid, in_specs=[qmeta_spec, kmeta_spec, q_spe...  8.11 us
    all_to_all x1, starting transfers between devices, shards(): lax.all_to_all(packed, 'inner', 0, 0, tiled=True).reshape(tok_dev, -1)  6.34 us
    ppermute x1, waiting for transfers between devices, shards(): from_partner = lax.ppermute(kv_grads[2].astype(low), 'inner', pairs_down)  5.08 us
    concatenate x1, other arithmetic, shards(): packed = jnp.roll(packed, -2 * outer_id, axis=0)  4.09 us
    ppermute x1, waiting for transfers between devices, shards(): kv_partner = lax.ppermute(kv_own, 'inner', pairs_up)  3.49 us
  transfers between devices with their start and end apart: 8, of which 4 were waited for; matrix products, arithmetic and copies ran while one was open for 6% of the time, Pallas kernels for 0%

profile of v12, /device:TPU:1, one launch (start us, length us, event | category | flops | bytes accessed | tf_op | source)
XLA Modules:
  0.0 128.5 jit_solution(4594057955548803462)
XLA Ops:
  0.7 4.1 %fusion.4 = bf16[8,64,1280]{2,1,0:T(8,128)(2,1)} fusion(s32[]{:T(128)S(6)} %select_n.152, bf16[8,64,512]{2,1,0:T(8,128)(2,1)} %bitcast.103, bf16[8,64,512]{2,1,0:T(8,128)(2,1)} %bitcast.104, bf16[8,64,128]{2,1,0:T(8,128)(2,1)} %bitcast.106, bf16[8,64,128]{2,1,0:T(8,128)(2,1)} %bitcast.107), kind=kLoop, calls=%fused_computation.24 | loop fusion | flops 10485760 | bytes 2621444 | tf_op jit(solution)/shard_map/jit(_roll_dynamic)/concatenate | solution.py:125
  4.8 6.3 %all-to-all-start = ((bf16[8,64,1280]{2,1,0:T(8,128)(2,1)}), bf16[8,64,1280]{2,1,0:T(8,128)(2,1)S(1)}, u32[]{:S(2)}, u32[]{:S(2)}) async-start(bf16[8,64,1280]{2,1,0:T(8,128)(2,1)} %fusion.4), calls=%async_computation | async-start | bytes 2621440 | tf_op jit(solution)/shard_map/all_to_all | solution.py:126
  11.2 0.1 reshape.292
  11.3 0.1 reduce.3
  11.4 0.1 reshape.250
  11.5 0.1 le.67
  11.6 0.1 convert_reduce_fusion
  11.7 0.1 fusion.15
  11.8 0.6 fusion.21
  12.5 0.6 iota_add_fusion.1
  13.1 0.1 reduce_min.29
  13.2 0.1 fusion.20
  13.4 1.9 %broadcast_subtract_fusion = (s32[4,1]{0,1:T(1,128)S(1)}, pred[4]{0:T(512)(128)(4,1)S(1)}) fusion(s32[4]{0:T(128)S(1)} %reduce_min.29, s32[]{:T(128)} %get-tuple-element.144, s32[4]{0:T(128)S(1)} %get-tuple-element.123, s32[]{:T(128)} %get-tuple-element.125, s32[4]{0:T(128)S(1)} %get-tuple-element.122, s32[]{:T(128)} %get-tuple-element.124), kind=kLoop, calls=%fused_computation.83 | loop fusion | flops 36 | bytes 80 | tf_op jit(solution)/shard_map/sub | solution.py:176
  15.4 0.2 reduce-window.11
  15.5 0.2 reduce-window.14
  15.7 0.6 convert_reduce_fusion.2
  16.4 0.6 bitcast_select_fusion
  17.0 0.1 select_reduce_fusion
  17.1 0.6 gather_fusion
  17.7 0.6 gather_fusion.1
  18.3 0.7 fusion.18
  19.0 22.7 %all-to-all-done = bf16[8,64,1280]{2,1,0:T(8,128)(2,1)S(1)} async-done(((bf16[8,64,1280]{2,1,0:T(8,128)(2,1)}), bf16[8,64,1280]{2,1,0:T(8,128)(2,1)S(1)}, u32[]{:S(2)}, u32[]{:S(2)}) %all-to-all-start) | async-done | bytes 1310752 | tf_op jit(solution)/shard_map/all_to_all | solution.py:126
  41.7 0.7 collective-permute-start
  42.4 0.7 collective-permute-start.1
  43.1 3.4 %collective-permute-start.2 = (bf16[512,256]{1,0:T(8,128)(2,1)S(1)}, bf16[512,256]{1,0:T(8,128)(2,1)S(1)}, u32[]{:S(2)}, u32[]{:S(2)}) collective-permute-start(bf16[512,256]{1,0:T(8,128)(2,1)S(1)} %get-tuple-element.136), channel_id=1, source_target_pairs={{0,1},{2,3},{4,5},{6,7},{8,9},{10,11},{12,13},{14,15},{16,17},{18,... | collective-permute-start | bytes 786440 | tf_op jit(solution)/shard_map/ppermute | solution.py:130
  47.3 3.5 %collective-permute-done.2 = bf16[512,256]{1,0:T(8,128)(2,1)S(1)} collective-permute-done((bf16[512,256]{1,0:T(8,128)(2,1)S(1)}, bf16[512,256]{1,0:T(8,128)(2,1)S(1)}, u32[]{:S(2)}, u32[]{:S(2)}) %collective-permute-start.2) | collective-permute-done | bytes 262176 | tf_op jit(solution)/shard_map/ppermute | solution.py:130
  50.8 0.7 copy-done.2
  51.5 1.1 pad_maximum_fusion.3
  52.6 0.6 gather_fusion.2
  53.2 11.7 %conditional.1 = (bf16[512,512]{1,0:T(8,128)(2,1)}, bf16[512,512]{1,0:T(8,128)(2,1)}, f32[4,512,256]{1,2,0:T(8,128)}) conditional(s32[]{:T(128)} %clamp.3, (s32[512,2]{0,1:T(2,128)S(1)}, s32[2,2048]{1,0:T(2,128)S(1)}, bf16[512,1280]{1,0:T(8,128)(2,1)S(1)}, bf16[2048,256]{1,0:T(8,128)(2,1)S(1)}) %tuple.63, ...), branch_computations={%region_13.15_spmd, %region_14.16_spmd, %region_15.17_spmd, %regio... | conditional | flops 524288 | bytes 13115420 | solution.py:201
  53.2 0.8 copy.34.qmeta_ref
  54.1 8.1 %branch_0_fun.1 = (bf16[512,512]{1,0:T(8,128)(2,1)}, bf16[512,512]{1,0:T(8,128)(2,1)}, f32[128,512]{1,0:T(8,128)}, f32[128,512]{1,0:T(8,128)}) custom-call(s32[512,2]{1,0:T(8,128)} %copy.34.qmeta_ref, s32[2,2048]{1,0:T(2,128)S(1)} %get-tuple-element.34.kmeta_ref, bf16[512,1280]{1,0:T(8,128)(2,1)S(1)} %get-tuple-element.35.q_ref.g_ref, ...), custom_call_target="tpu_custom_call" | custom-call | tf_op jit(solution)/shard_map/cond/branch_0_fun/pallas_call | solution.py:92
  62.2 1.1 maximum_bitcast_fusion
  63.2 1.6 %concatenate.26 = f32[4,512,256]{1,2,0:T(8,128)} pad(f32[1,512,256]{1,2,0:T(8,128)S(1)} %maximum_bitcast_fusion, f32[]{:T(128)} %constant.79.clone), padding=0_3x0_0x0_0 | pad | bytes 2621444 | tf_op jit(solution)/shard_map/cond/branch_0_fun/concatenate | solution.py:194
  64.9 2.3 %gather_fusion.3 = f32[4,512,256]{1,2,0:T(8,128)S(1)} fusion(f32[4,512,256]{1,2,0:T(8,128)} %get-tuple-element.74, s32[1024]{0:T(1024)S(1)} %pad_clamp_fusion), kind=kCustom, calls=%fused_computation.3 | custom fusion | bytes 4194320 | tf_op jit(solution)/shard_map/gather | solution.py:204
  67.2 0.1 fusion.14
  67.3 1.4 %collective-permute-start.3 = (bf16[512,256]{0,1:T(8,128)(2,1)S(1)}, bf16[512,256]{0,1:T(8,128)(2,1)S(1)}, u32[]{:S(2)}, u32[]{:S(2)}) collective-permute-start(bf16[512,256]{0,1:T(8,128)(2,1)S(1)} %get-tuple-element.129), channel_id=1, source_target_pairs={{1,0},{3,2},{5,4},{7,6},{9,8},{11,10},{13,12},{15,14},{17,16},{19,... | collective-permute-start | bytes 786440 | tf_op jit(solution)/shard_map/ppermute | solution.py:208
  68.7 0.7 collective-permute-start.4
  69.4 0.7 collective-permute-start.5
  70.1 5.1 %collective-permute-done.3 = bf16[512,256]{0,1:T(8,128)(2,1)S(1)} collective-permute-done((bf16[512,256]{0,1:T(8,128)(2,1)S(1)}, bf16[512,256]{0,1:T(8,128)(2,1)S(1)}, u32[]{:S(2)}, u32[]{:S(2)}) %collective-permute-start.3) | collective-permute-done | bytes 262176 | tf_op jit(solution)/shard_map/ppermute | solution.py:208
  75.1 0.1 fusion.11
  75.3 0.1 copy.38
  75.4 1.1 pad_maximum_fusion.2
  76.6 17.8 %all-to-all-start.1 = ((bf16[8,64,1280]{2,1,0:T(8,128)(2,1)}), bf16[8,64,1280]{2,1,0:T(8,128)(2,1)S(1)}, u32[]{:S(2)}, u32[]{:S(2)}) async-start(bf16[8,64,1280]{2,1,0:T(8,128)(2,1)} %bitcast.33), calls=%async_computation.1 | async-start | bytes 2621440 | tf_op jit(solution)/shard_map/all_to_all | solution.py:226
  94.4 31.8 %all-to-all-done.1 = bf16[8,64,1280]{2,1,0:T(8,128)(2,1)S(1)} async-done(((bf16[8,64,1280]{2,1,0:T(8,128)(2,1)}), bf16[8,64,1280]{2,1,0:T(8,128)(2,1)S(1)}, u32[]{:S(2)}, u32[]{:S(2)}) %all-to-all-start.1) | async-done | bytes 1310752 | tf_op jit(solution)/shard_map/all_to_all | solution.py:226
  126.2 0.5 fusion
  126.7 1.1 slice_bitcast_fusion
  127.8 0.8 slice_bitcast_fusion.3
  (32 shorter events, 0.3 us)
Async XLA Ops:
  0.7 10.4 %copy-start.3 = (s32[4,8,4]{1,2,0:T(4,128)S(1)}, s32[4,8,4]{1,2,0:T(4,128)}, u32[]{:S(2)}) copy-start(s32[4,8,4]{1,2,0:T(4,128)} %param.15) | copy-start | bytes 1540
  4.8 36.9 %all-to-all-start = ((bf16[8,64,1280]{2,1,0:T(8,128)(2,1)}), bf16[8,64,1280]{2,1,0:T(8,128)(2,1)S(1)}, u32[]{:S(2)}, u32[]{:S(2)}) async-start(bf16[8,64,1280]{2,1,0:T(8,128)(2,1)} %fusion.4), calls=%async_computation | async-start | bytes 2621440 | tf_op jit(solution)/shard_map/all_to_all | solution.py:126
  41.7 5.5 %collective-permute-start = (bf16[512,256]{1,0:T(8,128)(2,1)S(1)}, bf16[512,256]{1,0:T(8,128)(2,1)S(1)}, u32[]{:S(2)}, u32[]{:S(2)}) collective-permute-start(bf16[512,256]{1,0:T(8,128)(2,1)S(1)} %get-tuple-element.136), channel_id=1, source_target_pairs={{6,14},{7,15},{12,20},{13,21},{18,26},{19,27}} | collective-permute-start | bytes 786440 | tf_op jit(solution)/shard_map/ppermute | solution.py:139
  42.4 4.8 %collective-permute-start.1 = (bf16[512,256]{1,0:T(8,128)(2,1)S(1)}, bf16[512,256]{1,0:T(8,128)(2,1)S(1)}, u32[]{:S(2)}, u32[]{:S(2)}) collective-permute-start(bf16[512,256]{1,0:T(8,128)(2,1)S(1)} %get-tuple-element.136), channel_id=1, source_target_pairs={{6,15},{7,14},{12,21},{13,20},{18,27},{19,26}} | collective-permute-start | bytes 786440 | tf_op jit(solution)/shard_map/ppermute | solution.py:140
  43.1 7.7 %collective-permute-start.2 = (bf16[512,256]{1,0:T(8,128)(2,1)S(1)}, bf16[512,256]{1,0:T(8,128)(2,1)S(1)}, u32[]{:S(2)}, u32[]{:S(2)}) collective-permute-start(bf16[512,256]{1,0:T(8,128)(2,1)S(1)} %get-tuple-element.136), channel_id=1, source_target_pairs={{0,1},{2,3},{4,5},{6,7},{8,9},{10,11},{12,13},{14,15},{16,17},{18,... | collective-permute-start | bytes 786440 | tf_op jit(solution)/shard_map/ppermute | solution.py:130
  50.8 0.7 copy-start.2
  67.1 8.3 %copy-start = (bf16[512,512]{1,0:T(8,128)(2,1)S(1)}, bf16[512,512]{1,0:T(8,128)(2,1)}, u32[]{:S(2)}) copy-start(bf16[512,512]{1,0:T(8,128)(2,1)} %get-tuple-element.72) | copy-start | bytes 1572868
  67.2 8.3 %copy-start.1 = (bf16[512,512]{1,0:T(8,128)(2,1)S(1)}, bf16[512,512]{1,0:T(8,128)(2,1)}, u32[]{:S(2)}) copy-start(bf16[512,512]{1,0:T(8,128)(2,1)} %get-tuple-element.73) | copy-start | bytes 1572868
  67.3 7.9 %collective-permute-start.3 = (bf16[512,256]{0,1:T(8,128)(2,1)S(1)}, bf16[512,256]{0,1:T(8,128)(2,1)S(1)}, u32[]{:S(2)}, u32[]{:S(2)}) collective-permute-start(bf16[512,256]{0,1:T(8,128)(2,1)S(1)} %get-tuple-element.129), channel_id=1, source_target_pairs={{1,0},{3,2},{5,4},{7,6},{9,8},{11,10},{13,12},{15,14},{17,16},{19,... | collective-permute-start | bytes 786440 | tf_op jit(solution)/shard_map/ppermute | solution.py:208
  68.7 6.5 %collective-permute-start.4 = (bf16[512,256]{0,1:T(8,128)(2,1)S(1)}, bf16[512,256]{0,1:T(8,128)(2,1)S(1)}, u32[]{:S(2)}, u32[]{:S(2)}) collective-permute-start(bf16[512,256]{0,1:T(8,128)(2,1)S(1)} %get-tuple-element.131), channel_id=1, source_target_pairs={{14,6},{15,7},{20,12},{21,13},{26,18},{27,19}} | collective-permute-start | bytes 786440 | tf_op jit(solution)/shard_map/ppermute | solution.py:213
  69.4 5.8 %collective-permute-start.5 = (bf16[512,256]{0,1:T(8,128)(2,1)S(1)}, bf16[512,256]{0,1:T(8,128)(2,1)S(1)}, u32[]{:S(2)}, u32[]{:S(2)}) collective-permute-start(bf16[512,256]{0,1:T(8,128)(2,1)S(1)} %get-tuple-element.130), channel_id=1, source_target_pairs={{15,6},{14,7},{21,12},{20,13},{27,18},{26,19}} | collective-permute-start | bytes 786440 | tf_op jit(solution)/shard_map/ppermute | solution.py:214
  76.6 49.6 %all-to-all-start.1 = ((bf16[8,64,1280]{2,1,0:T(8,128)(2,1)}), bf16[8,64,1280]{2,1,0:T(8,128)(2,1)S(1)}, u32[]{:S(2)}, u32[]{:S(2)}) async-start(bf16[8,64,1280]{2,1,0:T(8,128)(2,1)} %bitcast.33), calls=%async_computation.1 | async-start | bytes 2621440 | tf_op jit(solution)/shard_map/all_to_all | solution.py:226

commit v13 on v12

--- a/solution.py
+++ b/solution.py
@@ -22,13 +22,16 @@
 
 
 def attention_kernel(
-    qmeta_ref, kmeta_ref, q_ref, g_ref, k_ref, v_ref,
-    o_ref, dq_ref, dkt_ref, dvt_ref, *, scaling, n_heads, head_dim
+    order_ref, qmeta_ref, kmeta_ref, q_ref, g_ref, k_ref, v_ref,
+    o_ref, dq_ref, dkv_ref, dkt_ref, dvt_ref, *, scaling, n_heads, head_dim, slot_len
 ):
-    @pl.when(pl.program_id(0) == 0)
+    step = pl.program_id(0)
+
+    @pl.when(step == 0)
     def _():
         dkt_ref[...] = jnp.zeros_like(dkt_ref)
         dvt_ref[...] = jnp.zeros_like(dvt_ref)
+        dkv_ref[...] = jnp.zeros_like(dkv_ref)
 
     k = k_ref[...]
     v = v_ref[...]
@@ -68,40 +71,57 @@
             g, probs_low, contract_first, preferred_element_type=jnp.float32
         )
 
-
-def attend(rows, qmeta, ctx_all, kmeta_all, n_keys, n_heads):
+    @pl.when(step == pl.num_programs(0) - 1)
+    def _():
+        for r in range(dkt_ref.shape[1] // slot_len):
+            cols = slice(r * slot_len, (r + 1) * slot_len)
+            slot = order_ref[r]
+            dkv_ref[slot, :, 0:head_dim] = dkt_ref[:, cols].T
+            dkv_ref[slot, :, head_dim : 2 * head_dim] = dvt_ref[:, cols].T
+
+
+def attend(rows, qmeta, ctx_all, kmeta_all, order, n_keys, n_heads):
     n_rows = rows.shape[0]
+    n_slots = order.shape[0]
+    slot_len = ctx_all.shape[0] // n_slots
     head_dim = ctx_all.shape[1] // 2
     width_q = n_heads * head_dim
     block_q = min(256, n_rows)
     grid = (n_rows // block_q,)
-    q_spec = pl.BlockSpec((block_q, width_q), lambda i: (i, 0))
-    g_spec = pl.BlockSpec((block_q, width_q), lambda i: (i, 1))
-    qmeta_spec = pl.BlockSpec((block_q, 2), lambda i: (i, 0))
-    kmeta_spec = pl.BlockSpec((2, n_keys), lambda i: (0, 0))
-    k_spec = pl.BlockSpec((n_keys, head_dim), lambda i: (0, 0))
-    v_spec = pl.BlockSpec((n_keys, head_dim), lambda i: (0, 1))
-    out_spec = pl.BlockSpec((block_q, width_q), lambda i: (i, 0))
-    key_t_spec = pl.BlockSpec((head_dim, n_keys), lambda i: (0, 0))
+    q_spec = pl.BlockSpec((block_q, width_q), lambda i, o: (i, 0))
+    g_spec = pl.BlockSpec((block_q, width_q), lambda i, o: (i, 1))
+    qmeta_spec = pl.BlockSpec((block_q, 2), lambda i, o: (i, 0))
+    kmeta_spec = pl.BlockSpec((2, n_keys), lambda i, o: (0, 0))
+    k_spec = pl.BlockSpec((n_keys, head_dim), lambda i, o: (0, 0))
+    v_spec = pl.BlockSpec((n_keys, head_dim), lambda i, o: (0, 1))
+    out_spec = pl.BlockSpec((block_q, width_q), lambda i, o: (i, 0))
+    grads_spec = pl.BlockSpec((n_slots, slot_len, 2 * head_dim), lambda i, o: (0, 0, 0))
     kernel = functools.partial(
         attention_kernel,
         scaling=1.0 / math.sqrt(head_dim),
         n_heads=n_heads,
         head_dim=head_dim,
+        slot_len=slot_len,
     )
     return pl.pallas_call(
         kernel,
-        grid=grid,
-        in_specs=[qmeta_spec, kmeta_spec, q_spec, g_spec, k_spec, v_spec],
-        out_specs=[out_spec, out_spec, key_t_spec, key_t_spec],
+        grid_spec=pltpu.PrefetchScalarGridSpec(
+            num_scalar_prefetch=1,
+            grid=grid,
+            in_specs=[qmeta_spec, kmeta_spec, q_spec, g_spec, k_spec, v_spec],
+            out_specs=[out_spec, out_spec, grads_spec],
+            scratch_shapes=[
+                pltpu.VMEM((head_dim, n_keys), jnp.float32),
+                pltpu.VMEM((head_dim, n_keys), jnp.float32),
+            ],
+        ),
         out_shape=[
             jax.ShapeDtypeStruct((n_rows, width_q), jnp.bfloat16),
             jax.ShapeDtypeStruct((n_rows, width_q), jnp.bfloat16),
-            jax.ShapeDtypeStruct((head_dim, n_keys), jnp.float32),
-            jax.ShapeDtypeStruct((head_dim, n_keys), jnp.float32),
+            jax.ShapeDtypeStruct((n_slots, slot_len, 2 * head_dim), jnp.float32),
         ],
         compiler_params=pltpu.CompilerParams(dimension_semantics=("arbitrary",)),
-    )(qmeta, kmeta_all, rows, rows, ctx_all, ctx_all)
+    )(order, qmeta, kmeta_all, rows, rows, ctx_all, ctx_all)
 
 
 def shards(queries, keys, values, grad_out, doc_starts):
@@ -184,24 +204,21 @@
     qmeta = jnp.stack([query_doc, query_pos], axis=1)
 
     def branch(n_used):
-        def run(kv_sorted, kmeta_sorted, qmeta):
-            attn, q_grads, k_grads_t, v_grads_t = attend(
-                arrived, qmeta, kv_sorted, kmeta_sorted, n_used * tok_dev, n_heads
+        def run(kv_sorted, kmeta_sorted, qmeta, order):
+            return attend(
+                arrived, qmeta, kv_sorted, kmeta_sorted, order, n_used * tok_dev, n_heads
             )
-            grads = jnp.concatenate([k_grads_t, v_grads_t], axis=0).T.reshape(
-                n_used, tok_dev, 2 * head_dim
-            )
-            grads = jnp.concatenate(
-                [grads, jnp.zeros((n_slots - n_used, tok_dev, 2 * head_dim), jnp.float32)]
-            )
-            return attn, q_grads, grads
 
         return run
 
-    attn, q_grads, grads_sorted = lax.switch(
-        count - 1, [branch(n) for n in range(1, n_slots + 1)], kv_sorted, kmeta_sorted, qmeta
-    )
-    kv_grads = grads_sorted[rank]
+    attn, q_grads, kv_grads = lax.switch(
+        count - 1,
+        [branch(n) for n in range(1, n_slots + 1)],
+        kv_sorted,
+        kmeta_sorted,
+        qmeta,
+        order,
+    )
 
     pairs_down = [(b, a) for a, b in pairs_up]
     low = jnp.bfloat16

time: 129 us -> 125 us (0.969); the launches traced: 129 us -> 123 us
  local copies, waits for them, and re-layouts: 9.5 us -> 4.78 us
  starting transfers between devices: 31.7 us -> 29.3 us
  Pallas kernels: 8.11 us -> 9.52 us
    all_to_all x1, starting transfers between devices: 17.8 us -> 14.8 us  [shards(): lax.all_to_all(result, 'inner', 0, 0, tiled=True)]
    gather x1 -> x0, local copies, waits for them, and re-layouts: 2.27 us -> none  [shards(): kv_grads = grads_sorted[rank]]
    convert_element_type x1, other arithmetic: 0.01 us -> 1.95 us  [shards(): needed_i = needed.astype(jnp.int32)]
    sub x1, other arithmetic: 1.95 us -> 0.01 us  [shards(): 1 - needed_i]
    concatenate x1 -> x0, local copies, waits for them, and re-layouts: 1.62 us -> none  [run(): jnp.concatenate([grads, jnp.zeros((n_slots - n_used, tok_dev, 2 * head_di...]
    pallas_call x1, Pallas kernels: 8.11 us -> 9.52 us  [attend(): pl.pallas_call(kernel, grid_spec=pltpu.PrefetchScalarGridSpec(num_scalar_...]
    convert_element_type x1, other arithmetic: 0.08 us -> 1.44 us  [shards(): from_partner = lax.ppermute(kv_grads[2].astype(low), 'inner', pairs_down)]
where the time goes in v13:
time: 125 us; the launch traced here: 123 us
  waiting for transfers between devices  62.5 us (50%)
  starting transfers between devices  29.3 us (23%)
  other arithmetic  15.1 us (12%)
  Pallas kernels  9.52 us (8%)
  local copies, waits for them, and re-layouts  4.78 us (4%)
  between operations  1.5 us (1%)
    all_to_all x1, waiting for transfers between devices, shards(): lax.all_to_all(result, 'inner', 0, 0, tiled=True)  31 us
    all_to_all x1, waiting for transfers between devices, shards(): lax.all_to_all(packed, 'inner', 0, 0, tiled=True).reshape(tok_dev, -1)  23.4 us
    all_to_all x1, starting transfers between devices, shards(): lax.all_to_all(result, 'inner', 0, 0, tiled=True)  14.8 us
    pallas_call x1, Pallas kernels, attend(): pl.pallas_call(kernel, grid_spec=pltpu.PrefetchScalarGridSpec(num_scalar_...  9.52 us
    all_to_all x1, starting transfers between devices, shards(): lax.all_to_all(packed, 'inner', 0, 0, tiled=True).reshape(tok_dev, -1)  6.34 us
    ppermute x1, waiting for transfers between devices, shards(): from_partner = lax.ppermute(kv_grads[2].astype(low), 'inner', pairs_down)  5.28 us
    ppermute x1, starting transfers between devices, shards(): kv_partner = lax.ppermute(kv_own, 'inner', pairs_up)  4.1 us
    concatenate x1, other arithmetic, shards(): packed = jnp.roll(packed, -2 * outer_id, axis=0)  4.09 us
  transfers between devices with their start and end apart: 8, of which 4 were waited for; matrix products, arithmetic and copies ran while one was open for 6% of the time, Pallas kernels for 0%

profile of v13, /device:TPU:1, one launch (start us, length us, event | category | flops | bytes accessed | tf_op | source)
XLA Modules:
  0.0 122.7 jit_solution(8477528885374404228)
XLA Ops:
  0.7 4.1 %fusion.4 = bf16[8,64,1280]{2,1,0:T(8,128)(2,1)} fusion(s32[]{:T(128)S(6)} %select_n.131, bf16[8,64,512]{2,1,0:T(8,128)(2,1)} %bitcast.76, bf16[8,64,512]{2,1,0:T(8,128)(2,1)} %bitcast.77, bf16[8,64,128]{2,1,0:T(8,128)(2,1)} %bitcast.78, bf16[8,64,128]{2,1,0:T(8,128)(2,1)} %bitcast.79), kind=kLoop, calls=%fused_computation.17 | loop fusion | flops 10485760 | bytes 2621444 | tf_op jit(solution)/shard_map/jit(_roll_dynamic)/concatenate | solution.py:145
  4.8 6.3 %all-to-all-start = ((bf16[8,64,1280]{2,1,0:T(8,128)(2,1)}), bf16[8,64,1280]{2,1,0:T(8,128)(2,1)S(1)}, u32[]{:S(2)}, u32[]{:S(2)}) async-start(bf16[8,64,1280]{2,1,0:T(8,128)(2,1)} %fusion.4), calls=%async_computation | async-start | bytes 2621440 | tf_op jit(solution)/shard_map/all_to_all | solution.py:146
  11.1 0.6 iota_add_fusion.1
  11.8 0.0 copy-done
  11.8 0.1 le.67
  11.9 0.1 reshape.272
  12.0 0.1 reduce-window.21
  12.0 0.1 reduce.3
  12.2 0.1 reshape.238
  12.2 0.1 convert_reduce_fusion
  12.4 0.1 fusion.14
  12.4 0.6 fusion.19
  13.1 0.1 reduce_min.29
  13.2 0.1 fusion.18
  13.4 1.9 %fusion.15 = (s32[4,1]{0,1:T(1,128)S(1)}, pred[4]{0:T(512)(128)(4,1)S(1)}) fusion(s32[4]{0:T(128)S(1)} %reduce_min.29, s32[]{:T(128)} %get-tuple-element.133, s32[4]{0:T(128)S(1)} %get-tuple-element.112, s32[]{:T(128)} %get-tuple-element.114, s32[4]{0:T(128)S(1)} %get-tuple-element.111, s32[]{:T(128)} %get-tuple-element.113), kind=kLoop, calls=%fused_computation.65 | loop fusion | flops 32 | bytes 80 | tf_op jit(solution)/shard_map/convert_element_type | solution.py:193
  15.3 0.2 reduce-window.22
  15.5 0.2 reduce-window.23
  15.7 0.6 convert_reduce_fusion.2
  16.3 0.6 bitcast_select_fusion
  17.0 0.1 select_reduce_fusion
  17.1 0.6 gather_fusion.1
  17.7 0.6 gather_fusion
  18.3 23.4 %all-to-all-done = bf16[8,64,1280]{2,1,0:T(8,128)(2,1)S(1)} async-done(((bf16[8,64,1280]{2,1,0:T(8,128)(2,1)}), bf16[8,64,1280]{2,1,0:T(8,128)(2,1)S(1)}, u32[]{:S(2)}, u32[]{:S(2)}) %all-to-all-start) | async-done | bytes 1310752 | tf_op jit(solution)/shard_map/all_to_all | solution.py:146
  41.7 0.7 collective-permute-start.1
  42.4 0.7 collective-permute-start
  43.1 4.1 %collective-permute-start.2 = (bf16[512,256]{1,0:T(8,128)(2,1)S(1)}, bf16[512,256]{1,0:T(8,128)(2,1)}, u32[]{:S(2)}, u32[]{:S(2)}) collective-permute-start(bf16[512,256]{1,0:T(8,128)(2,1)S(1)} %get-tuple-element.125), channel_id=1, source_target_pairs={{0,1},{2,3},{4,5},{6,7},{8,9},{10,11},{12,13},{14,15},{16,17},{18,... | collective-permute-start | bytes 786440 | tf_op jit(solution)/shard_map/ppermute | solution.py:150
  47.9 0.0 collective-permute-done.1
  47.9 0.0 collective-permute-done
  48.0 2.8 %collective-permute-done.2 = bf16[512,256]{1,0:T(8,128)(2,1)} collective-permute-done((bf16[512,256]{1,0:T(8,128)(2,1)S(1)}, bf16[512,256]{1,0:T(8,128)(2,1)}, u32[]{:S(2)}, u32[]{:S(2)}) %collective-permute-start.2) | collective-permute-done | bytes 262176 | tf_op jit(solution)/shard_map/ppermute | solution.py:150
  50.8 1.1 pad_maximum_fusion.1
  51.9 0.6 gather_fusion.2
  52.5 10.4 %conditional.1 = ((bf16[512,512]{1,0:T(8,128)(2,1)S(1)}, bf16[512,512]{1,0:T(8,128)(2,1)S(1)}, f32[4,512,256]{2,1,0:T(8,128)})) conditional(s32[]{:T(128)} %clamp.3, (s32[4]{0:T(128)S(1)}, s32[512,2]{0,1:T(2,128)S(1)}, s32[2,2048]{1,0:T(2,128)S(1)}, bf16[512,1280]{1,0:T(8,128)(2,1)S(1)}, ...), branch_computations={%region_13.15_spmd, %region_14.16_spmd, %region_15.17_spmd, %regio... | conditional | bytes 8200 | solution.py:214
  52.5 0.9 copy.21.qmeta_ref
  53.4 9.5 %branch_0_fun.1 = (bf16[512,512]{1,0:T(8,128)(2,1)S(1)}, bf16[512,512]{1,0:T(8,128)(2,1)S(1)}, f32[4,512,256]{2,1,0:T(8,128)}) custom-call(s32[4]{0:T(128)S(1)} %get-tuple-element.34.order_ref, s32[512,2]{1,0:T(8,128)} %copy.21.qmeta_ref, s32[2,2048]{1,0:T(2,128)S(1)} %get-tuple-element.43.kmeta_ref, bf16[512,1280]{1,0:T(8,128)(2,1)S(1)} %get-tuple-element.44.q_ref.g_ref, ...), custom_call_target="tpu_custom_call" | custom-call | tf_op jit(solution)/shard_map/cond/branch_0_fun/pallas_call | solution.py:106
  62.9 1.4 %fusion.13 = (bf16[512,256]{1,0:T(8,128)(2,1)S(1)}, bf16[512,256]{1,0:T(8,128)(2,1)S(1)}, bf16[512,256]{1,0:T(8,128)(2,1)S(1)}) fusion(f32[4,512,256]{2,1,0:T(8,128)} %get-tuple-element.70, pred[]{:T(512)S(6)} %eq.54), kind=kLoop, calls=%fused_computation.34 | loop fusion | flops 262144 | bytes 1572865 | tf_op jit(solution)/shard_map/convert_element_type | solution.py:225
  64.3 1.3 %collective-permute-start.3 = (bf16[512,256]{1,0:T(8,128)(2,1)S(1)}, bf16[512,256]{1,0:T(8,128)(2,1)S(1)}, u32[]{:S(2)}, u32[]{:S(2)}) collective-permute-start(bf16[512,256]{1,0:T(8,128)(2,1)S(1)} %get-tuple-element.118), channel_id=1, source_target_pairs={{1,0},{3,2},{5,4},{7,6},{9,8},{11,10},{13,12},{15,14},{17,16},{19,... | collective-permute-start | bytes 786440 | tf_op jit(solution)/shard_map/ppermute | solution.py:225
  65.7 0.7 collective-permute-start.4
  66.3 0.7 collective-permute-start.5
  67.0 5.3 %collective-permute-done.3 = bf16[512,256]{1,0:T(8,128)(2,1)S(1)} collective-permute-done((bf16[512,256]{1,0:T(8,128)(2,1)S(1)}, bf16[512,256]{1,0:T(8,128)(2,1)S(1)}, u32[]{:S(2)}, u32[]{:S(2)}) %collective-permute-start.3) | collective-permute-done | bytes 262176 | tf_op jit(solution)/shard_map/ppermute | solution.py:225
  72.3 0.0 collective-permute-done.4
  72.3 0.0 collective-permute-done.5
  72.3 1.2 fusion.10
  73.5 1.1 pad_maximum_fusion
  74.6 14.8 %all-to-all-start.1 = ((bf16[8,64,1280]{2,1,0:T(8,128)(2,1)}), bf16[8,64,1280]{2,1,0:T(8,128)(2,1)S(1)}, u32[]{:S(2)}, u32[]{:S(2)}) async-start(bf16[8,64,1280]{2,1,0:T(8,128)(2,1)} %bitcast.25), calls=%async_computation.1 | async-start | bytes 2621440 | tf_op jit(solution)/shard_map/all_to_all | solution.py:243
  89.4 31.0 %all-to-all-done.1 = bf16[8,64,1280]{2,1,0:T(8,128)(2,1)S(1)} async-done(((bf16[8,64,1280]{2,1,0:T(8,128)(2,1)}), bf16[8,64,1280]{2,1,0:T(8,128)(2,1)S(1)}, u32[]{:S(2)}, u32[]{:S(2)}) %all-to-all-start.1) | async-done | bytes 1310752 | tf_op jit(solution)/shard_map/all_to_all | solution.py:243
  120.4 0.5 fusion
  120.9 0.8 slice_bitcast_fusion.2
  121.6 1.1 slice_bitcast_fusion
  (20 shorter events, 0.2 us)
Async XLA Ops:
  0.7 11.1 %copy-start = (s32[4,8,4]{1,2,0:T(4,128)S(1)}, s32[4,8,4]{1,2,0:T(4,128)}, u32[]{:S(2)}) copy-start(s32[4,8,4]{1,2,0:T(4,128)} %param.15) | copy-start | bytes 1540
  4.8 36.9 %all-to-all-start = ((bf16[8,64,1280]{2,1,0:T(8,128)(2,1)}), bf16[8,64,1280]{2,1,0:T(8,128)(2,1)S(1)}, u32[]{:S(2)}, u32[]{:S(2)}) async-start(bf16[8,64,1280]{2,1,0:T(8,128)(2,1)} %fusion.4), calls=%async_computation | async-start | bytes 2621440 | tf_op jit(solution)/shard_map/all_to_all | solution.py:146
  41.7 6.2 %collective-permute-start.1 = (bf16[512,256]{1,0:T(8,128)(2,1)S(1)}, bf16[512,256]{1,0:T(8,128)(2,1)S(1)}, u32[]{:S(2)}, u32[]{:S(2)}) collective-permute-start(bf16[512,256]{1,0:T(8,128)(2,1)S(1)} %get-tuple-element.125), channel_id=1, source_target_pairs={{6,15},{7,14},{12,21},{13,20},{18,27},{19,26}} | collective-permute-start | bytes 786440 | tf_op jit(solution)/shard_map/ppermute | solution.py:160
  42.4 5.5 %collective-permute-start = (bf16[512,256]{1,0:T(8,128)(2,1)S(1)}, bf16[512,256]{1,0:T(8,128)(2,1)S(1)}, u32[]{:S(2)}, u32[]{:S(2)}) collective-permute-start(bf16[512,256]{1,0:T(8,128)(2,1)S(1)} %get-tuple-element.125), channel_id=1, source_target_pairs={{6,14},{7,15},{12,20},{13,21},{18,26},{19,27}} | collective-permute-start | bytes 786440 | tf_op jit(solution)/shard_map/ppermute | solution.py:159
  43.1 7.7 %collective-permute-start.2 = (bf16[512,256]{1,0:T(8,128)(2,1)S(1)}, bf16[512,256]{1,0:T(8,128)(2,1)}, u32[]{:S(2)}, u32[]{:S(2)}) collective-permute-start(bf16[512,256]{1,0:T(8,128)(2,1)S(1)} %get-tuple-element.125), channel_id=1, source_target_pairs={{0,1},{2,3},{4,5},{6,7},{8,9},{10,11},{12,13},{14,15},{16,17},{18,... | collective-permute-start | bytes 786440 | tf_op jit(solution)/shard_map/ppermute | solution.py:150
  64.3 7.9 %collective-permute-start.3 = (bf16[512,256]{1,0:T(8,128)(2,1)S(1)}, bf16[512,256]{1,0:T(8,128)(2,1)S(1)}, u32[]{:S(2)}, u32[]{:S(2)}) collective-permute-start(bf16[512,256]{1,0:T(8,128)(2,1)S(1)} %get-tuple-element.118), channel_id=1, source_target_pairs={{1,0},{3,2},{5,4},{7,6},{9,8},{11,10},{13,12},{15,14},{17,16},{19,... | collective-permute-start | bytes 786440 | tf_op jit(solution)/shard_map/ppermute | solution.py:225
  65.7 6.7 %collective-permute-start.4 = (bf16[512,256]{1,0:T(8,128)(2,1)S(1)}, bf16[512,256]{1,0:T(8,128)(2,1)S(1)}, u32[]{:S(2)}, u32[]{:S(2)}) collective-permute-start(bf16[512,256]{1,0:T(8,128)(2,1)S(1)} %get-tuple-element.119), channel_id=1, source_target_pairs={{14,6},{15,7},{20,12},{21,13},{26,18},{27,19}} | collective-permute-start | bytes 786440 | tf_op jit(solution)/shard_map/ppermute | solution.py:230
  66.3 6.0 %collective-permute-start.5 = (bf16[512,256]{1,0:T(8,128)(2,1)S(1)}, bf16[512,256]{1,0:T(8,128)(2,1)S(1)}, u32[]{:S(2)}, u32[]{:S(2)}) collective-permute-start(bf16[512,256]{1,0:T(8,128)(2,1)S(1)} %get-tuple-element.120), channel_id=1, source_target_pairs={{15,6},{14,7},{21,12},{20,13},{27,18},{26,19}} | collective-permute-start | bytes 786440 | tf_op jit(solution)/shard_map/ppermute | solution.py:231
  74.6 45.8 %all-to-all-start.1 = ((bf16[8,64,1280]{2,1,0:T(8,128)(2,1)}), bf16[8,64,1280]{2,1,0:T(8,128)(2,1)S(1)}, u32[]{:S(2)}, u32[]{:S(2)}) async-start(bf16[8,64,1280]{2,1,0:T(8,128)(2,1)} %bitcast.25), calls=%async_computation.1 | async-start | bytes 2621440 | tf_op jit(solution)/shard_map/all_to_all | solution.py:243

commit v14 on v13

--- a/solution.py
+++ b/solution.py
@@ -31,15 +31,15 @@
     def _():
         dkt_ref[...] = jnp.zeros_like(dkt_ref)
         dvt_ref[...] = jnp.zeros_like(dvt_ref)
-        dkv_ref[...] = jnp.zeros_like(dkv_ref)
 
     k = k_ref[...]
     v = v_ref[...]
     kt = k.T
     vt = v.T
     contract_first = (((0,), (0,)), ((), ()))
+    lanes = qmeta_ref.shape[1] // 2
     allowed = (qmeta_ref[:, 0:1] == kmeta_ref[0:1, :]) & (
-        kmeta_ref[1:2, :] <= qmeta_ref[:, 1:2]
+        kmeta_ref[1:2, :] <= qmeta_ref[:, lanes : lanes + 1]
     )
     for h in range(n_heads):
         cols = slice(h * head_dim, (h + 1) * head_dim)
@@ -73,11 +73,14 @@
 
     @pl.when(step == pl.num_programs(0) - 1)
     def _():
-        for r in range(dkt_ref.shape[1] // slot_len):
+        n_used = dkt_ref.shape[1] // slot_len
+        for r in range(n_used):
             cols = slice(r * slot_len, (r + 1) * slot_len)
             slot = order_ref[r]
             dkv_ref[slot, :, 0:head_dim] = dkt_ref[:, cols].T
             dkv_ref[slot, :, head_dim : 2 * head_dim] = dvt_ref[:, cols].T
+        for r in range(n_used, dkv_ref.shape[0]):
+            dkv_ref[order_ref[r]] = jnp.zeros(dkv_ref.shape[1:], dkv_ref.dtype)
 
 
 def attend(rows, qmeta, ctx_all, kmeta_all, order, n_keys, n_heads):
@@ -90,7 +93,7 @@
     grid = (n_rows // block_q,)
     q_spec = pl.BlockSpec((block_q, width_q), lambda i, o: (i, 0))
     g_spec = pl.BlockSpec((block_q, width_q), lambda i, o: (i, 1))
-    qmeta_spec = pl.BlockSpec((block_q, 2), lambda i, o: (i, 0))
+    qmeta_spec = pl.BlockSpec((block_q, qmeta.shape[1]), lambda i, o: (i, 0))
     kmeta_spec = pl.BlockSpec((2, n_keys), lambda i, o: (0, 0))
     k_spec = pl.BlockSpec((n_keys, head_dim), lambda i, o: (0, 0))
     v_spec = pl.BlockSpec((n_keys, head_dim), lambda i, o: (0, 1))
@@ -201,7 +204,14 @@
     )
     kv_sorted = slot_kv[order].reshape(n_slots * tok_dev, 2 * head_dim)
     kmeta_sorted = jnp.stack([slot_doc[order].reshape(-1), slot_pos[order].reshape(-1)])
-    qmeta = jnp.stack([query_doc, query_pos], axis=1)
+    lane_width = 128
+    qmeta = jnp.concatenate(
+        [
+            jnp.broadcast_to(query_doc[:, None], (tok_dev, lane_width)),
+            jnp.broadcast_to(query_pos[:, None], (tok_dev, lane_width)),
+        ],
+        axis=1,
+    )
 
     def branch(n_used):
         def run(kv_sorted, kmeta_sorted, qmeta, order):

time: 125 us -> 125 us (level)
  starting transfers between devices: 29.3 us -> 23.8 us
  waiting for transfers between devices: 62.5 us -> 67.6 us
    all_to_all x1, starting transfers between devices: 14.8 us -> 10 us  [shards(): lax.all_to_all(result, 'inner', 0, 0, tiled=True)]
    ppermute x1, waiting for transfers between devices: 5.28 us -> 9.96 us  [shards(): from_partner = lax.ppermute(kv_grads[2].astype(low), 'inner', pairs_down)]
where the time goes in v14:
time: 125 us; the launch traced here: 122 us
  waiting for transfers between devices  67.6 us (54%)
  starting transfers between devices  23.8 us (19%)
  other arithmetic  15.3 us (12%)
  Pallas kernels  8.83 us (7%)
  local copies, waits for them, and re-layouts  5.39 us (4%)
  between operations  1.53 us (1%)
    all_to_all x1, waiting for transfers between devices, shards(): lax.all_to_all(result, 'inner', 0, 0, tiled=True)  31 us
    all_to_all x1, waiting for transfers between devices, shards(): lax.all_to_all(packed, 'inner', 0, 0, tiled=True).reshape(tok_dev, -1)  23.4 us
    all_to_all x1, starting transfers between devices, shards(): lax.all_to_all(result, 'inner', 0, 0, tiled=True)  10 us
    ppermute x1, waiting for transfers between devices, shards(): from_partner = lax.ppermute(kv_grads[2].astype(low), 'inner', pairs_down)  9.96 us
    pallas_call x1, Pallas kernels, attend(): pl.pallas_call(kernel, grid_spec=pltpu.PrefetchScalarGridSpec(num_scalar_...  8.83 us
    all_to_all x1, starting transfers between devices, shards(): lax.all_to_all(packed, 'inner', 0, 0, tiled=True).reshape(tok_dev, -1)  6.34 us
    concatenate x1, other arithmetic, shards(): packed = jnp.roll(packed, -2 * outer_id, axis=0)  4.09 us
    ppermute x1, starting transfers between devices, shards(): kv_partner = lax.ppermute(kv_own, 'inner', pairs_up)  3.41 us
  transfers between devices with their start and end apart: 8, of which 4 were waited for; matrix products, arithmetic and copies ran while one was open for 6% of the time, Pallas kernels for 0%

profile of v14, /device:TPU:1, one launch (start us, length us, event | category | flops | bytes accessed | tf_op | source)
XLA Modules:
  0.0 122.4 jit_solution(14467672076859163684)
XLA Ops:
  0.7 4.1 %fusion.4 = bf16[8,64,1280]{2,1,0:T(8,128)(2,1)} fusion(s32[]{:T(128)S(6)} %select_n.131, bf16[8,64,512]{2,1,0:T(8,128)(2,1)} %bitcast.75, bf16[8,64,512]{2,1,0:T(8,128)(2,1)} %bitcast.76, bf16[8,64,128]{2,1,0:T(8,128)(2,1)} %bitcast.78, bf16[8,64,128]{2,1,0:T(8,128)(2,1)} %bitcast.79), kind=kLoop, calls=%fused_computation.17 | loop fusion | flops 10485760 | bytes 2621444 | tf_op jit(solution)/shard_map/jit(_roll_dynamic)/concatenate | solution.py:148
  4.8 6.3 %all-to-all-start = ((bf16[8,64,1280]{2,1,0:T(8,128)(2,1)}), bf16[8,64,1280]{2,1,0:T(8,128)(2,1)S(1)}, u32[]{:S(2)}, u32[]{:S(2)}) async-start(bf16[8,64,1280]{2,1,0:T(8,128)(2,1)} %fusion.4), calls=%async_computation | async-start | bytes 2621440 | tf_op jit(solution)/shard_map/all_to_all | solution.py:149
  11.1 0.6 iota_add_fusion
  11.8 0.1 le.67
  11.9 0.1 reshape.270
  12.0 0.1 reduce-window.21
  12.0 0.1 reduce.3
  12.2 0.1 reshape.236
  12.2 0.1 convert_reduce_fusion
  12.4 0.1 fusion.14
  12.4 0.6 fusion.19
  13.1 0.1 reduce_min.29
  13.2 0.1 fusion.18
  13.4 1.9 %fusion.15 = (s32[4,1]{0,1:T(1,128)S(1)}, pred[4]{0:T(512)(128)(4,1)S(1)}) fusion(s32[4]{0:T(128)S(1)} %reduce_min.29, s32[]{:T(128)} %get-tuple-element.93, s32[4]{0:T(128)S(1)} %get-tuple-element.72, s32[]{:T(128)} %get-tuple-element.74, s32[4]{0:T(128)S(1)} %get-tuple-element.71, s32[]{:T(128)} %get-tuple-element.73), kind=kLoop, calls=%fused_computation.64 | loop fusion | flops 32 | bytes 80 | tf_op jit(solution)/shard_map/convert_element_type | solution.py:196
  15.3 0.2 reduce-window.22
  15.5 0.2 reduce-window.23
  15.7 0.6 convert_reduce_fusion.2
  16.3 0.6 bitcast_select_fusion
  17.0 0.1 select_reduce_fusion
  17.1 0.6 gather_fusion.1
  17.7 0.6 gather_fusion
  18.3 23.4 %all-to-all-done = bf16[8,64,1280]{2,1,0:T(8,128)(2,1)S(1)} async-done(((bf16[8,64,1280]{2,1,0:T(8,128)(2,1)}), bf16[8,64,1280]{2,1,0:T(8,128)(2,1)S(1)}, u32[]{:S(2)}, u32[]{:S(2)}) %all-to-all-start) | async-done | bytes 1310752 | tf_op jit(solution)/shard_map/all_to_all | solution.py:149
  41.7 0.7 collective-permute-start.1
  42.4 0.7 collective-permute-start
  43.1 3.4 %collective-permute-start.2 = (bf16[512,256]{1,0:T(8,128)(2,1)S(1)}, bf16[512,256]{1,0:T(8,128)(2,1)S(1)}, u32[]{:S(2)}, u32[]{:S(2)}) collective-permute-start(bf16[512,256]{1,0:T(8,128)(2,1)S(1)} %get-tuple-element.85), channel_id=1, source_target_pairs={{0,1},{2,3},{4,5},{6,7},{8,9},{10,11},{12,13},{14,15},{16,17},{18,... | collective-permute-start | bytes 786440 | tf_op jit(solution)/shard_map/ppermute | solution.py:153
  46.5 0.1 broadcast_in_dim.46
  46.7 0.1 broadcast_in_dim.47
  47.5 0.0 collective-permute-done.1
  47.5 0.0 collective-permute-done
  47.6 3.2 %collective-permute-done.2 = bf16[512,256]{1,0:T(8,128)(2,1)S(1)} collective-permute-done((bf16[512,256]{1,0:T(8,128)(2,1)S(1)}, bf16[512,256]{1,0:T(8,128)(2,1)S(1)}, u32[]{:S(2)}, u32[]{:S(2)}) %collective-permute-start.2) | collective-permute-done | bytes 262176 | tf_op jit(solution)/shard_map/ppermute | solution.py:153
  50.8 1.1 pad_maximum_fusion.1
  51.9 1.8 %gather_fusion.2 = bf16[4,512,256]{2,1,0:T(8,128)(2,1)S(1)} fusion(bf16[4,512,256]{2,1,0:T(8,128)(2,1)} %pad_maximum_fusion.1, s32[1024]{0:T(1024)S(1)} %pad_clamp_fusion), kind=kCustom, calls=%fused_computation.2 | custom fusion | bytes 2097168 | tf_op jit(solution)/shard_map/gather | solution.py:205
  53.7 8.9 %conditional.1 = ((bf16[512,512]{1,0:T(8,128)(2,1)S(1)}, bf16[512,512]{1,0:T(8,128)(2,1)}, f32[4,512,256]{2,1,0:T(8,128)})) conditional(s32[]{:T(128)} %clamp.3, (s32[4]{0:T(128)S(1)}, s32[512,256]{1,0:T(8,128)S(1)}, s32[2,2048]{1,0:T(2,128)S(1)}, bf16[512,1280]{1,0:T(8,128)(2,1)S(1)}, ...), branch_computations={%region_13.15_spmd, %region_14.16_spmd, %region_15.17_spmd, %regio... | conditional | bytes 8 | solution.py:224
  53.8 8.8 %branch_0_fun.1 = (bf16[512,512]{1,0:T(8,128)(2,1)S(1)}, bf16[512,512]{1,0:T(8,128)(2,1)}, f32[4,512,256]{2,1,0:T(8,128)}) custom-call(s32[4]{0:T(128)S(1)} %get-tuple-element.34.order_ref, s32[512,256]{1,0:T(8,128)S(1)} %get-tuple-element.42.qmeta_ref, s32[2,2048]{1,0:T(2,128)S(1)} %get-tuple-element.43.kmeta_ref, ...), custom_call_target="tpu_custom_call" | custom-call | tf_op jit(solution)/shard_map/cond/branch_0_fun/pallas_call | solution.py:109
  62.6 1.5 %fusion.13 = (bf16[512,256]{1,0:T(8,128)(2,1)S(1)}, bf16[512,256]{1,0:T(8,128)(2,1)S(1)}, bf16[512,256]{1,0:T(8,128)(2,1)S(1)}) fusion(f32[4,512,256]{2,1,0:T(8,128)} %get-tuple-element.70, pred[]{:T(512)S(6)} %eq.54), kind=kLoop, calls=%fused_computation.35 | loop fusion | flops 262144 | bytes 1572865 | tf_op jit(solution)/shard_map/convert_element_type | solution.py:235
  64.1 1.3 %collective-permute-start.3 = (bf16[512,256]{1,0:T(8,128)(2,1)S(1)}, bf16[512,256]{1,0:T(8,128)(2,1)S(1)}, u32[]{:S(2)}, u32[]{:S(2)}) collective-permute-start(bf16[512,256]{1,0:T(8,128)(2,1)S(1)} %get-tuple-element.78), channel_id=1, source_target_pairs={{1,0},{3,2},{5,4},{7,6},{9,8},{11,10},{13,12},{15,14},{17,16},{19,... | collective-permute-start | bytes 786440 | tf_op jit(solution)/shard_map/ppermute | solution.py:235
  65.4 0.7 collective-permute-start.4
  66.1 0.7 collective-permute-start.5
  66.8 10.0 %collective-permute-done.3 = bf16[512,256]{1,0:T(8,128)(2,1)S(1)} collective-permute-done((bf16[512,256]{1,0:T(8,128)(2,1)S(1)}, bf16[512,256]{1,0:T(8,128)(2,1)S(1)}, u32[]{:S(2)}, u32[]{:S(2)}) %collective-permute-start.3) | collective-permute-done | bytes 262176 | tf_op jit(solution)/shard_map/ppermute | solution.py:235
  76.7 0.0 collective-permute-done.4
  76.7 0.0 collective-permute-done.5
  76.7 1.2 fusion.10
  77.9 1.1 pad_maximum_fusion
  79.1 10.0 %all-to-all-start.1 = ((bf16[8,64,1280]{2,1,0:T(8,128)(2,1)}), bf16[8,64,1280]{2,1,0:T(8,128)(2,1)S(1)}, u32[]{:S(2)}, u32[]{:S(2)}) async-start(bf16[8,64,1280]{2,1,0:T(8,128)(2,1)} %bitcast.24), calls=%async_computation.1 | async-start | bytes 2621440 | tf_op jit(solution)/shard_map/all_to_all | solution.py:253
  89.1 31.0 %all-to-all-done.1 = bf16[8,64,1280]{2,1,0:T(8,128)(2,1)S(1)} async-done(((bf16[8,64,1280]{2,1,0:T(8,128)(2,1)}), bf16[8,64,1280]{2,1,0:T(8,128)(2,1)S(1)}, u32[]{:S(2)}, u32[]{:S(2)}) %all-to-all-start.1) | async-done | bytes 1310752 | tf_op jit(solution)/shard_map/all_to_all | solution.py:253
  120.0 0.5 fusion
  120.5 0.8 slice_bitcast_fusion.2
  121.3 1.1 slice_bitcast_fusion
  (22 shorter events, 0.3 us)
Async XLA Ops:
  0.7 11.1 %copy-start.1 = (s32[4,8,4]{1,2,0:T(4,128)S(1)}, s32[4,8,4]{1,2,0:T(4,128)}, u32[]{:S(2)}) copy-start(s32[4,8,4]{1,2,0:T(4,128)} %param.15) | copy-start | bytes 1540
  4.8 36.9 %all-to-all-start = ((bf16[8,64,1280]{2,1,0:T(8,128)(2,1)}), bf16[8,64,1280]{2,1,0:T(8,128)(2,1)S(1)}, u32[]{:S(2)}, u32[]{:S(2)}) async-start(bf16[8,64,1280]{2,1,0:T(8,128)(2,1)} %fusion.4), calls=%async_computation | async-start | bytes 2621440 | tf_op jit(solution)/shard_map/all_to_all | solution.py:149
  41.7 5.8 %collective-permute-start.1 = (bf16[512,256]{1,0:T(8,128)(2,1)S(1)}, bf16[512,256]{1,0:T(8,128)(2,1)S(1)}, u32[]{:S(2)}, u32[]{:S(2)}) collective-permute-start(bf16[512,256]{1,0:T(8,128)(2,1)S(1)} %get-tuple-element.85), channel_id=1, source_target_pairs={{6,15},{7,14},{12,21},{13,20},{18,27},{19,26}} | collective-permute-start | bytes 786440 | tf_op jit(solution)/shard_map/ppermute | solution.py:163
  42.4 5.1 %collective-permute-start = (bf16[512,256]{1,0:T(8,128)(2,1)S(1)}, bf16[512,256]{1,0:T(8,128)(2,1)S(1)}, u32[]{:S(2)}, u32[]{:S(2)}) collective-permute-start(bf16[512,256]{1,0:T(8,128)(2,1)S(1)} %get-tuple-element.85), channel_id=1, source_target_pairs={{6,14},{7,15},{12,20},{13,21},{18,26},{19,27}} | collective-permute-start | bytes 786440 | tf_op jit(solution)/shard_map/ppermute | solution.py:162
  43.1 7.7 %collective-permute-start.2 = (bf16[512,256]{1,0:T(8,128)(2,1)S(1)}, bf16[512,256]{1,0:T(8,128)(2,1)S(1)}, u32[]{:S(2)}, u32[]{:S(2)}) collective-permute-start(bf16[512,256]{1,0:T(8,128)(2,1)S(1)} %get-tuple-element.85), channel_id=1, source_target_pairs={{0,1},{2,3},{4,5},{6,7},{8,9},{10,11},{12,13},{14,15},{16,17},{18,... | collective-permute-start | bytes 786440 | tf_op jit(solution)/shard_map/ppermute | solution.py:153
  62.6 15.3 %copy-start = (bf16[512,512]{1,0:T(8,128)(2,1)S(1)}, bf16[512,512]{1,0:T(8,128)(2,1)}, u32[]{:S(2)}) copy-start(bf16[512,512]{1,0:T(8,128)(2,1)} %get-tuple-element.69) | copy-start | bytes 1572868
  64.1 12.6 %collective-permute-start.3 = (bf16[512,256]{1,0:T(8,128)(2,1)S(1)}, bf16[512,256]{1,0:T(8,128)(2,1)S(1)}, u32[]{:S(2)}, u32[]{:S(2)}) collective-permute-start(bf16[512,256]{1,0:T(8,128)(2,1)S(1)} %get-tuple-element.78), channel_id=1, source_target_pairs={{1,0},{3,2},{5,4},{7,6},{9,8},{11,10},{13,12},{15,14},{17,16},{19,... | collective-permute-start | bytes 786440 | tf_op jit(solution)/shard_map/ppermute | solution.py:235
  65.4 11.3 %collective-permute-start.4 = (bf16[512,256]{1,0:T(8,128)(2,1)S(1)}, bf16[512,256]{1,0:T(8,128)(2,1)S(1)}, u32[]{:S(2)}, u32[]{:S(2)}) collective-permute-start(bf16[512,256]{1,0:T(8,128)(2,1)S(1)} %get-tuple-element.79), channel_id=1, source_target_pairs={{14,6},{15,7},{20,12},{21,13},{26,18},{27,19}} | collective-permute-start | bytes 786440 | tf_op jit(solution)/shard_map/ppermute | solution.py:240
  66.1 10.7 %collective-permute-start.5 = (bf16[512,256]{1,0:T(8,128)(2,1)S(1)}, bf16[512,256]{1,0:T(8,128)(2,1)S(1)}, u32[]{:S(2)}, u32[]{:S(2)}) collective-permute-start(bf16[512,256]{1,0:T(8,128)(2,1)S(1)} %get-tuple-element.80), channel_id=1, source_target_pairs={{15,6},{14,7},{21,12},{20,13},{27,18},{26,19}} | collective-permute-start | bytes 786440 | tf_op jit(solution)/shard_map/ppermute | solution.py:241
  79.1 41.0 %all-to-all-start.1 = ((bf16[8,64,1280]{2,1,0:T(8,128)(2,1)}), bf16[8,64,1280]{2,1,0:T(8,128)(2,1)S(1)}, u32[]{:S(2)}, u32[]{:S(2)}) async-start(bf16[8,64,1280]{2,1,0:T(8,128)(2,1)} %bitcast.24), calls=%async_computation.1 | async-start | bytes 2621440 | tf_op jit(solution)/shard_map/all_to_all | solution.py:253

commit v15 on v14

--- a/solution.py
+++ b/solution.py
@@ -141,11 +141,21 @@
     docs_all = doc_table(doc_starts, tok_dev)
     offsets = jnp.arange(tok_dev, dtype=jnp.int32)
 
-    packed = jnp.concatenate(
-        [queries[0, :, 0], grad_out[0, :, 0], keys[0, :, 0], values[0, :, 0]], axis=-1
+    def packed_for(shift):
+        def pack(q, g, k, v):
+            return jnp.roll(jnp.concatenate([q, g, k, v], axis=-1), -2 * shift, axis=0)
+
+        return pack
+
+    packed = lax.switch(
+        outer_id,
+        [packed_for(o) for o in range(n_outer)],
+        queries[0, :, 0],
+        grad_out[0, :, 0],
+        keys[0, :, 0],
+        values[0, :, 0],
     )
     unit_local = (inner_id + 2 * outer_id) % n_units
-    packed = jnp.roll(packed, -2 * outer_id, axis=0)
     arrived = lax.all_to_all(packed, "inner", 0, 0, tiled=True).reshape(tok_dev, -1)
     kv_own = arrived[:, 2 * width_q :]
 

time: 125 us -> 123 us (0.984)
  starting transfers between devices: 23.8 us -> 29.2 us
  waiting for transfers between devices: 67.6 us -> 62.3 us
  other arithmetic: 15.3 us -> 12.3 us
  local copies, waits for them, and re-layouts: 5.39 us -> 6.76 us
    ppermute x1, waiting for transfers between devices: 9.96 us -> 4.57 us  [shards(): from_partner = lax.ppermute(kv_grads[2].astype(low), 'inner', pairs_down)]
    all_to_all x1, starting transfers between devices: 10 us -> 15.4 us  [shards(): lax.all_to_all(result, 'inner', 0, 0, tiled=True)]
    concatenate x1, other arithmetic: 4.09 us -> 1.18 us  [pack(): return jnp.roll(jnp.concatenate([q, g, k, v], axis=-1), -2 * shift, axis=0)]
where the time goes in v15:
time: 123 us; the launch traced here: 121 us
  waiting for transfers between devices  62.3 us (51%)
  starting transfers between devices  29.2 us (24%)
  other arithmetic  12.3 us (10%)
  Pallas kernels  8.82 us (7%)
  local copies, waits for them, and re-layouts  6.76 us (5%)
  between operations  1.51 us (1%)
    all_to_all x1, waiting for transfers between devices, shards(): lax.all_to_all(result, 'inner', 0, 0, tiled=True)  31 us
    all_to_all x1, waiting for transfers between devices, shards(): lax.all_to_all(packed, 'inner', 0, 0, tiled=True).reshape(tok_dev, -1)  23.5 us
    all_to_all x1, starting transfers between devices, shards(): lax.all_to_all(result, 'inner', 0, 0, tiled=True)  15.4 us
    pallas_call x1, Pallas kernels, attend(): pl.pallas_call(kernel, grid_spec=pltpu.PrefetchScalarGridSpec(num_scalar_...  8.82 us
    all_to_all x1, starting transfers between devices, shards(): lax.all_to_all(packed, 'inner', 0, 0, tiled=True).reshape(tok_dev, -1)  6.47 us
    ppermute x1, waiting for transfers between devices, shards(): from_partner = lax.ppermute(kv_grads[2].astype(low), 'inner', pairs_down)  4.57 us
    ppermute x1, starting transfers between devices, shards(): kv_partner = lax.ppermute(kv_own, 'inner', pairs_up)  3.3 us
    ppermute x1, waiting for transfers between devices, shards(): kv_partner = lax.ppermute(kv_own, 'inner', pairs_up)  3.2 us
  transfers between devices with their start and end apart: 8, of which 4 were waited for; matrix products, arithmetic and copies ran while one was open for 6% of the time, Pallas kernels for 0%

profile of v15, /device:TPU:1, one launch (start us, length us, event | category | flops | bytes accessed | tf_op | source)
XLA Modules:
  0.0 121.0 jit_solution(3305524477100272009)
XLA Ops:
  0.6 2.7 %conditional.2 = (bf16[8,64,1280]{2,1,0:T(8,128)(2,1)}) conditional(s32[]{:T(128)} %clamp.7, (bf16[8,64,512]{2,1,0:T(8,128)(2,1)}, bf16[8,64,512]{2,1,0:T(8,128)(2,1)}, bf16[8,64,128]{2,1,0:T(8,128)(2,1)}, bf16[8,64,128]{2,1,0:T(8,128)(2,1)}) %tuple.83, (bf16[8,64,512]{2,1,0:T(8,128)(2,1)}, ...), branch_computations={%region_13.14_spmd, %region_14.15_spmd, %region_15.16_spmd, %regio... | conditional | flops 5242880 | bytes 11010140 | solution.py:150
  0.7 1.1 constant_dynamic-update-slice_fusion.3
  1.8 0.0 copy-done
  2.0 0.1 slice.69
  2.1 1.2 pad_maximum_fusion.1
  3.3 6.5 %all-to-all-start = ((bf16[8,64,1280]{2,1,0:T(8,128)(2,1)}), bf16[8,64,1280]{2,1,0:T(8,128)(2,1)S(1)}, u32[]{:S(2)}, u32[]{:S(2)}) async-start(bf16[8,64,1280]{2,1,0:T(8,128)(2,1)} %get-tuple-element.162), calls=%async_computation | async-start | bytes 2621440 | tf_op jit(solution)/shard_map/all_to_all | solution.py:159
  9.8 0.6 iota_add_fusion
  10.5 0.1 le.67
  10.6 0.1 reshape.270
  10.6 0.1 reduce-window.21
  10.7 0.1 reduce.3
  10.8 0.1 reshape.236
  10.9 0.1 convert_reduce_fusion
  11.0 0.1 fusion.7
  11.1 0.6 fusion.12
  11.8 0.1 reduce_min.29
  11.9 0.1 fusion.11
  12.0 1.9 %fusion.8 = (s32[4,1]{0,1:T(1,128)S(1)}, pred[4]{0:T(512)(128)(4,1)S(1)}) fusion(s32[4]{0:T(128)S(1)} %reduce_min.29, s32[]{:T(128)} %get-tuple-element.147, s32[4]{0:T(128)S(1)} %get-tuple-element.124, s32[]{:T(128)} %get-tuple-element.126, s32[4]{0:T(128)S(1)} %get-tuple-element.123, s32[]{:T(128)} %get-tuple-element.125), kind=kLoop, calls=%fused_computation.61 | loop fusion | flops 32 | bytes 80 | tf_op jit(solution)/shard_map/convert_element_type | solution.py:206
  14.0 0.2 reduce-window.22
  14.2 0.2 reduce-window.23
  14.4 0.6 convert_reduce_fusion.2
  15.0 0.6 bitcast_select_fusion
  15.6 0.1 select_reduce_fusion
  15.8 0.6 gather_fusion.1
  16.3 0.6 gather_fusion
  16.9 23.5 %all-to-all-done = bf16[8,64,1280]{2,1,0:T(8,128)(2,1)S(1)} async-done(((bf16[8,64,1280]{2,1,0:T(8,128)(2,1)}), bf16[8,64,1280]{2,1,0:T(8,128)(2,1)S(1)}, u32[]{:S(2)}, u32[]{:S(2)}) %all-to-all-start) | async-done | bytes 1310752 | tf_op jit(solution)/shard_map/all_to_all | solution.py:159
  40.5 0.7 collective-permute-start.1
  41.2 0.7 collective-permute-start
  41.9 3.3 %collective-permute-start.2 = (bf16[512,256]{1,0:T(8,128)(2,1)S(1)}, bf16[512,256]{1,0:T(8,128)(2,1)S(1)}, u32[]{:S(2)}, u32[]{:S(2)}) collective-permute-start(bf16[512,256]{1,0:T(8,128)(2,1)S(1)} %get-tuple-element.139), channel_id=1, source_target_pairs={{0,1},{2,3},{4,5},{6,7},{8,9},{10,11},{12,13},{14,15},{16,17},{18,... | collective-permute-start | bytes 786440 | tf_op jit(solution)/shard_map/ppermute | solution.py:163
  45.2 0.1 broadcast_in_dim.46
  45.3 0.1 broadcast_in_dim.47
  46.2 3.2 %collective-permute-done.2 = bf16[512,256]{1,0:T(8,128)(2,1)S(1)} collective-permute-done((bf16[512,256]{1,0:T(8,128)(2,1)S(1)}, bf16[512,256]{1,0:T(8,128)(2,1)S(1)}, u32[]{:S(2)}, u32[]{:S(2)}) %collective-permute-start.2) | collective-permute-done | bytes 262176 | tf_op jit(solution)/shard_map/ppermute | solution.py:163
  49.4 1.1 pad_maximum_fusion.5
  50.6 1.8 %gather_fusion.2 = bf16[4,512,256]{2,1,0:T(8,128)(2,1)S(1)} fusion(bf16[4,512,256]{2,1,0:T(8,128)(2,1)} %pad_maximum_fusion.5, s32[1024]{0:T(1024)S(1)} %pad_clamp_fusion), kind=kCustom, calls=%fused_computation.2 | custom fusion | bytes 2097168 | tf_op jit(solution)/shard_map/gather | solution.py:215
  52.4 8.8 %conditional.3 = ((bf16[512,512]{1,0:T(8,128)(2,1)S(1)}, bf16[512,512]{1,0:T(8,128)(2,1)}, f32[4,512,256]{2,1,0:T(8,128)})) conditional(s32[]{:T(128)} %clamp.6, (s32[4]{0:T(128)S(1)}, s32[512,256]{1,0:T(8,128)S(1)}, s32[2,2048]{1,0:T(2,128)S(1)}, bf16[512,1280]{1,0:T(8,128)(2,1)S(1)}, ...), branch_computations={%region_17.18_spmd, %region_18.19_spmd, %region_19.20_spmd, %regio... | conditional | bytes 8 | solution.py:234
  52.4 8.8 %branch_0_fun.1 = (bf16[512,512]{1,0:T(8,128)(2,1)S(1)}, bf16[512,512]{1,0:T(8,128)(2,1)}, f32[4,512,256]{2,1,0:T(8,128)}) custom-call(s32[4]{0:T(128)S(1)} %get-tuple-element.93.order_ref, s32[512,256]{1,0:T(8,128)S(1)} %get-tuple-element.94.qmeta_ref, s32[2,2048]{1,0:T(2,128)S(1)} %get-tuple-element.95.kmeta_ref, ...), custom_call_target="tpu_custom_call" | custom-call | tf_op jit(solution)/shard_map/cond/branch_0_fun/pallas_call | solution.py:109
  61.2 1.5 %fusion.6 = (bf16[512,256]{1,0:T(8,128)(2,1)S(1)}, bf16[512,256]{1,0:T(8,128)(2,1)S(1)}, bf16[512,256]{1,0:T(8,128)(2,1)S(1)}) fusion(f32[4,512,256]{2,1,0:T(8,128)} %get-tuple-element.122, pred[]{:T(512)S(6)} %eq.55), kind=kLoop, calls=%fused_computation.36 | loop fusion | flops 262144 | bytes 1572865 | tf_op jit(solution)/shard_map/convert_element_type | solution.py:245
  62.7 1.3 %collective-permute-start.3 = (bf16[512,256]{1,0:T(8,128)(2,1)S(1)}, bf16[512,256]{1,0:T(8,128)(2,1)S(1)}, u32[]{:S(2)}, u32[]{:S(2)}) collective-permute-start(bf16[512,256]{1,0:T(8,128)(2,1)S(1)} %get-tuple-element.132), channel_id=1, source_target_pairs={{1,0},{3,2},{5,4},{7,6},{9,8},{11,10},{13,12},{15,14},{17,16},{19,... | collective-permute-start | bytes 786440 | tf_op jit(solution)/shard_map/ppermute | solution.py:245
  64.0 0.7 collective-permute-start.4
  64.7 0.7 collective-permute-start.5
  65.4 4.6 %collective-permute-done.3 = bf16[512,256]{1,0:T(8,128)(2,1)S(1)} collective-permute-done((bf16[512,256]{1,0:T(8,128)(2,1)S(1)}, bf16[512,256]{1,0:T(8,128)(2,1)S(1)}, u32[]{:S(2)}, u32[]{:S(2)}) %collective-permute-start.3) | collective-permute-done | bytes 262176 | tf_op jit(solution)/shard_map/ppermute | solution.py:245
  70.0 1.2 fusion.3
  71.2 1.2 pad_maximum_fusion.4
  72.3 15.4 %all-to-all-start.1 = ((bf16[8,64,1280]{2,1,0:T(8,128)(2,1)}), bf16[8,64,1280]{2,1,0:T(8,128)(2,1)S(1)}, u32[]{:S(2)}, u32[]{:S(2)}) async-start(bf16[8,64,1280]{2,1,0:T(8,128)(2,1)} %bitcast.24), calls=%async_computation.1 | async-start | bytes 2621440 | tf_op jit(solution)/shard_map/all_to_all | solution.py:263
  87.7 31.0 %all-to-all-done.1 = bf16[8,64,1280]{2,1,0:T(8,128)(2,1)S(1)} async-done(((bf16[8,64,1280]{2,1,0:T(8,128)(2,1)}), bf16[8,64,1280]{2,1,0:T(8,128)(2,1)S(1)}, u32[]{:S(2)}, u32[]{:S(2)}) %all-to-all-start.1) | async-done | bytes 1310752 | tf_op jit(solution)/shard_map/all_to_all | solution.py:263
  118.7 0.5 fusion
  119.2 0.8 slice_bitcast_fusion.2
  119.9 1.1 slice_bitcast_fusion
  (35 shorter events, 0.4 us)
Async XLA Ops:
  0.7 1.2 copy-start
  0.7 1.2 %copy-start.3 = (bf16[8,64,128]{2,1,0:T(8,128)(2,1)S(1)}, bf16[8,64,128]{2,1,0:T(8,128)(2,1)}, u32[]{:S(2)}) copy-start(bf16[8,64,128]{2,1,0:T(8,128)(2,1)} %get-tuple-element.83) | copy-start | bytes 393220 | tf_op jit(solution)/shard_map/cond
  0.7 1.3 %copy-start.6 = (bf16[8,64,128]{2,1,0:T(8,128)(2,1)S(1)}, bf16[8,64,128]{2,1,0:T(8,128)(2,1)}, u32[]{:S(2)}) copy-start(bf16[8,64,128]{2,1,0:T(8,128)(2,1)} %get-tuple-element.84) | copy-start | bytes 393220 | tf_op jit(solution)/shard_map/cond
  3.3 7.1 %copy-start.10 = (s32[4,8,4]{1,2,0:T(4,128)S(1)}, s32[4,8,4]{1,2,0:T(4,128)}, u32[]{:S(2)}) copy-start(s32[4,8,4]{1,2,0:T(4,128)} %param.17) | copy-start | bytes 1540
  3.3 37.2 %all-to-all-start = ((bf16[8,64,1280]{2,1,0:T(8,128)(2,1)}), bf16[8,64,1280]{2,1,0:T(8,128)(2,1)S(1)}, u32[]{:S(2)}, u32[]{:S(2)}) async-start(bf16[8,64,1280]{2,1,0:T(8,128)(2,1)} %get-tuple-element.162), calls=%async_computation | async-start | bytes 2621440 | tf_op jit(solution)/shard_map/all_to_all | solution.py:159
  40.5 5.7 %collective-permute-start.1 = (bf16[512,256]{1,0:T(8,128)(2,1)S(1)}, bf16[512,256]{1,0:T(8,128)(2,1)S(1)}, u32[]{:S(2)}, u32[]{:S(2)}) collective-permute-start(bf16[512,256]{1,0:T(8,128)(2,1)S(1)} %get-tuple-element.139), channel_id=1, source_target_pairs={{6,15},{7,14},{12,21},{13,20},{18,27},{19,26}} | collective-permute-start | bytes 786440 | tf_op jit(solution)/shard_map/ppermute | solution.py:173
  41.2 5.0 %collective-permute-start = (bf16[512,256]{1,0:T(8,128)(2,1)S(1)}, bf16[512,256]{1,0:T(8,128)(2,1)S(1)}, u32[]{:S(2)}, u32[]{:S(2)}) collective-permute-start(bf16[512,256]{1,0:T(8,128)(2,1)S(1)} %get-tuple-element.139), channel_id=1, source_target_pairs={{6,14},{7,15},{12,20},{13,21},{18,26},{19,27}} | collective-permute-start | bytes 786440 | tf_op jit(solution)/shard_map/ppermute | solution.py:172
  41.9 7.5 %collective-permute-start.2 = (bf16[512,256]{1,0:T(8,128)(2,1)S(1)}, bf16[512,256]{1,0:T(8,128)(2,1)S(1)}, u32[]{:S(2)}, u32[]{:S(2)}) collective-permute-start(bf16[512,256]{1,0:T(8,128)(2,1)S(1)} %get-tuple-element.139), channel_id=1, source_target_pairs={{0,1},{2,3},{4,5},{6,7},{8,9},{10,11},{12,13},{14,15},{16,17},{18,... | collective-permute-start | bytes 786440 | tf_op jit(solution)/shard_map/ppermute | solution.py:163
  61.2 9.9 %copy-start.9 = (bf16[512,512]{1,0:T(8,128)(2,1)S(1)}, bf16[512,512]{1,0:T(8,128)(2,1)}, u32[]{:S(2)}) copy-start(bf16[512,512]{1,0:T(8,128)(2,1)} %get-tuple-element.121) | copy-start | bytes 1572868
  62.7 7.2 %collective-permute-start.3 = (bf16[512,256]{1,0:T(8,128)(2,1)S(1)}, bf16[512,256]{1,0:T(8,128)(2,1)S(1)}, u32[]{:S(2)}, u32[]{:S(2)}) collective-permute-start(bf16[512,256]{1,0:T(8,128)(2,1)S(1)} %get-tuple-element.132), channel_id=1, source_target_pairs={{1,0},{3,2},{5,4},{7,6},{9,8},{11,10},{13,12},{15,14},{17,16},{19,... | collective-permute-start | bytes 786440 | tf_op jit(solution)/shard_map/ppermute | solution.py:245
  64.0 5.9 %collective-permute-start.4 = (bf16[512,256]{1,0:T(8,128)(2,1)S(1)}, bf16[512,256]{1,0:T(8,128)(2,1)S(1)}, u32[]{:S(2)}, u32[]{:S(2)}) collective-permute-start(bf16[512,256]{1,0:T(8,128)(2,1)S(1)} %get-tuple-element.133), channel_id=1, source_target_pairs={{14,6},{15,7},{20,12},{21,13},{26,18},{27,19}} | collective-permute-start | bytes 786440 | tf_op jit(solution)/shard_map/ppermute | solution.py:250
  64.7 5.3 %collective-permute-start.5 = (bf16[512,256]{1,0:T(8,128)(2,1)S(1)}, bf16[512,256]{1,0:T(8,128)(2,1)S(1)}, u32[]{:S(2)}, u32[]{:S(2)}) collective-permute-start(bf16[512,256]{1,0:T(8,128)(2,1)S(1)} %get-tuple-element.134), channel_id=1, source_target_pairs={{15,6},{14,7},{21,12},{20,13},{27,18},{26,19}} | collective-permute-start | bytes 786440 | tf_op jit(solution)/shard_map/ppermute | solution.py:251
  72.3 46.4 %all-to-all-start.1 = ((bf16[8,64,1280]{2,1,0:T(8,128)(2,1)}), bf16[8,64,1280]{2,1,0:T(8,128)(2,1)S(1)}, u32[]{:S(2)}, u32[]{:S(2)}) async-start(bf16[8,64,1280]{2,1,0:T(8,128)(2,1)} %bitcast.24), calls=%async_computation.1 | async-start | bytes 2621440 | tf_op jit(solution)/shard_map/all_to_all | solution.py:263

commit v16 on v15

--- a/solution.py
+++ b/solution.py
@@ -23,7 +23,7 @@
 
 def attention_kernel(
     order_ref, qmeta_ref, kmeta_ref, q_ref, g_ref, k_ref, v_ref,
-    o_ref, dq_ref, dkv_ref, dkt_ref, dvt_ref, *, scaling, n_heads, head_dim, slot_len
+    out_ref, dkv_ref, dkt_ref, dvt_ref, *, scaling, n_heads, head_dim, slot_len
 ):
     step = pl.program_id(0)
 
@@ -54,13 +54,14 @@
         probs = jnp.exp(scores - log_total)
         probs_low = probs.astype(jnp.bfloat16)
         attn = jnp.dot(probs_low, v, preferred_element_type=jnp.float32).astype(jnp.bfloat16)
-        o_ref[:, cols] = attn
+        out_ref[:, cols] = attn
         inner_prod = jnp.sum(
             g.astype(jnp.float32) * attn.astype(jnp.float32), axis=1, keepdims=True
         )
         grad_probs = jnp.dot(g, vt, preferred_element_type=jnp.float32)
         score_grads = (probs * (grad_probs - inner_prod)).astype(jnp.bfloat16)
-        dq_ref[:, cols] = (
+        dq_cols = slice((n_heads + h) * head_dim, (n_heads + h + 1) * head_dim)
+        out_ref[:, dq_cols] = (
             jnp.dot(score_grads, k, preferred_element_type=jnp.float32) * scaling
         ).astype(jnp.bfloat16)
         dkt_ref[...] += (
@@ -97,7 +98,8 @@
     kmeta_spec = pl.BlockSpec((2, n_keys), lambda i, o: (0, 0))
     k_spec = pl.BlockSpec((n_keys, head_dim), lambda i, o: (0, 0))
     v_spec = pl.BlockSpec((n_keys, head_dim), lambda i, o: (0, 1))
-    out_spec = pl.BlockSpec((block_q, width_q), lambda i, o: (i, 0))
+    out_width = 2 * width_q + 2 * head_dim
+    out_spec = pl.BlockSpec((block_q, out_width), lambda i, o: (i, 0))
     grads_spec = pl.BlockSpec((n_slots, slot_len, 2 * head_dim), lambda i, o: (0, 0, 0))
     kernel = functools.partial(
         attention_kernel,
@@ -112,15 +114,14 @@
             num_scalar_prefetch=1,
             grid=grid,
             in_specs=[qmeta_spec, kmeta_spec, q_spec, g_spec, k_spec, v_spec],
-            out_specs=[out_spec, out_spec, grads_spec],
+            out_specs=[out_spec, grads_spec],
             scratch_shapes=[
                 pltpu.VMEM((head_dim, n_keys), jnp.float32),
                 pltpu.VMEM((head_dim, n_keys), jnp.float32),
             ],
         ),
         out_shape=[
-            jax.ShapeDtypeStruct((n_rows, width_q), jnp.bfloat16),
-            jax.ShapeDtypeStruct((n_rows, width_q), jnp.bfloat16),
+            jax.ShapeDtypeStruct((n_rows, out_width), jnp.bfloat16),
             jax.ShapeDtypeStruct((n_slots, slot_len, 2 * head_dim), jnp.float32),
         ],
         compiler_params=pltpu.CompilerParams(dimension_semantics=("arbitrary",)),
@@ -231,7 +232,7 @@
 
         return run
 
-    attn, q_grads, kv_grads = lax.switch(
+    out_rows, kv_grads = lax.switch(
         count - 1,
         [branch(n) for n in range(1, n_slots + 1)],
         kv_sorted,
@@ -256,7 +257,7 @@
         + from_next_b.astype(jnp.float32)
     ).astype(jnp.bfloat16)
 
-    result = jnp.concatenate([attn, q_grads, kv_total], axis=-1).reshape(
+    result = out_rows.at[:, 2 * width_q :].set(kv_total).reshape(
         n_inner, piece_len, -1
     )
     returned = jnp.roll(

time: 123 us -> 123 us (level)
    scatter x0 -> x1, other arithmetic: none -> 1.9 us  [shards(): out_rows.at[:, 2 * width_q:].set(kv_total).reshape(n_inner, piece_len, -1)]
where the time goes in v16:
time: 123 us; the launch traced here: 121 us
  waiting for transfers between devices  61.7 us (50%)
  starting transfers between devices  29.9 us (24%)
  other arithmetic  11.9 us (10%)
  Pallas kernels  9.79 us (8%)
  local copies, waits for them, and re-layouts  6.54 us (5%)
  between operations  1.48 us (1%)
    all_to_all x1, waiting for transfers between devices, shards(): lax.all_to_all(result, 'inner', 0, 0, tiled=True)  31 us
    all_to_all x1, waiting for transfers between devices, shards(): lax.all_to_all(packed, 'inner', 0, 0, tiled=True).reshape(tok_dev, -1)  23.5 us
    all_to_all x1, starting transfers between devices, shards(): lax.all_to_all(result, 'inner', 0, 0, tiled=True)  15.4 us
    pallas_call x1, Pallas kernels, attend(): pl.pallas_call(kernel, grid_spec=pltpu.PrefetchScalarGridSpec(num_scalar_...  9.79 us
    all_to_all x1, starting transfers between devices, shards(): lax.all_to_all(packed, 'inner', 0, 0, tiled=True).reshape(tok_dev, -1)  6.47 us
    ppermute x1, waiting for transfers between devices, shards(): from_partner = lax.ppermute(kv_grads[2].astype(low), 'inner', pairs_down)  4.67 us
    ppermute x1, starting transfers between devices, shards(): kv_partner = lax.ppermute(kv_own, 'inner', pairs_up)  3.98 us
    ppermute x1, waiting for transfers between devices, shards(): kv_partner = lax.ppermute(kv_own, 'inner', pairs_up)  2.53 us
  transfers between devices with their start and end apart: 8, of which 4 were waited for; matrix products, arithmetic and copies ran while one was open for 6% of the time, Pallas kernels for 0%

profile of v16, /device:TPU:1, one launch (start us, length us, event | category | flops | bytes accessed | tf_op | source)
XLA Modules:
  0.0 121.4 jit_solution(1565703754595343339)
XLA Ops:
  0.6 2.7 %conditional.2 = (bf16[8,64,1280]{2,1,0:T(8,128)(2,1)}) conditional(s32[]{:T(128)} %clamp.7, (bf16[8,64,512]{2,1,0:T(8,128)(2,1)}, bf16[8,64,512]{2,1,0:T(8,128)(2,1)}, bf16[8,64,128]{2,1,0:T(8,128)(2,1)}, bf16[8,64,128]{2,1,0:T(8,128)(2,1)}) %tuple.113, (bf16[8,64,512]{2,1,0:T(8,128)(2,1)}, ...), branch_computations={%region_13.14_spmd, %region_14.15_spmd, %region_15.16_spmd, %regio... | conditional | flops 5242880 | bytes 11010140 | solution.py:151
  0.7 0.0 copy-start.3
  0.7 1.1 constant_dynamic-update-slice_fusion.3
  1.8 0.0 copy-done
  2.0 0.1 slice.96
  2.1 1.2 pad_maximum_fusion.1
  3.3 6.5 %all-to-all-start = ((bf16[8,64,1280]{2,1,0:T(8,128)(2,1)}), bf16[8,64,1280]{2,1,0:T(8,128)(2,1)S(1)}, u32[]{:S(2)}, u32[]{:S(2)}) async-start(bf16[8,64,1280]{2,1,0:T(8,128)(2,1)} %get-tuple-element.271), calls=%async_computation | async-start | bytes 2621440 | tf_op jit(solution)/shard_map/all_to_all | solution.py:160
  9.8 0.6 iota_add_fusion
  10.5 0.1 le.67
  10.6 0.1 reshape.337
  10.6 0.1 reduce-window.21
  10.7 0.1 reduce.5
  10.8 0.1 reshape.276
  10.9 0.1 convert_reduce_fusion
  11.0 0.1 fusion.8
  11.1 0.6 fusion.13
  11.8 0.1 reduce_min.29
  11.9 0.1 fusion.12
  12.0 1.9 %fusion.9 = (s32[4,1]{0,1:T(1,128)S(1)}, pred[4]{0:T(512)(128)(4,1)S(1)}) fusion(s32[4]{0:T(128)S(1)} %reduce_min.29, s32[]{:T(128)} %get-tuple-element.260, s32[4]{0:T(128)S(1)} %get-tuple-element.235, s32[]{:T(128)} %get-tuple-element.237, s32[4]{0:T(128)S(1)} %get-tuple-element.234, s32[]{:T(128)} %get-tuple-element.236), kind=kLoop, calls=%fused_computation.68 | loop fusion | flops 32 | bytes 80 | tf_op jit(solution)/shard_map/convert_element_type | solution.py:207
  14.0 0.2 reduce-window.22
  14.2 0.2 reduce-window.23
  14.4 0.6 convert_reduce_fusion.2
  15.0 0.6 bitcast_select_fusion
  15.6 0.1 select_reduce_fusion
  15.8 0.6 gather_fusion.5
  16.3 0.6 gather_fusion.4
  16.9 23.5 %all-to-all-done = bf16[8,64,1280]{2,1,0:T(8,128)(2,1)S(1)} async-done(((bf16[8,64,1280]{2,1,0:T(8,128)(2,1)}), bf16[8,64,1280]{2,1,0:T(8,128)(2,1)S(1)}, u32[]{:S(2)}, u32[]{:S(2)}) %all-to-all-start) | async-done | bytes 1310752 | tf_op jit(solution)/shard_map/all_to_all | solution.py:160
  40.5 0.7 collective-permute-start.1
  41.2 0.7 collective-permute-start
  41.9 4.0 %collective-permute-start.2 = (bf16[512,256]{1,0:T(8,128)(2,1)S(1)}, bf16[512,256]{1,0:T(8,128)(2,1)}, u32[]{:S(2)}, u32[]{:S(2)}) collective-permute-start(bf16[512,256]{1,0:T(8,128)(2,1)S(1)} %get-tuple-element.250), channel_id=1, source_target_pairs={{0,1},{2,3},{4,5},{6,7},{8,9},{10,11},{12,13},{14,15},{16,17},{18,... | collective-permute-start | bytes 786440 | tf_op jit(solution)/shard_map/ppermute | solution.py:164
  45.9 0.1 broadcast_in_dim.46
  46.0 0.1 broadcast_in_dim.47
  46.9 2.5 %collective-permute-done.2 = bf16[512,256]{1,0:T(8,128)(2,1)} collective-permute-done((bf16[512,256]{1,0:T(8,128)(2,1)S(1)}, bf16[512,256]{1,0:T(8,128)(2,1)}, u32[]{:S(2)}, u32[]{:S(2)}) %collective-permute-start.2) | collective-permute-done | bytes 262176 | tf_op jit(solution)/shard_map/ppermute | solution.py:164
  49.4 1.1 pad_maximum_fusion.4
  50.5 11.4 %conditional.3 = ((bf16[512,1280]{1,0:T(8,128)(2,1)}, f32[4,512,256]{2,1,0:T(8,128)})) conditional(s32[]{:T(128)} %clamp.6, (bf16[4,512,256]{2,1,0:T(8,128)(2,1)S(1)}, s32[4,1]{0,1:T(1,128)S(1)}, s32[4]{0:T(128)S(1)}, s32[512,256]{1,0:T(8,128)S(1)}, s32[2,2048]{1,0:T(2,128)S(1)}, ...), branch_computations={%region_17.18_spmd.clone, %region_18.19_spmd.clone, %region_19.20_... | conditional | flops 1024 | bytes 2101288 | solution.py:235
  50.6 1.6 %gather_fusion = bf16[4,512,256]{2,1,0:T(8,128)(2,1)} fusion(bf16[4,512,256]{2,1,0:T(8,128)(2,1)S(1)} %get-tuple-element.198, s32[1024]{0:T(1024)S(1)} %pad_clamp_fusion), kind=kCustom, calls=%fused_computation | custom fusion | bytes 2097168 | tf_op jit(solution)/shard_map/gather | solution.py:216
  52.2 9.8 %branch_0_fun.2 = (bf16[512,1280]{1,0:T(8,128)(2,1)}, f32[4,512,256]{2,1,0:T(8,128)}) custom-call(s32[4]{0:T(128)S(1)} %get-tuple-element.194.order_ref, s32[512,256]{1,0:T(8,128)S(1)} %get-tuple-element.195.qmeta_ref, s32[2,2048]{1,0:T(2,128)S(1)} %get-tuple-element.196.kmeta_ref, bf16[512,1280]{1,0:T(8,128)(2,1)S(1)} %get-tuple-element.197.q_ref.g_ref, ...), custom_call_target="tpu_custom_call" | custom-call | tf_op jit(solution)/shard_map/cond/branch_0_fun/pallas_call | solution.py:111
  62.0 1.4 %fusion.7 = (bf16[512,256]{1,0:T(8,128)(2,1)S(1)}, bf16[512,256]{1,0:T(8,128)(2,1)S(1)}, bf16[512,256]{1,0:T(8,128)(2,1)S(1)}) fusion(f32[4,512,256]{2,1,0:T(8,128)} %get-tuple-element.193, pred[]{:T(512)S(6)} %eq.51), kind=kLoop, calls=%fused_computation.43 | loop fusion | flops 262144 | bytes 1572865 | tf_op jit(solution)/shard_map/convert_element_type | solution.py:246
  63.4 1.3 %collective-permute-start.3 = (bf16[512,256]{1,0:T(8,128)(2,1)S(1)}, bf16[512,256]{1,0:T(8,128)(2,1)S(1)}, u32[]{:S(2)}, u32[]{:S(2)}) collective-permute-start(bf16[512,256]{1,0:T(8,128)(2,1)S(1)} %get-tuple-element.243), channel_id=1, source_target_pairs={{1,0},{3,2},{5,4},{7,6},{9,8},{11,10},{13,12},{15,14},{17,16},{19,... | collective-permute-start | bytes 786440 | tf_op jit(solution)/shard_map/ppermute | solution.py:246
  64.7 0.7 collective-permute-start.4
  65.4 0.7 collective-permute-start.5
  66.1 4.7 %collective-permute-done.3 = bf16[512,256]{1,0:T(8,128)(2,1)S(1)} collective-permute-done((bf16[512,256]{1,0:T(8,128)(2,1)S(1)}, bf16[512,256]{1,0:T(8,128)(2,1)S(1)}, u32[]{:S(2)}, u32[]{:S(2)}) %collective-permute-start.3) | collective-permute-done | bytes 262176 | tf_op jit(solution)/shard_map/ppermute | solution.py:246
  70.8 1.9 %fusion.6 = bf16[512,1280]{1,0:T(8,128)(2,1)} fusion(bf16[512,1280]{1,0:T(8,128)(2,1)} %get-tuple-element.192, bf16[512,256]{1,0:T(8,128)(2,1)S(1)} %collective-permute-done.5, bf16[512,256]{1,0:T(8,128)(2,1)S(1)} %collective-permute-done.4, bf16[512,256]{1,0:T(8,128)(2,1)S(1)} %collective-permute-done.3, f32[4,512,256]{2,1,0:T(8,128)} %get-tuple-element.193), kind=kLoop, calls=%fused_computation.42 | loop fusion | flops 917504 | bytes 1572864 | tf_op jit(solution)/shard_map/scatter | solution.py:260
  72.7 15.4 %all-to-all-start.1 = ((bf16[8,64,1280]{2,1,0:T(8,128)(2,1)}), bf16[8,64,1280]{2,1,0:T(8,128)(2,1)S(1)}, u32[]{:S(2)}, u32[]{:S(2)}) async-start(bf16[8,64,1280]{2,1,0:T(8,128)(2,1)} %bitcast.23), calls=%async_computation.1 | async-start | bytes 2621440 | tf_op jit(solution)/shard_map/all_to_all | solution.py:264
  88.1 31.0 %all-to-all-done.1 = bf16[8,64,1280]{2,1,0:T(8,128)(2,1)S(1)} async-done(((bf16[8,64,1280]{2,1,0:T(8,128)(2,1)}), bf16[8,64,1280]{2,1,0:T(8,128)(2,1)S(1)}, u32[]{:S(2)}, u32[]{:S(2)}) %all-to-all-start.1) | async-done | bytes 1310752 | tf_op jit(solution)/shard_map/all_to_all | solution.py:264
  119.1 0.5 fusion
  119.6 0.8 slice_bitcast_fusion.2
  120.3 1.1 slice_bitcast_fusion
  (33 shorter events, 0.4 us)
Async XLA Ops:
  0.7 1.2 copy-start
  0.7 1.2 %copy-start.3 = (bf16[8,64,128]{2,1,0:T(8,128)(2,1)S(1)}, bf16[8,64,128]{2,1,0:T(8,128)(2,1)}, u32[]{:S(2)}) copy-start(bf16[8,64,128]{2,1,0:T(8,128)(2,1)} %get-tuple-element.144) | copy-start | bytes 393220 | tf_op jit(solution)/shard_map/cond
  0.7 1.3 %copy-start.6 = (bf16[8,64,128]{2,1,0:T(8,128)(2,1)S(1)}, bf16[8,64,128]{2,1,0:T(8,128)(2,1)}, u32[]{:S(2)}) copy-start(bf16[8,64,128]{2,1,0:T(8,128)(2,1)} %get-tuple-element.145) | copy-start | bytes 393220 | tf_op jit(solution)/shard_map/cond
  3.3 7.1 %copy-start.9 = (s32[4,8,4]{1,2,0:T(4,128)S(1)}, s32[4,8,4]{1,2,0:T(4,128)}, u32[]{:S(2)}) copy-start(s32[4,8,4]{1,2,0:T(4,128)} %param.19) | copy-start | bytes 1540
  3.3 37.2 %all-to-all-start = ((bf16[8,64,1280]{2,1,0:T(8,128)(2,1)}), bf16[8,64,1280]{2,1,0:T(8,128)(2,1)S(1)}, u32[]{:S(2)}, u32[]{:S(2)}) async-start(bf16[8,64,1280]{2,1,0:T(8,128)(2,1)} %get-tuple-element.271), calls=%async_computation | async-start | bytes 2621440 | tf_op jit(solution)/shard_map/all_to_all | solution.py:160
  40.5 6.3 %collective-permute-start.1 = (bf16[512,256]{1,0:T(8,128)(2,1)S(1)}, bf16[512,256]{1,0:T(8,128)(2,1)S(1)}, u32[]{:S(2)}, u32[]{:S(2)}) collective-permute-start(bf16[512,256]{1,0:T(8,128)(2,1)S(1)} %get-tuple-element.250), channel_id=1, source_target_pairs={{6,15},{7,14},{12,21},{13,20},{18,27},{19,26}} | collective-permute-start | bytes 786440 | tf_op jit(solution)/shard_map/ppermute | solution.py:174
  41.2 5.7 %collective-permute-start = (bf16[512,256]{1,0:T(8,128)(2,1)S(1)}, bf16[512,256]{1,0:T(8,128)(2,1)S(1)}, u32[]{:S(2)}, u32[]{:S(2)}) collective-permute-start(bf16[512,256]{1,0:T(8,128)(2,1)S(1)} %get-tuple-element.250), channel_id=1, source_target_pairs={{6,14},{7,15},{12,20},{13,21},{18,26},{19,27}} | collective-permute-start | bytes 786440 | tf_op jit(solution)/shard_map/ppermute | solution.py:173
  41.9 7.5 %collective-permute-start.2 = (bf16[512,256]{1,0:T(8,128)(2,1)S(1)}, bf16[512,256]{1,0:T(8,128)(2,1)}, u32[]{:S(2)}, u32[]{:S(2)}) collective-permute-start(bf16[512,256]{1,0:T(8,128)(2,1)S(1)} %get-tuple-element.250), channel_id=1, source_target_pairs={{0,1},{2,3},{4,5},{6,7},{8,9},{10,11},{12,13},{14,15},{16,17},{18,... | collective-permute-start | bytes 786440 | tf_op jit(solution)/shard_map/ppermute | solution.py:164
  63.4 7.3 %collective-permute-start.3 = (bf16[512,256]{1,0:T(8,128)(2,1)S(1)}, bf16[512,256]{1,0:T(8,128)(2,1)S(1)}, u32[]{:S(2)}, u32[]{:S(2)}) collective-permute-start(bf16[512,256]{1,0:T(8,128)(2,1)S(1)} %get-tuple-element.243), channel_id=1, source_target_pairs={{1,0},{3,2},{5,4},{7,6},{9,8},{11,10},{13,12},{15,14},{17,16},{19,... | collective-permute-start | bytes 786440 | tf_op jit(solution)/shard_map/ppermute | solution.py:246
  64.7 6.0 %collective-permute-start.4 = (bf16[512,256]{1,0:T(8,128)(2,1)S(1)}, bf16[512,256]{1,0:T(8,128)(2,1)S(1)}, u32[]{:S(2)}, u32[]{:S(2)}) collective-permute-start(bf16[512,256]{1,0:T(8,128)(2,1)S(1)} %get-tuple-element.244), channel_id=1, source_target_pairs={{14,6},{15,7},{20,12},{21,13},{26,18},{27,19}} | collective-permute-start | bytes 786440 | tf_op jit(solution)/shard_map/ppermute | solution.py:251
  65.4 5.4 %collective-permute-start.5 = (bf16[512,256]{1,0:T(8,128)(2,1)S(1)}, bf16[512,256]{1,0:T(8,128)(2,1)S(1)}, u32[]{:S(2)}, u32[]{:S(2)}) collective-permute-start(bf16[512,256]{1,0:T(8,128)(2,1)S(1)} %get-tuple-element.245), channel_id=1, source_target_pairs={{15,6},{14,7},{21,12},{20,13},{27,18},{26,19}} | collective-permute-start | bytes 786440 | tf_op jit(solution)/shard_map/ppermute | solution.py:252
  72.7 46.4 %all-to-all-start.1 = ((bf16[8,64,1280]{2,1,0:T(8,128)(2,1)}), bf16[8,64,1280]{2,1,0:T(8,128)(2,1)S(1)}, u32[]{:S(2)}, u32[]{:S(2)}) async-start(bf16[8,64,1280]{2,1,0:T(8,128)(2,1)} %bitcast.23), calls=%async_computation.1 | async-start | bytes 2621440 | tf_op jit(solution)/shard_map/all_to_all | solution.py:264

commit v17 on v15

--- a/solution.py
+++ b/solution.py
@@ -89,7 +89,7 @@
     slot_len = ctx_all.shape[0] // n_slots
     head_dim = ctx_all.shape[1] // 2
     width_q = n_heads * head_dim
-    block_q = min(256, n_rows)
+    block_q = min(128, n_rows)
     grid = (n_rows // block_q,)
     q_spec = pl.BlockSpec((block_q, width_q), lambda i, o: (i, 0))
     g_spec = pl.BlockSpec((block_q, width_q), lambda i, o: (i, 1))

time: 123 us -> 129 us (1.049); the launches traced: 121 us -> 128 us
  Pallas kernels: 8.82 us -> 14 us
  starting transfers between devices: 29.2 us -> 31.4 us
    pallas_call x1, Pallas kernels: 8.82 us -> 14 us  [attend(): pl.pallas_call(kernel, grid_spec=pltpu.PrefetchScalarGridSpec(num_scalar_...]
    all_to_all x1, starting transfers between devices: 15.4 us -> 17.6 us  [shards(): lax.all_to_all(result, 'inner', 0, 0, tiled=True)]
where the time goes in v17:
time: 129 us; the launch traced here: 128 us
  waiting for transfers between devices  62.3 us (48%)
  starting transfers between devices  31.4 us (24%)
  Pallas kernels  14 us (11%)
  other arithmetic  12.3 us (10%)
  local copies, waits for them, and re-layouts  6.76 us (5%)
  between operations  1.51 us (1%)
    all_to_all x1, waiting for transfers between devices, shards(): lax.all_to_all(result, 'inner', 0, 0, tiled=True)  31 us
    all_to_all x1, waiting for transfers between devices, shards(): lax.all_to_all(packed, 'inner', 0, 0, tiled=True).reshape(tok_dev, -1)  23.5 us
    all_to_all x1, starting transfers between devices, shards(): lax.all_to_all(result, 'inner', 0, 0, tiled=True)  17.6 us
    pallas_call x1, Pallas kernels, attend(): pl.pallas_call(kernel, grid_spec=pltpu.PrefetchScalarGridSpec(num_scalar_...  14 us
    all_to_all x1, starting transfers between devices, shards(): lax.all_to_all(packed, 'inner', 0, 0, tiled=True).reshape(tok_dev, -1)  6.47 us
    ppermute x1, waiting for transfers between devices, shards(): from_partner = lax.ppermute(kv_grads[2].astype(low), 'inner', pairs_down)  4.57 us
    ppermute x1, starting transfers between devices, shards(): kv_partner = lax.ppermute(kv_own, 'inner', pairs_up)  3.3 us
    ppermute x1, waiting for transfers between devices, shards(): kv_partner = lax.ppermute(kv_own, 'inner', pairs_up)  3.2 us
  transfers between devices with their start and end apart: 8, of which 4 were waited for; matrix products, arithmetic and copies ran while one was open for 6% of the time, Pallas kernels for 0%

profile of v17, /device:TPU:1, one launch (start us, length us, event | category | flops | bytes accessed | tf_op | source)
XLA Modules:
  0.0 128.4 jit_solution(10723372465316350631)
XLA Ops:
  0.6 2.7 %conditional.2 = (bf16[8,64,1280]{2,1,0:T(8,128)(2,1)}) conditional(s32[]{:T(128)} %clamp.7, (bf16[8,64,512]{2,1,0:T(8,128)(2,1)}, bf16[8,64,512]{2,1,0:T(8,128)(2,1)}, bf16[8,64,128]{2,1,0:T(8,128)(2,1)}, bf16[8,64,128]{2,1,0:T(8,128)(2,1)}) %tuple.83, (bf16[8,64,512]{2,1,0:T(8,128)(2,1)}, ...), branch_computations={%region_13.14_spmd, %region_14.15_spmd, %region_15.16_spmd, %regio... | conditional | flops 5242880 | bytes 11010140 | solution.py:150
  0.7 1.1 constant_dynamic-update-slice_fusion.3
  1.8 0.0 copy-done
  2.0 0.1 slice.69
  2.1 1.2 pad_maximum_fusion.1
  3.3 6.5 %all-to-all-start = ((bf16[8,64,1280]{2,1,0:T(8,128)(2,1)}), bf16[8,64,1280]{2,1,0:T(8,128)(2,1)S(1)}, u32[]{:S(2)}, u32[]{:S(2)}) async-start(bf16[8,64,1280]{2,1,0:T(8,128)(2,1)} %get-tuple-element.162), calls=%async_computation | async-start | bytes 2621440 | tf_op jit(solution)/shard_map/all_to_all | solution.py:159
  9.8 0.6 iota_add_fusion
  10.5 0.1 le.67
  10.6 0.1 reshape.270
  10.6 0.1 reduce-window.21
  10.7 0.1 reduce.3
  10.8 0.1 reshape.236
  10.9 0.1 convert_reduce_fusion
  11.0 0.1 fusion.7
  11.1 0.6 fusion.12
  11.8 0.1 reduce_min.29
  11.9 0.1 fusion.11
  12.0 1.9 %fusion.8 = (s32[4,1]{0,1:T(1,128)S(1)}, pred[4]{0:T(512)(128)(4,1)S(1)}) fusion(s32[4]{0:T(128)S(1)} %reduce_min.29, s32[]{:T(128)} %get-tuple-element.147, s32[4]{0:T(128)S(1)} %get-tuple-element.124, s32[]{:T(128)} %get-tuple-element.126, s32[4]{0:T(128)S(1)} %get-tuple-element.123, s32[]{:T(128)} %get-tuple-element.125), kind=kLoop, calls=%fused_computation.61 | loop fusion | flops 32 | bytes 80 | tf_op jit(solution)/shard_map/convert_element_type | solution.py:206
  14.0 0.2 reduce-window.22
  14.2 0.2 reduce-window.23
  14.4 0.6 convert_reduce_fusion.2
  15.0 0.6 bitcast_select_fusion
  15.6 0.1 select_reduce_fusion
  15.8 0.6 gather_fusion.1
  16.3 0.6 gather_fusion
  16.9 23.5 %all-to-all-done = bf16[8,64,1280]{2,1,0:T(8,128)(2,1)S(1)} async-done(((bf16[8,64,1280]{2,1,0:T(8,128)(2,1)}), bf16[8,64,1280]{2,1,0:T(8,128)(2,1)S(1)}, u32[]{:S(2)}, u32[]{:S(2)}) %all-to-all-start) | async-done | bytes 1310752 | tf_op jit(solution)/shard_map/all_to_all | solution.py:159
  40.5 0.7 collective-permute-start.1
  41.2 0.7 collective-permute-start
  41.9 3.3 %collective-permute-start.2 = (bf16[512,256]{1,0:T(8,128)(2,1)S(1)}, bf16[512,256]{1,0:T(8,128)(2,1)S(1)}, u32[]{:S(2)}, u32[]{:S(2)}) collective-permute-start(bf16[512,256]{1,0:T(8,128)(2,1)S(1)} %get-tuple-element.139), channel_id=1, source_target_pairs={{0,1},{2,3},{4,5},{6,7},{8,9},{10,11},{12,13},{14,15},{16,17},{18,... | collective-permute-start | bytes 786440 | tf_op jit(solution)/shard_map/ppermute | solution.py:163
  45.2 0.1 broadcast_in_dim.46
  45.3 0.1 broadcast_in_dim.47
  46.2 3.2 %collective-permute-done.2 = bf16[512,256]{1,0:T(8,128)(2,1)S(1)} collective-permute-done((bf16[512,256]{1,0:T(8,128)(2,1)S(1)}, bf16[512,256]{1,0:T(8,128)(2,1)S(1)}, u32[]{:S(2)}, u32[]{:S(2)}) %collective-permute-start.2) | collective-permute-done | bytes 262176 | tf_op jit(solution)/shard_map/ppermute | solution.py:163
  49.4 1.1 pad_maximum_fusion.5
  50.6 1.8 %gather_fusion.2 = bf16[4,512,256]{2,1,0:T(8,128)(2,1)S(1)} fusion(bf16[4,512,256]{2,1,0:T(8,128)(2,1)} %pad_maximum_fusion.5, s32[1024]{0:T(1024)S(1)} %pad_clamp_fusion), kind=kCustom, calls=%fused_computation.2 | custom fusion | bytes 2097168 | tf_op jit(solution)/shard_map/gather | solution.py:215
  52.4 14.0 %conditional.3 = ((bf16[512,512]{1,0:T(8,128)(2,1)S(1)}, bf16[512,512]{1,0:T(8,128)(2,1)}, f32[4,512,256]{2,1,0:T(8,128)})) conditional(s32[]{:T(128)} %clamp.6, (s32[4]{0:T(128)S(1)}, s32[512,256]{1,0:T(8,128)S(1)}, s32[2,2048]{1,0:T(2,128)S(1)}, bf16[512,1280]{1,0:T(8,128)(2,1)S(1)}, ...), branch_computations={%region_17.18_spmd, %region_18.19_spmd, %region_19.20_spmd, %regio... | conditional | bytes 8 | solution.py:234
  52.4 14.0 %branch_0_fun.1 = (bf16[512,512]{1,0:T(8,128)(2,1)S(1)}, bf16[512,512]{1,0:T(8,128)(2,1)}, f32[4,512,256]{2,1,0:T(8,128)}) custom-call(s32[4]{0:T(128)S(1)} %get-tuple-element.93.order_ref, s32[512,256]{1,0:T(8,128)S(1)} %get-tuple-element.94.qmeta_ref, s32[2,2048]{1,0:T(2,128)S(1)} %get-tuple-element.95.kmeta_ref, ...), custom_call_target="tpu_custom_call" | custom-call | tf_op jit(solution)/shard_map/cond/branch_0_fun/pallas_call | solution.py:109
  66.4 1.5 %fusion.6 = (bf16[512,256]{1,0:T(8,128)(2,1)S(1)}, bf16[512,256]{1,0:T(8,128)(2,1)S(1)}, bf16[512,256]{1,0:T(8,128)(2,1)S(1)}) fusion(f32[4,512,256]{2,1,0:T(8,128)} %get-tuple-element.122, pred[]{:T(512)S(6)} %eq.55), kind=kLoop, calls=%fused_computation.36 | loop fusion | flops 262144 | bytes 1572865 | tf_op jit(solution)/shard_map/convert_element_type | solution.py:245
  67.9 1.3 %collective-permute-start.3 = (bf16[512,256]{1,0:T(8,128)(2,1)S(1)}, bf16[512,256]{1,0:T(8,128)(2,1)S(1)}, u32[]{:S(2)}, u32[]{:S(2)}) collective-permute-start(bf16[512,256]{1,0:T(8,128)(2,1)S(1)} %get-tuple-element.132), channel_id=1, source_target_pairs={{1,0},{3,2},{5,4},{7,6},{9,8},{11,10},{13,12},{15,14},{17,16},{19,... | collective-permute-start | bytes 786440 | tf_op jit(solution)/shard_map/ppermute | solution.py:245
  69.2 0.7 collective-permute-start.4
  69.9 0.7 collective-permute-start.5
  70.6 4.6 %collective-permute-done.3 = bf16[512,256]{1,0:T(8,128)(2,1)S(1)} collective-permute-done((bf16[512,256]{1,0:T(8,128)(2,1)S(1)}, bf16[512,256]{1,0:T(8,128)(2,1)S(1)}, u32[]{:S(2)}, u32[]{:S(2)}) %collective-permute-start.3) | collective-permute-done | bytes 262176 | tf_op jit(solution)/shard_map/ppermute | solution.py:245
  75.2 1.2 fusion.3
  76.3 1.2 pad_maximum_fusion.4
  77.5 17.6 %all-to-all-start.1 = ((bf16[8,64,1280]{2,1,0:T(8,128)(2,1)}), bf16[8,64,1280]{2,1,0:T(8,128)(2,1)S(1)}, u32[]{:S(2)}, u32[]{:S(2)}) async-start(bf16[8,64,1280]{2,1,0:T(8,128)(2,1)} %bitcast.24), calls=%async_computation.1 | async-start | bytes 2621440 | tf_op jit(solution)/shard_map/all_to_all | solution.py:263
  95.1 31.0 %all-to-all-done.1 = bf16[8,64,1280]{2,1,0:T(8,128)(2,1)S(1)} async-done(((bf16[8,64,1280]{2,1,0:T(8,128)(2,1)}), bf16[8,64,1280]{2,1,0:T(8,128)(2,1)S(1)}, u32[]{:S(2)}, u32[]{:S(2)}) %all-to-all-start.1) | async-done | bytes 1310752 | tf_op jit(solution)/shard_map/all_to_all | solution.py:263
  126.1 0.5 fusion
  126.6 0.8 slice_bitcast_fusion.2
  127.3 1.1 slice_bitcast_fusion
  (35 shorter events, 0.4 us)
Async XLA Ops:
  0.7 1.2 copy-start
  0.7 1.2 copy-start.3
  0.7 1.3 copy-start.6
  3.3 7.1 %copy-start.10 = (s32[4,8,4]{1,2,0:T(4,128)S(1)}, s32[4,8,4]{1,2,0:T(4,128)}, u32[]{:S(2)}) copy-start(s32[4,8,4]{1,2,0:T(4,128)} %param.17) | copy-start | bytes 1540
  3.3 37.2 %all-to-all-start = ((bf16[8,64,1280]{2,1,0:T(8,128)(2,1)}), bf16[8,64,1280]{2,1,0:T(8,128)(2,1)S(1)}, u32[]{:S(2)}, u32[]{:S(2)}) async-start(bf16[8,64,1280]{2,1,0:T(8,128)(2,1)} %get-tuple-element.162), calls=%async_computation | async-start | bytes 2621440 | tf_op jit(solution)/shard_map/all_to_all | solution.py:159
  40.5 5.7 %collective-permute-start.1 = (bf16[512,256]{1,0:T(8,128)(2,1)S(1)}, bf16[512,256]{1,0:T(8,128)(2,1)S(1)}, u32[]{:S(2)}, u32[]{:S(2)}) collective-permute-start(bf16[512,256]{1,0:T(8,128)(2,1)S(1)} %get-tuple-element.139), channel_id=1, source_target_pairs={{6,15},{7,14},{12,21},{13,20},{18,27},{19,26}} | collective-permute-start | bytes 786440 | tf_op jit(solution)/shard_map/ppermute | solution.py:173
  41.2 5.0 %collective-permute-start = (bf16[512,256]{1,0:T(8,128)(2,1)S(1)}, bf16[512,256]{1,0:T(8,128)(2,1)S(1)}, u32[]{:S(2)}, u32[]{:S(2)}) collective-permute-start(bf16[512,256]{1,0:T(8,128)(2,1)S(1)} %get-tuple-element.139), channel_id=1, source_target_pairs={{6,14},{7,15},{12,20},{13,21},{18,26},{19,27}} | collective-permute-start | bytes 786440 | tf_op jit(solution)/shard_map/ppermute | solution.py:172
  41.9 7.5 %collective-permute-start.2 = (bf16[512,256]{1,0:T(8,128)(2,1)S(1)}, bf16[512,256]{1,0:T(8,128)(2,1)S(1)}, u32[]{:S(2)}, u32[]{:S(2)}) collective-permute-start(bf16[512,256]{1,0:T(8,128)(2,1)S(1)} %get-tuple-element.139), channel_id=1, source_target_pairs={{0,1},{2,3},{4,5},{6,7},{8,9},{10,11},{12,13},{14,15},{16,17},{18,... | collective-permute-start | bytes 786440 | tf_op jit(solution)/shard_map/ppermute | solution.py:163
  66.4 9.9 %copy-start.9 = (bf16[512,512]{1,0:T(8,128)(2,1)S(1)}, bf16[512,512]{1,0:T(8,128)(2,1)}, u32[]{:S(2)}) copy-start(bf16[512,512]{1,0:T(8,128)(2,1)} %get-tuple-element.121) | copy-start | bytes 1572868
  67.9 7.2 %collective-permute-start.3 = (bf16[512,256]{1,0:T(8,128)(2,1)S(1)}, bf16[512,256]{1,0:T(8,128)(2,1)S(1)}, u32[]{:S(2)}, u32[]{:S(2)}) collective-permute-start(bf16[512,256]{1,0:T(8,128)(2,1)S(1)} %get-tuple-element.132), channel_id=1, source_target_pairs={{1,0},{3,2},{5,4},{7,6},{9,8},{11,10},{13,12},{15,14},{17,16},{19,... | collective-permute-start | bytes 786440 | tf_op jit(solution)/shard_map/ppermute | solution.py:245
  69.2 5.9 %collective-permute-start.4 = (bf16[512,256]{1,0:T(8,128)(2,1)S(1)}, bf16[512,256]{1,0:T(8,128)(2,1)S(1)}, u32[]{:S(2)}, u32[]{:S(2)}) collective-permute-start(bf16[512,256]{1,0:T(8,128)(2,1)S(1)} %get-tuple-element.133), channel_id=1, source_target_pairs={{14,6},{15,7},{20,12},{21,13},{26,18},{27,19}} | collective-permute-start | bytes 786440 | tf_op jit(solution)/shard_map/ppermute | solution.py:250
  69.9 5.3 %collective-permute-start.5 = (bf16[512,256]{1,0:T(8,128)(2,1)S(1)}, bf16[512,256]{1,0:T(8,128)(2,1)S(1)}, u32[]{:S(2)}, u32[]{:S(2)}) collective-permute-start(bf16[512,256]{1,0:T(8,128)(2,1)S(1)} %get-tuple-element.134), channel_id=1, source_target_pairs={{15,6},{14,7},{21,12},{20,13},{27,18},{26,19}} | collective-permute-start | bytes 786440 | tf_op jit(solution)/shard_map/ppermute | solution.py:251
  77.5 48.6 %all-to-all-start.1 = ((bf16[8,64,1280]{2,1,0:T(8,128)(2,1)}), bf16[8,64,1280]{2,1,0:T(8,128)(2,1)S(1)}, u32[]{:S(2)}, u32[]{:S(2)}) async-start(bf16[8,64,1280]{2,1,0:T(8,128)(2,1)} %bitcast.24), calls=%async_computation.1 | async-start | bytes 2621440 | tf_op jit(solution)/shard_map/all_to_all | solution.py:263
